TPU v7x, 512 devices: a whole 4x4x16 slice. The times are simulated.
512 devices in a mesh: band: 32 (over x, z_lo), grid: 16 (over z_hi, y, core).
Axes of the slice: x: 4, y: 4, z: 16 (z_hi: 2, z_lo: 8; z = z_hi * 8 + z_lo), core: 2. Of those that a mesh axis runs over, the one named last changes fastest.
Arguments:
- trial_bands: float32 [64, 160, 32, 128], P('band', 'grid'), may hold values from -6 to 6
- potential: float32 [160, 32, 128], P('grid'), may hold values from -2 to 0
Outputs:
- filtered: float32 [64, 160, 32, 128], P('band', 'grid')
- projected: float32 [64, 64], P('band')
- residual_norms: float32 [64], P('band')
All inputs are finite; a program needn't handle non-finite values.
Results may differ from a plain program's by a relative error of at most 0.00016.
Values sent between devices are 32-bit elements; how exact they have to be, the bound alone decides.
No kernel may reach another device: no remote copies, remote signals or barrier semaphores. Data moves between devices by JAX's collectives and lax.ppermute only.
A program may use at most 64 MiB of HBM per device.

v0:
```python
import jax
import jax.numpy as jnp
from jax import lax
from jax.sharding import PartitionSpec as P

CENTER = 4.25
HALF_WIDTH = 3.75
LOWEST = -2.0
SIGMA_ONE = HALF_WIDTH / (LOWEST - CENTER)
FOUR_THIRDS = 4.0 / 3.0
TWELFTH = 1.0 / 12.0
filter_degree = 4


def padded_2(cells, sides, width):
    for axis, dim in sides:
        count = lax.axis_size(axis)
        head = lax.slice_in_dim(cells, 0, width, axis=dim)
        tail = lax.slice_in_dim(cells, cells.shape[dim] - width, cells.shape[dim], axis=dim)
        cells = jnp.concatenate(
            [
                lax.ppermute(tail, axis, [(i, (i + 1) % count) for i in range(count)]),
                cells,
                lax.ppermute(head, axis, [((i + 1) % count, i) for i in range(count)]),
            ],
            axis=dim,
        )
    return cells


def operate(field_in, potential):
    padded = padded_2(field_in, (("grid", 1),), 2)
    plane_count = field_in.shape[1]
    near_sum = padded[:, 1 : 1 + plane_count] + padded[:, 3 : 3 + plane_count]
    near_sum = near_sum + jnp.roll(field_in, 1, 2) + jnp.roll(field_in, -1, 2)
    near_sum = near_sum + jnp.roll(field_in, 1, 3) + jnp.roll(field_in, -1, 3)
    far_sum = padded[:, 0:plane_count] + padded[:, 4 : 4 + plane_count]
    far_sum = far_sum + jnp.roll(field_in, 2, 2) + jnp.roll(field_in, -2, 2)
    far_sum = far_sum + jnp.roll(field_in, 2, 3) + jnp.roll(field_in, -2, 3)
    kinetic = 0.5 * (7.5 * field_in - FOUR_THIRDS * near_sum + TWELFTH * far_sum)
    return kinetic + potential * field_in


def on_device(trial_bands, potential):
    sigma_now = SIGMA_ONE
    previous = trial_bands
    current = (operate(trial_bands, potential) - CENTER * trial_bands) * (SIGMA_ONE / HALF_WIDTH)
    for repeat_index in range(filter_degree - 1):
        sigma_next = 1.0 / (2.0 / SIGMA_ONE - sigma_now)
        following = (operate(current, potential) - CENTER * current) * (
            2.0 * sigma_next / HALF_WIDTH
        ) - sigma_now * sigma_next * previous
        previous, current, sigma_now = (current, following, sigma_next)
    applied = operate(current, potential)
    band_count = current.shape[0]
    flat_bands = current.reshape(band_count, -1)
    flat_image = applied.reshape(band_count, -1)
    cell_total = flat_bands.shape[1] * lax.axis_size("grid")
    inverse_cells = 1.0 / cell_total
    first_band = lax.axis_index("band") * band_count
    local_norms = jnp.sum(flat_image * flat_image, axis=1)
    panel_piece = lax.all_gather(current, "band", axis=0, tiled=True)
    flat_piece = panel_piece.reshape(panel_piece.shape[0], -1)
    margin_part = jnp.dot(
        flat_bands,
        flat_piece.T,
        precision=lax.Precision.HIGHEST,
        preferred_element_type=jnp.float32,
    )
    image_part = jnp.dot(
        flat_image,
        flat_piece.T,
        precision=lax.Precision.HIGHEST,
        preferred_element_type=jnp.float32,
    )
    margin_rows = margin_part
    image_rows = image_part
    margin_rows, image_rows, norm_rows = lax.psum((margin_rows, image_rows, local_norms), "grid")
    margin, subspace, image_norms = (
        lax.all_gather(margin_rows, "band", axis=0, tiled=True),
        lax.all_gather(image_rows, "band", axis=0, tiled=True),
        lax.all_gather(norm_rows, "band", axis=0, tiled=True),
    )
    margin = margin * inverse_cells
    subspace = subspace * inverse_cells
    image_norms = image_norms * inverse_cells
    factor = jnp.linalg.cholesky(margin)
    coefficients = lax.linalg.triangular_solve(factor, subspace.T, left_side=True, lower=True)
    projected = lax.linalg.triangular_solve(factor, coefficients.T, left_side=True, lower=True)
    residual_norms = image_norms - jnp.sum(coefficients * coefficients, axis=0)
    projected_rows = lax.dynamic_slice_in_dim(projected, first_band, band_count, 0)
    residual_rows = lax.dynamic_slice_in_dim(residual_norms, first_band, band_count, 0)
    return (current, projected_rows, residual_rows)


def solution(mesh):
    in_specs = (P("band", "grid", None, None), P("grid", None, None))
    out_specs = (P("band", "grid", None, None), P("band", None), P("band"))
    return jax.shard_map(
        on_device, mesh=mesh, in_specs=in_specs, out_specs=out_specs, check_vma=False
    )
```

profile of v0, /device:TPU:24, one launch (start us, length us, event | category | flops | bytes accessed | tf_op | source)
XLA Modules:
  0.0 821.3 jit_solution(4509007590177282399)
XLA Ops:
  8.1 1.9 collective-permute-start
  10.0 3.6 collective-permute-start.1
  13.7 1.2 fusion.160
  14.9 1.2 fusion.161
  18.3 1.3 fusion.155
  19.6 1.2 fusion.156
  24.9 1.3 collective-permute-done.1
  26.3 1.7 broadcast_multiply_fusion
  28.8 1.9 collective-permute-start.3
  30.7 16.1 %collective-permute-start.2 = (f32[2,2,32,128]{3,2,1,0:T(8,128)S(1)}, f32[2,2,32,128]{3,2,1,0:T(8,128)S(1)}, u32[]{:S(2)}, u32[]{:S(2)}) collective-permute-start(f32[2,2,32,128]{3,2,1,0:T(8,128)S(1)} %get-tuple-element.87), channel_id=1, source_target_pairs={{0,1},{1,2},{2,3},{3,4},{4,5},{5,6},{6,7},{7,8},{8,9},{9,10},{10,1... | collective-permute-start | bytes 196616 | tf_op jit(solution)/shard_map/ppermute | solution.py:22
  49.2 1.9 collective-permute-start.5
  51.1 15.2 %collective-permute-start.4 = (f32[2,2,32,128]{3,2,1,0:T(8,128)S(1)}, f32[2,2,32,128]{3,2,1,0:T(8,128)S(1)}, u32[]{:S(2)}, u32[]{:S(2)}) collective-permute-start(f32[2,2,32,128]{3,2,1,0:T(8,128)S(1)} %get-tuple-element.69), channel_id=1, source_target_pairs={{0,1},{1,2},{2,3},{3,4},{4,5},{5,6},{6,7},{7,8},{8,9},{9,10},{10,1... | collective-permute-start | bytes 196616 | tf_op jit(solution)/shard_map/ppermute | solution.py:22
  68.7 1.9 collective-permute-start.7
  70.7 15.7 %collective-permute-start.6 = (f32[2,2,32,128]{3,2,1,0:T(8,128)S(1)}, f32[2,2,32,128]{3,2,1,0:T(8,128)S(1)}, u32[]{:S(2)}, u32[]{:S(2)}) collective-permute-start(f32[2,2,32,128]{3,2,1,0:T(8,128)S(1)} %get-tuple-element.51), channel_id=1, source_target_pairs={{0,1},{1,2},{2,3},{3,4},{4,5},{5,6},{6,7},{7,8},{8,9},{9,10},{10,1... | collective-permute-start | bytes 196616 | tf_op jit(solution)/shard_map/ppermute | solution.py:22
  87.3 1.4 fusion.35
  88.7 1.3 dynamic-slice
  91.5 1.9 collective-permute-start.9
  93.5 15.7 %collective-permute-start.8 = (f32[2,2,32,128]{3,2,1,0:T(8,128)S(1)}, f32[2,2,32,128]{3,2,1,0:T(8,128)S(1)}, u32[]{:S(2)}, u32[]{:S(2)}) collective-permute-start(f32[2,2,32,128]{3,2,1,0:T(8,128)S(1)} %get-tuple-element.25), channel_id=1, source_target_pairs={{0,1},{1,2},{2,3},{3,4},{4,5},{5,6},{6,7},{7,8},{8,9},{9,10},{10,1... | collective-permute-start | bytes 196616 | tf_op jit(solution)/shard_map/ppermute | solution.py:22
  110.1 1.2 fusion.124
  111.4 1.2 fusion.125
  113.7 1.2 fusion.119
  115.0 1.2 fusion.120
  118.3 2.4 multiply_reduce_fusion
  120.7 252.5 %all-gather.4.cloned.1.call-done = f32[64,10,32,128]{3,2,1,0:T(8,128)} async-done(((f32[2,10,32,128]{3,2,1,0:T(8,128)}), f32[64,10,32,128]{3,2,1,0:T(8,128)}) %all-gather.4.cloned.1.call-update) | async-done | bytes 10485776 | tf_op jit(solution)/shard_map/all_gather | solution.py:62
  373.2 17.0 %fusion.4 = f32[2,64]{1,0:T(2,128)S(1)} fusion(f32[64,10,32,128]{3,2,1,0:T(8,128)} %all-gather.4.cloned.1.call-done, f32[2,10,32,128]{3,2,1,0:T(8,128)S(1)} %copy-done), kind=kOutput, calls=%fused_computation.4 | convolution fusion | flops 62914560 | bytes 10813952 | tf_op jit(solution)/shard_map/dot_general | solution.py:64
  390.2 12.8 %fusion.7 = f32[2,64]{1,0:T(2,128)S(1)} fusion(f32[64,10,32,128]{3,2,1,0:T(8,128)S(1)} %copy-done.2, f32[2,10,32,128]{3,2,1,0:T(8,128)S(1)} %get-tuple-element.14), kind=kOutput, calls=%fused_computation.5 | convolution fusion | flops 62914560 | bytes 10813952 | tf_op jit(solution)/shard_map/dot_general | solution.py:70
  403.0 54.6 %all-reduce.1 = (f32[2,64]{1,0:T(2,128)S(1)}, f32[2,64]{1,0:T(2,128)S(1)}, f32[2]{0:T(128)S(1)}) all-reduce(f32[2,64]{1,0:T(2,128)S(1)} %fusion.7, f32[2,64]{1,0:T(2,128)S(1)} %fusion.4, f32[2]{0:T(128)S(1)} %get-tuple-element.13), channel_id=1, replica_groups=mesh['band'=32,'grid'=16] {'grid'}, use_global_device_ids=true, to_apply=%region_3.4 | all-reduce | flops 258 | bytes 2064 | tf_op jit(solution)/shard_map/psum | solution.py:78
  457.6 116.2 %all-gather.1 = f32[32,2,64]{2,1,0:T(2,128)S(1)} all-gather(f32[1,2,64]{2,1,0:T(2,128)S(1)} %bitcast.38), channel_id=1, replica_groups=mesh['band'=32,'grid'=16] {'band'}, dimensions={0}, use_global_device_ids=true | all-gather | bytes 16896 | tf_op jit(solution)/shard_map/all_gather | solution.py:81
  573.9 111.3 %all-gather = f32[32,2,64]{2,1,0:T(2,128)S(1)} all-gather(f32[1,2,64]{2,1,0:T(2,128)S(1)} %bitcast.37), channel_id=1, replica_groups=mesh['band'=32,'grid'=16] {'band'}, dimensions={0}, use_global_device_ids=true | all-gather | bytes 16896 | tf_op jit(solution)/shard_map/all_gather | solution.py:80
  685.3 5.8 cholesky.18
  692.5 4.9 custom-call.8
  698.2 115.1 %all-reduce = f32[64]{0:T(128)S(1)} all-reduce(f32[64]{0:T(128)S(1)} %dynamic-update-slice.3), channel_id=1, replica_groups=mesh['band'=32,'grid'=16] {'band'}, use_global_device_ids=true, to_apply=%add | all-reduce | flops 64 | bytes 512
  (76 shorter events, 21.9 us)
Async XLA Ops:
  7.2 366.0 %all-gather.4.cloned.1.call-start = ((), (), s32[]{:S(2)}) async-start(), calls=%async_computation | async-start | bytes 10813440 | tf_op jit(solution)/shard_map/all_gather | solution.py:62
  8.1 15.7 %collective-permute-start = (f32[2,2,32,128]{3,2,1,0:T(8,128)S(1)}, f32[2,2,32,128]{3,2,1,0:T(8,128)S(1)}, u32[]{:S(2)}, u32[]{:S(2)}) collective-permute-start(f32[2,2,32,128]{3,2,1,0:T(8,128)S(1)} %get-tuple-element.99), channel_id=1, source_target_pairs={{0,1},{1,2},{2,3},{3,4},{4,5},{5,6},{6,7},{7,8},{8,9},{9,10},{10,1... | collective-permute-start | bytes 196616 | tf_op jit(solution)/shard_map/ppermute | solution.py:22
  10.0 16.2 %collective-permute-start.1 = (f32[2,2,32,128]{3,2,1,0:T(8,128)S(1)}, f32[2,2,32,128]{3,2,1,0:T(8,128)S(1)}, u32[]{:S(2)}, u32[]{:S(2)}) collective-permute-start(f32[2,2,32,128]{3,2,1,0:T(8,128)S(1)} %get-tuple-element.100), channel_id=1, source_target_pairs={{1,0},{2,1},{3,2},{4,3},{5,4},{6,5},{7,6},{8,7},{9,8},{10,9},{11,1... | collective-permute-start | bytes 196616 | tf_op jit(solution)/shard_map/ppermute | solution.py:24
  18.3 29.4 %copy-start.1 = (f32[2,10,32,128]{3,2,1,0:T(8,128)S(1)}, f32[2,10,32,128]{3,2,1,0:T(8,128)}, u32[]{:S(2)}) copy-start(f32[2,10,32,128]{3,2,1,0:T(8,128)} %param.4) | copy-start | bytes 983044
  28.0 39.2 %copy-start.3 = (f32[10,32,128]{2,1,0:T(8,128)S(1)}, f32[10,32,128]{2,1,0:T(8,128)}, u32[]{:S(2)}) copy-start(f32[10,32,128]{2,1,0:T(8,128)} %param.5) | copy-start | bytes 491524
  28.8 18.0 %collective-permute-start.3 = (f32[2,2,32,128]{3,2,1,0:T(8,128)S(1)}, f32[2,2,32,128]{3,2,1,0:T(8,128)S(1)}, u32[]{:S(2)}, u32[]{:S(2)}) collective-permute-start(f32[2,2,32,128]{3,2,1,0:T(8,128)S(1)} %get-tuple-element.88), channel_id=1, source_target_pairs={{1,0},{2,1},{3,2},{4,3},{5,4},{6,5},{7,6},{8,7},{9,8},{10,9},{11,1... | collective-permute-start | bytes 196616 | tf_op jit(solution)/shard_map/ppermute | solution.py:24
  30.7 16.9 %collective-permute-start.2 = (f32[2,2,32,128]{3,2,1,0:T(8,128)S(1)}, f32[2,2,32,128]{3,2,1,0:T(8,128)S(1)}, u32[]{:S(2)}, u32[]{:S(2)}) collective-permute-start(f32[2,2,32,128]{3,2,1,0:T(8,128)S(1)} %get-tuple-element.87), channel_id=1, source_target_pairs={{0,1},{1,2},{2,3},{3,4},{4,5},{5,6},{6,7},{7,8},{8,9},{9,10},{10,1... | collective-permute-start | bytes 196616 | tf_op jit(solution)/shard_map/ppermute | solution.py:22
  49.2 17.2 %collective-permute-start.5 = (f32[2,2,32,128]{3,2,1,0:T(8,128)S(1)}, f32[2,2,32,128]{3,2,1,0:T(8,128)S(1)}, u32[]{:S(2)}, u32[]{:S(2)}) collective-permute-start(f32[2,2,32,128]{3,2,1,0:T(8,128)S(1)} %get-tuple-element.70), channel_id=1, source_target_pairs={{1,0},{2,1},{3,2},{4,3},{5,4},{6,5},{7,6},{8,7},{9,8},{10,9},{11,1... | collective-permute-start | bytes 196616 | tf_op jit(solution)/shard_map/ppermute | solution.py:24
  51.1 16.1 %collective-permute-start.4 = (f32[2,2,32,128]{3,2,1,0:T(8,128)S(1)}, f32[2,2,32,128]{3,2,1,0:T(8,128)S(1)}, u32[]{:S(2)}, u32[]{:S(2)}) collective-permute-start(f32[2,2,32,128]{3,2,1,0:T(8,128)S(1)} %get-tuple-element.69), channel_id=1, source_target_pairs={{0,1},{1,2},{2,3},{3,4},{4,5},{5,6},{6,7},{7,8},{8,9},{9,10},{10,1... | collective-permute-start | bytes 196616 | tf_op jit(solution)/shard_map/ppermute | solution.py:22
  68.7 17.7 %collective-permute-start.7 = (f32[2,2,32,128]{3,2,1,0:T(8,128)S(1)}, f32[2,2,32,128]{3,2,1,0:T(8,128)S(1)}, u32[]{:S(2)}, u32[]{:S(2)}) collective-permute-start(f32[2,2,32,128]{3,2,1,0:T(8,128)S(1)} %get-tuple-element.52), channel_id=1, source_target_pairs={{1,0},{2,1},{3,2},{4,3},{5,4},{6,5},{7,6},{8,7},{9,8},{10,9},{11,1... | collective-permute-start | bytes 196616 | tf_op jit(solution)/shard_map/ppermute | solution.py:24
  70.7 16.6 %collective-permute-start.6 = (f32[2,2,32,128]{3,2,1,0:T(8,128)S(1)}, f32[2,2,32,128]{3,2,1,0:T(8,128)S(1)}, u32[]{:S(2)}, u32[]{:S(2)}) collective-permute-start(f32[2,2,32,128]{3,2,1,0:T(8,128)S(1)} %get-tuple-element.51), channel_id=1, source_target_pairs={{0,1},{1,2},{2,3},{3,4},{4,5},{5,6},{6,7},{7,8},{8,9},{9,10},{10,1... | collective-permute-start | bytes 196616 | tf_op jit(solution)/shard_map/ppermute | solution.py:22
  88.7 284.5 %copy-start = (f32[2,10,32,128]{3,2,1,0:T(8,128)S(1)}, f32[2,10,32,128]{3,2,1,0:T(8,128)}, u32[]{:S(2)}) copy-start(f32[2,10,32,128]{3,2,1,0:T(8,128)} %fusion.35) | copy-start | bytes 983044
  91.5 26.7 %collective-permute-start.9 = (f32[2,2,32,128]{3,2,1,0:T(8,128)S(1)}, f32[2,2,32,128]{3,2,1,0:T(8,128)S(1)}, u32[]{:S(2)}, u32[]{:S(2)}) collective-permute-start(f32[2,2,32,128]{3,2,1,0:T(8,128)S(1)} %get-tuple-element.26), channel_id=1, source_target_pairs={{1,0},{2,1},{3,2},{4,3},{5,4},{6,5},{7,6},{8,7},{9,8},{10,9},{11,1... | collective-permute-start | bytes 196616 | tf_op jit(solution)/shard_map/ppermute | solution.py:24
  93.5 24.8 %collective-permute-start.8 = (f32[2,2,32,128]{3,2,1,0:T(8,128)S(1)}, f32[2,2,32,128]{3,2,1,0:T(8,128)S(1)}, u32[]{:S(2)}, u32[]{:S(2)}) collective-permute-start(f32[2,2,32,128]{3,2,1,0:T(8,128)S(1)} %get-tuple-element.25), channel_id=1, source_target_pairs={{0,1},{1,2},{2,3},{3,4},{4,5},{5,6},{6,7},{7,8},{8,9},{9,10},{10,1... | collective-permute-start | bytes 196616 | tf_op jit(solution)/shard_map/ppermute | solution.py:22
  373.2 17.0 %copy-start.2 = (f32[64,10,32,128]{3,2,1,0:T(8,128)S(1)}, f32[64,10,32,128]{3,2,1,0:T(8,128)}, u32[]{:S(2)}) copy-start(f32[64,10,32,128]{3,2,1,0:T(8,128)} %all-gather.4.cloned.1.call-done) | copy-start | bytes 31457284
Sparse Core Ops, SparseCore 0:
  88.8 284.3 all-gather.3
where the time goes:
time: 829 us; the launch traced here: 821 us
  blocking collectives  397 us (48%)
  waiting for transfers between devices  256 us (31%)
  starting transfers between devices  76 us (9%)
  matrix products  30.4 us (4%)
  local copies, waits for them, and re-layouts  26.3 us (3%)
  other arithmetic  19.9 us (2%)
  between operations  15.1 us (2%)
    all_gather x1, waiting for transfers between devices, on_device(): panel_piece = lax.all_gather(current, 'band', axis=0, tiled=True)  252 us
    all_gather x1, blocking collectives, on_device(): lax.all_gather(image_rows, 'band', axis=0, tiled=True)  116 us
    unnamed x1, blocking collectives  115 us
    all_gather x1, blocking collectives, on_device(): lax.all_gather(margin_rows, 'band', axis=0, tiled=True)  111 us
    ppermute x5, starting transfers between devices, padded_2(): lax.ppermute(tail, axis, [(i, (i + 1) % count) for i in range(count)])  64.7 us
    psum x1, blocking collectives, on_device(): lax.psum((margin_rows, image_rows, local_norms), 'grid')  54.6 us
    dot_general x1, matrix products, on_device(): jnp.dot(flat_bands, flat_piece.T, precision=lax.Precision.HIGHEST, prefer...  17 us
  transfers between devices with their start and end apart: 11, of which 5 were waited for; matrix products, arithmetic and copies ran while one was open for 3% of the time, Pallas kernels for 0%

commit v1 on v0

--- a/solution.py
+++ b/solution.py
@@ -53,37 +53,31 @@
         previous, current, sigma_now = (current, following, sigma_next)
     applied = operate(current, potential)
     band_count = current.shape[0]
-    flat_bands = current.reshape(band_count, -1)
-    flat_image = applied.reshape(band_count, -1)
-    cell_total = flat_bands.shape[1] * lax.axis_size("grid")
+    band_devices = lax.axis_size("band")
+    total_bands = band_count * band_devices
+    cell_count = current.shape[1] * current.shape[2] * current.shape[3]
+    cell_total = cell_count * lax.axis_size("grid")
     inverse_cells = 1.0 / cell_total
     first_band = lax.axis_index("band") * band_count
-    local_norms = jnp.sum(flat_image * flat_image, axis=1)
-    panel_piece = lax.all_gather(current, "band", axis=0, tiled=True)
-    flat_piece = panel_piece.reshape(panel_piece.shape[0], -1)
+    both = jnp.stack(
+        [current.reshape(band_count, cell_count), applied.reshape(band_count, cell_count)]
+    ).reshape(2, band_count, band_devices, cell_count // band_devices)
+    moved = lax.all_to_all(both, "band", 2, 1, tiled=True)
+    bands_here = moved[0].reshape(total_bands, -1)
+    image_here = moved[1].reshape(total_bands, -1)
     margin_part = jnp.dot(
-        flat_bands,
-        flat_piece.T,
-        precision=lax.Precision.HIGHEST,
-        preferred_element_type=jnp.float32,
+        bands_here, bands_here.T, precision=lax.Precision.HIGHEST, preferred_element_type=jnp.float32
     )
     image_part = jnp.dot(
-        flat_image,
-        flat_piece.T,
-        precision=lax.Precision.HIGHEST,
-        preferred_element_type=jnp.float32,
+        image_here, bands_here.T, precision=lax.Precision.HIGHEST, preferred_element_type=jnp.float32
     )
-    margin_rows = margin_part
-    image_rows = image_part
-    margin_rows, image_rows, norm_rows = lax.psum((margin_rows, image_rows, local_norms), "grid")
-    margin, subspace, image_norms = (
-        lax.all_gather(margin_rows, "band", axis=0, tiled=True),
-        lax.all_gather(image_rows, "band", axis=0, tiled=True),
-        lax.all_gather(norm_rows, "band", axis=0, tiled=True),
-    )
-    margin = margin * inverse_cells
-    subspace = subspace * inverse_cells
-    image_norms = image_norms * inverse_cells
+    norm_part = jnp.sum(image_here * image_here, axis=1)
+    packed = jnp.concatenate([margin_part.reshape(-1), image_part.reshape(-1), norm_part])
+    packed = lax.psum(packed, ("band", "grid")) * inverse_cells
+    square = total_bands * total_bands
+    margin = packed[:square].reshape(total_bands, total_bands)
+    subspace = packed[square : 2 * square].reshape(total_bands, total_bands)
+    image_norms = packed[2 * square :]
     factor = jnp.linalg.cholesky(margin)
     coefficients = lax.linalg.triangular_solve(factor, subspace.T, left_side=True, lower=True)
     projected = lax.linalg.triangular_solve(factor, coefficients.T, left_side=True, lower=True)

time: 829 us -> 276 us (0.33)
  blocking collectives: 397 us -> 116 us
  waiting for transfers between devices: 256 us -> 40 us
  matrix products: 30.4 us -> 1.31 us
  between operations: 15.1 us -> 1.09 us
  local copies, waits for them, and re-layouts: 26.3 us -> 15.7 us
    all_gather x1 -> x0, waiting for transfers between devices: 252 us -> none  [on_device(): panel_piece = lax.all_gather(current, 'band', axis=0, tiled=True)]
    all_gather x2 -> x0, blocking collectives: 228 us -> none  [the longest x1 116 us: on_device(): lax.all_gather(image_rows, 'band', axis=0, tiled=True)]
    unnamed x1 -> x0, blocking collectives: 115 us -> none
    psum x1, blocking collectives: 54.6 us -> 116 us  [on_device(): packed = lax.psum(packed, ('band', 'grid')) * inverse_cells]
    dot_general x2, matrix products: 29.8 us -> 0.82 us  [the longest x1 0.41 us: on_device(): jnp.dot(bands_here, bands_here.T, precision=lax.Precision.HIGHEST, prefer...]
    all_to_all x0 -> x1, waiting for transfers between devices: none -> 23.9 us  [on_device(): moved = lax.all_to_all(both, 'band', 2, 1, tiled=True)]
    ppermute x5, waiting for transfers between devices: 1.34 us -> 16.2 us  [padded_2(): lax.ppermute(head, axis, [((i + 1) % count, i) for i in range(count)])]
  transfers between devices with their start and end apart: 11 -> 11, of which waited for: 5 -> 6; matrix products, arithmetic and copies ran while one was open for 3% -> 1% of each run, Pallas kernels for 0% -> 0%
where the time goes in v1:
time: 276 us; the launch traced here: 274 us
  blocking collectives  116 us (42%)
  starting transfers between devices  82.4 us (30%)
  waiting for transfers between devices  40 us (14%)
  other arithmetic  17.6 us (6%)
  local copies, waits for them, and re-layouts  15.7 us (6%)
    psum x1, blocking collectives, on_device(): packed = lax.psum(packed, ('band', 'grid')) * inverse_cells  116 us
    ppermute x5, starting transfers between devices, padded_2(): lax.ppermute(tail, axis, [(i, (i + 1) % count) for i in range(count)])  62.9 us
    all_to_all x1, waiting for transfers between devices, on_device(): moved = lax.all_to_all(both, 'band', 2, 1, tiled=True)  23.9 us
    ppermute x5, waiting for transfers between devices, padded_2(): lax.ppermute(head, axis, [((i + 1) % count, i) for i in range(count)])  16.2 us
    ppermute x5, starting transfers between devices, padded_2(): lax.ppermute(head, axis, [((i + 1) % count, i) for i in range(count)])  11.5 us
    all_to_all x1, starting transfers between devices, on_device(): moved = lax.all_to_all(both, 'band', 2, 1, tiled=True)  8.06 us
    another operation x3, other arithmetic, on_device(): factor = jnp.linalg.cholesky(margin)  6.52 us
    another operation x2, other arithmetic, on_device(): lax.linalg.triangular_solve(factor, coefficients.T, left_side=True, lower...  5.55 us
  transfers between devices with their start and end apart: 11, of which 6 were waited for; matrix products, arithmetic and copies ran while one was open for 1% of the time, Pallas kernels for 0%

profile of v1, /device:TPU:24, one launch (start us, length us, event | category | flops | bytes accessed | tf_op | source)
XLA Modules:
  0.0 274.3 jit_solution(5035472801133282586)
XLA Ops:
  0.6 0.9 fusion.146
  1.5 1.9 collective-permute-start
  3.5 3.8 %collective-permute-start.1 = (f32[2,2,32,128]{3,2,1,0:T(8,128)S(1)}, f32[2,2,32,128]{3,2,1,0:T(8,128)S(1)}, u32[]{:S(2)}, u32[]{:S(2)}) collective-permute-start(f32[2,2,32,128]{3,2,1,0:T(8,128)S(1)} %get-tuple-element.92), channel_id=1, source_target_pairs={{1,0},{2,1},{3,2},{4,3},{5,4},{6,5},{7,6},{8,7},{9,8},{10,9},{11,1... | collective-permute-start | bytes 196616 | tf_op jit(solution)/shard_map/ppermute | solution.py:24
  7.2 1.2 fusion.150
  9.1 0.7 copy-done.2
  10.0 9.8 %collective-permute-done.1 = f32[2,2,32,128]{3,2,1,0:T(8,128)S(1)} collective-permute-done((f32[2,2,32,128]{3,2,1,0:T(8,128)S(1)}, f32[2,2,32,128]{3,2,1,0:T(8,128)S(1)}, u32[]{:S(2)}, u32[]{:S(2)}) %collective-permute-start.1) | collective-permute-done | bytes 65568 | tf_op jit(solution)/shard_map/ppermute | solution.py:24
  21.3 16.1 %collective-permute-start.2 = (f32[2,2,32,128]{3,2,1,0:T(8,128)S(1)}, f32[2,2,32,128]{3,2,1,0:T(8,128)S(1)}, u32[]{:S(2)}, u32[]{:S(2)}) collective-permute-start(f32[2,2,32,128]{3,2,1,0:T(8,128)S(1)} %get-tuple-element.79), channel_id=1, source_target_pairs={{0,1},{1,2},{2,3},{3,4},{4,5},{5,6},{6,7},{7,8},{8,9},{9,10},{10,1... | collective-permute-start | bytes 196616 | tf_op jit(solution)/shard_map/ppermute | solution.py:22
  37.4 1.9 collective-permute-start.3
  39.4 1.8 collective-permute-done.3
  41.2 0.7 fusion.55
  42.7 15.4 %collective-permute-start.4 = (f32[2,2,32,128]{3,2,1,0:T(8,128)S(1)}, f32[2,2,32,128]{3,2,1,0:T(8,128)S(1)}, u32[]{:S(2)}, u32[]{:S(2)}) collective-permute-start(f32[2,2,32,128]{3,2,1,0:T(8,128)S(1)} %get-tuple-element.61), channel_id=1, source_target_pairs={{0,1},{1,2},{2,3},{3,4},{4,5},{5,6},{6,7},{7,8},{8,9},{9,10},{10,1... | collective-permute-start | bytes 196616 | tf_op jit(solution)/shard_map/ppermute | solution.py:22
  58.1 1.9 collective-permute-start.5
  60.1 1.8 collective-permute-done.5
  63.4 15.0 %collective-permute-start.6 = (f32[2,2,32,128]{3,2,1,0:T(8,128)S(1)}, f32[2,2,32,128]{3,2,1,0:T(8,128)S(1)}, u32[]{:S(2)}, u32[]{:S(2)}) collective-permute-start(f32[2,2,32,128]{3,2,1,0:T(8,128)S(1)} %get-tuple-element.43), channel_id=1, source_target_pairs={{0,1},{1,2},{2,3},{3,4},{4,5},{5,6},{6,7},{7,8},{8,9},{9,10},{10,1... | collective-permute-start | bytes 196616 | tf_op jit(solution)/shard_map/ppermute | solution.py:22
  78.4 1.9 collective-permute-start.7
  80.4 1.8 collective-permute-done.7
  83.5 0.9 fusion.111
  84.4 0.9 fusion.112
  85.3 0.7 fusion.114
  86.0 14.5 %collective-permute-start.8 = (f32[2,2,32,128]{3,2,1,0:T(8,128)}, f32[2,2,32,128]{3,2,1,0:T(8,128)S(1)}, u32[]{:S(2)}, u32[]{:S(2)}) collective-permute-start(f32[2,2,32,128]{3,2,1,0:T(8,128)} %get-tuple-element.25), channel_id=1, source_target_pairs={{0,1},{1,2},{2,3},{3,4},{4,5},{5,6},{6,7},{7,8},{8,9},{9,10},{10,1... | collective-permute-start | bytes 196616 | tf_op jit(solution)/shard_map/ppermute | solution.py:22
  100.5 1.9 collective-permute-start.9
  103.0 0.8 stack.7
  103.8 0.8 collective-permute-done.9
  104.6 0.7 copy-done.4
  105.3 2.5 fusion.10
  107.8 1.1 stack.8
  109.0 1.4 copy.10
  110.3 8.1 %all-to-all-start = ((f32[2,2,32,1280]{3,1,0,2:T(2,128)}), f32[2,2,32,1280]{3,1,0,2:T(2,128)S(1)}, u32[]{:S(2)}, u32[]{:S(2)}) async-start(f32[2,2,32,1280]{3,1,0,2:T(2,128)} %copy.10), calls=%async_computation | async-start | bytes 1310720 | tf_op jit(solution)/shard_map/all_to_all | solution.py:65
  118.4 23.9 %all-to-all-done = f32[2,2,32,1280]{3,1,0,2:T(2,128)S(1)} async-done(((f32[2,2,32,1280]{3,1,0,2:T(2,128)}), f32[2,2,32,1280]{3,1,0,2:T(2,128)S(1)}, u32[]{:S(2)}, u32[]{:S(2)}) %all-to-all-start) | async-done | bytes 655392 | tf_op jit(solution)/shard_map/all_to_all | solution.py:65
  144.1 116.2 %psum.7 = f32[8256]{0:T(1024)S(1)} all-reduce(f32[8256]{0:T(1024)S(1)} %pad_maximum_fusion.9), channel_id=1, replica_groups=mesh['band'=32,'grid'=16] {'band','grid'}, use_global_device_ids=true, to_apply=%region_1.2 | all-reduce | flops 8256 | bytes 66048 | tf_op jit(solution)/shard_map/psum | solution.py:76
  260.5 5.8 %cholesky.18 = f32[64,64]{1,0:T(8,128)S(1)} custom-call(f32[64,64]{1,0:T(8,128)S(1)} %fusion.103), custom_call_target="Cholesky" | custom-call | tf_op jit(solution)/shard_map/jit(cholesky)/cholesky | solution.py:81
  267.7 4.9 %custom-call.8 = f32[1,64,64]{1,2,0:T(8,128)S(1)} custom-call(f32[1,64,64]{2,1,0:T(8,128)S(1)} %fusion.96), custom_call_target="InvertDiagBlocksLowerTriangular" | custom-call | tf_op jit(solution)/shard_map/triangular_solve/custom-call.0 | solution.py:83
  (86 shorter events, 11.4 us)
Async XLA Ops:
  1.5 8.4 %collective-permute-start = (f32[2,2,32,128]{3,2,1,0:T(8,128)S(1)}, f32[2,2,32,128]{3,2,1,0:T(8,128)S(1)}, u32[]{:S(2)}, u32[]{:S(2)}) collective-permute-start(f32[2,2,32,128]{3,2,1,0:T(8,128)S(1)} %get-tuple-element.91), channel_id=1, source_target_pairs={{0,1},{1,2},{2,3},{3,4},{4,5},{5,6},{6,7},{7,8},{8,9},{9,10},{10,1... | collective-permute-start | bytes 196616 | tf_op jit(solution)/shard_map/ppermute | solution.py:22
  3.5 5.0 %copy-start.1 = (f32[2,10,32,128]{3,2,1,0:T(8,128)S(1)}, f32[2,10,32,128]{3,2,1,0:T(8,128)}, u32[]{:S(2)}) copy-start(f32[2,10,32,128]{3,2,1,0:T(8,128)} %param.4) | copy-start | bytes 983044
  3.5 16.4 %collective-permute-start.1 = (f32[2,2,32,128]{3,2,1,0:T(8,128)S(1)}, f32[2,2,32,128]{3,2,1,0:T(8,128)S(1)}, u32[]{:S(2)}, u32[]{:S(2)}) collective-permute-start(f32[2,2,32,128]{3,2,1,0:T(8,128)S(1)} %get-tuple-element.92), channel_id=1, source_target_pairs={{1,0},{2,1},{3,2},{4,3},{5,4},{6,5},{7,6},{8,7},{9,8},{10,9},{11,1... | collective-permute-start | bytes 196616 | tf_op jit(solution)/shard_map/ppermute | solution.py:24
  8.9 0.9 copy-start.2
  21.3 18.0 %collective-permute-start.2 = (f32[2,2,32,128]{3,2,1,0:T(8,128)S(1)}, f32[2,2,32,128]{3,2,1,0:T(8,128)S(1)}, u32[]{:S(2)}, u32[]{:S(2)}) collective-permute-start(f32[2,2,32,128]{3,2,1,0:T(8,128)S(1)} %get-tuple-element.79), channel_id=1, source_target_pairs={{0,1},{1,2},{2,3},{3,4},{4,5},{5,6},{6,7},{7,8},{8,9},{9,10},{10,1... | collective-permute-start | bytes 196616 | tf_op jit(solution)/shard_map/ppermute | solution.py:22
  37.4 3.8 %collective-permute-start.3 = (f32[2,2,32,128]{3,2,1,0:T(8,128)S(1)}, f32[2,2,32,128]{3,2,1,0:T(8,128)S(1)}, u32[]{:S(2)}, u32[]{:S(2)}) collective-permute-start(f32[2,2,32,128]{3,2,1,0:T(8,128)S(1)} %get-tuple-element.80), channel_id=1, source_target_pairs={{1,0},{2,1},{3,2},{4,3},{5,4},{6,5},{7,6},{8,7},{9,8},{10,9},{11,1... | collective-permute-start | bytes 196616 | tf_op jit(solution)/shard_map/ppermute | solution.py:24
  42.7 17.3 %collective-permute-start.4 = (f32[2,2,32,128]{3,2,1,0:T(8,128)S(1)}, f32[2,2,32,128]{3,2,1,0:T(8,128)S(1)}, u32[]{:S(2)}, u32[]{:S(2)}) collective-permute-start(f32[2,2,32,128]{3,2,1,0:T(8,128)S(1)} %get-tuple-element.61), channel_id=1, source_target_pairs={{0,1},{1,2},{2,3},{3,4},{4,5},{5,6},{6,7},{7,8},{8,9},{9,10},{10,1... | collective-permute-start | bytes 196616 | tf_op jit(solution)/shard_map/ppermute | solution.py:22
  58.1 3.8 %collective-permute-start.5 = (f32[2,2,32,128]{3,2,1,0:T(8,128)S(1)}, f32[2,2,32,128]{3,2,1,0:T(8,128)S(1)}, u32[]{:S(2)}, u32[]{:S(2)}) collective-permute-start(f32[2,2,32,128]{3,2,1,0:T(8,128)S(1)} %get-tuple-element.62), channel_id=1, source_target_pairs={{1,0},{2,1},{3,2},{4,3},{5,4},{6,5},{7,6},{8,7},{9,8},{10,9},{11,1... | collective-permute-start | bytes 196616 | tf_op jit(solution)/shard_map/ppermute | solution.py:24
  63.4 17.0 %collective-permute-start.6 = (f32[2,2,32,128]{3,2,1,0:T(8,128)S(1)}, f32[2,2,32,128]{3,2,1,0:T(8,128)S(1)}, u32[]{:S(2)}, u32[]{:S(2)}) collective-permute-start(f32[2,2,32,128]{3,2,1,0:T(8,128)S(1)} %get-tuple-element.43), channel_id=1, source_target_pairs={{0,1},{1,2},{2,3},{3,4},{4,5},{5,6},{6,7},{7,8},{8,9},{9,10},{10,1... | collective-permute-start | bytes 196616 | tf_op jit(solution)/shard_map/ppermute | solution.py:22
  78.4 3.8 %collective-permute-start.7 = (f32[2,2,32,128]{3,2,1,0:T(8,128)S(1)}, f32[2,2,32,128]{3,2,1,0:T(8,128)S(1)}, u32[]{:S(2)}, u32[]{:S(2)}) collective-permute-start(f32[2,2,32,128]{3,2,1,0:T(8,128)S(1)} %get-tuple-element.44), channel_id=1, source_target_pairs={{1,0},{2,1},{3,2},{4,3},{5,4},{6,5},{7,6},{8,7},{9,8},{10,9},{11,1... | collective-permute-start | bytes 196616 | tf_op jit(solution)/shard_map/ppermute | solution.py:24
  82.9 21.7 %copy-start = (f32[2,10,32,128]{3,2,1,0:T(8,128)}, f32[2,10,32,128]{3,2,1,0:T(8,128)S(1)}, u32[]{:S(2)}) copy-start(f32[2,10,32,128]{3,2,1,0:T(8,128)S(1)} %fusion.25) | copy-start | bytes 983044
  86.0 17.9 %collective-permute-start.8 = (f32[2,2,32,128]{3,2,1,0:T(8,128)}, f32[2,2,32,128]{3,2,1,0:T(8,128)S(1)}, u32[]{:S(2)}, u32[]{:S(2)}) collective-permute-start(f32[2,2,32,128]{3,2,1,0:T(8,128)} %get-tuple-element.25), channel_id=1, source_target_pairs={{0,1},{1,2},{2,3},{3,4},{4,5},{5,6},{6,7},{7,8},{8,9},{9,10},{10,1... | collective-permute-start | bytes 196616 | tf_op jit(solution)/shard_map/ppermute | solution.py:22
  100.5 4.1 %collective-permute-start.9 = (f32[2,2,32,128]{3,2,1,0:T(8,128)}, f32[2,2,32,128]{3,2,1,0:T(8,128)}, u32[]{:S(2)}, u32[]{:S(2)}) collective-permute-start(f32[2,2,32,128]{3,2,1,0:T(8,128)} %get-tuple-element.26), channel_id=1, source_target_pairs={{1,0},{2,1},{3,2},{4,3},{5,4},{6,5},{7,6},{8,7},{9,8},{10,9},{11,1... | collective-permute-start | bytes 196616 | tf_op jit(solution)/shard_map/ppermute | solution.py:24
  104.6 0.7 copy-start.4
  104.6 0.7 copy-start.5
  107.8 1.1 copy-start.3
  110.3 31.9 %all-to-all-start = ((f32[2,2,32,1280]{3,1,0,2:T(2,128)}), f32[2,2,32,1280]{3,1,0,2:T(2,128)S(1)}, u32[]{:S(2)}, u32[]{:S(2)}) async-start(f32[2,2,32,1280]{3,1,0,2:T(2,128)} %copy.10), calls=%async_computation | async-start | bytes 1310720 | tf_op jit(solution)/shard_map/all_to_all | solution.py:65

commit v2 on v1

--- a/solution.py
+++ b/solution.py
@@ -26,6 +26,15 @@
             axis=dim,
         )
     return cells
+
+
+def butterfly_sum(values, axis):
+    count = lax.axis_size(axis)
+    step = 1
+    while step < count:
+        values = values + lax.ppermute(values, axis, [(i, i ^ step) for i in range(count)])
+        step *= 2
+    return values
 
 
 def operate(field_in, potential):
@@ -73,7 +82,7 @@
     )
     norm_part = jnp.sum(image_here * image_here, axis=1)
     packed = jnp.concatenate([margin_part.reshape(-1), image_part.reshape(-1), norm_part])
-    packed = lax.psum(packed, ("band", "grid")) * inverse_cells
+    packed = butterfly_sum(butterfly_sum(packed, "grid"), "band") * inverse_cells
     square = total_bands * total_bands
     margin = packed[:square].reshape(total_bands, total_bands)
     subspace = packed[square : 2 * square].reshape(total_bands, total_bands)

time: 276 us -> 242 us (0.88)
  blocking collectives: 116 us -> 31.6 us
  starting transfers between devices: 82.4 us -> 111 us
  waiting for transfers between devices: 40 us -> 63.6 us
    psum x1 -> x0, blocking collectives: 116 us -> none  [on_device(): packed = lax.psum(packed, ('band', 'grid')) * inverse_cells]
    ppermute x0 -> x9, waiting for transfers between devices: none -> 47.5 us  [butterfly_sum(): lax.ppermute(values, axis, [(i, i ^ step) for i in range(count)])]
    ppermute x0 -> x9, starting transfers between devices: none -> 37 us  [butterfly_sum(): lax.ppermute(values, axis, [(i, i ^ step) for i in range(count)])]
    all_to_all x0 -> x1, blocking collectives: none -> 31.6 us  [on_device(): moved = lax.all_to_all(both, 'band', 2, 1, tiled=True)]
    all_to_all x1 -> x0, waiting for transfers between devices: 23.9 us -> none  [on_device(): moved = lax.all_to_all(both, 'band', 2, 1, tiled=True)]
    all_to_all x1 -> x0, starting transfers between devices: 8.06 us -> none  [on_device(): moved = lax.all_to_all(both, 'band', 2, 1, tiled=True)]
  transfers between devices with their start and end apart: 11 -> 19, of which waited for: 6 -> 14; matrix products, arithmetic and copies ran while one was open for 1% -> 1% of each run, Pallas kernels for 0% -> 0%
where the time goes in v2:
time: 242 us
  starting transfers between devices  111 us (46%)
  waiting for transfers between devices  63.6 us (26%)
  blocking collectives  31.6 us (13%)
  other arithmetic  17.6 us (7%)
  local copies, waits for them, and re-layouts  14.8 us (6%)
    ppermute x5, starting transfers between devices, padded_2(): lax.ppermute(tail, axis, [(i, (i + 1) % count) for i in range(count)])  62.9 us
    ppermute x9, waiting for transfers between devices, butterfly_sum(): lax.ppermute(values, axis, [(i, i ^ step) for i in range(count)])  47.5 us
    ppermute x9, starting transfers between devices, butterfly_sum(): lax.ppermute(values, axis, [(i, i ^ step) for i in range(count)])  37 us
    all_to_all x1, blocking collectives, on_device(): moved = lax.all_to_all(both, 'band', 2, 1, tiled=True)  31.6 us
    ppermute x5, waiting for transfers between devices, padded_2(): lax.ppermute(head, axis, [((i + 1) % count, i) for i in range(count)])  16.1 us
    ppermute x5, starting transfers between devices, padded_2(): lax.ppermute(head, axis, [((i + 1) % count, i) for i in range(count)])  11.5 us
    another operation x3, other arithmetic, on_device(): factor = jnp.linalg.cholesky(margin)  6.52 us
    another operation x2, other arithmetic, on_device(): lax.linalg.triangular_solve(factor, coefficients.T, left_side=True, lower...  5.55 us
  transfers between devices with their start and end apart: 19, of which 14 were waited for; matrix products, arithmetic and copies ran while one was open for 1% of the time, Pallas kernels for 0%

profile of v2, /device:TPU:24, one launch (start us, length us, event | category | flops | bytes accessed | tf_op | source)
XLA Modules:
  0.0 241.5 jit_solution(17557738878988345218)
XLA Ops:
  1.5 1.9 collective-permute-start
  3.5 3.8 %collective-permute-start.1 = (f32[2,2,32,128]{3,2,1,0:T(8,128)S(1)}, f32[2,2,32,128]{3,2,1,0:T(8,128)S(1)}, u32[]{:S(2)}, u32[]{:S(2)}) collective-permute-start(f32[2,2,32,128]{3,2,1,0:T(8,128)S(1)} %get-tuple-element.92), channel_id=1, source_target_pairs={{1,0},{2,1},{3,2},{4,3},{5,4},{6,5},{7,6},{8,7},{9,8},{10,9},{11,1... | collective-permute-start | bytes 196616 | tf_op jit(solution)/shard_map/ppermute | solution.py:24
  10.0 9.8 %collective-permute-done.1 = f32[2,2,32,128]{3,2,1,0:T(8,128)S(1)} collective-permute-done((f32[2,2,32,128]{3,2,1,0:T(8,128)S(1)}, f32[2,2,32,128]{3,2,1,0:T(8,128)S(1)}, u32[]{:S(2)}, u32[]{:S(2)}) %collective-permute-start.1) | collective-permute-done | bytes 65568 | tf_op jit(solution)/shard_map/ppermute | solution.py:24
  21.3 16.1 %collective-permute-start.2 = (f32[2,2,32,128]{3,2,1,0:T(8,128)S(1)}, f32[2,2,32,128]{3,2,1,0:T(8,128)S(1)}, u32[]{:S(2)}, u32[]{:S(2)}) collective-permute-start(f32[2,2,32,128]{3,2,1,0:T(8,128)S(1)} %get-tuple-element.79), channel_id=1, source_target_pairs={{0,1},{1,2},{2,3},{3,4},{4,5},{5,6},{6,7},{7,8},{8,9},{9,10},{10,1... | collective-permute-start | bytes 196616 | tf_op jit(solution)/shard_map/ppermute | solution.py:22
  37.4 1.9 collective-permute-start.3
  42.7 15.4 %collective-permute-start.4 = (f32[2,2,32,128]{3,2,1,0:T(8,128)S(1)}, f32[2,2,32,128]{3,2,1,0:T(8,128)S(1)}, u32[]{:S(2)}, u32[]{:S(2)}) collective-permute-start(f32[2,2,32,128]{3,2,1,0:T(8,128)S(1)} %get-tuple-element.61), channel_id=1, source_target_pairs={{0,1},{1,2},{2,3},{3,4},{4,5},{5,6},{6,7},{7,8},{8,9},{9,10},{10,1... | collective-permute-start | bytes 196616 | tf_op jit(solution)/shard_map/ppermute | solution.py:22
  58.1 1.9 collective-permute-start.5
  63.4 15.0 %collective-permute-start.6 = (f32[2,2,32,128]{3,2,1,0:T(8,128)S(1)}, f32[2,2,32,128]{3,2,1,0:T(8,128)S(1)}, u32[]{:S(2)}, u32[]{:S(2)}) collective-permute-start(f32[2,2,32,128]{3,2,1,0:T(8,128)S(1)} %get-tuple-element.43), channel_id=1, source_target_pairs={{0,1},{1,2},{2,3},{3,4},{4,5},{5,6},{6,7},{7,8},{8,9},{9,10},{10,1... | collective-permute-start | bytes 196616 | tf_op jit(solution)/shard_map/ppermute | solution.py:22
  78.4 1.9 collective-permute-start.7
  85.9 14.5 %collective-permute-start.8 = (f32[2,2,32,128]{3,2,1,0:T(8,128)}, f32[2,2,32,128]{3,2,1,0:T(8,128)S(1)}, u32[]{:S(2)}, u32[]{:S(2)}) collective-permute-start(f32[2,2,32,128]{3,2,1,0:T(8,128)} %get-tuple-element.25), channel_id=1, source_target_pairs={{0,1},{1,2},{2,3},{3,4},{4,5},{5,6},{6,7},{7,8},{8,9},{9,10},{10,1... | collective-permute-start | bytes 196616 | tf_op jit(solution)/shard_map/ppermute | solution.py:22
  100.5 1.9 collective-permute-start.9
  105.3 2.5 %fusion.10 = f32[2,10,32,128]{3,2,1,0:T(8,128)} fusion(f32[2,10,32,128]{3,2,1,0:T(8,128)S(1)} %fusion.25, f32[2,2,32,128]{3,2,1,0:T(8,128)} %collective-permute-done.9, f32[2,2,32,128]{3,2,1,0:T(8,128)S(1)} %collective-permute-done.8, f32[2,10,31,128]{3,2,1,0:T(8,128)} %get-tuple-element.22, f32[2,10,1,128]{3,2,1,0:T(1,128)S(1)} %copy-done.5, ...), kind=kLoop, calls=%fused_computation.27 | loop fusion | flops 2457600 | bytes 3571712 | tf_op jit(solution)/shard_map/add | solution.py:50
  109.5 31.6 %all_to_all.15 = f32[2,2,32,1280]{3,1,0,2:T(2,128)S(1)} all-to-all(f32[2,2,32,1280]{3,1,0,2:T(2,128)S(1)} %copy.10), channel_id=1, replica_groups=mesh['band'=32,'grid'=16] {'band'}, dimensions={2} | all-to-all | bytes 1310720 | tf_op jit(solution)/shard_map/all_to_all | solution.py:74
  142.9 20.0 %collective-permute-start.10 = (f32[8256]{0:T(1024)S(1)}, f32[8256]{0:T(1024)S(1)}, u32[]{:S(2)}, u32[]{:S(2)}) collective-permute-start(f32[8256]{0:T(1024)S(1)} %constant_dynamic-update-slice_fusion.5), channel_id=1, source_target_pairs={{0,1},{1,0},{2,3},{3,2},{4,5},{5,4},{6,7},{7,6},{8,9},{9,8},{10,11... | collective-permute-start | bytes 99080 | tf_op jit(solution)/shard_map/ppermute | solution.py:35
  163.7 1.9 collective-permute-start.11
  165.6 3.9 %collective-permute-done.11 = f32[8256]{0:T(1024)S(1)} collective-permute-done((f32[8256]{0:T(1024)S(1)}, f32[8256]{0:T(1024)S(1)}, u32[]{:S(2)}, u32[]{:S(2)}) %collective-permute-start.11) | collective-permute-done | bytes 33056 | tf_op jit(solution)/shard_map/ppermute | solution.py:35
  169.5 1.9 collective-permute-start.12
  171.4 5.4 %collective-permute-done.12 = f32[8256]{0:T(1024)S(1)} collective-permute-done((f32[8256]{0:T(1024)S(1)}, f32[8256]{0:T(1024)S(1)}, u32[]{:S(2)}, u32[]{:S(2)}) %collective-permute-start.12) | collective-permute-done | bytes 33056 | tf_op jit(solution)/shard_map/ppermute | solution.py:35
  176.9 1.9 collective-permute-start.13
  178.8 12.7 %collective-permute-done.13 = f32[8256]{0:T(1024)S(1)} collective-permute-done((f32[8256]{0:T(1024)S(1)}, f32[8256]{0:T(1024)S(1)}, u32[]{:S(2)}, u32[]{:S(2)}) %collective-permute-start.13) | collective-permute-done | bytes 33056 | tf_op jit(solution)/shard_map/ppermute | solution.py:35
  191.5 1.9 collective-permute-start.14
  193.4 3.9 %collective-permute-done.14 = f32[8256]{0:T(1024)S(1)} collective-permute-done((f32[8256]{0:T(1024)S(1)}, f32[8256]{0:T(1024)S(1)}, u32[]{:S(2)}, u32[]{:S(2)}) %collective-permute-start.14) | collective-permute-done | bytes 33056 | tf_op jit(solution)/shard_map/ppermute | solution.py:35
  197.3 2.3 collective-permute-start.15
  199.6 4.5 %collective-permute-done.15 = f32[8256]{0:T(1024)S(1)} collective-permute-done((f32[8256]{0:T(1024)S(1)}, f32[8256]{0:T(1024)S(1)}, u32[]{:S(2)}, u32[]{:S(2)}) %collective-permute-start.15) | collective-permute-done | bytes 33056 | tf_op jit(solution)/shard_map/ppermute | solution.py:35
  204.1 1.9 collective-permute-start.16
  206.0 8.3 %collective-permute-done.16 = f32[8256]{0:T(1024)S(1)} collective-permute-done((f32[8256]{0:T(1024)S(1)}, f32[8256]{0:T(1024)S(1)}, u32[]{:S(2)}, u32[]{:S(2)}) %collective-permute-start.16) | collective-permute-done | bytes 33056 | tf_op jit(solution)/shard_map/ppermute | solution.py:35
  214.3 1.9 collective-permute-start.17
  216.2 3.9 %collective-permute-done.17 = f32[8256]{0:T(1024)S(1)} collective-permute-done((f32[8256]{0:T(1024)S(1)}, f32[8256]{0:T(1024)S(1)}, u32[]{:S(2)}, u32[]{:S(2)}) %collective-permute-start.17) | collective-permute-done | bytes 33056 | tf_op jit(solution)/shard_map/ppermute | solution.py:35
  220.1 3.3 %collective-permute-start.18 = (f32[8256]{0:T(1024)S(1)}, f32[8256]{0:T(1024)S(1)}, u32[]{:S(2)}, u32[]{:S(2)}) collective-permute-start(f32[8256]{0:T(1024)S(1)} %add.288), channel_id=1, source_target_pairs={{0,256},{16,272},{32,288},{48,304},{64,320},{80,336},{96,352},{112... | collective-permute-start | bytes 99080 | tf_op jit(solution)/shard_map/ppermute | solution.py:35
  223.5 4.0 %collective-permute-done.18 = f32[8256]{0:T(1024)S(1)} collective-permute-done((f32[8256]{0:T(1024)S(1)}, f32[8256]{0:T(1024)S(1)}, u32[]{:S(2)}, u32[]{:S(2)}) %collective-permute-start.18) | collective-permute-done | bytes 33056 | tf_op jit(solution)/shard_map/ppermute | solution.py:35
  227.7 5.8 %cholesky.18 = f32[64,64]{1,0:T(8,128)S(1)} custom-call(f32[64,64]{1,0:T(8,128)S(1)} %fusion.103), custom_call_target="Cholesky" | custom-call | tf_op jit(solution)/shard_map/jit(cholesky)/cholesky | solution.py:90
  234.9 4.9 %custom-call.8 = f32[1,64,64]{1,2,0:T(8,128)S(1)} custom-call(f32[1,64,64]{2,1,0:T(8,128)S(1)} %fusion.96), custom_call_target="InvertDiagBlocksLowerTriangular" | custom-call | tf_op jit(solution)/shard_map/triangular_solve/custom-call.0 | solution.py:92
  (112 shorter events, 27.7 us)
Async XLA Ops:
  1.5 8.4 %collective-permute-start = (f32[2,2,32,128]{3,2,1,0:T(8,128)S(1)}, f32[2,2,32,128]{3,2,1,0:T(8,128)S(1)}, u32[]{:S(2)}, u32[]{:S(2)}) collective-permute-start(f32[2,2,32,128]{3,2,1,0:T(8,128)S(1)} %get-tuple-element.91), channel_id=1, source_target_pairs={{0,1},{1,2},{2,3},{3,4},{4,5},{5,6},{6,7},{7,8},{8,9},{9,10},{10,1... | collective-permute-start | bytes 196616 | tf_op jit(solution)/shard_map/ppermute | solution.py:22
  3.5 5.0 %copy-start.1 = (f32[2,10,32,128]{3,2,1,0:T(8,128)S(1)}, f32[2,10,32,128]{3,2,1,0:T(8,128)}, u32[]{:S(2)}) copy-start(f32[2,10,32,128]{3,2,1,0:T(8,128)} %param.4) | copy-start | bytes 983044
  3.5 16.4 %collective-permute-start.1 = (f32[2,2,32,128]{3,2,1,0:T(8,128)S(1)}, f32[2,2,32,128]{3,2,1,0:T(8,128)S(1)}, u32[]{:S(2)}, u32[]{:S(2)}) collective-permute-start(f32[2,2,32,128]{3,2,1,0:T(8,128)S(1)} %get-tuple-element.92), channel_id=1, source_target_pairs={{1,0},{2,1},{3,2},{4,3},{5,4},{6,5},{7,6},{8,7},{9,8},{10,9},{11,1... | collective-permute-start | bytes 196616 | tf_op jit(solution)/shard_map/ppermute | solution.py:24
  8.9 0.9 copy-start.2
  21.3 18.0 %collective-permute-start.2 = (f32[2,2,32,128]{3,2,1,0:T(8,128)S(1)}, f32[2,2,32,128]{3,2,1,0:T(8,128)S(1)}, u32[]{:S(2)}, u32[]{:S(2)}) collective-permute-start(f32[2,2,32,128]{3,2,1,0:T(8,128)S(1)} %get-tuple-element.79), channel_id=1, source_target_pairs={{0,1},{1,2},{2,3},{3,4},{4,5},{5,6},{6,7},{7,8},{8,9},{9,10},{10,1... | collective-permute-start | bytes 196616 | tf_op jit(solution)/shard_map/ppermute | solution.py:22
  37.4 3.8 %collective-permute-start.3 = (f32[2,2,32,128]{3,2,1,0:T(8,128)S(1)}, f32[2,2,32,128]{3,2,1,0:T(8,128)S(1)}, u32[]{:S(2)}, u32[]{:S(2)}) collective-permute-start(f32[2,2,32,128]{3,2,1,0:T(8,128)S(1)} %get-tuple-element.80), channel_id=1, source_target_pairs={{1,0},{2,1},{3,2},{4,3},{5,4},{6,5},{7,6},{8,7},{9,8},{10,9},{11,1... | collective-permute-start | bytes 196616 | tf_op jit(solution)/shard_map/ppermute | solution.py:24
  42.7 17.3 %collective-permute-start.4 = (f32[2,2,32,128]{3,2,1,0:T(8,128)S(1)}, f32[2,2,32,128]{3,2,1,0:T(8,128)S(1)}, u32[]{:S(2)}, u32[]{:S(2)}) collective-permute-start(f32[2,2,32,128]{3,2,1,0:T(8,128)S(1)} %get-tuple-element.61), channel_id=1, source_target_pairs={{0,1},{1,2},{2,3},{3,4},{4,5},{5,6},{6,7},{7,8},{8,9},{9,10},{10,1... | collective-permute-start | bytes 196616 | tf_op jit(solution)/shard_map/ppermute | solution.py:22
  58.1 3.8 %collective-permute-start.5 = (f32[2,2,32,128]{3,2,1,0:T(8,128)S(1)}, f32[2,2,32,128]{3,2,1,0:T(8,128)S(1)}, u32[]{:S(2)}, u32[]{:S(2)}) collective-permute-start(f32[2,2,32,128]{3,2,1,0:T(8,128)S(1)} %get-tuple-element.62), channel_id=1, source_target_pairs={{1,0},{2,1},{3,2},{4,3},{5,4},{6,5},{7,6},{8,7},{9,8},{10,9},{11,1... | collective-permute-start | bytes 196616 | tf_op jit(solution)/shard_map/ppermute | solution.py:24
  63.4 17.0 %collective-permute-start.6 = (f32[2,2,32,128]{3,2,1,0:T(8,128)S(1)}, f32[2,2,32,128]{3,2,1,0:T(8,128)S(1)}, u32[]{:S(2)}, u32[]{:S(2)}) collective-permute-start(f32[2,2,32,128]{3,2,1,0:T(8,128)S(1)} %get-tuple-element.43), channel_id=1, source_target_pairs={{0,1},{1,2},{2,3},{3,4},{4,5},{5,6},{6,7},{7,8},{8,9},{9,10},{10,1... | collective-permute-start | bytes 196616 | tf_op jit(solution)/shard_map/ppermute | solution.py:22
  78.4 3.8 %collective-permute-start.7 = (f32[2,2,32,128]{3,2,1,0:T(8,128)S(1)}, f32[2,2,32,128]{3,2,1,0:T(8,128)S(1)}, u32[]{:S(2)}, u32[]{:S(2)}) collective-permute-start(f32[2,2,32,128]{3,2,1,0:T(8,128)S(1)} %get-tuple-element.44), channel_id=1, source_target_pairs={{1,0},{2,1},{3,2},{4,3},{5,4},{6,5},{7,6},{8,7},{9,8},{10,9},{11,1... | collective-permute-start | bytes 196616 | tf_op jit(solution)/shard_map/ppermute | solution.py:24
  82.9 21.7 %copy-start = (f32[2,10,32,128]{3,2,1,0:T(8,128)}, f32[2,10,32,128]{3,2,1,0:T(8,128)S(1)}, u32[]{:S(2)}) copy-start(f32[2,10,32,128]{3,2,1,0:T(8,128)S(1)} %fusion.25) | copy-start | bytes 983044
  85.9 17.9 %collective-permute-start.8 = (f32[2,2,32,128]{3,2,1,0:T(8,128)}, f32[2,2,32,128]{3,2,1,0:T(8,128)S(1)}, u32[]{:S(2)}, u32[]{:S(2)}) collective-permute-start(f32[2,2,32,128]{3,2,1,0:T(8,128)} %get-tuple-element.25), channel_id=1, source_target_pairs={{0,1},{1,2},{2,3},{3,4},{4,5},{5,6},{6,7},{7,8},{8,9},{9,10},{10,1... | collective-permute-start | bytes 196616 | tf_op jit(solution)/shard_map/ppermute | solution.py:22
  100.5 4.1 %collective-permute-start.9 = (f32[2,2,32,128]{3,2,1,0:T(8,128)}, f32[2,2,32,128]{3,2,1,0:T(8,128)}, u32[]{:S(2)}, u32[]{:S(2)}) collective-permute-start(f32[2,2,32,128]{3,2,1,0:T(8,128)} %get-tuple-element.26), channel_id=1, source_target_pairs={{1,0},{2,1},{3,2},{4,3},{5,4},{6,5},{7,6},{8,7},{9,8},{10,9},{11,1... | collective-permute-start | bytes 196616 | tf_op jit(solution)/shard_map/ppermute | solution.py:24
  104.6 0.7 copy-start.4
  104.6 0.7 copy-start.5
  107.8 1.1 copy-start.3
  142.9 20.8 %collective-permute-start.10 = (f32[8256]{0:T(1024)S(1)}, f32[8256]{0:T(1024)S(1)}, u32[]{:S(2)}, u32[]{:S(2)}) collective-permute-start(f32[8256]{0:T(1024)S(1)} %constant_dynamic-update-slice_fusion.5), channel_id=1, source_target_pairs={{0,1},{1,0},{2,3},{3,2},{4,5},{5,4},{6,7},{7,6},{8,9},{9,8},{10,11... | collective-permute-start | bytes 99080 | tf_op jit(solution)/shard_map/ppermute | solution.py:35
  163.7 5.8 %collective-permute-start.11 = (f32[8256]{0:T(1024)S(1)}, f32[8256]{0:T(1024)S(1)}, u32[]{:S(2)}, u32[]{:S(2)}) collective-permute-start(f32[8256]{0:T(1024)S(1)} %add.281), channel_id=1, source_target_pairs={{0,2},{1,3},{2,0},{3,1},{4,6},{5,7},{6,4},{7,5},{8,10},{9,11},{10,... | collective-permute-start | bytes 99080 | tf_op jit(solution)/shard_map/ppermute | solution.py:35
  169.5 7.3 %collective-permute-start.12 = (f32[8256]{0:T(1024)S(1)}, f32[8256]{0:T(1024)S(1)}, u32[]{:S(2)}, u32[]{:S(2)}) collective-permute-start(f32[8256]{0:T(1024)S(1)} %add.282), channel_id=1, source_target_pairs={{0,4},{1,5},{2,6},{3,7},{4,0},{5,1},{6,2},{7,3},{8,12},{9,13},{10,... | collective-permute-start | bytes 99080 | tf_op jit(solution)/shard_map/ppermute | solution.py:35
  176.9 14.6 %collective-permute-start.13 = (f32[8256]{0:T(1024)S(1)}, f32[8256]{0:T(1024)S(1)}, u32[]{:S(2)}, u32[]{:S(2)}) collective-permute-start(f32[8256]{0:T(1024)S(1)} %add.283), channel_id=1, source_target_pairs={{0,8},{1,9},{2,10},{3,11},{4,12},{5,13},{6,14},{7,15},{8,0},{9,1},... | collective-permute-start | bytes 99080 | tf_op jit(solution)/shard_map/ppermute | solution.py:35
  191.5 5.8 %collective-permute-start.14 = (f32[8256]{0:T(1024)S(1)}, f32[8256]{0:T(1024)S(1)}, u32[]{:S(2)}, u32[]{:S(2)}) collective-permute-start(f32[8256]{0:T(1024)S(1)} %add.284), channel_id=1, source_target_pairs={{0,16},{16,0},{32,48},{48,32},{64,80},{80,64},{96,112},{112,96},{1... | collective-permute-start | bytes 99080 | tf_op jit(solution)/shard_map/ppermute | solution.py:35
  197.3 6.7 %collective-permute-start.15 = (f32[8256]{0:T(1024)S(1)}, f32[8256]{0:T(1024)S(1)}, u32[]{:S(2)}, u32[]{:S(2)}) collective-permute-start(f32[8256]{0:T(1024)S(1)} %add.285), channel_id=1, source_target_pairs={{0,32},{16,48},{32,0},{48,16},{64,96},{80,112},{96,64},{112,80},{1... | collective-permute-start | bytes 99080 | tf_op jit(solution)/shard_map/ppermute | solution.py:35
  204.1 10.2 %collective-permute-start.16 = (f32[8256]{0:T(1024)S(1)}, f32[8256]{0:T(1024)S(1)}, u32[]{:S(2)}, u32[]{:S(2)}) collective-permute-start(f32[8256]{0:T(1024)S(1)} %add.286), channel_id=1, source_target_pairs={{0,64},{16,80},{32,96},{48,112},{64,0},{80,16},{96,32},{112,48},{1... | collective-permute-start | bytes 99080 | tf_op jit(solution)/shard_map/ppermute | solution.py:35
  214.3 5.8 %collective-permute-start.17 = (f32[8256]{0:T(1024)S(1)}, f32[8256]{0:T(1024)S(1)}, u32[]{:S(2)}, u32[]{:S(2)}) collective-permute-start(f32[8256]{0:T(1024)S(1)} %add.287), channel_id=1, source_target_pairs={{0,128},{16,144},{32,160},{48,176},{64,192},{80,208},{96,224},{112... | collective-permute-start | bytes 99080 | tf_op jit(solution)/shard_map/ppermute | solution.py:35
  220.1 7.3 %collective-permute-start.18 = (f32[8256]{0:T(1024)S(1)}, f32[8256]{0:T(1024)S(1)}, u32[]{:S(2)}, u32[]{:S(2)}) collective-permute-start(f32[8256]{0:T(1024)S(1)} %add.288), channel_id=1, source_target_pairs={{0,256},{16,272},{32,288},{48,304},{64,320},{80,336},{96,352},{112... | collective-permute-start | bytes 99080 | tf_op jit(solution)/shard_map/ppermute | solution.py:35

commit v3 on v2

--- a/solution.py
+++ b/solution.py
@@ -12,22 +12,6 @@
 filter_degree = 4
 
 
-def padded_2(cells, sides, width):
-    for axis, dim in sides:
-        count = lax.axis_size(axis)
-        head = lax.slice_in_dim(cells, 0, width, axis=dim)
-        tail = lax.slice_in_dim(cells, cells.shape[dim] - width, cells.shape[dim], axis=dim)
-        cells = jnp.concatenate(
-            [
-                lax.ppermute(tail, axis, [(i, (i + 1) % count) for i in range(count)]),
-                cells,
-                lax.ppermute(head, axis, [((i + 1) % count, i) for i in range(count)]),
-            ],
-            axis=dim,
-        )
-    return cells
-
-
 def butterfly_sum(values, axis):
     count = lax.axis_size(axis)
     step = 1
@@ -37,31 +21,67 @@
     return values
 
 
+def widened(cells, width):
+    count = lax.axis_size("grid")
+    head = cells[:, :width]
+    tail = cells[:, cells.shape[1] - width :]
+    return jnp.concatenate(
+        [
+            lax.ppermute(tail, "grid", [(i, (i + 1) % count) for i in range(count)]),
+            cells,
+            lax.ppermute(head, "grid", [((i + 1) % count, i) for i in range(count)]),
+        ],
+        axis=1,
+    )
+
+
 def operate(field_in, potential):
-    padded = padded_2(field_in, (("grid", 1),), 2)
-    plane_count = field_in.shape[1]
-    near_sum = padded[:, 1 : 1 + plane_count] + padded[:, 3 : 3 + plane_count]
-    near_sum = near_sum + jnp.roll(field_in, 1, 2) + jnp.roll(field_in, -1, 2)
-    near_sum = near_sum + jnp.roll(field_in, 1, 3) + jnp.roll(field_in, -1, 3)
-    far_sum = padded[:, 0:plane_count] + padded[:, 4 : 4 + plane_count]
-    far_sum = far_sum + jnp.roll(field_in, 2, 2) + jnp.roll(field_in, -2, 2)
-    far_sum = far_sum + jnp.roll(field_in, 2, 3) + jnp.roll(field_in, -2, 3)
-    kinetic = 0.5 * (7.5 * field_in - FOUR_THIRDS * near_sum + TWELFTH * far_sum)
-    return kinetic + potential * field_in
+    plane_count = field_in.shape[1] - 4
+    centre = field_in[:, 2 : 2 + plane_count]
+    near_sum = field_in[:, 1 : 1 + plane_count] + field_in[:, 3 : 3 + plane_count]
+    near_sum = near_sum + jnp.roll(centre, 1, 2) + jnp.roll(centre, -1, 2)
+    near_sum = near_sum + jnp.roll(centre, 1, 3) + jnp.roll(centre, -1, 3)
+    far_sum = field_in[:, 0:plane_count] + field_in[:, 4 : 4 + plane_count]
+    far_sum = far_sum + jnp.roll(centre, 2, 2) + jnp.roll(centre, -2, 2)
+    far_sum = far_sum + jnp.roll(centre, 2, 3) + jnp.roll(centre, -2, 3)
+    kinetic = 0.5 * (7.5 * centre - FOUR_THIRDS * near_sum + TWELFTH * far_sum)
+    return kinetic + potential * centre
 
 
 def on_device(trial_bands, potential):
+    band_count, own_planes = trial_bands.shape[0], trial_bands.shape[1]
+    width = 2 * (filter_degree + 1)
+    payload = jnp.concatenate([trial_bands, potential[None]], axis=0)
+    wide = widened(payload, width)
+    wide_bands, wide_potential = wide[:band_count], wide[band_count]
+    offset = [0]
+
+    def step(field_in):
+        first = offset[0] + 2
+        result = operate(field_in, wide_potential[first : first + field_in.shape[1] - 4])
+        return result, first
+
+    def trim(values, at, first, count):
+        return values[:, first - at : first - at + count]
+
     sigma_now = SIGMA_ONE
-    previous = trial_bands
-    current = (operate(trial_bands, potential) - CENTER * trial_bands) * (SIGMA_ONE / HALF_WIDTH)
+    previous, previous_at = wide_bands, 0
+    image_in, first = step(wide_bands)
+    current = (image_in - CENTER * trim(wide_bands, 0, first, image_in.shape[1])) * (SIGMA_ONE / HALF_WIDTH)
+    current_at = first
     for repeat_index in range(filter_degree - 1):
         sigma_next = 1.0 / (2.0 / SIGMA_ONE - sigma_now)
-        following = (operate(current, potential) - CENTER * current) * (
+        offset[0] = current_at
+        image_in, first = step(current)
+        count = image_in.shape[1]
+        following = (image_in - CENTER * trim(current, current_at, first, count)) * (
             2.0 * sigma_next / HALF_WIDTH
-        ) - sigma_now * sigma_next * previous
-        previous, current, sigma_now = (current, following, sigma_next)
-    applied = operate(current, potential)
-    band_count = current.shape[0]
+        ) - sigma_now * sigma_next * trim(previous, previous_at, first, count)
+        previous, previous_at = current, current_at
+        current, current_at, sigma_now = following, first, sigma_next
+    offset[0] = current_at
+    applied, first = step(current)
+    current = trim(current, current_at, first, own_planes)
     band_devices = lax.axis_size("band")
     total_bands = band_count * band_devices
     cell_count = current.shape[1] * current.shape[2] * current.shape[3]

time: 242 us -> 183 us (0.76)
  starting transfers between devices: 111 us -> 58.5 us
  local copies, waits for them, and re-layouts: 14.8 us -> 9.45 us
  waiting for transfers between devices: 63.6 us -> 59.1 us
  other arithmetic: 17.6 us -> 21.2 us
    ppermute x10 -> x2, starting transfers between devices: 74.4 us -> 5.56 us  [the longest x1 3.64 us: widened(): lax.ppermute(head, 'grid', [((i + 1) % count, i) for i in range(count)])]
    ppermute x9, starting transfers between devices: 37 us -> 52.9 us  [butterfly_sum(): lax.ppermute(values, axis, [(i, i ^ step) for i in range(count)])]
    ppermute x10 -> x2, waiting for transfers between devices: 16.1 us -> 13.2 us  [the longest x1 8.61 us: widened(): lax.ppermute(head, 'grid', [((i + 1) % count, i) for i in range(count)])]
    slice x45 -> x38, local copies, waits for them, and re-layouts: 8.82 us -> 5.96 us  [the longest x10 2.32 us: operate(): near_sum = near_sum + jnp.roll(centre, 1, 3) + jnp.roll(centre, -1, 3)]
  transfers between devices with their start and end apart: 19 -> 11, of which waited for: 14 -> 11; matrix products, arithmetic and copies ran while one was open for 1% -> 0% of each run, Pallas kernels for 0% -> 0%
where the time goes in v3:
time: 183 us
  waiting for transfers between devices  59.1 us (32%)
  starting transfers between devices  58.5 us (32%)
  blocking collectives  31.9 us (17%)
  other arithmetic  21.2 us (12%)
  local copies, waits for them, and re-layouts  9.45 us (5%)
    ppermute x9, starting transfers between devices, butterfly_sum(): lax.ppermute(values, axis, [(i, i ^ step) for i in range(count)])  52.9 us
    ppermute x9, waiting for transfers between devices, butterfly_sum(): lax.ppermute(values, axis, [(i, i ^ step) for i in range(count)])  45.9 us
    all_to_all x1, blocking collectives, on_device(): moved = lax.all_to_all(both, 'band', 2, 1, tiled=True)  31.9 us
    ppermute x1, waiting for transfers between devices, widened(): lax.ppermute(head, 'grid', [((i + 1) % count, i) for i in range(count)])  8.61 us
    another operation x3, other arithmetic, on_device(): factor = jnp.linalg.cholesky(margin)  6.52 us
    another operation x2, other arithmetic, on_device(): lax.linalg.triangular_solve(factor, coefficients.T, left_side=True, lower...  5.55 us
    ppermute x1, waiting for transfers between devices, widened(): lax.ppermute(tail, 'grid', [(i, (i + 1) % count) for i in range(count)])  4.57 us
  transfers between devices with their start and end apart: 11, of which 11 were waited for; matrix products, arithmetic and copies ran while one was open for 0% of the time, Pallas kernels for 0%

profile of v3, /device:TPU:24, one launch (start us, length us, event | category | flops | bytes accessed | tf_op | source)
XLA Modules:
  0.0 182.7 jit_solution(14323409402619208073)
XLA Ops:
  0.6 1.1 pad_maximum_fusion.14
  1.7 1.9 %collective-permute-start = (f32[3,10,32,128]{3,2,1,0:T(8,128)S(1)}, f32[3,10,32,128]{3,2,1,0:T(8,128)S(1)}, u32[]{:S(2)}, u32[]{:S(2)}) collective-permute-start(f32[3,10,32,128]{3,2,1,0:T(8,128)S(1)} %pad_maximum_fusion.14), channel_id=1, source_target_pairs={{0,1},{1,2},{2,3},{3,4},{4,5},{5,6},{6,7},{7,8},{8,9},{9,10},{10,1... | collective-permute-start | bytes 1474568 | tf_op jit(solution)/shard_map/ppermute | solution.py:30
  3.7 3.6 %collective-permute-start.1 = (f32[3,10,32,128]{3,2,1,0:T(8,128)S(1)}, f32[3,10,32,128]{3,2,1,0:T(8,128)S(1)}, u32[]{:S(2)}, u32[]{:S(2)}) collective-permute-start(f32[3,10,32,128]{3,2,1,0:T(8,128)S(1)} %pad_maximum_fusion.14), channel_id=1, source_target_pairs={{1,0},{2,1},{3,2},{4,3},{5,4},{6,5},{7,6},{8,7},{9,8},{10,9},{11,1... | collective-permute-start | bytes 1474568 | tf_op jit(solution)/shard_map/ppermute | solution.py:32
  7.3 4.6 %collective-permute-done = f32[3,10,32,128]{3,2,1,0:T(8,128)S(1)} collective-permute-done((f32[3,10,32,128]{3,2,1,0:T(8,128)S(1)}, f32[3,10,32,128]{3,2,1,0:T(8,128)S(1)}, u32[]{:S(2)}, u32[]{:S(2)}) %collective-permute-start) | collective-permute-done | bytes 491552 | tf_op jit(solution)/shard_map/ppermute | solution.py:30
  11.9 8.6 %collective-permute-done.1 = f32[3,10,32,128]{3,2,1,0:T(8,128)S(1)} collective-permute-done((f32[3,10,32,128]{3,2,1,0:T(8,128)S(1)}, f32[3,10,32,128]{3,2,1,0:T(8,128)S(1)}, u32[]{:S(2)}, u32[]{:S(2)}) %collective-permute-start.1) | collective-permute-done | bytes 491552 | tf_op jit(solution)/shard_map/ppermute | solution.py:32
  20.5 1.2 pad_maximum_fusion
  24.0 2.3 %fusion.9 = f32[2,26,32,128]{3,2,1,0:T(8,128)S(1)} fusion(f32[3,10,32,128]{3,2,1,0:T(8,128)S(1)} %collective-permute-done.1, f32[3,10,32,128]{3,2,1,0:T(8,128)S(1)} %collective-permute-done, f32[1,10,32,128]{3,2,1,0:T(8,128)S(1)} %bitcast.49, f32[2,10,32,128]{3,2,1,0:T(8,128)S(1)} %copy-done, f32[3,30,32,128]{3,2,1,0:T(8,128)S(1)} %pad_maximum_fusion, ...), kind=kLoop, calls=%fused_computation.11 | loop fusion | flops 8732672 | bytes 13668352 | tf_op jit(solution)/shard_map/mul | solution.py:70
  27.8 1.4 fusion.20
  30.5 1.2 fusion.37
  32.7 0.9 fusion.54
  34.5 0.7 fusion.78
  35.9 31.9 %all_to_all.15 = f32[2,2,32,1280]{3,1,0,2:T(2,128)S(1)} all-to-all(f32[2,2,32,1280]{3,1,0,2:T(2,128)S(1)} %copy.10), channel_id=1, replica_groups=mesh['band'=32,'grid'=16] {'band'}, dimensions={2} | all-to-all | bytes 1310720 | tf_op jit(solution)/shard_map/all_to_all | solution.py:94
  69.7 34.3 %collective-permute-start.2 = (f32[8256]{0:T(1024)S(1)}, f32[8256]{0:T(1024)S(1)}, u32[]{:S(2)}, u32[]{:S(2)}) collective-permute-start(f32[8256]{0:T(1024)S(1)} %constant_dynamic-update-slice_fusion), channel_id=1, source_target_pairs={{0,1},{1,0},{2,3},{3,2},{4,5},{5,4},{6,7},{7,6},{8,9},{9,8},{10,11... | collective-permute-start | bytes 99080 | tf_op jit(solution)/shard_map/ppermute | solution.py:19
  104.0 0.8 collective-permute-done.2
  104.8 1.9 %collective-permute-start.3 = (f32[8256]{0:T(1024)S(1)}, f32[8256]{0:T(1024)S(1)}, u32[]{:S(2)}, u32[]{:S(2)}) collective-permute-start(f32[8256]{0:T(1024)S(1)} %add.281), channel_id=1, source_target_pairs={{0,2},{1,3},{2,0},{3,1},{4,6},{5,7},{6,4},{7,5},{8,10},{9,11},{10,... | collective-permute-start | bytes 99080 | tf_op jit(solution)/shard_map/ppermute | solution.py:19
  106.7 3.9 %collective-permute-done.3 = f32[8256]{0:T(1024)S(1)} collective-permute-done((f32[8256]{0:T(1024)S(1)}, f32[8256]{0:T(1024)S(1)}, u32[]{:S(2)}, u32[]{:S(2)}) %collective-permute-start.3) | collective-permute-done | bytes 33056 | tf_op jit(solution)/shard_map/ppermute | solution.py:19
  110.7 1.9 %collective-permute-start.4 = (f32[8256]{0:T(1024)S(1)}, f32[8256]{0:T(1024)S(1)}, u32[]{:S(2)}, u32[]{:S(2)}) collective-permute-start(f32[8256]{0:T(1024)S(1)} %add.282), channel_id=1, source_target_pairs={{0,4},{1,5},{2,6},{3,7},{4,0},{5,1},{6,2},{7,3},{8,12},{9,13},{10,... | collective-permute-start | bytes 99080 | tf_op jit(solution)/shard_map/ppermute | solution.py:19
  112.6 5.4 %collective-permute-done.4 = f32[8256]{0:T(1024)S(1)} collective-permute-done((f32[8256]{0:T(1024)S(1)}, f32[8256]{0:T(1024)S(1)}, u32[]{:S(2)}, u32[]{:S(2)}) %collective-permute-start.4) | collective-permute-done | bytes 33056 | tf_op jit(solution)/shard_map/ppermute | solution.py:19
  118.0 3.6 %collective-permute-start.5 = (f32[8256]{0:T(1024)S(1)}, f32[8256]{0:T(1024)S(1)}, u32[]{:S(2)}, u32[]{:S(2)}) collective-permute-start(f32[8256]{0:T(1024)S(1)} %add.283), channel_id=1, source_target_pairs={{0,8},{1,9},{2,10},{3,11},{4,12},{5,13},{6,14},{7,15},{8,0},{9,1},... | collective-permute-start | bytes 99080 | tf_op jit(solution)/shard_map/ppermute | solution.py:19
  121.6 11.1 %collective-permute-done.5 = f32[8256]{0:T(1024)S(1)} collective-permute-done((f32[8256]{0:T(1024)S(1)}, f32[8256]{0:T(1024)S(1)}, u32[]{:S(2)}, u32[]{:S(2)}) %collective-permute-start.5) | collective-permute-done | bytes 33056 | tf_op jit(solution)/shard_map/ppermute | solution.py:19
  132.7 1.9 %collective-permute-start.6 = (f32[8256]{0:T(1024)S(1)}, f32[8256]{0:T(1024)S(1)}, u32[]{:S(2)}, u32[]{:S(2)}) collective-permute-start(f32[8256]{0:T(1024)S(1)} %add.284), channel_id=1, source_target_pairs={{0,16},{16,0},{32,48},{48,32},{64,80},{80,64},{96,112},{112,96},{1... | collective-permute-start | bytes 99080 | tf_op jit(solution)/shard_map/ppermute | solution.py:19
  134.6 3.9 %collective-permute-done.6 = f32[8256]{0:T(1024)S(1)} collective-permute-done((f32[8256]{0:T(1024)S(1)}, f32[8256]{0:T(1024)S(1)}, u32[]{:S(2)}, u32[]{:S(2)}) %collective-permute-start.6) | collective-permute-done | bytes 33056 | tf_op jit(solution)/shard_map/ppermute | solution.py:19
  138.5 2.3 %collective-permute-start.7 = (f32[8256]{0:T(1024)S(1)}, f32[8256]{0:T(1024)S(1)}, u32[]{:S(2)}, u32[]{:S(2)}) collective-permute-start(f32[8256]{0:T(1024)S(1)} %add.285), channel_id=1, source_target_pairs={{0,32},{16,48},{32,0},{48,16},{64,96},{80,112},{96,64},{112,80},{1... | collective-permute-start | bytes 99080 | tf_op jit(solution)/shard_map/ppermute | solution.py:19
  140.8 4.5 %collective-permute-done.7 = f32[8256]{0:T(1024)S(1)} collective-permute-done((f32[8256]{0:T(1024)S(1)}, f32[8256]{0:T(1024)S(1)}, u32[]{:S(2)}, u32[]{:S(2)}) %collective-permute-start.7) | collective-permute-done | bytes 33056 | tf_op jit(solution)/shard_map/ppermute | solution.py:19
  145.3 1.9 %collective-permute-start.8 = (f32[8256]{0:T(1024)S(1)}, f32[8256]{0:T(1024)S(1)}, u32[]{:S(2)}, u32[]{:S(2)}) collective-permute-start(f32[8256]{0:T(1024)S(1)} %add.286), channel_id=1, source_target_pairs={{0,64},{16,80},{32,96},{48,112},{64,0},{80,16},{96,32},{112,48},{1... | collective-permute-start | bytes 99080 | tf_op jit(solution)/shard_map/ppermute | solution.py:19
  147.2 8.3 %collective-permute-done.8 = f32[8256]{0:T(1024)S(1)} collective-permute-done((f32[8256]{0:T(1024)S(1)}, f32[8256]{0:T(1024)S(1)}, u32[]{:S(2)}, u32[]{:S(2)}) %collective-permute-start.8) | collective-permute-done | bytes 33056 | tf_op jit(solution)/shard_map/ppermute | solution.py:19
  155.5 1.9 %collective-permute-start.9 = (f32[8256]{0:T(1024)S(1)}, f32[8256]{0:T(1024)S(1)}, u32[]{:S(2)}, u32[]{:S(2)}) collective-permute-start(f32[8256]{0:T(1024)S(1)} %add.287), channel_id=1, source_target_pairs={{0,128},{16,144},{32,160},{48,176},{64,192},{80,208},{96,224},{112... | collective-permute-start | bytes 99080 | tf_op jit(solution)/shard_map/ppermute | solution.py:19
  157.4 3.9 %collective-permute-done.9 = f32[8256]{0:T(1024)S(1)} collective-permute-done((f32[8256]{0:T(1024)S(1)}, f32[8256]{0:T(1024)S(1)}, u32[]{:S(2)}, u32[]{:S(2)}) %collective-permute-start.9) | collective-permute-done | bytes 33056 | tf_op jit(solution)/shard_map/ppermute | solution.py:19
  161.3 3.2 %collective-permute-start.10 = (f32[8256]{0:T(1024)S(1)}, f32[8256]{0:T(1024)S(1)}, u32[]{:S(2)}, u32[]{:S(2)}) collective-permute-start(f32[8256]{0:T(1024)S(1)} %add.288), channel_id=1, source_target_pairs={{0,256},{16,272},{32,288},{48,304},{64,320},{80,336},{96,352},{112... | collective-permute-start | bytes 99080 | tf_op jit(solution)/shard_map/ppermute | solution.py:19
  164.6 4.1 %collective-permute-done.10 = f32[8256]{0:T(1024)S(1)} collective-permute-done((f32[8256]{0:T(1024)S(1)}, f32[8256]{0:T(1024)S(1)}, u32[]{:S(2)}, u32[]{:S(2)}) %collective-permute-start.10) | collective-permute-done | bytes 33056 | tf_op jit(solution)/shard_map/ppermute | solution.py:19
  168.9 5.8 %cholesky.18 = f32[64,64]{1,0:T(8,128)S(1)} custom-call(f32[64,64]{1,0:T(8,128)S(1)} %fusion.92), custom_call_target="Cholesky" | custom-call | tf_op jit(solution)/shard_map/jit(cholesky)/cholesky | solution.py:110
  176.0 4.9 %custom-call.8 = f32[1,64,64]{1,2,0:T(8,128)S(1)} custom-call(f32[1,64,64]{2,1,0:T(8,128)S(1)} %fusion.85), custom_call_target="InvertDiagBlocksLowerTriangular" | custom-call | tf_op jit(solution)/shard_map/triangular_solve/custom-call.0 | solution.py:112
  (85 shorter events, 12.5 us)
Async XLA Ops:
  1.7 10.1 %collective-permute-start = (f32[3,10,32,128]{3,2,1,0:T(8,128)S(1)}, f32[3,10,32,128]{3,2,1,0:T(8,128)S(1)}, u32[]{:S(2)}, u32[]{:S(2)}) collective-permute-start(f32[3,10,32,128]{3,2,1,0:T(8,128)S(1)} %pad_maximum_fusion.14), channel_id=1, source_target_pairs={{0,1},{1,2},{2,3},{3,4},{4,5},{5,6},{6,7},{7,8},{8,9},{9,10},{10,1... | collective-permute-start | bytes 1474568 | tf_op jit(solution)/shard_map/ppermute | solution.py:30
  3.7 16.8 %collective-permute-start.1 = (f32[3,10,32,128]{3,2,1,0:T(8,128)S(1)}, f32[3,10,32,128]{3,2,1,0:T(8,128)S(1)}, u32[]{:S(2)}, u32[]{:S(2)}) collective-permute-start(f32[3,10,32,128]{3,2,1,0:T(8,128)S(1)} %pad_maximum_fusion.14), channel_id=1, source_target_pairs={{1,0},{2,1},{3,2},{4,3},{5,4},{6,5},{7,6},{8,7},{9,8},{10,9},{11,1... | collective-permute-start | bytes 1474568 | tf_op jit(solution)/shard_map/ppermute | solution.py:32
  23.0 1.0 copy-start
  23.0 1.0 copy-start.1
  35.2 0.7 copy-start.2
  69.7 35.1 %collective-permute-start.2 = (f32[8256]{0:T(1024)S(1)}, f32[8256]{0:T(1024)S(1)}, u32[]{:S(2)}, u32[]{:S(2)}) collective-permute-start(f32[8256]{0:T(1024)S(1)} %constant_dynamic-update-slice_fusion), channel_id=1, source_target_pairs={{0,1},{1,0},{2,3},{3,2},{4,5},{5,4},{6,7},{7,6},{8,9},{9,8},{10,11... | collective-permute-start | bytes 99080 | tf_op jit(solution)/shard_map/ppermute | solution.py:19
  104.8 5.8 %collective-permute-start.3 = (f32[8256]{0:T(1024)S(1)}, f32[8256]{0:T(1024)S(1)}, u32[]{:S(2)}, u32[]{:S(2)}) collective-permute-start(f32[8256]{0:T(1024)S(1)} %add.281), channel_id=1, source_target_pairs={{0,2},{1,3},{2,0},{3,1},{4,6},{5,7},{6,4},{7,5},{8,10},{9,11},{10,... | collective-permute-start | bytes 99080 | tf_op jit(solution)/shard_map/ppermute | solution.py:19
  110.7 7.3 %collective-permute-start.4 = (f32[8256]{0:T(1024)S(1)}, f32[8256]{0:T(1024)S(1)}, u32[]{:S(2)}, u32[]{:S(2)}) collective-permute-start(f32[8256]{0:T(1024)S(1)} %add.282), channel_id=1, source_target_pairs={{0,4},{1,5},{2,6},{3,7},{4,0},{5,1},{6,2},{7,3},{8,12},{9,13},{10,... | collective-permute-start | bytes 99080 | tf_op jit(solution)/shard_map/ppermute | solution.py:19
  118.0 14.7 %collective-permute-start.5 = (f32[8256]{0:T(1024)S(1)}, f32[8256]{0:T(1024)S(1)}, u32[]{:S(2)}, u32[]{:S(2)}) collective-permute-start(f32[8256]{0:T(1024)S(1)} %add.283), channel_id=1, source_target_pairs={{0,8},{1,9},{2,10},{3,11},{4,12},{5,13},{6,14},{7,15},{8,0},{9,1},... | collective-permute-start | bytes 99080 | tf_op jit(solution)/shard_map/ppermute | solution.py:19
  132.7 5.8 %collective-permute-start.6 = (f32[8256]{0:T(1024)S(1)}, f32[8256]{0:T(1024)S(1)}, u32[]{:S(2)}, u32[]{:S(2)}) collective-permute-start(f32[8256]{0:T(1024)S(1)} %add.284), channel_id=1, source_target_pairs={{0,16},{16,0},{32,48},{48,32},{64,80},{80,64},{96,112},{112,96},{1... | collective-permute-start | bytes 99080 | tf_op jit(solution)/shard_map/ppermute | solution.py:19
  138.5 6.7 %collective-permute-start.7 = (f32[8256]{0:T(1024)S(1)}, f32[8256]{0:T(1024)S(1)}, u32[]{:S(2)}, u32[]{:S(2)}) collective-permute-start(f32[8256]{0:T(1024)S(1)} %add.285), channel_id=1, source_target_pairs={{0,32},{16,48},{32,0},{48,16},{64,96},{80,112},{96,64},{112,80},{1... | collective-permute-start | bytes 99080 | tf_op jit(solution)/shard_map/ppermute | solution.py:19
  145.3 10.2 %collective-permute-start.8 = (f32[8256]{0:T(1024)S(1)}, f32[8256]{0:T(1024)S(1)}, u32[]{:S(2)}, u32[]{:S(2)}) collective-permute-start(f32[8256]{0:T(1024)S(1)} %add.286), channel_id=1, source_target_pairs={{0,64},{16,80},{32,96},{48,112},{64,0},{80,16},{96,32},{112,48},{1... | collective-permute-start | bytes 99080 | tf_op jit(solution)/shard_map/ppermute | solution.py:19
  155.5 5.8 %collective-permute-start.9 = (f32[8256]{0:T(1024)S(1)}, f32[8256]{0:T(1024)S(1)}, u32[]{:S(2)}, u32[]{:S(2)}) collective-permute-start(f32[8256]{0:T(1024)S(1)} %add.287), channel_id=1, source_target_pairs={{0,128},{16,144},{32,160},{48,176},{64,192},{80,208},{96,224},{112... | collective-permute-start | bytes 99080 | tf_op jit(solution)/shard_map/ppermute | solution.py:19
  161.3 7.3 %collective-permute-start.10 = (f32[8256]{0:T(1024)S(1)}, f32[8256]{0:T(1024)S(1)}, u32[]{:S(2)}, u32[]{:S(2)}) collective-permute-start(f32[8256]{0:T(1024)S(1)} %add.288), channel_id=1, source_target_pairs={{0,256},{16,272},{32,288},{48,304},{64,320},{80,336},{96,352},{112... | collective-permute-start | bytes 99080 | tf_op jit(solution)/shard_map/ppermute | solution.py:19

commit v4 on v3

--- a/solution.py
+++ b/solution.py
@@ -12,13 +12,24 @@
 filter_degree = 4
 
 
-def butterfly_sum(values, axis):
+def butterfly_sum(values, axis, partner_rounds):
     count = lax.axis_size(axis)
-    step = 1
-    while step < count:
-        values = values + lax.ppermute(values, axis, [(i, i ^ step) for i in range(count)])
-        step *= 2
+    for partner in partner_rounds:
+        pairs = [(i, partner(i)) for i in range(count)]
+        values = values + lax.ppermute(values, axis, pairs)
     return values
+
+
+def flip(bit):
+    return lambda i: i ^ bit
+
+
+def ring_of_four(low, stride):
+    def partner(i):
+        place = (i // stride) % 4
+        return i + (3 - 2 * place) * stride
+
+    return partner
 
 
 def widened(cells, width):
@@ -102,7 +113,9 @@
     )
     norm_part = jnp.sum(image_here * image_here, axis=1)
     packed = jnp.concatenate([margin_part.reshape(-1), image_part.reshape(-1), norm_part])
-    packed = butterfly_sum(butterfly_sum(packed, "grid"), "band") * inverse_cells
+    packed = butterfly_sum(packed, "grid", [flip(1), flip(2), ring_of_four(0, 2), flip(8)])
+    packed = butterfly_sum(packed, "band", [flip(1), flip(2), flip(4), flip(8), ring_of_four(0, 8)])
+    packed = packed * inverse_cells
     square = total_bands * total_bands
     margin = packed[:square].reshape(total_bands, total_bands)
     subspace = packed[square : 2 * square].reshape(total_bands, total_bands)

time: 183 us -> 183 us (level)
  no operation moved by 1% of the time
where the time goes in v4:
time: 183 us; the launch traced here: 182 us
  waiting for transfers between devices  59.3 us (32%)
  starting transfers between devices  57.7 us (32%)
  blocking collectives  31.9 us (17%)
  other arithmetic  21.2 us (12%)
  local copies, waits for them, and re-layouts  9.45 us (5%)
    ppermute x9, starting transfers between devices, butterfly_sum(): values = values + lax.ppermute(values, axis, pairs)  52.1 us
    ppermute x9, waiting for transfers between devices, butterfly_sum(): values = values + lax.ppermute(values, axis, pairs)  46.2 us
    all_to_all x1, blocking collectives, on_device(): moved = lax.all_to_all(both, 'band', 2, 1, tiled=True)  31.9 us
    ppermute x1, waiting for transfers between devices, widened(): lax.ppermute(head, 'grid', [((i + 1) % count, i) for i in range(count)])  8.61 us
    another operation x3, other arithmetic, on_device(): factor = jnp.linalg.cholesky(margin)  6.52 us
    another operation x2, other arithmetic, on_device(): lax.linalg.triangular_solve(factor, coefficients.T, left_side=True, lower...  5.55 us
    ppermute x1, waiting for transfers between devices, widened(): lax.ppermute(tail, 'grid', [(i, (i + 1) % count) for i in range(count)])  4.57 us
  transfers between devices with their start and end apart: 11, of which 11 were waited for; matrix products, arithmetic and copies ran while one was open for 0% of the time, Pallas kernels for 0%

profile of v4, /device:TPU:24, one launch (start us, length us, event | category | flops | bytes accessed | tf_op | source)
XLA Modules:
  0.0 182.1 jit_solution(17271284618675652617)
XLA Ops:
  0.6 1.1 pad_maximum_fusion.14
  1.7 1.9 %collective-permute-start = (f32[3,10,32,128]{3,2,1,0:T(8,128)S(1)}, f32[3,10,32,128]{3,2,1,0:T(8,128)S(1)}, u32[]{:S(2)}, u32[]{:S(2)}) collective-permute-start(f32[3,10,32,128]{3,2,1,0:T(8,128)S(1)} %pad_maximum_fusion.14), channel_id=1, source_target_pairs={{0,1},{1,2},{2,3},{3,4},{4,5},{5,6},{6,7},{7,8},{8,9},{9,10},{10,1... | collective-permute-start | bytes 1474568 | tf_op jit(solution)/shard_map/ppermute | solution.py:41
  3.7 3.6 %collective-permute-start.1 = (f32[3,10,32,128]{3,2,1,0:T(8,128)S(1)}, f32[3,10,32,128]{3,2,1,0:T(8,128)S(1)}, u32[]{:S(2)}, u32[]{:S(2)}) collective-permute-start(f32[3,10,32,128]{3,2,1,0:T(8,128)S(1)} %pad_maximum_fusion.14), channel_id=1, source_target_pairs={{1,0},{2,1},{3,2},{4,3},{5,4},{6,5},{7,6},{8,7},{9,8},{10,9},{11,1... | collective-permute-start | bytes 1474568 | tf_op jit(solution)/shard_map/ppermute | solution.py:43
  7.3 4.6 %collective-permute-done = f32[3,10,32,128]{3,2,1,0:T(8,128)S(1)} collective-permute-done((f32[3,10,32,128]{3,2,1,0:T(8,128)S(1)}, f32[3,10,32,128]{3,2,1,0:T(8,128)S(1)}, u32[]{:S(2)}, u32[]{:S(2)}) %collective-permute-start) | collective-permute-done | bytes 491552 | tf_op jit(solution)/shard_map/ppermute | solution.py:41
  11.9 8.6 %collective-permute-done.1 = f32[3,10,32,128]{3,2,1,0:T(8,128)S(1)} collective-permute-done((f32[3,10,32,128]{3,2,1,0:T(8,128)S(1)}, f32[3,10,32,128]{3,2,1,0:T(8,128)S(1)}, u32[]{:S(2)}, u32[]{:S(2)}) %collective-permute-start.1) | collective-permute-done | bytes 491552 | tf_op jit(solution)/shard_map/ppermute | solution.py:43
  20.5 1.2 pad_maximum_fusion
  24.0 2.3 %fusion.9 = f32[2,26,32,128]{3,2,1,0:T(8,128)S(1)} fusion(f32[3,10,32,128]{3,2,1,0:T(8,128)S(1)} %collective-permute-done.1, f32[3,10,32,128]{3,2,1,0:T(8,128)S(1)} %collective-permute-done, f32[1,10,32,128]{3,2,1,0:T(8,128)S(1)} %bitcast.49, f32[2,10,32,128]{3,2,1,0:T(8,128)S(1)} %copy-done, f32[3,30,32,128]{3,2,1,0:T(8,128)S(1)} %pad_maximum_fusion, ...), kind=kLoop, calls=%fused_computation.11 | loop fusion | flops 8732672 | bytes 13668352 | tf_op jit(solution)/shard_map/mul | solution.py:81
  27.8 1.4 fusion.20
  30.5 1.2 fusion.37
  32.7 0.9 fusion.54
  34.5 0.7 fusion.78
  35.9 31.9 %all_to_all.15 = f32[2,2,32,1280]{3,1,0,2:T(2,128)S(1)} all-to-all(f32[2,2,32,1280]{3,1,0,2:T(2,128)S(1)} %copy.10), channel_id=1, replica_groups=mesh['band'=32,'grid'=16] {'band'}, dimensions={2} | all-to-all | bytes 1310720 | tf_op jit(solution)/shard_map/all_to_all | solution.py:105
  69.7 34.3 %collective-permute-start.2 = (f32[8256]{0:T(1024)S(1)}, f32[8256]{0:T(1024)S(1)}, u32[]{:S(2)}, u32[]{:S(2)}) collective-permute-start(f32[8256]{0:T(1024)S(1)} %constant_dynamic-update-slice_fusion), channel_id=1, source_target_pairs={{0,1},{1,0},{2,3},{3,2},{4,5},{5,4},{6,7},{7,6},{8,9},{9,8},{10,11... | collective-permute-start | bytes 99080 | tf_op jit(solution)/shard_map/ppermute | solution.py:19
  104.0 0.8 collective-permute-done.2
  104.8 1.9 %collective-permute-start.3 = (f32[8256]{0:T(1024)S(1)}, f32[8256]{0:T(1024)S(1)}, u32[]{:S(2)}, u32[]{:S(2)}) collective-permute-start(f32[8256]{0:T(1024)S(1)} %add.281), channel_id=1, source_target_pairs={{0,2},{1,3},{2,0},{3,1},{4,6},{5,7},{6,4},{7,5},{8,10},{9,11},{10,... | collective-permute-start | bytes 99080 | tf_op jit(solution)/shard_map/ppermute | solution.py:19
  106.7 3.9 %collective-permute-done.3 = f32[8256]{0:T(1024)S(1)} collective-permute-done((f32[8256]{0:T(1024)S(1)}, f32[8256]{0:T(1024)S(1)}, u32[]{:S(2)}, u32[]{:S(2)}) %collective-permute-start.3) | collective-permute-done | bytes 33056 | tf_op jit(solution)/shard_map/ppermute | solution.py:19
  110.7 1.9 %collective-permute-start.4 = (f32[8256]{0:T(1024)S(1)}, f32[8256]{0:T(1024)S(1)}, u32[]{:S(2)}, u32[]{:S(2)}) collective-permute-start(f32[8256]{0:T(1024)S(1)} %add.282), channel_id=1, source_target_pairs={{0,6},{1,7},{2,4},{3,5},{4,2},{5,3},{6,0},{7,1},{8,14},{9,15},{10,... | collective-permute-start | bytes 99080 | tf_op jit(solution)/shard_map/ppermute | solution.py:19
  112.6 5.1 %collective-permute-done.4 = f32[8256]{0:T(1024)S(1)} collective-permute-done((f32[8256]{0:T(1024)S(1)}, f32[8256]{0:T(1024)S(1)}, u32[]{:S(2)}, u32[]{:S(2)}) %collective-permute-start.4) | collective-permute-done | bytes 33056 | tf_op jit(solution)/shard_map/ppermute | solution.py:19
  117.7 3.6 %collective-permute-start.5 = (f32[8256]{0:T(1024)S(1)}, f32[8256]{0:T(1024)S(1)}, u32[]{:S(2)}, u32[]{:S(2)}) collective-permute-start(f32[8256]{0:T(1024)S(1)} %add.283), channel_id=1, source_target_pairs={{0,8},{1,9},{2,10},{3,11},{4,12},{5,13},{6,14},{7,15},{8,0},{9,1},... | collective-permute-start | bytes 99080 | tf_op jit(solution)/shard_map/ppermute | solution.py:19
  121.3 11.1 %collective-permute-done.5 = f32[8256]{0:T(1024)S(1)} collective-permute-done((f32[8256]{0:T(1024)S(1)}, f32[8256]{0:T(1024)S(1)}, u32[]{:S(2)}, u32[]{:S(2)}) %collective-permute-start.5) | collective-permute-done | bytes 33056 | tf_op jit(solution)/shard_map/ppermute | solution.py:19
  132.4 1.9 %collective-permute-start.6 = (f32[8256]{0:T(1024)S(1)}, f32[8256]{0:T(1024)S(1)}, u32[]{:S(2)}, u32[]{:S(2)}) collective-permute-start(f32[8256]{0:T(1024)S(1)} %add.284), channel_id=1, source_target_pairs={{0,16},{16,0},{32,48},{48,32},{64,80},{80,64},{96,112},{112,96},{1... | collective-permute-start | bytes 99080 | tf_op jit(solution)/shard_map/ppermute | solution.py:19
  134.3 3.9 %collective-permute-done.6 = f32[8256]{0:T(1024)S(1)} collective-permute-done((f32[8256]{0:T(1024)S(1)}, f32[8256]{0:T(1024)S(1)}, u32[]{:S(2)}, u32[]{:S(2)}) %collective-permute-start.6) | collective-permute-done | bytes 33056 | tf_op jit(solution)/shard_map/ppermute | solution.py:19
  138.2 2.3 %collective-permute-start.7 = (f32[8256]{0:T(1024)S(1)}, f32[8256]{0:T(1024)S(1)}, u32[]{:S(2)}, u32[]{:S(2)}) collective-permute-start(f32[8256]{0:T(1024)S(1)} %add.285), channel_id=1, source_target_pairs={{0,32},{16,48},{32,0},{48,16},{64,96},{80,112},{96,64},{112,80},{1... | collective-permute-start | bytes 99080 | tf_op jit(solution)/shard_map/ppermute | solution.py:19
  140.5 4.5 %collective-permute-done.7 = f32[8256]{0:T(1024)S(1)} collective-permute-done((f32[8256]{0:T(1024)S(1)}, f32[8256]{0:T(1024)S(1)}, u32[]{:S(2)}, u32[]{:S(2)}) %collective-permute-start.7) | collective-permute-done | bytes 33056 | tf_op jit(solution)/shard_map/ppermute | solution.py:19
  145.0 1.9 %collective-permute-start.8 = (f32[8256]{0:T(1024)S(1)}, f32[8256]{0:T(1024)S(1)}, u32[]{:S(2)}, u32[]{:S(2)}) collective-permute-start(f32[8256]{0:T(1024)S(1)} %add.286), channel_id=1, source_target_pairs={{0,64},{16,80},{32,96},{48,112},{64,0},{80,16},{96,32},{112,48},{1... | collective-permute-start | bytes 99080 | tf_op jit(solution)/shard_map/ppermute | solution.py:19
  146.9 8.3 %collective-permute-done.8 = f32[8256]{0:T(1024)S(1)} collective-permute-done((f32[8256]{0:T(1024)S(1)}, f32[8256]{0:T(1024)S(1)}, u32[]{:S(2)}, u32[]{:S(2)}) %collective-permute-start.8) | collective-permute-done | bytes 33056 | tf_op jit(solution)/shard_map/ppermute | solution.py:19
  155.2 1.9 %collective-permute-start.9 = (f32[8256]{0:T(1024)S(1)}, f32[8256]{0:T(1024)S(1)}, u32[]{:S(2)}, u32[]{:S(2)}) collective-permute-start(f32[8256]{0:T(1024)S(1)} %add.287), channel_id=1, source_target_pairs={{0,128},{16,144},{32,160},{48,176},{64,192},{80,208},{96,224},{112... | collective-permute-start | bytes 99080 | tf_op jit(solution)/shard_map/ppermute | solution.py:19
  157.1 3.9 %collective-permute-done.9 = f32[8256]{0:T(1024)S(1)} collective-permute-done((f32[8256]{0:T(1024)S(1)}, f32[8256]{0:T(1024)S(1)}, u32[]{:S(2)}, u32[]{:S(2)}) %collective-permute-start.9) | collective-permute-done | bytes 33056 | tf_op jit(solution)/shard_map/ppermute | solution.py:19
  161.0 2.4 %collective-permute-start.10 = (f32[8256]{0:T(1024)S(1)}, f32[8256]{0:T(1024)S(1)}, u32[]{:S(2)}, u32[]{:S(2)}) collective-permute-start(f32[8256]{0:T(1024)S(1)} %add.288), channel_id=1, source_target_pairs={{0,384},{16,400},{32,416},{48,432},{64,448},{80,464},{96,480},{112... | collective-permute-start | bytes 99080 | tf_op jit(solution)/shard_map/ppermute | solution.py:19
  163.5 4.6 %collective-permute-done.10 = f32[8256]{0:T(1024)S(1)} collective-permute-done((f32[8256]{0:T(1024)S(1)}, f32[8256]{0:T(1024)S(1)}, u32[]{:S(2)}, u32[]{:S(2)}) %collective-permute-start.10) | collective-permute-done | bytes 33056 | tf_op jit(solution)/shard_map/ppermute | solution.py:19
  168.3 5.8 %cholesky.18 = f32[64,64]{1,0:T(8,128)S(1)} custom-call(f32[64,64]{1,0:T(8,128)S(1)} %fusion.92), custom_call_target="Cholesky" | custom-call | tf_op jit(solution)/shard_map/jit(cholesky)/cholesky | solution.py:123
  175.5 4.9 %custom-call.8 = f32[1,64,64]{1,2,0:T(8,128)S(1)} custom-call(f32[1,64,64]{2,1,0:T(8,128)S(1)} %fusion.85), custom_call_target="InvertDiagBlocksLowerTriangular" | custom-call | tf_op jit(solution)/shard_map/triangular_solve/custom-call.0 | solution.py:125
  (85 shorter events, 12.5 us)
Async XLA Ops:
  1.7 10.1 %collective-permute-start = (f32[3,10,32,128]{3,2,1,0:T(8,128)S(1)}, f32[3,10,32,128]{3,2,1,0:T(8,128)S(1)}, u32[]{:S(2)}, u32[]{:S(2)}) collective-permute-start(f32[3,10,32,128]{3,2,1,0:T(8,128)S(1)} %pad_maximum_fusion.14), channel_id=1, source_target_pairs={{0,1},{1,2},{2,3},{3,4},{4,5},{5,6},{6,7},{7,8},{8,9},{9,10},{10,1... | collective-permute-start | bytes 1474568 | tf_op jit(solution)/shard_map/ppermute | solution.py:41
  3.7 16.8 %collective-permute-start.1 = (f32[3,10,32,128]{3,2,1,0:T(8,128)S(1)}, f32[3,10,32,128]{3,2,1,0:T(8,128)S(1)}, u32[]{:S(2)}, u32[]{:S(2)}) collective-permute-start(f32[3,10,32,128]{3,2,1,0:T(8,128)S(1)} %pad_maximum_fusion.14), channel_id=1, source_target_pairs={{1,0},{2,1},{3,2},{4,3},{5,4},{6,5},{7,6},{8,7},{9,8},{10,9},{11,1... | collective-permute-start | bytes 1474568 | tf_op jit(solution)/shard_map/ppermute | solution.py:43
  23.0 1.0 copy-start
  23.0 1.0 copy-start.1
  35.2 0.7 copy-start.2
  69.7 35.1 %collective-permute-start.2 = (f32[8256]{0:T(1024)S(1)}, f32[8256]{0:T(1024)S(1)}, u32[]{:S(2)}, u32[]{:S(2)}) collective-permute-start(f32[8256]{0:T(1024)S(1)} %constant_dynamic-update-slice_fusion), channel_id=1, source_target_pairs={{0,1},{1,0},{2,3},{3,2},{4,5},{5,4},{6,7},{7,6},{8,9},{9,8},{10,11... | collective-permute-start | bytes 99080 | tf_op jit(solution)/shard_map/ppermute | solution.py:19
  104.8 5.8 %collective-permute-start.3 = (f32[8256]{0:T(1024)S(1)}, f32[8256]{0:T(1024)S(1)}, u32[]{:S(2)}, u32[]{:S(2)}) collective-permute-start(f32[8256]{0:T(1024)S(1)} %add.281), channel_id=1, source_target_pairs={{0,2},{1,3},{2,0},{3,1},{4,6},{5,7},{6,4},{7,5},{8,10},{9,11},{10,... | collective-permute-start | bytes 99080 | tf_op jit(solution)/shard_map/ppermute | solution.py:19
  110.7 7.1 %collective-permute-start.4 = (f32[8256]{0:T(1024)S(1)}, f32[8256]{0:T(1024)S(1)}, u32[]{:S(2)}, u32[]{:S(2)}) collective-permute-start(f32[8256]{0:T(1024)S(1)} %add.282), channel_id=1, source_target_pairs={{0,6},{1,7},{2,4},{3,5},{4,2},{5,3},{6,0},{7,1},{8,14},{9,15},{10,... | collective-permute-start | bytes 99080 | tf_op jit(solution)/shard_map/ppermute | solution.py:19
  117.7 14.7 %collective-permute-start.5 = (f32[8256]{0:T(1024)S(1)}, f32[8256]{0:T(1024)S(1)}, u32[]{:S(2)}, u32[]{:S(2)}) collective-permute-start(f32[8256]{0:T(1024)S(1)} %add.283), channel_id=1, source_target_pairs={{0,8},{1,9},{2,10},{3,11},{4,12},{5,13},{6,14},{7,15},{8,0},{9,1},... | collective-permute-start | bytes 99080 | tf_op jit(solution)/shard_map/ppermute | solution.py:19
  132.4 5.8 %collective-permute-start.6 = (f32[8256]{0:T(1024)S(1)}, f32[8256]{0:T(1024)S(1)}, u32[]{:S(2)}, u32[]{:S(2)}) collective-permute-start(f32[8256]{0:T(1024)S(1)} %add.284), channel_id=1, source_target_pairs={{0,16},{16,0},{32,48},{48,32},{64,80},{80,64},{96,112},{112,96},{1... | collective-permute-start | bytes 99080 | tf_op jit(solution)/shard_map/ppermute | solution.py:19
  138.2 6.7 %collective-permute-start.7 = (f32[8256]{0:T(1024)S(1)}, f32[8256]{0:T(1024)S(1)}, u32[]{:S(2)}, u32[]{:S(2)}) collective-permute-start(f32[8256]{0:T(1024)S(1)} %add.285), channel_id=1, source_target_pairs={{0,32},{16,48},{32,0},{48,16},{64,96},{80,112},{96,64},{112,80},{1... | collective-permute-start | bytes 99080 | tf_op jit(solution)/shard_map/ppermute | solution.py:19
  145.0 10.2 %collective-permute-start.8 = (f32[8256]{0:T(1024)S(1)}, f32[8256]{0:T(1024)S(1)}, u32[]{:S(2)}, u32[]{:S(2)}) collective-permute-start(f32[8256]{0:T(1024)S(1)} %add.286), channel_id=1, source_target_pairs={{0,64},{16,80},{32,96},{48,112},{64,0},{80,16},{96,32},{112,48},{1... | collective-permute-start | bytes 99080 | tf_op jit(solution)/shard_map/ppermute | solution.py:19
  155.2 5.8 %collective-permute-start.9 = (f32[8256]{0:T(1024)S(1)}, f32[8256]{0:T(1024)S(1)}, u32[]{:S(2)}, u32[]{:S(2)}) collective-permute-start(f32[8256]{0:T(1024)S(1)} %add.287), channel_id=1, source_target_pairs={{0,128},{16,144},{32,160},{48,176},{64,192},{80,208},{96,224},{112... | collective-permute-start | bytes 99080 | tf_op jit(solution)/shard_map/ppermute | solution.py:19
  161.0 7.1 %collective-permute-start.10 = (f32[8256]{0:T(1024)S(1)}, f32[8256]{0:T(1024)S(1)}, u32[]{:S(2)}, u32[]{:S(2)}) collective-permute-start(f32[8256]{0:T(1024)S(1)} %add.288), channel_id=1, source_target_pairs={{0,384},{16,400},{32,416},{48,432},{64,448},{80,464},{96,480},{112... | collective-permute-start | bytes 99080 | tf_op jit(solution)/shard_map/ppermute | solution.py:19

commit v5 on v4

--- a/solution.py
+++ b/solution.py
@@ -1,6 +1,8 @@
 import jax
 import jax.numpy as jnp
 from jax import lax
+from jax.experimental import pallas as pl
+from jax.experimental.pallas import tpu as pltpu
 from jax.sharding import PartitionSpec as P
 
 CENTER = 4.25
@@ -32,67 +34,81 @@
     return partner
 
 
-def widened(cells, width):
-    count = lax.axis_size("grid")
-    head = cells[:, :width]
-    tail = cells[:, cells.shape[1] - width :]
-    return jnp.concatenate(
-        [
-            lax.ppermute(tail, "grid", [(i, (i + 1) % count) for i in range(count)]),
-            cells,
-            lax.ppermute(head, "grid", [((i + 1) % count, i) for i in range(count)]),
-        ],
-        axis=1,
-    )
+def filter_kernel(below_ref, own_ref, above_ref, filtered_ref, image_ref, first_buf, second_buf, third_buf, wide_pot):
+    band_count, own_planes = filtered_ref.shape[0], filtered_ref.shape[1]
+    width = below_ref.shape[1]
+    for at, source in ((0, below_ref), (width, own_ref), (width + own_planes, above_ref)):
+        first_buf[:, at : at + source.shape[1]] = source[:band_count]
+        wide_pot[at : at + source.shape[1]] = source[band_count]
+    rows, lanes = first_buf.shape[2], first_buf.shape[3]
+
+    def apply(field, band, plane):
+        centre = field[band, plane]
+        near_sum = field[band, plane - 1] + field[band, plane + 1]
+        near_sum = near_sum + pltpu.roll(centre, 1, 0) + pltpu.roll(centre, rows - 1, 0)
+        near_sum = near_sum + pltpu.roll(centre, 1, 1) + pltpu.roll(centre, lanes - 1, 1)
+        far_sum = field[band, plane - 2] + field[band, plane + 2]
+        far_sum = far_sum + pltpu.roll(centre, 2, 0) + pltpu.roll(centre, rows - 2, 0)
+        far_sum = far_sum + pltpu.roll(centre, 2, 1) + pltpu.roll(centre, lanes - 2, 1)
+        kinetic = 0.5 * (7.5 * centre - FOUR_THIRDS * near_sum + TWELFTH * far_sum)
+        return kinetic + wide_pot[plane] * centre, centre
+
+    def sweep(field, older, out, lo, hi, scale, carry_scale):
+        @pl.loop(lo, hi)
+        def _(plane):
+            for band in range(band_count):
+                applied, centre = apply(field, band, plane)
+                value = (applied - CENTER * centre) * scale
+                if older is not None:
+                    value = value - carry_scale * older[band, plane]
+                out[band, plane] = value
+
+    total = first_buf.shape[1]
+    sweep(first_buf, None, second_buf, 2, total - 2, SIGMA_ONE / HALF_WIDTH, 0.0)
+    bufs = [first_buf, second_buf, third_buf]
+    older, field, spare = 0, 1, 2
+    sigma_now = SIGMA_ONE
+    for repeat_index in range(filter_degree - 1):
+        sigma_next = 1.0 / (2.0 / SIGMA_ONE - sigma_now)
+        margin = 2 * (repeat_index + 2)
+        sweep(bufs[field], bufs[older], bufs[spare], margin, total - margin,
+              2.0 * sigma_next / HALF_WIDTH, sigma_now * sigma_next)
+        older, field, spare = field, spare, older
+        sigma_now = sigma_next
+    final = bufs[field]
+    filtered_ref[...] = final[:, width : width + own_planes]
+
+    @pl.loop(width, width + own_planes)
+    def _(plane):
+        for band in range(band_count):
+            image_ref[band, plane - width], _ = apply(final, band, plane)
 
 
-def operate(field_in, potential):
-    plane_count = field_in.shape[1] - 4
-    centre = field_in[:, 2 : 2 + plane_count]
-    near_sum = field_in[:, 1 : 1 + plane_count] + field_in[:, 3 : 3 + plane_count]
-    near_sum = near_sum + jnp.roll(centre, 1, 2) + jnp.roll(centre, -1, 2)
-    near_sum = near_sum + jnp.roll(centre, 1, 3) + jnp.roll(centre, -1, 3)
-    far_sum = field_in[:, 0:plane_count] + field_in[:, 4 : 4 + plane_count]
-    far_sum = far_sum + jnp.roll(centre, 2, 2) + jnp.roll(centre, -2, 2)
-    far_sum = far_sum + jnp.roll(centre, 2, 3) + jnp.roll(centre, -2, 3)
-    kinetic = 0.5 * (7.5 * centre - FOUR_THIRDS * near_sum + TWELFTH * far_sum)
-    return kinetic + potential * centre
+def filter_and_image(below, own, above):
+    band_count = own.shape[0] - 1
+    own_planes, rows, lanes = own.shape[1], own.shape[2], own.shape[3]
+    total = below.shape[1] + own_planes + above.shape[1]
+    shape = (band_count, own_planes, rows, lanes)
+    cells = band_count * total * rows * lanes
+    return pl.pallas_call(
+        filter_kernel,
+        out_shape=(jax.ShapeDtypeStruct(shape, jnp.float32), jax.ShapeDtypeStruct(shape, jnp.float32)),
+        in_specs=[pl.BlockSpec(memory_space=pltpu.VMEM)] * 3,
+        out_specs=(pl.BlockSpec(memory_space=pltpu.VMEM), pl.BlockSpec(memory_space=pltpu.VMEM)),
+        scratch_shapes=[pltpu.VMEM((band_count, total, rows, lanes), jnp.float32)] * 3
+        + [pltpu.VMEM((total, rows, lanes), jnp.float32)],
+        cost_estimate=pl.CostEstimate(flops=30 * cells * 4, transcendentals=0, bytes_accessed=4 * cells * 3),
+    )(below, own, above)
 
 
 def on_device(trial_bands, potential):
-    band_count, own_planes = trial_bands.shape[0], trial_bands.shape[1]
+    band_count = trial_bands.shape[0]
     width = 2 * (filter_degree + 1)
+    count = lax.axis_size("grid")
     payload = jnp.concatenate([trial_bands, potential[None]], axis=0)
-    wide = widened(payload, width)
-    wide_bands, wide_potential = wide[:band_count], wide[band_count]
-    offset = [0]
-
-    def step(field_in):
-        first = offset[0] + 2
-        result = operate(field_in, wide_potential[first : first + field_in.shape[1] - 4])
-        return result, first
-
-    def trim(values, at, first, count):
-        return values[:, first - at : first - at + count]
-
-    sigma_now = SIGMA_ONE
-    previous, previous_at = wide_bands, 0
-    image_in, first = step(wide_bands)
-    current = (image_in - CENTER * trim(wide_bands, 0, first, image_in.shape[1])) * (SIGMA_ONE / HALF_WIDTH)
-    current_at = first
-    for repeat_index in range(filter_degree - 1):
-        sigma_next = 1.0 / (2.0 / SIGMA_ONE - sigma_now)
-        offset[0] = current_at
-        image_in, first = step(current)
-        count = image_in.shape[1]
-        following = (image_in - CENTER * trim(current, current_at, first, count)) * (
-            2.0 * sigma_next / HALF_WIDTH
-        ) - sigma_now * sigma_next * trim(previous, previous_at, first, count)
-        previous, previous_at = current, current_at
-        current, current_at, sigma_now = following, first, sigma_next
-    offset[0] = current_at
-    applied, first = step(current)
-    current = trim(current, current_at, first, own_planes)
+    below = lax.ppermute(payload[:, payload.shape[1] - width :], "grid", [(i, (i + 1) % count) for i in range(count)])
+    above = lax.ppermute(payload[:, :width], "grid", [((i + 1) % count, i) for i in range(count)])
+    current, applied = filter_and_image(below, payload, above)
     band_devices = lax.axis_size("band")
     total_bands = band_count * band_devices
     cell_count = current.shape[1] * current.shape[2] * current.shape[3]

time: 183 us -> 183 us (level)
  Pallas kernels: 0 us -> 12 us
  other arithmetic: 21.2 us -> 13.8 us
  local copies, waits for them, and re-layouts: 9.45 us -> 5.2 us
    pallas_call x0 -> x1, Pallas kernels: none -> 12 us  [filter_and_image(): pl.pallas_call(filter_kernel, out_shape=(jax.ShapeDtypeStruct(shape, jnp....]
    slice x38 -> x0, local copies, waits for them, and re-layouts: 5.96 us -> none  [the longest x10 2.32 us: operate(): near_sum = near_sum + jnp.roll(centre, 1, 3) + jnp.roll(centre, -1, 3)]
    sub x3 -> x0, other arithmetic: 3.56 us -> none  [on_device(): (image_in - CENTER * trim(current, current_at, first, count)) * (2.0 * si...]
    mul x1 -> x0, other arithmetic: 2.31 us -> none  [on_device(): (image_in - CENTER * trim(wide_bands, 0, first, image_in.shape[1])) * (SI...]
where the time goes in v5:
time: 183 us; the launch traced here: 182 us
  waiting for transfers between devices  59.3 us (32%)
  starting transfers between devices  57.7 us (32%)
  blocking collectives  31.9 us (17%)
  other arithmetic  13.8 us (8%)
  Pallas kernels  12 us (7%)
  local copies, waits for them, and re-layouts  5.2 us (3%)
    ppermute x9, starting transfers between devices, butterfly_sum(): values = values + lax.ppermute(values, axis, pairs)  52.1 us
    ppermute x9, waiting for transfers between devices, butterfly_sum(): values = values + lax.ppermute(values, axis, pairs)  46.1 us
    all_to_all x1, blocking collectives, on_device(): moved = lax.all_to_all(both, 'band', 2, 1, tiled=True)  31.9 us
    pallas_call x1, Pallas kernels, filter_and_image(): pl.pallas_call(filter_kernel, out_shape=(jax.ShapeDtypeStruct(shape, jnp....  12 us
    ppermute x1, waiting for transfers between devices, on_device(): lax.ppermute(payload[:, :width], 'grid', [((i + 1) % count, i) for i in r...  8.61 us
    another operation x3, other arithmetic, on_device(): factor = jnp.linalg.cholesky(margin)  6.52 us
    another operation x2, other arithmetic, on_device(): lax.linalg.triangular_solve(factor, coefficients.T, left_side=True, lower...  5.55 us
    ppermute x1, waiting for transfers between devices, on_device(): lax.ppermute(payload[:, payload.shape[1] - width:], 'grid', [(i, (i + 1)...  4.57 us
  transfers between devices with their start and end apart: 11, of which 11 were waited for; matrix products, arithmetic and copies ran while one was open for 0% of the time, Pallas kernels for 0%

profile of v5, /device:TPU:24, one launch (start us, length us, event | category | flops | bytes accessed | tf_op | source)
XLA Modules:
  0.0 182.1 jit_solution(15516836445088087144)
XLA Ops:
  0.6 1.1 pad_maximum_fusion.1.own_ref
  1.7 1.9 %collective-permute-start = (f32[3,10,32,128]{3,2,1,0:T(8,128)S(1)}, f32[3,10,32,128]{3,2,1,0:T(8,128)S(1)}, u32[]{:S(2)}, u32[]{:S(2)}) collective-permute-start(f32[3,10,32,128]{3,2,1,0:T(8,128)S(1)} %pad_maximum_fusion.1.own_ref), channel_id=1, source_target_pairs={{0,1},{1,2},{2,3},{3,4},{4,5},{5,6},{6,7},{7,8},{8,9},{9,10},{10,1... | collective-permute-start | bytes 1474568 | tf_op jit(solution)/shard_map/ppermute | solution.py:109
  3.7 3.6 %collective-permute-start.1 = (f32[3,10,32,128]{3,2,1,0:T(8,128)S(1)}, f32[3,10,32,128]{3,2,1,0:T(8,128)S(1)}, u32[]{:S(2)}, u32[]{:S(2)}) collective-permute-start(f32[3,10,32,128]{3,2,1,0:T(8,128)S(1)} %pad_maximum_fusion.1.own_ref), channel_id=1, source_target_pairs={{1,0},{2,1},{3,2},{4,3},{5,4},{6,5},{7,6},{8,7},{9,8},{10,9},{11,1... | collective-permute-start | bytes 1474568 | tf_op jit(solution)/shard_map/ppermute | solution.py:110
  7.3 4.6 %collective-permute-done.below_ref = f32[3,10,32,128]{3,2,1,0:T(8,128)S(1)} collective-permute-done((f32[3,10,32,128]{3,2,1,0:T(8,128)S(1)}, f32[3,10,32,128]{3,2,1,0:T(8,128)S(1)}, u32[]{:S(2)}, u32[]{:S(2)}) %collective-permute-start) | collective-permute-done | bytes 491552 | tf_op jit(solution)/shard_map/ppermute | solution.py:109
  11.9 8.6 %collective-permute-done.1.above_ref = f32[3,10,32,128]{3,2,1,0:T(8,128)S(1)} collective-permute-done((f32[3,10,32,128]{3,2,1,0:T(8,128)S(1)}, f32[3,10,32,128]{3,2,1,0:T(8,128)S(1)}, u32[]{:S(2)}, u32[]{:S(2)}) %collective-permute-start.1) | collective-permute-done | bytes 491552 | tf_op jit(solution)/shard_map/ppermute | solution.py:110
  20.5 0.8 copy-done.2
  21.3 12.0 %shard_map.49 = (f32[2,10,32,128]{3,2,1,0:T(8,128)}, f32[2,10,32,128]{3,2,1,0:T(8,128)}) custom-call(f32[3,10,32,128]{3,2,1,0:T(8,128)} %copy-done.1, f32[3,10,32,128]{3,2,1,0:T(8,128)} %copy-done, f32[3,10,32,128]{3,2,1,0:T(8,128)} %copy-done.2), custom_call_target="tpu_custom_call" | custom-call | flops 29491200 | bytes 2949120 | tf_op jit(solution)/shard_map/pallas_call | solution.py:93
  33.3 1.0 stack.7
  34.6 0.7 copy-done.3
  35.9 31.9 %all_to_all.15 = f32[2,2,32,1280]{3,1,0,2:T(2,128)S(1)} all-to-all(f32[2,2,32,1280]{3,1,0,2:T(2,128)S(1)} %pad_maximum_fusion), channel_id=1, replica_groups=mesh['band'=32,'grid'=16] {'band'}, dimensions={2} | all-to-all | bytes 1310720 | tf_op jit(solution)/shard_map/all_to_all | solution.py:121
  69.7 34.3 %collective-permute-start.2 = (f32[8256]{0:T(1024)S(1)}, f32[8256]{0:T(1024)S(1)}, u32[]{:S(2)}, u32[]{:S(2)}) collective-permute-start(f32[8256]{0:T(1024)S(1)} %constant_dynamic-update-slice_fusion), channel_id=1, source_target_pairs={{0,1},{1,0},{2,3},{3,2},{4,5},{5,4},{6,7},{7,6},{8,9},{9,8},{10,11... | collective-permute-start | bytes 99080 | tf_op jit(solution)/shard_map/ppermute | solution.py:21
  103.9 0.8 collective-permute-done.2
  104.8 1.9 %collective-permute-start.3 = (f32[8256]{0:T(1024)S(1)}, f32[8256]{0:T(1024)S(1)}, u32[]{:S(2)}, u32[]{:S(2)}) collective-permute-start(f32[8256]{0:T(1024)S(1)} %add.41), channel_id=1, source_target_pairs={{0,2},{1,3},{2,0},{3,1},{4,6},{5,7},{6,4},{7,5},{8,10},{9,11},{10,... | collective-permute-start | bytes 99080 | tf_op jit(solution)/shard_map/ppermute | solution.py:21
  106.7 3.9 %collective-permute-done.3 = f32[8256]{0:T(1024)S(1)} collective-permute-done((f32[8256]{0:T(1024)S(1)}, f32[8256]{0:T(1024)S(1)}, u32[]{:S(2)}, u32[]{:S(2)}) %collective-permute-start.3) | collective-permute-done | bytes 33056 | tf_op jit(solution)/shard_map/ppermute | solution.py:21
  110.6 1.9 %collective-permute-start.4 = (f32[8256]{0:T(1024)S(1)}, f32[8256]{0:T(1024)S(1)}, u32[]{:S(2)}, u32[]{:S(2)}) collective-permute-start(f32[8256]{0:T(1024)S(1)} %add.42), channel_id=1, source_target_pairs={{0,6},{1,7},{2,4},{3,5},{4,2},{5,3},{6,0},{7,1},{8,14},{9,15},{10,... | collective-permute-start | bytes 99080 | tf_op jit(solution)/shard_map/ppermute | solution.py:21
  112.5 5.1 %collective-permute-done.4 = f32[8256]{0:T(1024)S(1)} collective-permute-done((f32[8256]{0:T(1024)S(1)}, f32[8256]{0:T(1024)S(1)}, u32[]{:S(2)}, u32[]{:S(2)}) %collective-permute-start.4) | collective-permute-done | bytes 33056 | tf_op jit(solution)/shard_map/ppermute | solution.py:21
  117.7 3.6 %collective-permute-start.5 = (f32[8256]{0:T(1024)S(1)}, f32[8256]{0:T(1024)S(1)}, u32[]{:S(2)}, u32[]{:S(2)}) collective-permute-start(f32[8256]{0:T(1024)S(1)} %add.43), channel_id=1, source_target_pairs={{0,8},{1,9},{2,10},{3,11},{4,12},{5,13},{6,14},{7,15},{8,0},{9,1},... | collective-permute-start | bytes 99080 | tf_op jit(solution)/shard_map/ppermute | solution.py:21
  121.3 11.0 %collective-permute-done.5 = f32[8256]{0:T(1024)S(1)} collective-permute-done((f32[8256]{0:T(1024)S(1)}, f32[8256]{0:T(1024)S(1)}, u32[]{:S(2)}, u32[]{:S(2)}) %collective-permute-start.5) | collective-permute-done | bytes 33056 | tf_op jit(solution)/shard_map/ppermute | solution.py:21
  132.3 1.9 %collective-permute-start.6 = (f32[8256]{0:T(1024)S(1)}, f32[8256]{0:T(1024)S(1)}, u32[]{:S(2)}, u32[]{:S(2)}) collective-permute-start(f32[8256]{0:T(1024)S(1)} %add.44), channel_id=1, source_target_pairs={{0,16},{16,0},{32,48},{48,32},{64,80},{80,64},{96,112},{112,96},{1... | collective-permute-start | bytes 99080 | tf_op jit(solution)/shard_map/ppermute | solution.py:21
  134.3 3.9 %collective-permute-done.6 = f32[8256]{0:T(1024)S(1)} collective-permute-done((f32[8256]{0:T(1024)S(1)}, f32[8256]{0:T(1024)S(1)}, u32[]{:S(2)}, u32[]{:S(2)}) %collective-permute-start.6) | collective-permute-done | bytes 33056 | tf_op jit(solution)/shard_map/ppermute | solution.py:21
  138.2 2.3 %collective-permute-start.7 = (f32[8256]{0:T(1024)S(1)}, f32[8256]{0:T(1024)S(1)}, u32[]{:S(2)}, u32[]{:S(2)}) collective-permute-start(f32[8256]{0:T(1024)S(1)} %add.45), channel_id=1, source_target_pairs={{0,32},{16,48},{32,0},{48,16},{64,96},{80,112},{96,64},{112,80},{1... | collective-permute-start | bytes 99080 | tf_op jit(solution)/shard_map/ppermute | solution.py:21
  140.5 4.5 %collective-permute-done.7 = f32[8256]{0:T(1024)S(1)} collective-permute-done((f32[8256]{0:T(1024)S(1)}, f32[8256]{0:T(1024)S(1)}, u32[]{:S(2)}, u32[]{:S(2)}) %collective-permute-start.7) | collective-permute-done | bytes 33056 | tf_op jit(solution)/shard_map/ppermute | solution.py:21
  144.9 1.9 %collective-permute-start.8 = (f32[8256]{0:T(1024)S(1)}, f32[8256]{0:T(1024)S(1)}, u32[]{:S(2)}, u32[]{:S(2)}) collective-permute-start(f32[8256]{0:T(1024)S(1)} %add.46), channel_id=1, source_target_pairs={{0,64},{16,80},{32,96},{48,112},{64,0},{80,16},{96,32},{112,48},{1... | collective-permute-start | bytes 99080 | tf_op jit(solution)/shard_map/ppermute | solution.py:21
  146.9 8.3 %collective-permute-done.8 = f32[8256]{0:T(1024)S(1)} collective-permute-done((f32[8256]{0:T(1024)S(1)}, f32[8256]{0:T(1024)S(1)}, u32[]{:S(2)}, u32[]{:S(2)}) %collective-permute-start.8) | collective-permute-done | bytes 33056 | tf_op jit(solution)/shard_map/ppermute | solution.py:21
  155.1 1.9 %collective-permute-start.9 = (f32[8256]{0:T(1024)S(1)}, f32[8256]{0:T(1024)S(1)}, u32[]{:S(2)}, u32[]{:S(2)}) collective-permute-start(f32[8256]{0:T(1024)S(1)} %add.47), channel_id=1, source_target_pairs={{0,128},{16,144},{32,160},{48,176},{64,192},{80,208},{96,224},{112... | collective-permute-start | bytes 99080 | tf_op jit(solution)/shard_map/ppermute | solution.py:21
  157.0 3.9 %collective-permute-done.9 = f32[8256]{0:T(1024)S(1)} collective-permute-done((f32[8256]{0:T(1024)S(1)}, f32[8256]{0:T(1024)S(1)}, u32[]{:S(2)}, u32[]{:S(2)}) %collective-permute-start.9) | collective-permute-done | bytes 33056 | tf_op jit(solution)/shard_map/ppermute | solution.py:21
  161.0 2.4 %collective-permute-start.10 = (f32[8256]{0:T(1024)S(1)}, f32[8256]{0:T(1024)S(1)}, u32[]{:S(2)}, u32[]{:S(2)}) collective-permute-start(f32[8256]{0:T(1024)S(1)} %add.48), channel_id=1, source_target_pairs={{0,384},{16,400},{32,416},{48,432},{64,448},{80,464},{96,480},{112... | collective-permute-start | bytes 99080 | tf_op jit(solution)/shard_map/ppermute | solution.py:21
  163.4 4.6 %collective-permute-done.10 = f32[8256]{0:T(1024)S(1)} collective-permute-done((f32[8256]{0:T(1024)S(1)}, f32[8256]{0:T(1024)S(1)}, u32[]{:S(2)}, u32[]{:S(2)}) %collective-permute-start.10) | collective-permute-done | bytes 33056 | tf_op jit(solution)/shard_map/ppermute | solution.py:21
  168.2 5.8 %cholesky.18 = f32[64,64]{1,0:T(8,128)S(1)} custom-call(f32[64,64]{1,0:T(8,128)S(1)} %fusion.7), custom_call_target="Cholesky" | custom-call | tf_op jit(solution)/shard_map/jit(cholesky)/cholesky | solution.py:139
  174.1 0.6 compare_reduce_fusion
  174.7 0.7 fusion
  175.4 4.9 %custom-call.8 = f32[1,64,64]{1,2,0:T(8,128)S(1)} custom-call(f32[1,64,64]{2,1,0:T(8,128)S(1)} %fusion), custom_call_target="InvertDiagBlocksLowerTriangular" | custom-call | tf_op jit(solution)/shard_map/triangular_solve/custom-call.0 | solution.py:141
  (41 shorter events, 4.6 us)
Async XLA Ops:
  1.7 18.8 %copy-start = (f32[3,10,32,128]{3,2,1,0:T(8,128)}, f32[3,10,32,128]{3,2,1,0:T(8,128)S(1)}, u32[]{:S(2)}) copy-start(f32[3,10,32,128]{3,2,1,0:T(8,128)S(1)} %pad_maximum_fusion.1.own_ref) | copy-start | bytes 1474564
  1.7 10.1 %collective-permute-start = (f32[3,10,32,128]{3,2,1,0:T(8,128)S(1)}, f32[3,10,32,128]{3,2,1,0:T(8,128)S(1)}, u32[]{:S(2)}, u32[]{:S(2)}) collective-permute-start(f32[3,10,32,128]{3,2,1,0:T(8,128)S(1)} %pad_maximum_fusion.1.own_ref), channel_id=1, source_target_pairs={{0,1},{1,2},{2,3},{3,4},{4,5},{5,6},{6,7},{7,8},{8,9},{9,10},{10,1... | collective-permute-start | bytes 1474568 | tf_op jit(solution)/shard_map/ppermute | solution.py:109
  3.7 16.8 %collective-permute-start.1 = (f32[3,10,32,128]{3,2,1,0:T(8,128)S(1)}, f32[3,10,32,128]{3,2,1,0:T(8,128)S(1)}, u32[]{:S(2)}, u32[]{:S(2)}) collective-permute-start(f32[3,10,32,128]{3,2,1,0:T(8,128)S(1)} %pad_maximum_fusion.1.own_ref), channel_id=1, source_target_pairs={{1,0},{2,1},{3,2},{4,3},{5,4},{6,5},{7,6},{8,7},{9,8},{10,9},{11,1... | collective-permute-start | bytes 1474568 | tf_op jit(solution)/shard_map/ppermute | solution.py:110
  11.9 8.6 %copy-start.1 = (f32[3,10,32,128]{3,2,1,0:T(8,128)}, f32[3,10,32,128]{3,2,1,0:T(8,128)S(1)}, u32[]{:S(2)}) copy-start(f32[3,10,32,128]{3,2,1,0:T(8,128)S(1)} %collective-permute-done.below_ref) | copy-start | bytes 1474564
  20.5 0.8 copy-start.2
  34.3 1.0 copy-start.3
  69.7 35.1 %collective-permute-start.2 = (f32[8256]{0:T(1024)S(1)}, f32[8256]{0:T(1024)S(1)}, u32[]{:S(2)}, u32[]{:S(2)}) collective-permute-start(f32[8256]{0:T(1024)S(1)} %constant_dynamic-update-slice_fusion), channel_id=1, source_target_pairs={{0,1},{1,0},{2,3},{3,2},{4,5},{5,4},{6,7},{7,6},{8,9},{9,8},{10,11... | collective-permute-start | bytes 99080 | tf_op jit(solution)/shard_map/ppermute | solution.py:21
  104.8 5.8 %collective-permute-start.3 = (f32[8256]{0:T(1024)S(1)}, f32[8256]{0:T(1024)S(1)}, u32[]{:S(2)}, u32[]{:S(2)}) collective-permute-start(f32[8256]{0:T(1024)S(1)} %add.41), channel_id=1, source_target_pairs={{0,2},{1,3},{2,0},{3,1},{4,6},{5,7},{6,4},{7,5},{8,10},{9,11},{10,... | collective-permute-start | bytes 99080 | tf_op jit(solution)/shard_map/ppermute | solution.py:21
  110.6 7.1 %collective-permute-start.4 = (f32[8256]{0:T(1024)S(1)}, f32[8256]{0:T(1024)S(1)}, u32[]{:S(2)}, u32[]{:S(2)}) collective-permute-start(f32[8256]{0:T(1024)S(1)} %add.42), channel_id=1, source_target_pairs={{0,6},{1,7},{2,4},{3,5},{4,2},{5,3},{6,0},{7,1},{8,14},{9,15},{10,... | collective-permute-start | bytes 99080 | tf_op jit(solution)/shard_map/ppermute | solution.py:21
  117.7 14.7 %collective-permute-start.5 = (f32[8256]{0:T(1024)S(1)}, f32[8256]{0:T(1024)S(1)}, u32[]{:S(2)}, u32[]{:S(2)}) collective-permute-start(f32[8256]{0:T(1024)S(1)} %add.43), channel_id=1, source_target_pairs={{0,8},{1,9},{2,10},{3,11},{4,12},{5,13},{6,14},{7,15},{8,0},{9,1},... | collective-permute-start | bytes 99080 | tf_op jit(solution)/shard_map/ppermute | solution.py:21
  132.3 5.8 %collective-permute-start.6 = (f32[8256]{0:T(1024)S(1)}, f32[8256]{0:T(1024)S(1)}, u32[]{:S(2)}, u32[]{:S(2)}) collective-permute-start(f32[8256]{0:T(1024)S(1)} %add.44), channel_id=1, source_target_pairs={{0,16},{16,0},{32,48},{48,32},{64,80},{80,64},{96,112},{112,96},{1... | collective-permute-start | bytes 99080 | tf_op jit(solution)/shard_map/ppermute | solution.py:21
  138.2 6.7 %collective-permute-start.7 = (f32[8256]{0:T(1024)S(1)}, f32[8256]{0:T(1024)S(1)}, u32[]{:S(2)}, u32[]{:S(2)}) collective-permute-start(f32[8256]{0:T(1024)S(1)} %add.45), channel_id=1, source_target_pairs={{0,32},{16,48},{32,0},{48,16},{64,96},{80,112},{96,64},{112,80},{1... | collective-permute-start | bytes 99080 | tf_op jit(solution)/shard_map/ppermute | solution.py:21
  144.9 10.2 %collective-permute-start.8 = (f32[8256]{0:T(1024)S(1)}, f32[8256]{0:T(1024)S(1)}, u32[]{:S(2)}, u32[]{:S(2)}) collective-permute-start(f32[8256]{0:T(1024)S(1)} %add.46), channel_id=1, source_target_pairs={{0,64},{16,80},{32,96},{48,112},{64,0},{80,16},{96,32},{112,48},{1... | collective-permute-start | bytes 99080 | tf_op jit(solution)/shard_map/ppermute | solution.py:21
  155.1 5.8 %collective-permute-start.9 = (f32[8256]{0:T(1024)S(1)}, f32[8256]{0:T(1024)S(1)}, u32[]{:S(2)}, u32[]{:S(2)}) collective-permute-start(f32[8256]{0:T(1024)S(1)} %add.47), channel_id=1, source_target_pairs={{0,128},{16,144},{32,160},{48,176},{64,192},{80,208},{96,224},{112... | collective-permute-start | bytes 99080 | tf_op jit(solution)/shard_map/ppermute | solution.py:21
  161.0 7.1 %collective-permute-start.10 = (f32[8256]{0:T(1024)S(1)}, f32[8256]{0:T(1024)S(1)}, u32[]{:S(2)}, u32[]{:S(2)}) collective-permute-start(f32[8256]{0:T(1024)S(1)} %add.48), channel_id=1, source_target_pairs={{0,384},{16,400},{32,416},{48,432},{64,448},{80,464},{96,480},{112... | collective-permute-start | bytes 99080 | tf_op jit(solution)/shard_map/ppermute | solution.py:21

commit v6 on v5

--- a/solution.py
+++ b/solution.py
@@ -34,12 +34,14 @@
     return partner
 
 
-def filter_kernel(below_ref, own_ref, above_ref, filtered_ref, image_ref, first_buf, second_buf, third_buf, wide_pot):
+def filter_kernel(below_ref, own_ref, above_ref, below_pot, own_pot, above_pot, filtered_ref, image_ref,
+                  first_buf, second_buf, third_buf, wide_pot):
     band_count, own_planes = filtered_ref.shape[0], filtered_ref.shape[1]
     width = below_ref.shape[1]
-    for at, source in ((0, below_ref), (width, own_ref), (width + own_planes, above_ref)):
-        first_buf[:, at : at + source.shape[1]] = source[:band_count]
-        wide_pot[at : at + source.shape[1]] = source[band_count]
+    for at, source, pot in ((0, below_ref, below_pot), (width, own_ref, own_pot),
+                            (width + own_planes, above_ref, above_pot)):
+        first_buf[:, at : at + source.shape[1]] = source[...]
+        wide_pot[at : at + source.shape[1]] = pot[...]
     rows, lanes = first_buf.shape[2], first_buf.shape[3]
 
     def apply(field, band, plane):
@@ -84,8 +86,8 @@
             image_ref[band, plane - width], _ = apply(final, band, plane)
 
 
-def filter_and_image(below, own, above):
-    band_count = own.shape[0] - 1
+def filter_and_image(below, own, above, below_pot, own_pot, above_pot):
+    band_count = own.shape[0]
     own_planes, rows, lanes = own.shape[1], own.shape[2], own.shape[3]
     total = below.shape[1] + own_planes + above.shape[1]
     shape = (band_count, own_planes, rows, lanes)
@@ -93,22 +95,35 @@
     return pl.pallas_call(
         filter_kernel,
         out_shape=(jax.ShapeDtypeStruct(shape, jnp.float32), jax.ShapeDtypeStruct(shape, jnp.float32)),
-        in_specs=[pl.BlockSpec(memory_space=pltpu.VMEM)] * 3,
+        in_specs=[pl.BlockSpec(memory_space=pltpu.VMEM)] * 6,
         out_specs=(pl.BlockSpec(memory_space=pltpu.VMEM), pl.BlockSpec(memory_space=pltpu.VMEM)),
         scratch_shapes=[pltpu.VMEM((band_count, total, rows, lanes), jnp.float32)] * 3
         + [pltpu.VMEM((total, rows, lanes), jnp.float32)],
         cost_estimate=pl.CostEstimate(flops=30 * cells * 4, transcendentals=0, bytes_accessed=4 * cells * 3),
-    )(below, own, above)
+    )(below, own, above, below_pot, own_pot, above_pot)
+
+
+def replica_pairs(direction):
+    grid_count, band_count = lax.axis_size("grid"), lax.axis_size("band")
+    pairs = []
+    for target_grid in range(grid_count):
+        source_grid = (target_grid - direction) % grid_count
+        far = source_grid // 8 != target_grid // 8
+        for target_band in range(band_count):
+            source_band = target_band ^ 4 if far else target_band
+            pairs.append((source_band * grid_count + source_grid, target_band * grid_count + target_grid))
+    return pairs
 
 
 def on_device(trial_bands, potential):
     band_count = trial_bands.shape[0]
     width = 2 * (filter_degree + 1)
     count = lax.axis_size("grid")
-    payload = jnp.concatenate([trial_bands, potential[None]], axis=0)
-    below = lax.ppermute(payload[:, payload.shape[1] - width :], "grid", [(i, (i + 1) % count) for i in range(count)])
-    above = lax.ppermute(payload[:, :width], "grid", [((i + 1) % count, i) for i in range(count)])
-    current, applied = filter_and_image(below, payload, above)
+    below = lax.ppermute(trial_bands[:, trial_bands.shape[1] - width :], "grid", [(i, (i + 1) % count) for i in range(count)])
+    above = lax.ppermute(trial_bands[:, :width], "grid", [((i + 1) % count, i) for i in range(count)])
+    below_pot = lax.ppermute(potential[potential.shape[0] - width :], ("band", "grid"), replica_pairs(1))
+    above_pot = lax.ppermute(potential[:width], ("band", "grid"), replica_pairs(-1))
+    current, applied = filter_and_image(below, trial_bands, above, below_pot, potential, above_pot)
     band_devices = lax.axis_size("band")
     total_bands = band_count * band_devices
     cell_count = current.shape[1] * current.shape[2] * current.shape[3]

time: 183 us -> 179 us (0.978)
  waiting for transfers between devices: 59.3 us -> 55.9 us
    ppermute x9, starting transfers between devices: 52.1 us -> 36 us  [butterfly_sum(): values = values + lax.ppermute(values, axis, pairs)]
    ppermute x2 -> x4, starting transfers between devices: 5.56 us -> 21.2 us  [the longest x1 13.8 us: on_device(): lax.ppermute(potential[potential.shape[0] - width:], ('band', 'grid'), re...]
    ppermute x2 -> x4, waiting for transfers between devices: 13.2 us -> 10.6 us  [the longest x1 10.6 us: on_device(): lax.ppermute(potential[:width], ('band', 'grid'), replica_pairs(-1))]
  transfers between devices with their start and end apart: 11 -> 13, of which waited for: 11 -> 10; matrix products, arithmetic and copies ran while one was open for 0% -> 0% of each run, Pallas kernels for 0% -> 0%
where the time goes in v6:
time: 179 us; the launch traced here: 178 us
  starting transfers between devices  57.2 us (32%)
  waiting for transfers between devices  55.9 us (31%)
  blocking collectives  32.5 us (18%)
  other arithmetic  12.7 us (7%)
  Pallas kernels  12 us (7%)
  local copies, waits for them, and re-layouts  5.89 us (3%)
    ppermute x9, waiting for transfers between devices, butterfly_sum(): values = values + lax.ppermute(values, axis, pairs)  45.3 us
    ppermute x9, starting transfers between devices, butterfly_sum(): values = values + lax.ppermute(values, axis, pairs)  36 us
    all_to_all x1, blocking collectives, on_device(): moved = lax.all_to_all(both, 'band', 2, 1, tiled=True)  32.5 us
    ppermute x1, starting transfers between devices, on_device(): lax.ppermute(potential[potential.shape[0] - width:], ('band', 'grid'), re...  13.8 us
    pallas_call x1, Pallas kernels, filter_and_image(): pl.pallas_call(filter_kernel, out_shape=(jax.ShapeDtypeStruct(shape, jnp....  12 us
    ppermute x1, waiting for transfers between devices, on_device(): lax.ppermute(potential[:width], ('band', 'grid'), replica_pairs(-1))  10.6 us
    another operation x3, other arithmetic, on_device(): factor = jnp.linalg.cholesky(margin)  6.52 us
    another operation x2, other arithmetic, on_device(): lax.linalg.triangular_solve(factor, coefficients.T, left_side=True, lower...  5.55 us
  transfers between devices with their start and end apart: 13, of which 10 were waited for; matrix products, arithmetic and copies ran while one was open for 0% of the time, Pallas kernels for 0%

profile of v6, /device:TPU:24, one launch (start us, length us, event | category | flops | bytes accessed | tf_op | source)
XLA Modules:
  0.0 178.4 jit_solution(6957984781163588158)
XLA Ops:
  0.6 1.9 %collective-permute-start = (f32[2,10,32,128]{3,2,1,0:T(8,128)}, f32[2,10,32,128]{3,2,1,0:T(8,128)S(1)}, u32[]{:S(2)}, u32[]{:S(2)}) collective-permute-start(f32[2,10,32,128]{3,2,1,0:T(8,128)} %own_ref.1), channel_id=1, source_target_pairs={{0,1},{1,2},{2,3},{3,4},{4,5},{5,6},{6,7},{7,8},{8,9},{9,10},{10,1... | collective-permute-start | bytes 983048 | tf_op jit(solution)/shard_map/ppermute | solution.py:122
  2.6 3.6 %collective-permute-start.1 = (f32[2,10,32,128]{3,2,1,0:T(8,128)}, f32[2,10,32,128]{3,2,1,0:T(8,128)S(1)}, u32[]{:S(2)}, u32[]{:S(2)}) collective-permute-start(f32[2,10,32,128]{3,2,1,0:T(8,128)} %own_ref.1), channel_id=1, source_target_pairs={{1,0},{2,1},{3,2},{4,3},{5,4},{6,5},{7,6},{8,7},{9,8},{10,9},{11,1... | collective-permute-start | bytes 983048 | tf_op jit(solution)/shard_map/ppermute | solution.py:123
  6.2 13.8 %collective-permute-start.2 = (f32[10,32,128]{2,1,0:T(8,128)}, f32[10,32,128]{2,1,0:T(8,128)S(1)}, u32[]{:S(2)}, u32[]{:S(2)}) collective-permute-start(f32[10,32,128]{2,1,0:T(8,128)} %own_pot.1), channel_id=1, source_target_pairs={{79,0},{95,16},{111,32},{127,48},{15,64},{31,80},{47,96},{63,112},... | collective-permute-start | bytes 491528 | tf_op jit(solution)/shard_map/ppermute | solution.py:124
  20.0 1.9 %collective-permute-start.3 = (f32[10,32,128]{2,1,0:T(8,128)}, f32[10,32,128]{2,1,0:T(8,128)S(1)}, u32[]{:S(2)}, u32[]{:S(2)}) collective-permute-start(f32[10,32,128]{2,1,0:T(8,128)} %own_pot.1), channel_id=1, source_target_pairs={{1,0},{17,16},{33,32},{49,48},{65,64},{81,80},{97,96},{113,112},{1... | collective-permute-start | bytes 491528 | tf_op jit(solution)/shard_map/ppermute | solution.py:125
  21.9 10.6 %collective-permute-done.3.above_pot = f32[10,32,128]{2,1,0:T(8,128)S(1)} collective-permute-done((f32[10,32,128]{2,1,0:T(8,128)}, f32[10,32,128]{2,1,0:T(8,128)S(1)}, u32[]{:S(2)}, u32[]{:S(2)}) %collective-permute-start.3) | collective-permute-done | bytes 163872 | tf_op jit(solution)/shard_map/ppermute | solution.py:125
  32.6 0.7 copy-done.4
  33.3 0.7 copy-done.2
  34.1 12.0 %shard_map.49 = (f32[2,10,32,128]{3,2,1,0:T(8,128)}, f32[2,10,32,128]{3,2,1,0:T(8,128)}) custom-call(f32[2,10,32,128]{3,2,1,0:T(8,128)} %copy-done.1, f32[2,10,32,128]{3,2,1,0:T(8,128)} %own_ref.1, f32[2,10,32,128]{3,2,1,0:T(8,128)} %copy-done.2, f32[10,32,128]{2,1,0:T(8,128)} %copy-done.3, f32[10,32,128]{2,1,0:T(8,128)} %own_pot.1, f32[10,32,128]{2,1,0:T(8,128)} %copy-done.4), custom_call_target="tpu_custom_call" | custom-call | flops 29491200 | bytes 2949120 | tf_op jit(solution)/shard_map/pallas_call | solution.py:95
  46.0 1.0 stack.7
  47.3 0.7 copy-done
  48.7 32.5 %all_to_all.15 = f32[2,2,32,1280]{3,1,0,2:T(2,128)S(1)} all-to-all(f32[2,2,32,1280]{3,1,0,2:T(2,128)S(1)} %pad_maximum_fusion), channel_id=1, replica_groups=mesh['band'=32,'grid'=16] {'band'}, dimensions={2} | all-to-all | bytes 1310720 | tf_op jit(solution)/shard_map/all_to_all | solution.py:136
  83.0 17.2 %collective-permute-start.4 = (f32[8256]{0:T(1024)S(1)}, f32[8256]{0:T(1024)S(1)}, u32[]{:S(2)}, u32[]{:S(2)}) collective-permute-start(f32[8256]{0:T(1024)S(1)} %constant_dynamic-update-slice_fusion), channel_id=1, source_target_pairs={{0,1},{1,0},{2,3},{3,2},{4,5},{5,4},{6,7},{7,6},{8,9},{9,8},{10,11... | collective-permute-start | bytes 99080 | tf_op jit(solution)/shard_map/ppermute | solution.py:21
  100.2 0.8 collective-permute-done.4
  101.0 1.9 %collective-permute-start.5 = (f32[8256]{0:T(1024)S(1)}, f32[8256]{0:T(1024)S(1)}, u32[]{:S(2)}, u32[]{:S(2)}) collective-permute-start(f32[8256]{0:T(1024)S(1)} %add.41), channel_id=1, source_target_pairs={{0,2},{1,3},{2,0},{3,1},{4,6},{5,7},{6,4},{7,5},{8,10},{9,11},{10,... | collective-permute-start | bytes 99080 | tf_op jit(solution)/shard_map/ppermute | solution.py:21
  102.9 3.9 %collective-permute-done.5 = f32[8256]{0:T(1024)S(1)} collective-permute-done((f32[8256]{0:T(1024)S(1)}, f32[8256]{0:T(1024)S(1)}, u32[]{:S(2)}, u32[]{:S(2)}) %collective-permute-start.5) | collective-permute-done | bytes 33056 | tf_op jit(solution)/shard_map/ppermute | solution.py:21
  106.9 1.9 %collective-permute-start.6 = (f32[8256]{0:T(1024)S(1)}, f32[8256]{0:T(1024)S(1)}, u32[]{:S(2)}, u32[]{:S(2)}) collective-permute-start(f32[8256]{0:T(1024)S(1)} %add.42), channel_id=1, source_target_pairs={{0,6},{1,7},{2,4},{3,5},{4,2},{5,3},{6,0},{7,1},{8,14},{9,15},{10,... | collective-permute-start | bytes 99080 | tf_op jit(solution)/shard_map/ppermute | solution.py:21
  108.8 5.1 %collective-permute-done.6 = f32[8256]{0:T(1024)S(1)} collective-permute-done((f32[8256]{0:T(1024)S(1)}, f32[8256]{0:T(1024)S(1)}, u32[]{:S(2)}, u32[]{:S(2)}) %collective-permute-start.6) | collective-permute-done | bytes 33056 | tf_op jit(solution)/shard_map/ppermute | solution.py:21
  113.9 4.5 %collective-permute-start.7 = (f32[8256]{0:T(1024)S(1)}, f32[8256]{0:T(1024)S(1)}, u32[]{:S(2)}, u32[]{:S(2)}) collective-permute-start(f32[8256]{0:T(1024)S(1)} %add.43), channel_id=1, source_target_pairs={{0,8},{1,9},{2,10},{3,11},{4,12},{5,13},{6,14},{7,15},{8,0},{9,1},... | collective-permute-start | bytes 99080 | tf_op jit(solution)/shard_map/ppermute | solution.py:21
  118.4 10.4 %collective-permute-done.7 = f32[8256]{0:T(1024)S(1)} collective-permute-done((f32[8256]{0:T(1024)S(1)}, f32[8256]{0:T(1024)S(1)}, u32[]{:S(2)}, u32[]{:S(2)}) %collective-permute-start.7) | collective-permute-done | bytes 33056 | tf_op jit(solution)/shard_map/ppermute | solution.py:21
  128.9 1.9 %collective-permute-start.8 = (f32[8256]{0:T(1024)S(1)}, f32[8256]{0:T(1024)S(1)}, u32[]{:S(2)}, u32[]{:S(2)}) collective-permute-start(f32[8256]{0:T(1024)S(1)} %add.44), channel_id=1, source_target_pairs={{0,16},{16,0},{32,48},{48,32},{64,80},{80,64},{96,112},{112,96},{1... | collective-permute-start | bytes 99080 | tf_op jit(solution)/shard_map/ppermute | solution.py:21
  130.8 3.9 %collective-permute-done.8 = f32[8256]{0:T(1024)S(1)} collective-permute-done((f32[8256]{0:T(1024)S(1)}, f32[8256]{0:T(1024)S(1)}, u32[]{:S(2)}, u32[]{:S(2)}) %collective-permute-start.8) | collective-permute-done | bytes 33056 | tf_op jit(solution)/shard_map/ppermute | solution.py:21
  134.7 1.9 %collective-permute-start.9 = (f32[8256]{0:T(1024)S(1)}, f32[8256]{0:T(1024)S(1)}, u32[]{:S(2)}, u32[]{:S(2)}) collective-permute-start(f32[8256]{0:T(1024)S(1)} %add.45), channel_id=1, source_target_pairs={{0,32},{16,48},{32,0},{48,16},{64,96},{80,112},{96,64},{112,80},{1... | collective-permute-start | bytes 99080 | tf_op jit(solution)/shard_map/ppermute | solution.py:21
  136.7 4.8 %collective-permute-done.9 = f32[8256]{0:T(1024)S(1)} collective-permute-done((f32[8256]{0:T(1024)S(1)}, f32[8256]{0:T(1024)S(1)}, u32[]{:S(2)}, u32[]{:S(2)}) %collective-permute-start.9) | collective-permute-done | bytes 33056 | tf_op jit(solution)/shard_map/ppermute | solution.py:21
  141.5 1.9 %collective-permute-start.10 = (f32[8256]{0:T(1024)S(1)}, f32[8256]{0:T(1024)S(1)}, u32[]{:S(2)}, u32[]{:S(2)}) collective-permute-start(f32[8256]{0:T(1024)S(1)} %add.46), channel_id=1, source_target_pairs={{0,64},{16,80},{32,96},{48,112},{64,0},{80,16},{96,32},{112,48},{1... | collective-permute-start | bytes 99080 | tf_op jit(solution)/shard_map/ppermute | solution.py:21
  143.4 8.1 %collective-permute-done.10 = f32[8256]{0:T(1024)S(1)} collective-permute-done((f32[8256]{0:T(1024)S(1)}, f32[8256]{0:T(1024)S(1)}, u32[]{:S(2)}, u32[]{:S(2)}) %collective-permute-start.10) | collective-permute-done | bytes 33056 | tf_op jit(solution)/shard_map/ppermute | solution.py:21
  151.5 1.9 %collective-permute-start.11 = (f32[8256]{0:T(1024)S(1)}, f32[8256]{0:T(1024)S(1)}, u32[]{:S(2)}, u32[]{:S(2)}) collective-permute-start(f32[8256]{0:T(1024)S(1)} %add.47), channel_id=1, source_target_pairs={{0,128},{16,144},{32,160},{48,176},{64,192},{80,208},{96,224},{112... | collective-permute-start | bytes 99080 | tf_op jit(solution)/shard_map/ppermute | solution.py:21
  153.4 3.9 %collective-permute-done.11 = f32[8256]{0:T(1024)S(1)} collective-permute-done((f32[8256]{0:T(1024)S(1)}, f32[8256]{0:T(1024)S(1)}, u32[]{:S(2)}, u32[]{:S(2)}) %collective-permute-start.11) | collective-permute-done | bytes 33056 | tf_op jit(solution)/shard_map/ppermute | solution.py:21
  157.3 2.9 %collective-permute-start.12 = (f32[8256]{0:T(1024)S(1)}, f32[8256]{0:T(1024)S(1)}, u32[]{:S(2)}, u32[]{:S(2)}) collective-permute-start(f32[8256]{0:T(1024)S(1)} %add.48), channel_id=1, source_target_pairs={{0,384},{16,400},{32,416},{48,432},{64,448},{80,464},{96,480},{112... | collective-permute-start | bytes 99080 | tf_op jit(solution)/shard_map/ppermute | solution.py:21
  160.2 4.2 %collective-permute-done.12 = f32[8256]{0:T(1024)S(1)} collective-permute-done((f32[8256]{0:T(1024)S(1)}, f32[8256]{0:T(1024)S(1)}, u32[]{:S(2)}, u32[]{:S(2)}) %collective-permute-start.12) | collective-permute-done | bytes 33056 | tf_op jit(solution)/shard_map/ppermute | solution.py:21
  164.6 5.8 %cholesky.18 = f32[64,64]{1,0:T(8,128)S(1)} custom-call(f32[64,64]{1,0:T(8,128)S(1)} %fusion.7), custom_call_target="Cholesky" | custom-call | tf_op jit(solution)/shard_map/jit(cholesky)/cholesky | solution.py:154
  171.1 0.7 fusion
  171.8 4.9 %custom-call.8 = f32[1,64,64]{1,2,0:T(8,128)S(1)} custom-call(f32[1,64,64]{2,1,0:T(8,128)S(1)} %fusion), custom_call_target="InvertDiagBlocksLowerTriangular" | custom-call | tf_op jit(solution)/shard_map/triangular_solve/custom-call.0 | solution.py:156
  (46 shorter events, 5.4 us)
Async XLA Ops:
  0.6 31.9 %collective-permute-start = (f32[2,10,32,128]{3,2,1,0:T(8,128)}, f32[2,10,32,128]{3,2,1,0:T(8,128)S(1)}, u32[]{:S(2)}, u32[]{:S(2)}) collective-permute-start(f32[2,10,32,128]{3,2,1,0:T(8,128)} %own_ref.1), channel_id=1, source_target_pairs={{0,1},{1,2},{2,3},{3,4},{4,5},{5,6},{6,7},{7,8},{8,9},{9,10},{10,1... | collective-permute-start | bytes 983048 | tf_op jit(solution)/shard_map/ppermute | solution.py:122
  2.6 30.0 %collective-permute-start.1 = (f32[2,10,32,128]{3,2,1,0:T(8,128)}, f32[2,10,32,128]{3,2,1,0:T(8,128)S(1)}, u32[]{:S(2)}, u32[]{:S(2)}) collective-permute-start(f32[2,10,32,128]{3,2,1,0:T(8,128)} %own_ref.1), channel_id=1, source_target_pairs={{1,0},{2,1},{3,2},{4,3},{5,4},{6,5},{7,6},{8,7},{9,8},{10,9},{11,1... | collective-permute-start | bytes 983048 | tf_op jit(solution)/shard_map/ppermute | solution.py:123
  6.2 15.7 %collective-permute-start.2 = (f32[10,32,128]{2,1,0:T(8,128)}, f32[10,32,128]{2,1,0:T(8,128)S(1)}, u32[]{:S(2)}, u32[]{:S(2)}) collective-permute-start(f32[10,32,128]{2,1,0:T(8,128)} %own_pot.1), channel_id=1, source_target_pairs={{79,0},{95,16},{111,32},{127,48},{15,64},{31,80},{47,96},{63,112},... | collective-permute-start | bytes 491528 | tf_op jit(solution)/shard_map/ppermute | solution.py:124
  20.0 12.6 %collective-permute-start.3 = (f32[10,32,128]{2,1,0:T(8,128)}, f32[10,32,128]{2,1,0:T(8,128)S(1)}, u32[]{:S(2)}, u32[]{:S(2)}) collective-permute-start(f32[10,32,128]{2,1,0:T(8,128)} %own_pot.1), channel_id=1, source_target_pairs={{1,0},{17,16},{33,32},{49,48},{65,64},{81,80},{97,96},{113,112},{1... | collective-permute-start | bytes 491528 | tf_op jit(solution)/shard_map/ppermute | solution.py:125
  21.9 10.6 %copy-start.3 = (f32[10,32,128]{2,1,0:T(8,128)}, f32[10,32,128]{2,1,0:T(8,128)S(1)}, u32[]{:S(2)}) copy-start(f32[10,32,128]{2,1,0:T(8,128)S(1)} %collective-permute-done.2.below_pot) | copy-start | bytes 491524
  32.5 0.7 copy-start.4
  32.6 0.8 copy-start.1
  33.3 0.7 copy-start.2
  47.1 1.0 copy-start
  83.0 18.0 %collective-permute-start.4 = (f32[8256]{0:T(1024)S(1)}, f32[8256]{0:T(1024)S(1)}, u32[]{:S(2)}, u32[]{:S(2)}) collective-permute-start(f32[8256]{0:T(1024)S(1)} %constant_dynamic-update-slice_fusion), channel_id=1, source_target_pairs={{0,1},{1,0},{2,3},{3,2},{4,5},{5,4},{6,7},{7,6},{8,9},{9,8},{10,11... | collective-permute-start | bytes 99080 | tf_op jit(solution)/shard_map/ppermute | solution.py:21
  101.0 5.8 %collective-permute-start.5 = (f32[8256]{0:T(1024)S(1)}, f32[8256]{0:T(1024)S(1)}, u32[]{:S(2)}, u32[]{:S(2)}) collective-permute-start(f32[8256]{0:T(1024)S(1)} %add.41), channel_id=1, source_target_pairs={{0,2},{1,3},{2,0},{3,1},{4,6},{5,7},{6,4},{7,5},{8,10},{9,11},{10,... | collective-permute-start | bytes 99080 | tf_op jit(solution)/shard_map/ppermute | solution.py:21
  106.9 7.1 %collective-permute-start.6 = (f32[8256]{0:T(1024)S(1)}, f32[8256]{0:T(1024)S(1)}, u32[]{:S(2)}, u32[]{:S(2)}) collective-permute-start(f32[8256]{0:T(1024)S(1)} %add.42), channel_id=1, source_target_pairs={{0,6},{1,7},{2,4},{3,5},{4,2},{5,3},{6,0},{7,1},{8,14},{9,15},{10,... | collective-permute-start | bytes 99080 | tf_op jit(solution)/shard_map/ppermute | solution.py:21
  113.9 14.9 %collective-permute-start.7 = (f32[8256]{0:T(1024)S(1)}, f32[8256]{0:T(1024)S(1)}, u32[]{:S(2)}, u32[]{:S(2)}) collective-permute-start(f32[8256]{0:T(1024)S(1)} %add.43), channel_id=1, source_target_pairs={{0,8},{1,9},{2,10},{3,11},{4,12},{5,13},{6,14},{7,15},{8,0},{9,1},... | collective-permute-start | bytes 99080 | tf_op jit(solution)/shard_map/ppermute | solution.py:21
  128.9 5.8 %collective-permute-start.8 = (f32[8256]{0:T(1024)S(1)}, f32[8256]{0:T(1024)S(1)}, u32[]{:S(2)}, u32[]{:S(2)}) collective-permute-start(f32[8256]{0:T(1024)S(1)} %add.44), channel_id=1, source_target_pairs={{0,16},{16,0},{32,48},{48,32},{64,80},{80,64},{96,112},{112,96},{1... | collective-permute-start | bytes 99080 | tf_op jit(solution)/shard_map/ppermute | solution.py:21
  134.7 6.7 %collective-permute-start.9 = (f32[8256]{0:T(1024)S(1)}, f32[8256]{0:T(1024)S(1)}, u32[]{:S(2)}, u32[]{:S(2)}) collective-permute-start(f32[8256]{0:T(1024)S(1)} %add.45), channel_id=1, source_target_pairs={{0,32},{16,48},{32,0},{48,16},{64,96},{80,112},{96,64},{112,80},{1... | collective-permute-start | bytes 99080 | tf_op jit(solution)/shard_map/ppermute | solution.py:21
  141.5 10.0 %collective-permute-start.10 = (f32[8256]{0:T(1024)S(1)}, f32[8256]{0:T(1024)S(1)}, u32[]{:S(2)}, u32[]{:S(2)}) collective-permute-start(f32[8256]{0:T(1024)S(1)} %add.46), channel_id=1, source_target_pairs={{0,64},{16,80},{32,96},{48,112},{64,0},{80,16},{96,32},{112,48},{1... | collective-permute-start | bytes 99080 | tf_op jit(solution)/shard_map/ppermute | solution.py:21
  151.5 5.8 %collective-permute-start.11 = (f32[8256]{0:T(1024)S(1)}, f32[8256]{0:T(1024)S(1)}, u32[]{:S(2)}, u32[]{:S(2)}) collective-permute-start(f32[8256]{0:T(1024)S(1)} %add.47), channel_id=1, source_target_pairs={{0,128},{16,144},{32,160},{48,176},{64,192},{80,208},{96,224},{112... | collective-permute-start | bytes 99080 | tf_op jit(solution)/shard_map/ppermute | solution.py:21
  157.3 7.1 %collective-permute-start.12 = (f32[8256]{0:T(1024)S(1)}, f32[8256]{0:T(1024)S(1)}, u32[]{:S(2)}, u32[]{:S(2)}) collective-permute-start(f32[8256]{0:T(1024)S(1)} %add.48), channel_id=1, source_target_pairs={{0,384},{16,400},{32,416},{48,432},{64,448},{80,464},{96,480},{112... | collective-permute-start | bytes 99080 | tf_op jit(solution)/shard_map/ppermute | solution.py:21

commit v7 on v6

--- a/solution.py
+++ b/solution.py
@@ -56,8 +56,7 @@
         return kinetic + wide_pot[plane] * centre, centre
 
     def sweep(field, older, out, lo, hi, scale, carry_scale):
-        @pl.loop(lo, hi)
-        def _(plane):
+        for plane in range(lo, hi):
             for band in range(band_count):
                 applied, centre = apply(field, band, plane)
                 value = (applied - CENTER * centre) * scale
@@ -80,8 +79,7 @@
     final = bufs[field]
     filtered_ref[...] = final[:, width : width + own_planes]
 
-    @pl.loop(width, width + own_planes)
-    def _(plane):
+    for plane in range(width, width + own_planes):
         for band in range(band_count):
             image_ref[band, plane - width], _ = apply(final, band, plane)
 

time: 179 us -> 173 us (0.966)
  Pallas kernels: 12 us -> 5.77 us
    pallas_call x1, Pallas kernels: 12 us -> 5.77 us  [filter_and_image(): pl.pallas_call(filter_kernel, out_shape=(jax.ShapeDtypeStruct(shape, jnp....]
where the time goes in v7:
time: 173 us; the launch traced here: 172 us
  starting transfers between devices  57.2 us (33%)
  waiting for transfers between devices  55.9 us (32%)
  blocking collectives  32.5 us (19%)
  other arithmetic  12.7 us (7%)
  local copies, waits for them, and re-layouts  5.89 us (3%)
  Pallas kernels  5.77 us (3%)
    ppermute x9, waiting for transfers between devices, butterfly_sum(): values = values + lax.ppermute(values, axis, pairs)  45.3 us
    ppermute x9, starting transfers between devices, butterfly_sum(): values = values + lax.ppermute(values, axis, pairs)  36 us
    all_to_all x1, blocking collectives, on_device(): moved = lax.all_to_all(both, 'band', 2, 1, tiled=True)  32.5 us
    ppermute x1, starting transfers between devices, on_device(): lax.ppermute(potential[potential.shape[0] - width:], ('band', 'grid'), re...  13.8 us
    ppermute x1, waiting for transfers between devices, on_device(): lax.ppermute(potential[:width], ('band', 'grid'), replica_pairs(-1))  10.6 us
    another operation x3, other arithmetic, on_device(): factor = jnp.linalg.cholesky(margin)  6.52 us
    pallas_call x1, Pallas kernels, filter_and_image(): pl.pallas_call(filter_kernel, out_shape=(jax.ShapeDtypeStruct(shape, jnp....  5.77 us
    another operation x2, other arithmetic, on_device(): lax.linalg.triangular_solve(factor, coefficients.T, left_side=True, lower...  5.55 us
  transfers between devices with their start and end apart: 13, of which 10 were waited for; matrix products, arithmetic and copies ran while one was open for 0% of the time, Pallas kernels for 0%

profile of v7, /device:TPU:24, one launch (start us, length us, event | category | flops | bytes accessed | tf_op | source)
XLA Modules:
  0.0 172.2 jit_solution(16750090327814004140)
XLA Ops:
  0.6 1.9 %collective-permute-start = (f32[2,10,32,128]{3,2,1,0:T(8,128)}, f32[2,10,32,128]{3,2,1,0:T(8,128)S(1)}, u32[]{:S(2)}, u32[]{:S(2)}) collective-permute-start(f32[2,10,32,128]{3,2,1,0:T(8,128)} %own_ref.1), channel_id=1, source_target_pairs={{0,1},{1,2},{2,3},{3,4},{4,5},{5,6},{6,7},{7,8},{8,9},{9,10},{10,1... | collective-permute-start | bytes 983048 | tf_op jit(solution)/shard_map/ppermute | solution.py:120
  2.6 3.6 %collective-permute-start.1 = (f32[2,10,32,128]{3,2,1,0:T(8,128)}, f32[2,10,32,128]{3,2,1,0:T(8,128)S(1)}, u32[]{:S(2)}, u32[]{:S(2)}) collective-permute-start(f32[2,10,32,128]{3,2,1,0:T(8,128)} %own_ref.1), channel_id=1, source_target_pairs={{1,0},{2,1},{3,2},{4,3},{5,4},{6,5},{7,6},{8,7},{9,8},{10,9},{11,1... | collective-permute-start | bytes 983048 | tf_op jit(solution)/shard_map/ppermute | solution.py:121
  6.2 13.8 %collective-permute-start.2 = (f32[10,32,128]{2,1,0:T(8,128)}, f32[10,32,128]{2,1,0:T(8,128)S(1)}, u32[]{:S(2)}, u32[]{:S(2)}) collective-permute-start(f32[10,32,128]{2,1,0:T(8,128)} %own_pot.1), channel_id=1, source_target_pairs={{79,0},{95,16},{111,32},{127,48},{15,64},{31,80},{47,96},{63,112},... | collective-permute-start | bytes 491528 | tf_op jit(solution)/shard_map/ppermute | solution.py:122
  20.0 1.9 %collective-permute-start.3 = (f32[10,32,128]{2,1,0:T(8,128)}, f32[10,32,128]{2,1,0:T(8,128)S(1)}, u32[]{:S(2)}, u32[]{:S(2)}) collective-permute-start(f32[10,32,128]{2,1,0:T(8,128)} %own_pot.1), channel_id=1, source_target_pairs={{1,0},{17,16},{33,32},{49,48},{65,64},{81,80},{97,96},{113,112},{1... | collective-permute-start | bytes 491528 | tf_op jit(solution)/shard_map/ppermute | solution.py:123
  21.9 10.6 %collective-permute-done.3.above_pot = f32[10,32,128]{2,1,0:T(8,128)S(1)} collective-permute-done((f32[10,32,128]{2,1,0:T(8,128)}, f32[10,32,128]{2,1,0:T(8,128)S(1)}, u32[]{:S(2)}, u32[]{:S(2)}) %collective-permute-start.3) | collective-permute-done | bytes 163872 | tf_op jit(solution)/shard_map/ppermute | solution.py:123
  32.6 0.7 copy-done.4
  33.3 0.7 copy-done.2
  34.1 5.8 %shard_map.49 = (f32[2,10,32,128]{3,2,1,0:T(8,128)}, f32[2,10,32,128]{3,2,1,0:T(8,128)}) custom-call(f32[2,10,32,128]{3,2,1,0:T(8,128)} %copy-done.1, f32[2,10,32,128]{3,2,1,0:T(8,128)} %own_ref.1, f32[2,10,32,128]{3,2,1,0:T(8,128)} %copy-done.2, f32[10,32,128]{2,1,0:T(8,128)} %copy-done.3, f32[10,32,128]{2,1,0:T(8,128)} %own_pot.1, f32[10,32,128]{2,1,0:T(8,128)} %copy-done.4), custom_call_target="tpu_custom_call" | custom-call | flops 29491200 | bytes 2949120 | tf_op jit(solution)/shard_map/pallas_call | solution.py:93
  39.8 1.0 stack.7
  41.1 0.7 copy-done
  42.4 32.5 %all_to_all.15 = f32[2,2,32,1280]{3,1,0,2:T(2,128)S(1)} all-to-all(f32[2,2,32,1280]{3,1,0,2:T(2,128)S(1)} %pad_maximum_fusion), channel_id=1, replica_groups=mesh['band'=32,'grid'=16] {'band'}, dimensions={2} | all-to-all | bytes 1310720 | tf_op jit(solution)/shard_map/all_to_all | solution.py:134
  76.8 17.2 %collective-permute-start.4 = (f32[8256]{0:T(1024)S(1)}, f32[8256]{0:T(1024)S(1)}, u32[]{:S(2)}, u32[]{:S(2)}) collective-permute-start(f32[8256]{0:T(1024)S(1)} %constant_dynamic-update-slice_fusion), channel_id=1, source_target_pairs={{0,1},{1,0},{2,3},{3,2},{4,5},{5,4},{6,7},{7,6},{8,9},{9,8},{10,11... | collective-permute-start | bytes 99080 | tf_op jit(solution)/shard_map/ppermute | solution.py:21
  94.0 0.8 collective-permute-done.4
  94.8 1.9 %collective-permute-start.5 = (f32[8256]{0:T(1024)S(1)}, f32[8256]{0:T(1024)S(1)}, u32[]{:S(2)}, u32[]{:S(2)}) collective-permute-start(f32[8256]{0:T(1024)S(1)} %add.41), channel_id=1, source_target_pairs={{0,2},{1,3},{2,0},{3,1},{4,6},{5,7},{6,4},{7,5},{8,10},{9,11},{10,... | collective-permute-start | bytes 99080 | tf_op jit(solution)/shard_map/ppermute | solution.py:21
  96.7 3.9 %collective-permute-done.5 = f32[8256]{0:T(1024)S(1)} collective-permute-done((f32[8256]{0:T(1024)S(1)}, f32[8256]{0:T(1024)S(1)}, u32[]{:S(2)}, u32[]{:S(2)}) %collective-permute-start.5) | collective-permute-done | bytes 33056 | tf_op jit(solution)/shard_map/ppermute | solution.py:21
  100.7 1.9 %collective-permute-start.6 = (f32[8256]{0:T(1024)S(1)}, f32[8256]{0:T(1024)S(1)}, u32[]{:S(2)}, u32[]{:S(2)}) collective-permute-start(f32[8256]{0:T(1024)S(1)} %add.42), channel_id=1, source_target_pairs={{0,6},{1,7},{2,4},{3,5},{4,2},{5,3},{6,0},{7,1},{8,14},{9,15},{10,... | collective-permute-start | bytes 99080 | tf_op jit(solution)/shard_map/ppermute | solution.py:21
  102.6 5.1 %collective-permute-done.6 = f32[8256]{0:T(1024)S(1)} collective-permute-done((f32[8256]{0:T(1024)S(1)}, f32[8256]{0:T(1024)S(1)}, u32[]{:S(2)}, u32[]{:S(2)}) %collective-permute-start.6) | collective-permute-done | bytes 33056 | tf_op jit(solution)/shard_map/ppermute | solution.py:21
  107.7 4.5 %collective-permute-start.7 = (f32[8256]{0:T(1024)S(1)}, f32[8256]{0:T(1024)S(1)}, u32[]{:S(2)}, u32[]{:S(2)}) collective-permute-start(f32[8256]{0:T(1024)S(1)} %add.43), channel_id=1, source_target_pairs={{0,8},{1,9},{2,10},{3,11},{4,12},{5,13},{6,14},{7,15},{8,0},{9,1},... | collective-permute-start | bytes 99080 | tf_op jit(solution)/shard_map/ppermute | solution.py:21
  112.2 10.5 %collective-permute-done.7 = f32[8256]{0:T(1024)S(1)} collective-permute-done((f32[8256]{0:T(1024)S(1)}, f32[8256]{0:T(1024)S(1)}, u32[]{:S(2)}, u32[]{:S(2)}) %collective-permute-start.7) | collective-permute-done | bytes 33056 | tf_op jit(solution)/shard_map/ppermute | solution.py:21
  122.7 1.9 %collective-permute-start.8 = (f32[8256]{0:T(1024)S(1)}, f32[8256]{0:T(1024)S(1)}, u32[]{:S(2)}, u32[]{:S(2)}) collective-permute-start(f32[8256]{0:T(1024)S(1)} %add.44), channel_id=1, source_target_pairs={{0,16},{16,0},{32,48},{48,32},{64,80},{80,64},{96,112},{112,96},{1... | collective-permute-start | bytes 99080 | tf_op jit(solution)/shard_map/ppermute | solution.py:21
  124.6 3.9 %collective-permute-done.8 = f32[8256]{0:T(1024)S(1)} collective-permute-done((f32[8256]{0:T(1024)S(1)}, f32[8256]{0:T(1024)S(1)}, u32[]{:S(2)}, u32[]{:S(2)}) %collective-permute-start.8) | collective-permute-done | bytes 33056 | tf_op jit(solution)/shard_map/ppermute | solution.py:21
  128.5 1.9 %collective-permute-start.9 = (f32[8256]{0:T(1024)S(1)}, f32[8256]{0:T(1024)S(1)}, u32[]{:S(2)}, u32[]{:S(2)}) collective-permute-start(f32[8256]{0:T(1024)S(1)} %add.45), channel_id=1, source_target_pairs={{0,32},{16,48},{32,0},{48,16},{64,96},{80,112},{96,64},{112,80},{1... | collective-permute-start | bytes 99080 | tf_op jit(solution)/shard_map/ppermute | solution.py:21
  130.4 4.8 %collective-permute-done.9 = f32[8256]{0:T(1024)S(1)} collective-permute-done((f32[8256]{0:T(1024)S(1)}, f32[8256]{0:T(1024)S(1)}, u32[]{:S(2)}, u32[]{:S(2)}) %collective-permute-start.9) | collective-permute-done | bytes 33056 | tf_op jit(solution)/shard_map/ppermute | solution.py:21
  135.3 1.9 %collective-permute-start.10 = (f32[8256]{0:T(1024)S(1)}, f32[8256]{0:T(1024)S(1)}, u32[]{:S(2)}, u32[]{:S(2)}) collective-permute-start(f32[8256]{0:T(1024)S(1)} %add.46), channel_id=1, source_target_pairs={{0,64},{16,80},{32,96},{48,112},{64,0},{80,16},{96,32},{112,48},{1... | collective-permute-start | bytes 99080 | tf_op jit(solution)/shard_map/ppermute | solution.py:21
  137.2 8.1 %collective-permute-done.10 = f32[8256]{0:T(1024)S(1)} collective-permute-done((f32[8256]{0:T(1024)S(1)}, f32[8256]{0:T(1024)S(1)}, u32[]{:S(2)}, u32[]{:S(2)}) %collective-permute-start.10) | collective-permute-done | bytes 33056 | tf_op jit(solution)/shard_map/ppermute | solution.py:21
  145.3 1.9 %collective-permute-start.11 = (f32[8256]{0:T(1024)S(1)}, f32[8256]{0:T(1024)S(1)}, u32[]{:S(2)}, u32[]{:S(2)}) collective-permute-start(f32[8256]{0:T(1024)S(1)} %add.47), channel_id=1, source_target_pairs={{0,128},{16,144},{32,160},{48,176},{64,192},{80,208},{96,224},{112... | collective-permute-start | bytes 99080 | tf_op jit(solution)/shard_map/ppermute | solution.py:21
  147.2 3.9 %collective-permute-done.11 = f32[8256]{0:T(1024)S(1)} collective-permute-done((f32[8256]{0:T(1024)S(1)}, f32[8256]{0:T(1024)S(1)}, u32[]{:S(2)}, u32[]{:S(2)}) %collective-permute-start.11) | collective-permute-done | bytes 33056 | tf_op jit(solution)/shard_map/ppermute | solution.py:21
  151.1 2.9 %collective-permute-start.12 = (f32[8256]{0:T(1024)S(1)}, f32[8256]{0:T(1024)S(1)}, u32[]{:S(2)}, u32[]{:S(2)}) collective-permute-start(f32[8256]{0:T(1024)S(1)} %add.48), channel_id=1, source_target_pairs={{0,384},{16,400},{32,416},{48,432},{64,448},{80,464},{96,480},{112... | collective-permute-start | bytes 99080 | tf_op jit(solution)/shard_map/ppermute | solution.py:21
  154.0 4.2 %collective-permute-done.12 = f32[8256]{0:T(1024)S(1)} collective-permute-done((f32[8256]{0:T(1024)S(1)}, f32[8256]{0:T(1024)S(1)}, u32[]{:S(2)}, u32[]{:S(2)}) %collective-permute-start.12) | collective-permute-done | bytes 33056 | tf_op jit(solution)/shard_map/ppermute | solution.py:21
  158.4 5.8 %cholesky.18 = f32[64,64]{1,0:T(8,128)S(1)} custom-call(f32[64,64]{1,0:T(8,128)S(1)} %fusion.7), custom_call_target="Cholesky" | custom-call | tf_op jit(solution)/shard_map/jit(cholesky)/cholesky | solution.py:152
  164.9 0.7 fusion
  165.5 4.9 %custom-call.8 = f32[1,64,64]{1,2,0:T(8,128)S(1)} custom-call(f32[1,64,64]{2,1,0:T(8,128)S(1)} %fusion), custom_call_target="InvertDiagBlocksLowerTriangular" | custom-call | tf_op jit(solution)/shard_map/triangular_solve/custom-call.0 | solution.py:154
  (46 shorter events, 5.4 us)
Async XLA Ops:
  0.6 31.9 %collective-permute-start = (f32[2,10,32,128]{3,2,1,0:T(8,128)}, f32[2,10,32,128]{3,2,1,0:T(8,128)S(1)}, u32[]{:S(2)}, u32[]{:S(2)}) collective-permute-start(f32[2,10,32,128]{3,2,1,0:T(8,128)} %own_ref.1), channel_id=1, source_target_pairs={{0,1},{1,2},{2,3},{3,4},{4,5},{5,6},{6,7},{7,8},{8,9},{9,10},{10,1... | collective-permute-start | bytes 983048 | tf_op jit(solution)/shard_map/ppermute | solution.py:120
  2.6 30.0 %collective-permute-start.1 = (f32[2,10,32,128]{3,2,1,0:T(8,128)}, f32[2,10,32,128]{3,2,1,0:T(8,128)S(1)}, u32[]{:S(2)}, u32[]{:S(2)}) collective-permute-start(f32[2,10,32,128]{3,2,1,0:T(8,128)} %own_ref.1), channel_id=1, source_target_pairs={{1,0},{2,1},{3,2},{4,3},{5,4},{6,5},{7,6},{8,7},{9,8},{10,9},{11,1... | collective-permute-start | bytes 983048 | tf_op jit(solution)/shard_map/ppermute | solution.py:121
  6.2 15.7 %collective-permute-start.2 = (f32[10,32,128]{2,1,0:T(8,128)}, f32[10,32,128]{2,1,0:T(8,128)S(1)}, u32[]{:S(2)}, u32[]{:S(2)}) collective-permute-start(f32[10,32,128]{2,1,0:T(8,128)} %own_pot.1), channel_id=1, source_target_pairs={{79,0},{95,16},{111,32},{127,48},{15,64},{31,80},{47,96},{63,112},... | collective-permute-start | bytes 491528 | tf_op jit(solution)/shard_map/ppermute | solution.py:122
  20.0 12.6 %collective-permute-start.3 = (f32[10,32,128]{2,1,0:T(8,128)}, f32[10,32,128]{2,1,0:T(8,128)S(1)}, u32[]{:S(2)}, u32[]{:S(2)}) collective-permute-start(f32[10,32,128]{2,1,0:T(8,128)} %own_pot.1), channel_id=1, source_target_pairs={{1,0},{17,16},{33,32},{49,48},{65,64},{81,80},{97,96},{113,112},{1... | collective-permute-start | bytes 491528 | tf_op jit(solution)/shard_map/ppermute | solution.py:123
  21.9 10.6 %copy-start.3 = (f32[10,32,128]{2,1,0:T(8,128)}, f32[10,32,128]{2,1,0:T(8,128)S(1)}, u32[]{:S(2)}) copy-start(f32[10,32,128]{2,1,0:T(8,128)S(1)} %collective-permute-done.2.below_pot) | copy-start | bytes 491524
  32.5 0.7 copy-start.4
  32.6 0.8 copy-start.1
  33.3 0.7 copy-start.2
  40.9 1.0 copy-start
  76.8 18.0 %collective-permute-start.4 = (f32[8256]{0:T(1024)S(1)}, f32[8256]{0:T(1024)S(1)}, u32[]{:S(2)}, u32[]{:S(2)}) collective-permute-start(f32[8256]{0:T(1024)S(1)} %constant_dynamic-update-slice_fusion), channel_id=1, source_target_pairs={{0,1},{1,0},{2,3},{3,2},{4,5},{5,4},{6,7},{7,6},{8,9},{9,8},{10,11... | collective-permute-start | bytes 99080 | tf_op jit(solution)/shard_map/ppermute | solution.py:21
  94.8 5.8 %collective-permute-start.5 = (f32[8256]{0:T(1024)S(1)}, f32[8256]{0:T(1024)S(1)}, u32[]{:S(2)}, u32[]{:S(2)}) collective-permute-start(f32[8256]{0:T(1024)S(1)} %add.41), channel_id=1, source_target_pairs={{0,2},{1,3},{2,0},{3,1},{4,6},{5,7},{6,4},{7,5},{8,10},{9,11},{10,... | collective-permute-start | bytes 99080 | tf_op jit(solution)/shard_map/ppermute | solution.py:21
  100.7 7.1 %collective-permute-start.6 = (f32[8256]{0:T(1024)S(1)}, f32[8256]{0:T(1024)S(1)}, u32[]{:S(2)}, u32[]{:S(2)}) collective-permute-start(f32[8256]{0:T(1024)S(1)} %add.42), channel_id=1, source_target_pairs={{0,6},{1,7},{2,4},{3,5},{4,2},{5,3},{6,0},{7,1},{8,14},{9,15},{10,... | collective-permute-start | bytes 99080 | tf_op jit(solution)/shard_map/ppermute | solution.py:21
  107.7 14.9 %collective-permute-start.7 = (f32[8256]{0:T(1024)S(1)}, f32[8256]{0:T(1024)S(1)}, u32[]{:S(2)}, u32[]{:S(2)}) collective-permute-start(f32[8256]{0:T(1024)S(1)} %add.43), channel_id=1, source_target_pairs={{0,8},{1,9},{2,10},{3,11},{4,12},{5,13},{6,14},{7,15},{8,0},{9,1},... | collective-permute-start | bytes 99080 | tf_op jit(solution)/shard_map/ppermute | solution.py:21
  122.7 5.8 %collective-permute-start.8 = (f32[8256]{0:T(1024)S(1)}, f32[8256]{0:T(1024)S(1)}, u32[]{:S(2)}, u32[]{:S(2)}) collective-permute-start(f32[8256]{0:T(1024)S(1)} %add.44), channel_id=1, source_target_pairs={{0,16},{16,0},{32,48},{48,32},{64,80},{80,64},{96,112},{112,96},{1... | collective-permute-start | bytes 99080 | tf_op jit(solution)/shard_map/ppermute | solution.py:21
  128.5 6.7 %collective-permute-start.9 = (f32[8256]{0:T(1024)S(1)}, f32[8256]{0:T(1024)S(1)}, u32[]{:S(2)}, u32[]{:S(2)}) collective-permute-start(f32[8256]{0:T(1024)S(1)} %add.45), channel_id=1, source_target_pairs={{0,32},{16,48},{32,0},{48,16},{64,96},{80,112},{96,64},{112,80},{1... | collective-permute-start | bytes 99080 | tf_op jit(solution)/shard_map/ppermute | solution.py:21
  135.3 10.0 %collective-permute-start.10 = (f32[8256]{0:T(1024)S(1)}, f32[8256]{0:T(1024)S(1)}, u32[]{:S(2)}, u32[]{:S(2)}) collective-permute-start(f32[8256]{0:T(1024)S(1)} %add.46), channel_id=1, source_target_pairs={{0,64},{16,80},{32,96},{48,112},{64,0},{80,16},{96,32},{112,48},{1... | collective-permute-start | bytes 99080 | tf_op jit(solution)/shard_map/ppermute | solution.py:21
  145.3 5.8 %collective-permute-start.11 = (f32[8256]{0:T(1024)S(1)}, f32[8256]{0:T(1024)S(1)}, u32[]{:S(2)}, u32[]{:S(2)}) collective-permute-start(f32[8256]{0:T(1024)S(1)} %add.47), channel_id=1, source_target_pairs={{0,128},{16,144},{32,160},{48,176},{64,192},{80,208},{96,224},{112... | collective-permute-start | bytes 99080 | tf_op jit(solution)/shard_map/ppermute | solution.py:21
  151.1 7.1 %collective-permute-start.12 = (f32[8256]{0:T(1024)S(1)}, f32[8256]{0:T(1024)S(1)}, u32[]{:S(2)}, u32[]{:S(2)}) collective-permute-start(f32[8256]{0:T(1024)S(1)} %add.48), channel_id=1, source_target_pairs={{0,384},{16,400},{32,416},{48,432},{64,448},{80,464},{96,480},{112... | collective-permute-start | bytes 99080 | tf_op jit(solution)/shard_map/ppermute | solution.py:21

commit v8 on v7

--- a/solution.py
+++ b/solution.py
@@ -99,6 +99,51 @@
         + [pltpu.VMEM((total, rows, lanes), jnp.float32)],
         cost_estimate=pl.CostEstimate(flops=30 * cells * 4, transcendentals=0, bytes_accessed=4 * cells * 3),
     )(below, own, above, below_pot, own_pot, above_pot)
+
+
+def rayleigh_ritz_kernel(margin_ref, subspace_ref, norms_ref, projected_ref, residual_ref):
+    size = margin_ref.shape[0]
+    work = margin_ref[...]
+    rows = lax.broadcasted_iota(jnp.int32, (size, size), 0)
+    cols = lax.broadcasted_iota(jnp.int32, (size, size), 1)
+    row_index = rows[:, :1]
+    col_index = cols[:1, :]
+    factor = jnp.zeros((size, size), jnp.float32)
+    factor_t = jnp.zeros((size, size), jnp.float32)
+    pivots = []
+    for k in range(size):
+        root = jnp.sqrt(work[k : k + 1, k : k + 1])
+        column = jnp.where(row_index >= k, work[:, k : k + 1] / root, 0.0)
+        row = jnp.where(col_index >= k, work[k : k + 1, :] / root, 0.0)
+        work = work - column * row
+        factor = jnp.where(cols == k, column, factor)
+        factor_t = jnp.where(rows == k, row, factor_t)
+        pivots.append(root)
+    rest = subspace_ref[...]
+    coeff_t = jnp.zeros((size, size), jnp.float32)
+    for j in range(size):
+        column = rest[:, j : j + 1] / pivots[j]
+        rest = rest - column * jnp.where(col_index > j, factor_t[j : j + 1, :], 0.0)
+        coeff_t = jnp.where(cols == j, column, coeff_t)
+    rest = coeff_t
+    projected = jnp.zeros((size, size), jnp.float32)
+    for i in range(size):
+        row = rest[i : i + 1, :] / pivots[i]
+        rest = rest - jnp.where(row_index > i, factor[:, i : i + 1], 0.0) * row
+        projected = jnp.where(rows == i, row, projected)
+    projected_ref[...] = projected
+    residual_ref[...] = norms_ref[...] - jnp.sum(coeff_t * coeff_t, axis=1, keepdims=True)
+
+
+def rayleigh_ritz(margin, subspace, image_norms):
+    size = margin.shape[0]
+    return pl.pallas_call(
+        rayleigh_ritz_kernel,
+        out_shape=(jax.ShapeDtypeStruct((size, size), jnp.float32), jax.ShapeDtypeStruct((size, 1), jnp.float32)),
+        in_specs=[pl.BlockSpec(memory_space=pltpu.VMEM)] * 3,
+        out_specs=(pl.BlockSpec(memory_space=pltpu.VMEM), pl.BlockSpec(memory_space=pltpu.VMEM)),
+        cost_estimate=pl.CostEstimate(flops=6 * size**3, transcendentals=size, bytes_accessed=4 * 4 * size * size),
+    )(margin, subspace, image_norms.reshape(size, 1))
 
 
 def replica_pairs(direction):
@@ -149,10 +194,9 @@
     margin = packed[:square].reshape(total_bands, total_bands)
     subspace = packed[square : 2 * square].reshape(total_bands, total_bands)
     image_norms = packed[2 * square :]
-    factor = jnp.linalg.cholesky(margin)
-    coefficients = lax.linalg.triangular_solve(factor, subspace.T, left_side=True, lower=True)
-    projected = lax.linalg.triangular_solve(factor, coefficients.T, left_side=True, lower=True)
-    residual_norms = image_norms - jnp.sum(coefficients * coefficients, axis=0)
+    margin = (margin + margin.T) / 2
+    projected, residual_norms = rayleigh_ritz(margin, subspace, image_norms)
+    residual_norms = residual_norms.reshape(-1)
     projected_rows = lax.dynamic_slice_in_dim(projected, first_band, band_count, 0)
     residual_rows = lax.dynamic_slice_in_dim(residual_norms, first_band, band_count, 0)
     return (current, projected_rows, residual_rows)

time: 173 us -> 173 us (level)
  other arithmetic: 12.7 us -> 1.22 us
  Pallas kernels: 5.77 us -> 15 us
  local copies, waits for them, and re-layouts: 5.89 us -> 8.58 us
    another operation x5 -> x0, other arithmetic: 12.1 us -> none  [the longest x3 6.52 us: on_device(): factor = jnp.linalg.cholesky(margin)]
    pallas_call x0 -> x1, Pallas kernels: none -> 9.24 us  [rayleigh_ritz(): pl.pallas_call(rayleigh_ritz_kernel, out_shape=(jax.ShapeDtypeStruct((siz...]
where the time goes in v8:
time: 173 us; the launch traced here: 172 us
  starting transfers between devices  57.2 us (33%)
  waiting for transfers between devices  55.9 us (32%)
  blocking collectives  32.5 us (19%)
  Pallas kernels  15 us (9%)
  local copies, waits for them, and re-layouts  8.58 us (5%)
    ppermute x9, waiting for transfers between devices, butterfly_sum(): values = values + lax.ppermute(values, axis, pairs)  45.3 us
    ppermute x9, starting transfers between devices, butterfly_sum(): values = values + lax.ppermute(values, axis, pairs)  36 us
    all_to_all x1, blocking collectives, on_device(): moved = lax.all_to_all(both, 'band', 2, 1, tiled=True)  32.5 us
    ppermute x1, starting transfers between devices, on_device(): lax.ppermute(potential[potential.shape[0] - width:], ('band', 'grid'), re...  13.8 us
    ppermute x1, waiting for transfers between devices, on_device(): lax.ppermute(potential[:width], ('band', 'grid'), replica_pairs(-1))  10.6 us
    pallas_call x1, Pallas kernels, rayleigh_ritz(): pl.pallas_call(rayleigh_ritz_kernel, out_shape=(jax.ShapeDtypeStruct((siz...  9.24 us
    pallas_call x1, Pallas kernels, filter_and_image(): pl.pallas_call(filter_kernel, out_shape=(jax.ShapeDtypeStruct(shape, jnp....  5.78 us
    ppermute x1, starting transfers between devices, on_device(): lax.ppermute(trial_bands[:, :width], 'grid', [((i + 1) % count, i) for i...  3.64 us
  transfers between devices with their start and end apart: 13, of which 10 were waited for; matrix products, arithmetic and copies ran while one was open for 0% of the time, Pallas kernels for 0%

profile of v8, /device:TPU:24, one launch (start us, length us, event | category | flops | bytes accessed | tf_op | source)
XLA Modules:
  0.0 172.1 jit_solution(1338185330555349904)
XLA Ops:
  0.6 1.9 %collective-permute-start = (f32[2,10,32,128]{3,2,1,0:T(8,128)}, f32[2,10,32,128]{3,2,1,0:T(8,128)S(1)}, u32[]{:S(2)}, u32[]{:S(2)}) collective-permute-start(f32[2,10,32,128]{3,2,1,0:T(8,128)} %own_ref.1), channel_id=1, source_target_pairs={{0,1},{1,2},{2,3},{3,4},{4,5},{5,6},{6,7},{7,8},{8,9},{9,10},{10,1... | collective-permute-start | bytes 983048 | tf_op jit(solution)/shard_map/ppermute | solution.py:165
  2.6 3.6 %collective-permute-start.1 = (f32[2,10,32,128]{3,2,1,0:T(8,128)}, f32[2,10,32,128]{3,2,1,0:T(8,128)S(1)}, u32[]{:S(2)}, u32[]{:S(2)}) collective-permute-start(f32[2,10,32,128]{3,2,1,0:T(8,128)} %own_ref.1), channel_id=1, source_target_pairs={{1,0},{2,1},{3,2},{4,3},{5,4},{6,5},{7,6},{8,7},{9,8},{10,9},{11,1... | collective-permute-start | bytes 983048 | tf_op jit(solution)/shard_map/ppermute | solution.py:166
  6.2 13.8 %collective-permute-start.2 = (f32[10,32,128]{2,1,0:T(8,128)}, f32[10,32,128]{2,1,0:T(8,128)S(1)}, u32[]{:S(2)}, u32[]{:S(2)}) collective-permute-start(f32[10,32,128]{2,1,0:T(8,128)} %own_pot.1), channel_id=1, source_target_pairs={{79,0},{95,16},{111,32},{127,48},{15,64},{31,80},{47,96},{63,112},... | collective-permute-start | bytes 491528 | tf_op jit(solution)/shard_map/ppermute | solution.py:167
  20.0 1.9 %collective-permute-start.3 = (f32[10,32,128]{2,1,0:T(8,128)}, f32[10,32,128]{2,1,0:T(8,128)S(1)}, u32[]{:S(2)}, u32[]{:S(2)}) collective-permute-start(f32[10,32,128]{2,1,0:T(8,128)} %own_pot.1), channel_id=1, source_target_pairs={{1,0},{17,16},{33,32},{49,48},{65,64},{81,80},{97,96},{113,112},{1... | collective-permute-start | bytes 491528 | tf_op jit(solution)/shard_map/ppermute | solution.py:168
  21.9 10.6 %collective-permute-done.3.above_pot = f32[10,32,128]{2,1,0:T(8,128)S(1)} collective-permute-done((f32[10,32,128]{2,1,0:T(8,128)}, f32[10,32,128]{2,1,0:T(8,128)S(1)}, u32[]{:S(2)}, u32[]{:S(2)}) %collective-permute-start.3) | collective-permute-done | bytes 163872 | tf_op jit(solution)/shard_map/ppermute | solution.py:168
  33.3 0.7 copy-done.2
  34.0 5.8 %shard_map.49 = (f32[2,10,32,128]{3,2,1,0:T(8,128)}, f32[2,10,32,128]{3,2,1,0:T(8,128)}) custom-call(f32[2,10,32,128]{3,2,1,0:T(8,128)} %copy-done.1, f32[2,10,32,128]{3,2,1,0:T(8,128)} %own_ref.1, f32[2,10,32,128]{3,2,1,0:T(8,128)} %copy-done.2, f32[10,32,128]{2,1,0:T(8,128)} %copy-done.3, f32[10,32,128]{2,1,0:T(8,128)} %own_pot.1, f32[10,32,128]{2,1,0:T(8,128)} %copy-done.4), custom_call_target="tpu_custom_call" | custom-call | flops 29491200 | bytes 2949120 | tf_op jit(solution)/shard_map/pallas_call | solution.py:93
  39.8 1.0 stack.7
  41.1 0.7 copy-done
  42.4 32.5 %all_to_all.15 = f32[2,2,32,1280]{3,1,0,2:T(2,128)S(1)} all-to-all(f32[2,2,32,1280]{3,1,0,2:T(2,128)S(1)} %pad_maximum_fusion), channel_id=1, replica_groups=mesh['band'=32,'grid'=16] {'band'}, dimensions={2} | all-to-all | bytes 1310720 | tf_op jit(solution)/shard_map/all_to_all | solution.py:179
  76.8 17.2 %collective-permute-start.4 = (f32[8256]{0:T(1024)S(1)}, f32[8256]{0:T(1024)S(1)}, u32[]{:S(2)}, u32[]{:S(2)}) collective-permute-start(f32[8256]{0:T(1024)S(1)} %constant_dynamic-update-slice_fusion), channel_id=1, source_target_pairs={{0,1},{1,0},{2,3},{3,2},{4,5},{5,4},{6,7},{7,6},{8,9},{9,8},{10,11... | collective-permute-start | bytes 99080 | tf_op jit(solution)/shard_map/ppermute | solution.py:21
  94.0 0.8 collective-permute-done.4
  94.8 1.9 %collective-permute-start.5 = (f32[8256]{0:T(1024)S(1)}, f32[8256]{0:T(1024)S(1)}, u32[]{:S(2)}, u32[]{:S(2)}) collective-permute-start(f32[8256]{0:T(1024)S(1)} %add.34), channel_id=1, source_target_pairs={{0,2},{1,3},{2,0},{3,1},{4,6},{5,7},{6,4},{7,5},{8,10},{9,11},{10,... | collective-permute-start | bytes 99080 | tf_op jit(solution)/shard_map/ppermute | solution.py:21
  96.7 3.9 %collective-permute-done.5 = f32[8256]{0:T(1024)S(1)} collective-permute-done((f32[8256]{0:T(1024)S(1)}, f32[8256]{0:T(1024)S(1)}, u32[]{:S(2)}, u32[]{:S(2)}) %collective-permute-start.5) | collective-permute-done | bytes 33056 | tf_op jit(solution)/shard_map/ppermute | solution.py:21
  100.7 1.9 %collective-permute-start.6 = (f32[8256]{0:T(1024)S(1)}, f32[8256]{0:T(1024)S(1)}, u32[]{:S(2)}, u32[]{:S(2)}) collective-permute-start(f32[8256]{0:T(1024)S(1)} %add.35), channel_id=1, source_target_pairs={{0,6},{1,7},{2,4},{3,5},{4,2},{5,3},{6,0},{7,1},{8,14},{9,15},{10,... | collective-permute-start | bytes 99080 | tf_op jit(solution)/shard_map/ppermute | solution.py:21
  102.6 5.1 %collective-permute-done.6 = f32[8256]{0:T(1024)S(1)} collective-permute-done((f32[8256]{0:T(1024)S(1)}, f32[8256]{0:T(1024)S(1)}, u32[]{:S(2)}, u32[]{:S(2)}) %collective-permute-start.6) | collective-permute-done | bytes 33056 | tf_op jit(solution)/shard_map/ppermute | solution.py:21
  107.7 4.5 %collective-permute-start.7 = (f32[8256]{0:T(1024)S(1)}, f32[8256]{0:T(1024)S(1)}, u32[]{:S(2)}, u32[]{:S(2)}) collective-permute-start(f32[8256]{0:T(1024)S(1)} %add.36), channel_id=1, source_target_pairs={{0,8},{1,9},{2,10},{3,11},{4,12},{5,13},{6,14},{7,15},{8,0},{9,1},... | collective-permute-start | bytes 99080 | tf_op jit(solution)/shard_map/ppermute | solution.py:21
  112.2 10.4 %collective-permute-done.7 = f32[8256]{0:T(1024)S(1)} collective-permute-done((f32[8256]{0:T(1024)S(1)}, f32[8256]{0:T(1024)S(1)}, u32[]{:S(2)}, u32[]{:S(2)}) %collective-permute-start.7) | collective-permute-done | bytes 33056 | tf_op jit(solution)/shard_map/ppermute | solution.py:21
  122.7 1.9 %collective-permute-start.8 = (f32[8256]{0:T(1024)S(1)}, f32[8256]{0:T(1024)S(1)}, u32[]{:S(2)}, u32[]{:S(2)}) collective-permute-start(f32[8256]{0:T(1024)S(1)} %add.37), channel_id=1, source_target_pairs={{0,16},{16,0},{32,48},{48,32},{64,80},{80,64},{96,112},{112,96},{1... | collective-permute-start | bytes 99080 | tf_op jit(solution)/shard_map/ppermute | solution.py:21
  124.6 3.9 %collective-permute-done.8 = f32[8256]{0:T(1024)S(1)} collective-permute-done((f32[8256]{0:T(1024)S(1)}, f32[8256]{0:T(1024)S(1)}, u32[]{:S(2)}, u32[]{:S(2)}) %collective-permute-start.8) | collective-permute-done | bytes 33056 | tf_op jit(solution)/shard_map/ppermute | solution.py:21
  128.5 1.9 %collective-permute-start.9 = (f32[8256]{0:T(1024)S(1)}, f32[8256]{0:T(1024)S(1)}, u32[]{:S(2)}, u32[]{:S(2)}) collective-permute-start(f32[8256]{0:T(1024)S(1)} %add.38), channel_id=1, source_target_pairs={{0,32},{16,48},{32,0},{48,16},{64,96},{80,112},{96,64},{112,80},{1... | collective-permute-start | bytes 99080 | tf_op jit(solution)/shard_map/ppermute | solution.py:21
  130.4 4.8 %collective-permute-done.9 = f32[8256]{0:T(1024)S(1)} collective-permute-done((f32[8256]{0:T(1024)S(1)}, f32[8256]{0:T(1024)S(1)}, u32[]{:S(2)}, u32[]{:S(2)}) %collective-permute-start.9) | collective-permute-done | bytes 33056 | tf_op jit(solution)/shard_map/ppermute | solution.py:21
  135.3 1.9 %collective-permute-start.10 = (f32[8256]{0:T(1024)S(1)}, f32[8256]{0:T(1024)S(1)}, u32[]{:S(2)}, u32[]{:S(2)}) collective-permute-start(f32[8256]{0:T(1024)S(1)} %add.39), channel_id=1, source_target_pairs={{0,64},{16,80},{32,96},{48,112},{64,0},{80,16},{96,32},{112,48},{1... | collective-permute-start | bytes 99080 | tf_op jit(solution)/shard_map/ppermute | solution.py:21
  137.2 8.1 %collective-permute-done.10 = f32[8256]{0:T(1024)S(1)} collective-permute-done((f32[8256]{0:T(1024)S(1)}, f32[8256]{0:T(1024)S(1)}, u32[]{:S(2)}, u32[]{:S(2)}) %collective-permute-start.10) | collective-permute-done | bytes 33056 | tf_op jit(solution)/shard_map/ppermute | solution.py:21
  145.3 1.9 %collective-permute-start.11 = (f32[8256]{0:T(1024)S(1)}, f32[8256]{0:T(1024)S(1)}, u32[]{:S(2)}, u32[]{:S(2)}) collective-permute-start(f32[8256]{0:T(1024)S(1)} %add.40), channel_id=1, source_target_pairs={{0,128},{16,144},{32,160},{48,176},{64,192},{80,208},{96,224},{112... | collective-permute-start | bytes 99080 | tf_op jit(solution)/shard_map/ppermute | solution.py:21
  147.2 3.9 %collective-permute-done.11 = f32[8256]{0:T(1024)S(1)} collective-permute-done((f32[8256]{0:T(1024)S(1)}, f32[8256]{0:T(1024)S(1)}, u32[]{:S(2)}, u32[]{:S(2)}) %collective-permute-start.11) | collective-permute-done | bytes 33056 | tf_op jit(solution)/shard_map/ppermute | solution.py:21
  151.1 2.9 %collective-permute-start.12 = (f32[8256]{0:T(1024)S(1)}, f32[8256]{0:T(1024)S(1)}, u32[]{:S(2)}, u32[]{:S(2)}) collective-permute-start(f32[8256]{0:T(1024)S(1)} %add.41), channel_id=1, source_target_pairs={{0,384},{16,400},{32,416},{48,432},{64,448},{80,464},{96,480},{112... | collective-permute-start | bytes 99080 | tf_op jit(solution)/shard_map/ppermute | solution.py:21
  154.0 4.2 %collective-permute-done.12 = f32[8256]{0:T(1024)S(1)} collective-permute-done((f32[8256]{0:T(1024)S(1)}, f32[8256]{0:T(1024)S(1)}, u32[]{:S(2)}, u32[]{:S(2)}) %collective-permute-start.12) | collective-permute-done | bytes 33056 | tf_op jit(solution)/shard_map/ppermute | solution.py:21
  159.7 0.7 copy.14.norms_ref
  160.4 9.2 %shard_map.50 = (f32[64,64]{1,0:T(8,128)}, f32[64,1]{1,0:T(8,128)}) custom-call(f32[64,64]{1,0:T(8,128)} %fusion.margin_ref, f32[64,64]{1,0:T(8,128)} %slice.42.subspace_ref, f32[64,1]{1,0:T(8,128)} %copy.14.norms_ref), custom_call_target="tpu_custom_call" | custom-call | flops 1572864 | bytes 65536 | tf_op jit(solution)/shard_map/pallas_call | solution.py:140
  169.6 1.3 dynamic-slice_reduce_fusion
  170.9 1.2 constant_dynamic-slice_fusion
  (41 shorter events, 4.9 us)
Async XLA Ops:
  0.6 31.9 %collective-permute-start = (f32[2,10,32,128]{3,2,1,0:T(8,128)}, f32[2,10,32,128]{3,2,1,0:T(8,128)S(1)}, u32[]{:S(2)}, u32[]{:S(2)}) collective-permute-start(f32[2,10,32,128]{3,2,1,0:T(8,128)} %own_ref.1), channel_id=1, source_target_pairs={{0,1},{1,2},{2,3},{3,4},{4,5},{5,6},{6,7},{7,8},{8,9},{9,10},{10,1... | collective-permute-start | bytes 983048 | tf_op jit(solution)/shard_map/ppermute | solution.py:165
  2.6 30.0 %collective-permute-start.1 = (f32[2,10,32,128]{3,2,1,0:T(8,128)}, f32[2,10,32,128]{3,2,1,0:T(8,128)S(1)}, u32[]{:S(2)}, u32[]{:S(2)}) collective-permute-start(f32[2,10,32,128]{3,2,1,0:T(8,128)} %own_ref.1), channel_id=1, source_target_pairs={{1,0},{2,1},{3,2},{4,3},{5,4},{6,5},{7,6},{8,7},{9,8},{10,9},{11,1... | collective-permute-start | bytes 983048 | tf_op jit(solution)/shard_map/ppermute | solution.py:166
  6.2 15.7 %collective-permute-start.2 = (f32[10,32,128]{2,1,0:T(8,128)}, f32[10,32,128]{2,1,0:T(8,128)S(1)}, u32[]{:S(2)}, u32[]{:S(2)}) collective-permute-start(f32[10,32,128]{2,1,0:T(8,128)} %own_pot.1), channel_id=1, source_target_pairs={{79,0},{95,16},{111,32},{127,48},{15,64},{31,80},{47,96},{63,112},... | collective-permute-start | bytes 491528 | tf_op jit(solution)/shard_map/ppermute | solution.py:167
  20.0 12.6 %collective-permute-start.3 = (f32[10,32,128]{2,1,0:T(8,128)}, f32[10,32,128]{2,1,0:T(8,128)S(1)}, u32[]{:S(2)}, u32[]{:S(2)}) collective-permute-start(f32[10,32,128]{2,1,0:T(8,128)} %own_pot.1), channel_id=1, source_target_pairs={{1,0},{17,16},{33,32},{49,48},{65,64},{81,80},{97,96},{113,112},{1... | collective-permute-start | bytes 491528 | tf_op jit(solution)/shard_map/ppermute | solution.py:168
  21.9 10.6 %copy-start.3 = (f32[10,32,128]{2,1,0:T(8,128)}, f32[10,32,128]{2,1,0:T(8,128)S(1)}, u32[]{:S(2)}) copy-start(f32[10,32,128]{2,1,0:T(8,128)S(1)} %collective-permute-done.2.below_pot) | copy-start | bytes 491524
  32.5 0.7 copy-start.4
  32.6 0.8 copy-start.1
  33.3 0.7 copy-start.2
  40.9 1.0 copy-start
  76.8 18.0 %collective-permute-start.4 = (f32[8256]{0:T(1024)S(1)}, f32[8256]{0:T(1024)S(1)}, u32[]{:S(2)}, u32[]{:S(2)}) collective-permute-start(f32[8256]{0:T(1024)S(1)} %constant_dynamic-update-slice_fusion), channel_id=1, source_target_pairs={{0,1},{1,0},{2,3},{3,2},{4,5},{5,4},{6,7},{7,6},{8,9},{9,8},{10,11... | collective-permute-start | bytes 99080 | tf_op jit(solution)/shard_map/ppermute | solution.py:21
  94.8 5.8 %collective-permute-start.5 = (f32[8256]{0:T(1024)S(1)}, f32[8256]{0:T(1024)S(1)}, u32[]{:S(2)}, u32[]{:S(2)}) collective-permute-start(f32[8256]{0:T(1024)S(1)} %add.34), channel_id=1, source_target_pairs={{0,2},{1,3},{2,0},{3,1},{4,6},{5,7},{6,4},{7,5},{8,10},{9,11},{10,... | collective-permute-start | bytes 99080 | tf_op jit(solution)/shard_map/ppermute | solution.py:21
  100.7 7.1 %collective-permute-start.6 = (f32[8256]{0:T(1024)S(1)}, f32[8256]{0:T(1024)S(1)}, u32[]{:S(2)}, u32[]{:S(2)}) collective-permute-start(f32[8256]{0:T(1024)S(1)} %add.35), channel_id=1, source_target_pairs={{0,6},{1,7},{2,4},{3,5},{4,2},{5,3},{6,0},{7,1},{8,14},{9,15},{10,... | collective-permute-start | bytes 99080 | tf_op jit(solution)/shard_map/ppermute | solution.py:21
  107.7 14.9 %collective-permute-start.7 = (f32[8256]{0:T(1024)S(1)}, f32[8256]{0:T(1024)S(1)}, u32[]{:S(2)}, u32[]{:S(2)}) collective-permute-start(f32[8256]{0:T(1024)S(1)} %add.36), channel_id=1, source_target_pairs={{0,8},{1,9},{2,10},{3,11},{4,12},{5,13},{6,14},{7,15},{8,0},{9,1},... | collective-permute-start | bytes 99080 | tf_op jit(solution)/shard_map/ppermute | solution.py:21
  122.7 5.8 %collective-permute-start.8 = (f32[8256]{0:T(1024)S(1)}, f32[8256]{0:T(1024)S(1)}, u32[]{:S(2)}, u32[]{:S(2)}) collective-permute-start(f32[8256]{0:T(1024)S(1)} %add.37), channel_id=1, source_target_pairs={{0,16},{16,0},{32,48},{48,32},{64,80},{80,64},{96,112},{112,96},{1... | collective-permute-start | bytes 99080 | tf_op jit(solution)/shard_map/ppermute | solution.py:21
  128.5 6.7 %collective-permute-start.9 = (f32[8256]{0:T(1024)S(1)}, f32[8256]{0:T(1024)S(1)}, u32[]{:S(2)}, u32[]{:S(2)}) collective-permute-start(f32[8256]{0:T(1024)S(1)} %add.38), channel_id=1, source_target_pairs={{0,32},{16,48},{32,0},{48,16},{64,96},{80,112},{96,64},{112,80},{1... | collective-permute-start | bytes 99080 | tf_op jit(solution)/shard_map/ppermute | solution.py:21
  135.3 10.0 %collective-permute-start.10 = (f32[8256]{0:T(1024)S(1)}, f32[8256]{0:T(1024)S(1)}, u32[]{:S(2)}, u32[]{:S(2)}) collective-permute-start(f32[8256]{0:T(1024)S(1)} %add.39), channel_id=1, source_target_pairs={{0,64},{16,80},{32,96},{48,112},{64,0},{80,16},{96,32},{112,48},{1... | collective-permute-start | bytes 99080 | tf_op jit(solution)/shard_map/ppermute | solution.py:21
  145.3 5.8 %collective-permute-start.11 = (f32[8256]{0:T(1024)S(1)}, f32[8256]{0:T(1024)S(1)}, u32[]{:S(2)}, u32[]{:S(2)}) collective-permute-start(f32[8256]{0:T(1024)S(1)} %add.40), channel_id=1, source_target_pairs={{0,128},{16,144},{32,160},{48,176},{64,192},{80,208},{96,224},{112... | collective-permute-start | bytes 99080 | tf_op jit(solution)/shard_map/ppermute | solution.py:21
  151.1 7.1 %collective-permute-start.12 = (f32[8256]{0:T(1024)S(1)}, f32[8256]{0:T(1024)S(1)}, u32[]{:S(2)}, u32[]{:S(2)}) collective-permute-start(f32[8256]{0:T(1024)S(1)} %add.41), channel_id=1, source_target_pairs={{0,384},{16,400},{32,416},{48,432},{64,448},{80,464},{96,480},{112... | collective-permute-start | bytes 99080 | tf_op jit(solution)/shard_map/ppermute | solution.py:21

commit v9 on v7

--- a/solution.py
+++ b/solution.py
@@ -99,6 +99,54 @@
         + [pltpu.VMEM((total, rows, lanes), jnp.float32)],
         cost_estimate=pl.CostEstimate(flops=30 * cells * 4, transcendentals=0, bytes_accessed=4 * cells * 3),
     )(below, own, above, below_pot, own_pot, above_pot)
+
+
+def rayleigh_ritz_kernel(first_ref, margin_ref, subspace_ref, norms_ref, projected_ref, residual_ref,
+                         projected_buf, residual_buf):
+    size = margin_ref.shape[0]
+    work = margin_ref[...]
+    rest = subspace_ref[...]
+    rows = lax.broadcasted_iota(jnp.int32, (size, size), 0)
+    cols = lax.broadcasted_iota(jnp.int32, (size, size), 1)
+    row_index = rows[:, :1]
+    col_index = cols[:1, :]
+    coeff_t = jnp.zeros((size, size), jnp.float32)
+    columns, inverses = [], []
+    for k in range(size):
+        inverse = 1.0 / jnp.sqrt(work[k : k + 1, k : k + 1])
+        column = jnp.where(row_index >= k, work[:, k : k + 1] * inverse, 0.0)
+        row = jnp.where(col_index >= k, work[k : k + 1, :] * inverse, 0.0)
+        work = work - column * row
+        solved = rest[:, k : k + 1] * inverse
+        rest = rest - solved * jnp.where(col_index > k, row, 0.0)
+        coeff_t = jnp.where(cols == k, solved, coeff_t)
+        columns.append(jnp.where(row_index > k, column, 0.0))
+        inverses.append(inverse)
+    rest = coeff_t
+    projected = jnp.zeros((size, size), jnp.float32)
+    for i in range(size):
+        row = rest[i : i + 1, :] * inverses[i]
+        rest = rest - columns[i] * row
+        projected = jnp.where(rows == i, row, projected)
+    projected_buf[...] = projected
+    residual_buf[...] = norms_ref[...] - jnp.sum(coeff_t * coeff_t, axis=1, keepdims=True)
+    first = first_ref[0]
+    count = projected_ref.shape[0]
+    projected_ref[...] = projected_buf[pl.ds(first, count), :]
+    residual_ref[...] = residual_buf[pl.ds(first, count), :]
+
+
+def rayleigh_ritz(first_band, band_count, margin, subspace, image_norms):
+    size = margin.shape[0]
+    return pl.pallas_call(
+        rayleigh_ritz_kernel,
+        out_shape=(jax.ShapeDtypeStruct((band_count, size), jnp.float32),
+                   jax.ShapeDtypeStruct((band_count, 1), jnp.float32)),
+        in_specs=[pl.BlockSpec(memory_space=pltpu.SMEM)] + [pl.BlockSpec(memory_space=pltpu.VMEM)] * 3,
+        out_specs=(pl.BlockSpec(memory_space=pltpu.VMEM), pl.BlockSpec(memory_space=pltpu.VMEM)),
+        scratch_shapes=[pltpu.VMEM((size, size), jnp.float32), pltpu.VMEM((size, 1), jnp.float32)],
+        cost_estimate=pl.CostEstimate(flops=6 * size**3, transcendentals=size, bytes_accessed=4 * 4 * size * size),
+    )(first_band.reshape(1).astype(jnp.int32), margin, subspace, image_norms.reshape(size, 1))
 
 
 def replica_pairs(direction):
@@ -149,12 +197,9 @@
     margin = packed[:square].reshape(total_bands, total_bands)
     subspace = packed[square : 2 * square].reshape(total_bands, total_bands)
     image_norms = packed[2 * square :]
-    factor = jnp.linalg.cholesky(margin)
-    coefficients = lax.linalg.triangular_solve(factor, subspace.T, left_side=True, lower=True)
-    projected = lax.linalg.triangular_solve(factor, coefficients.T, left_side=True, lower=True)
-    residual_norms = image_norms - jnp.sum(coefficients * coefficients, axis=0)
-    projected_rows = lax.dynamic_slice_in_dim(projected, first_band, band_count, 0)
-    residual_rows = lax.dynamic_slice_in_dim(residual_norms, first_band, band_count, 0)
+    margin = (margin + margin.T) / 2
+    projected_rows, residual_rows = rayleigh_ritz(first_band, band_count, margin, subspace, image_norms)
+    residual_rows = residual_rows.reshape(-1)
     return (current, projected_rows, residual_rows)
 
 

time: 173 us -> 171 us (0.988)
  other arithmetic: 12.7 us -> 1.85 us
  Pallas kernels: 5.77 us -> 14.2 us
    another operation x5 -> x0, other arithmetic: 12.1 us -> none  [the longest x3 6.52 us: on_device(): factor = jnp.linalg.cholesky(margin)]
    pallas_call x0 -> x1, Pallas kernels: none -> 8.4 us  [rayleigh_ritz(): pl.pallas_call(rayleigh_ritz_kernel, out_shape=(jax.ShapeDtypeStruct((ban...]
where the time goes in v9:
time: 171 us; the launch traced here: 170 us
  starting transfers between devices  57.2 us (33%)
  waiting for transfers between devices  55.9 us (33%)
  blocking collectives  32.5 us (19%)
  Pallas kernels  14.2 us (8%)
  local copies, waits for them, and re-layouts  6.69 us (4%)
  other arithmetic  1.85 us (1%)
    ppermute x9, waiting for transfers between devices, butterfly_sum(): values = values + lax.ppermute(values, axis, pairs)  45.3 us
    ppermute x9, starting transfers between devices, butterfly_sum(): values = values + lax.ppermute(values, axis, pairs)  36 us
    all_to_all x1, blocking collectives, on_device(): moved = lax.all_to_all(both, 'band', 2, 1, tiled=True)  32.5 us
    ppermute x1, starting transfers between devices, on_device(): lax.ppermute(potential[potential.shape[0] - width:], ('band', 'grid'), re...  13.8 us
    ppermute x1, waiting for transfers between devices, on_device(): lax.ppermute(potential[:width], ('band', 'grid'), replica_pairs(-1))  10.6 us
    pallas_call x1, Pallas kernels, rayleigh_ritz(): pl.pallas_call(rayleigh_ritz_kernel, out_shape=(jax.ShapeDtypeStruct((ban...  8.4 us
    pallas_call x1, Pallas kernels, filter_and_image(): pl.pallas_call(filter_kernel, out_shape=(jax.ShapeDtypeStruct(shape, jnp....  5.77 us
    ppermute x1, starting transfers between devices, on_device(): lax.ppermute(trial_bands[:, :width], 'grid', [((i + 1) % count, i) for i...  3.64 us
  transfers between devices with their start and end apart: 13, of which 10 were waited for; matrix products, arithmetic and copies ran while one was open for 0% of the time, Pallas kernels for 0%

profile of v9, /device:TPU:24, one launch (start us, length us, event | category | flops | bytes accessed | tf_op | source)
XLA Modules:
  0.0 170.0 jit_solution(10055143905140828467)
XLA Ops:
  0.6 1.9 %collective-permute-start = (f32[2,10,32,128]{3,2,1,0:T(8,128)}, f32[2,10,32,128]{3,2,1,0:T(8,128)S(1)}, u32[]{:S(2)}, u32[]{:S(2)}) collective-permute-start(f32[2,10,32,128]{3,2,1,0:T(8,128)} %own_ref.1), channel_id=1, source_target_pairs={{0,1},{1,2},{2,3},{3,4},{4,5},{5,6},{6,7},{7,8},{8,9},{9,10},{10,1... | collective-permute-start | bytes 983048 | tf_op jit(solution)/shard_map/ppermute | solution.py:168
  2.6 3.6 %collective-permute-start.1 = (f32[2,10,32,128]{3,2,1,0:T(8,128)}, f32[2,10,32,128]{3,2,1,0:T(8,128)S(1)}, u32[]{:S(2)}, u32[]{:S(2)}) collective-permute-start(f32[2,10,32,128]{3,2,1,0:T(8,128)} %own_ref.1), channel_id=1, source_target_pairs={{1,0},{2,1},{3,2},{4,3},{5,4},{6,5},{7,6},{8,7},{9,8},{10,9},{11,1... | collective-permute-start | bytes 983048 | tf_op jit(solution)/shard_map/ppermute | solution.py:169
  6.2 13.8 %collective-permute-start.2 = (f32[10,32,128]{2,1,0:T(8,128)}, f32[10,32,128]{2,1,0:T(8,128)S(1)}, u32[]{:S(2)}, u32[]{:S(2)}) collective-permute-start(f32[10,32,128]{2,1,0:T(8,128)} %own_pot.1), channel_id=1, source_target_pairs={{79,0},{95,16},{111,32},{127,48},{15,64},{31,80},{47,96},{63,112},... | collective-permute-start | bytes 491528 | tf_op jit(solution)/shard_map/ppermute | solution.py:170
  20.0 1.9 %collective-permute-start.3 = (f32[10,32,128]{2,1,0:T(8,128)}, f32[10,32,128]{2,1,0:T(8,128)S(1)}, u32[]{:S(2)}, u32[]{:S(2)}) collective-permute-start(f32[10,32,128]{2,1,0:T(8,128)} %own_pot.1), channel_id=1, source_target_pairs={{1,0},{17,16},{33,32},{49,48},{65,64},{81,80},{97,96},{113,112},{1... | collective-permute-start | bytes 491528 | tf_op jit(solution)/shard_map/ppermute | solution.py:171
  21.9 10.6 %collective-permute-done.3.above_pot = f32[10,32,128]{2,1,0:T(8,128)S(1)} collective-permute-done((f32[10,32,128]{2,1,0:T(8,128)}, f32[10,32,128]{2,1,0:T(8,128)S(1)}, u32[]{:S(2)}, u32[]{:S(2)}) %collective-permute-start.3) | collective-permute-done | bytes 163872 | tf_op jit(solution)/shard_map/ppermute | solution.py:171
  33.3 0.7 copy-done.2
  34.0 5.8 %shard_map.49 = (f32[2,10,32,128]{3,2,1,0:T(8,128)}, f32[2,10,32,128]{3,2,1,0:T(8,128)}) custom-call(f32[2,10,32,128]{3,2,1,0:T(8,128)} %copy-done.1, f32[2,10,32,128]{3,2,1,0:T(8,128)} %own_ref.1, f32[2,10,32,128]{3,2,1,0:T(8,128)} %copy-done.2, f32[10,32,128]{2,1,0:T(8,128)} %copy-done.3, f32[10,32,128]{2,1,0:T(8,128)} %own_pot.1, f32[10,32,128]{2,1,0:T(8,128)} %copy-done.4), custom_call_target="tpu_custom_call" | custom-call | flops 29491200 | bytes 2949120 | tf_op jit(solution)/shard_map/pallas_call | solution.py:93
  39.8 1.0 stack.7
  41.1 0.7 copy-done
  42.4 32.5 %all_to_all.15 = f32[2,2,32,1280]{3,1,0,2:T(2,128)S(1)} all-to-all(f32[2,2,32,1280]{3,1,0,2:T(2,128)S(1)} %pad_maximum_fusion), channel_id=1, replica_groups=mesh['band'=32,'grid'=16] {'band'}, dimensions={2} | all-to-all | bytes 1310720 | tf_op jit(solution)/shard_map/all_to_all | solution.py:182
  76.8 17.2 %collective-permute-start.4 = (f32[8256]{0:T(1024)S(1)}, f32[8256]{0:T(1024)S(1)}, u32[]{:S(2)}, u32[]{:S(2)}) collective-permute-start(f32[8256]{0:T(1024)S(1)} %constant_dynamic-update-slice_fusion), channel_id=1, source_target_pairs={{0,1},{1,0},{2,3},{3,2},{4,5},{5,4},{6,7},{7,6},{8,9},{9,8},{10,11... | collective-permute-start | bytes 99080 | tf_op jit(solution)/shard_map/ppermute | solution.py:21
  93.9 0.8 collective-permute-done.4
  94.8 1.9 %collective-permute-start.5 = (f32[8256]{0:T(1024)S(1)}, f32[8256]{0:T(1024)S(1)}, u32[]{:S(2)}, u32[]{:S(2)}) collective-permute-start(f32[8256]{0:T(1024)S(1)} %add.30), channel_id=1, source_target_pairs={{0,2},{1,3},{2,0},{3,1},{4,6},{5,7},{6,4},{7,5},{8,10},{9,11},{10,... | collective-permute-start | bytes 99080 | tf_op jit(solution)/shard_map/ppermute | solution.py:21
  96.7 3.9 %collective-permute-done.5 = f32[8256]{0:T(1024)S(1)} collective-permute-done((f32[8256]{0:T(1024)S(1)}, f32[8256]{0:T(1024)S(1)}, u32[]{:S(2)}, u32[]{:S(2)}) %collective-permute-start.5) | collective-permute-done | bytes 33056 | tf_op jit(solution)/shard_map/ppermute | solution.py:21
  100.6 1.9 %collective-permute-start.6 = (f32[8256]{0:T(1024)S(1)}, f32[8256]{0:T(1024)S(1)}, u32[]{:S(2)}, u32[]{:S(2)}) collective-permute-start(f32[8256]{0:T(1024)S(1)} %add.31), channel_id=1, source_target_pairs={{0,6},{1,7},{2,4},{3,5},{4,2},{5,3},{6,0},{7,1},{8,14},{9,15},{10,... | collective-permute-start | bytes 99080 | tf_op jit(solution)/shard_map/ppermute | solution.py:21
  102.6 5.1 %collective-permute-done.6 = f32[8256]{0:T(1024)S(1)} collective-permute-done((f32[8256]{0:T(1024)S(1)}, f32[8256]{0:T(1024)S(1)}, u32[]{:S(2)}, u32[]{:S(2)}) %collective-permute-start.6) | collective-permute-done | bytes 33056 | tf_op jit(solution)/shard_map/ppermute | solution.py:21
  107.7 4.5 %collective-permute-start.7 = (f32[8256]{0:T(1024)S(1)}, f32[8256]{0:T(1024)S(1)}, u32[]{:S(2)}, u32[]{:S(2)}) collective-permute-start(f32[8256]{0:T(1024)S(1)} %add.32), channel_id=1, source_target_pairs={{0,8},{1,9},{2,10},{3,11},{4,12},{5,13},{6,14},{7,15},{8,0},{9,1},... | collective-permute-start | bytes 99080 | tf_op jit(solution)/shard_map/ppermute | solution.py:21
  112.2 10.4 %collective-permute-done.7 = f32[8256]{0:T(1024)S(1)} collective-permute-done((f32[8256]{0:T(1024)S(1)}, f32[8256]{0:T(1024)S(1)}, u32[]{:S(2)}, u32[]{:S(2)}) %collective-permute-start.7) | collective-permute-done | bytes 33056 | tf_op jit(solution)/shard_map/ppermute | solution.py:21
  122.7 1.9 %collective-permute-start.8 = (f32[8256]{0:T(1024)S(1)}, f32[8256]{0:T(1024)S(1)}, u32[]{:S(2)}, u32[]{:S(2)}) collective-permute-start(f32[8256]{0:T(1024)S(1)} %add.33), channel_id=1, source_target_pairs={{0,16},{16,0},{32,48},{48,32},{64,80},{80,64},{96,112},{112,96},{1... | collective-permute-start | bytes 99080 | tf_op jit(solution)/shard_map/ppermute | solution.py:21
  124.6 3.9 %collective-permute-done.8 = f32[8256]{0:T(1024)S(1)} collective-permute-done((f32[8256]{0:T(1024)S(1)}, f32[8256]{0:T(1024)S(1)}, u32[]{:S(2)}, u32[]{:S(2)}) %collective-permute-start.8) | collective-permute-done | bytes 33056 | tf_op jit(solution)/shard_map/ppermute | solution.py:21
  128.5 1.9 %collective-permute-start.9 = (f32[8256]{0:T(1024)S(1)}, f32[8256]{0:T(1024)S(1)}, u32[]{:S(2)}, u32[]{:S(2)}) collective-permute-start(f32[8256]{0:T(1024)S(1)} %add.34), channel_id=1, source_target_pairs={{0,32},{16,48},{32,0},{48,16},{64,96},{80,112},{96,64},{112,80},{1... | collective-permute-start | bytes 99080 | tf_op jit(solution)/shard_map/ppermute | solution.py:21
  130.4 4.8 %collective-permute-done.9 = f32[8256]{0:T(1024)S(1)} collective-permute-done((f32[8256]{0:T(1024)S(1)}, f32[8256]{0:T(1024)S(1)}, u32[]{:S(2)}, u32[]{:S(2)}) %collective-permute-start.9) | collective-permute-done | bytes 33056 | tf_op jit(solution)/shard_map/ppermute | solution.py:21
  135.3 1.9 %collective-permute-start.10 = (f32[8256]{0:T(1024)S(1)}, f32[8256]{0:T(1024)S(1)}, u32[]{:S(2)}, u32[]{:S(2)}) collective-permute-start(f32[8256]{0:T(1024)S(1)} %add.35), channel_id=1, source_target_pairs={{0,64},{16,80},{32,96},{48,112},{64,0},{80,16},{96,32},{112,48},{1... | collective-permute-start | bytes 99080 | tf_op jit(solution)/shard_map/ppermute | solution.py:21
  137.2 8.1 %collective-permute-done.10 = f32[8256]{0:T(1024)S(1)} collective-permute-done((f32[8256]{0:T(1024)S(1)}, f32[8256]{0:T(1024)S(1)}, u32[]{:S(2)}, u32[]{:S(2)}) %collective-permute-start.10) | collective-permute-done | bytes 33056 | tf_op jit(solution)/shard_map/ppermute | solution.py:21
  145.2 1.9 %collective-permute-start.11 = (f32[8256]{0:T(1024)S(1)}, f32[8256]{0:T(1024)S(1)}, u32[]{:S(2)}, u32[]{:S(2)}) collective-permute-start(f32[8256]{0:T(1024)S(1)} %add.36), channel_id=1, source_target_pairs={{0,128},{16,144},{32,160},{48,176},{64,192},{80,208},{96,224},{112... | collective-permute-start | bytes 99080 | tf_op jit(solution)/shard_map/ppermute | solution.py:21
  147.2 3.9 %collective-permute-done.11 = f32[8256]{0:T(1024)S(1)} collective-permute-done((f32[8256]{0:T(1024)S(1)}, f32[8256]{0:T(1024)S(1)}, u32[]{:S(2)}, u32[]{:S(2)}) %collective-permute-start.11) | collective-permute-done | bytes 33056 | tf_op jit(solution)/shard_map/ppermute | solution.py:21
  151.1 2.9 %collective-permute-start.12 = (f32[8256]{0:T(1024)S(1)}, f32[8256]{0:T(1024)S(1)}, u32[]{:S(2)}, u32[]{:S(2)}) collective-permute-start(f32[8256]{0:T(1024)S(1)} %add.37), channel_id=1, source_target_pairs={{0,384},{16,400},{32,416},{48,432},{64,448},{80,464},{96,480},{112... | collective-permute-start | bytes 99080 | tf_op jit(solution)/shard_map/ppermute | solution.py:21
  154.0 4.2 %collective-permute-done.12 = f32[8256]{0:T(1024)S(1)} collective-permute-done((f32[8256]{0:T(1024)S(1)}, f32[8256]{0:T(1024)S(1)}, u32[]{:S(2)}, u32[]{:S(2)}) %collective-permute-start.12) | collective-permute-done | bytes 33056 | tf_op jit(solution)/shard_map/ppermute | solution.py:21
  159.0 0.7 slice.42.subspace_ref
  159.6 0.7 copy.14.norms_ref
  160.3 8.4 %shard_map.50 = (f32[2,64]{1,0:T(2,128)}, f32[2,1]{1,0:T(2,128)}) custom-call(s32[1]{0:T(128)} %bitcast.first_ref, f32[64,64]{1,0:T(8,128)} %fusion.margin_ref, f32[64,64]{1,0:T(8,128)} %slice.42.subspace_ref, f32[64,1]{1,0:T(8,128)} %copy.14.norms_ref), custom_call_target="tpu_custom_call" | custom-call | flops 1572864 | bytes 65536 | tf_op jit(solution)/shard_map/pallas_call | solution.py:141
  168.7 0.7 copy-done.5
  (42 shorter events, 4.9 us)
Async XLA Ops:
  0.6 31.9 %collective-permute-start = (f32[2,10,32,128]{3,2,1,0:T(8,128)}, f32[2,10,32,128]{3,2,1,0:T(8,128)S(1)}, u32[]{:S(2)}, u32[]{:S(2)}) collective-permute-start(f32[2,10,32,128]{3,2,1,0:T(8,128)} %own_ref.1), channel_id=1, source_target_pairs={{0,1},{1,2},{2,3},{3,4},{4,5},{5,6},{6,7},{7,8},{8,9},{9,10},{10,1... | collective-permute-start | bytes 983048 | tf_op jit(solution)/shard_map/ppermute | solution.py:168
  2.6 30.0 %collective-permute-start.1 = (f32[2,10,32,128]{3,2,1,0:T(8,128)}, f32[2,10,32,128]{3,2,1,0:T(8,128)S(1)}, u32[]{:S(2)}, u32[]{:S(2)}) collective-permute-start(f32[2,10,32,128]{3,2,1,0:T(8,128)} %own_ref.1), channel_id=1, source_target_pairs={{1,0},{2,1},{3,2},{4,3},{5,4},{6,5},{7,6},{8,7},{9,8},{10,9},{11,1... | collective-permute-start | bytes 983048 | tf_op jit(solution)/shard_map/ppermute | solution.py:169
  6.2 15.7 %collective-permute-start.2 = (f32[10,32,128]{2,1,0:T(8,128)}, f32[10,32,128]{2,1,0:T(8,128)S(1)}, u32[]{:S(2)}, u32[]{:S(2)}) collective-permute-start(f32[10,32,128]{2,1,0:T(8,128)} %own_pot.1), channel_id=1, source_target_pairs={{79,0},{95,16},{111,32},{127,48},{15,64},{31,80},{47,96},{63,112},... | collective-permute-start | bytes 491528 | tf_op jit(solution)/shard_map/ppermute | solution.py:170
  20.0 12.6 %collective-permute-start.3 = (f32[10,32,128]{2,1,0:T(8,128)}, f32[10,32,128]{2,1,0:T(8,128)S(1)}, u32[]{:S(2)}, u32[]{:S(2)}) collective-permute-start(f32[10,32,128]{2,1,0:T(8,128)} %own_pot.1), channel_id=1, source_target_pairs={{1,0},{17,16},{33,32},{49,48},{65,64},{81,80},{97,96},{113,112},{1... | collective-permute-start | bytes 491528 | tf_op jit(solution)/shard_map/ppermute | solution.py:171
  21.9 10.6 %copy-start.3 = (f32[10,32,128]{2,1,0:T(8,128)}, f32[10,32,128]{2,1,0:T(8,128)S(1)}, u32[]{:S(2)}) copy-start(f32[10,32,128]{2,1,0:T(8,128)S(1)} %collective-permute-done.2.below_pot) | copy-start | bytes 491524
  32.5 0.7 copy-start.4
  32.6 0.8 copy-start.1
  33.3 0.7 copy-start.2
  40.8 1.0 copy-start
  76.8 18.0 %collective-permute-start.4 = (f32[8256]{0:T(1024)S(1)}, f32[8256]{0:T(1024)S(1)}, u32[]{:S(2)}, u32[]{:S(2)}) collective-permute-start(f32[8256]{0:T(1024)S(1)} %constant_dynamic-update-slice_fusion), channel_id=1, source_target_pairs={{0,1},{1,0},{2,3},{3,2},{4,5},{5,4},{6,7},{7,6},{8,9},{9,8},{10,11... | collective-permute-start | bytes 99080 | tf_op jit(solution)/shard_map/ppermute | solution.py:21
  94.8 5.8 %collective-permute-start.5 = (f32[8256]{0:T(1024)S(1)}, f32[8256]{0:T(1024)S(1)}, u32[]{:S(2)}, u32[]{:S(2)}) collective-permute-start(f32[8256]{0:T(1024)S(1)} %add.30), channel_id=1, source_target_pairs={{0,2},{1,3},{2,0},{3,1},{4,6},{5,7},{6,4},{7,5},{8,10},{9,11},{10,... | collective-permute-start | bytes 99080 | tf_op jit(solution)/shard_map/ppermute | solution.py:21
  100.6 7.1 %collective-permute-start.6 = (f32[8256]{0:T(1024)S(1)}, f32[8256]{0:T(1024)S(1)}, u32[]{:S(2)}, u32[]{:S(2)}) collective-permute-start(f32[8256]{0:T(1024)S(1)} %add.31), channel_id=1, source_target_pairs={{0,6},{1,7},{2,4},{3,5},{4,2},{5,3},{6,0},{7,1},{8,14},{9,15},{10,... | collective-permute-start | bytes 99080 | tf_op jit(solution)/shard_map/ppermute | solution.py:21
  107.7 14.9 %collective-permute-start.7 = (f32[8256]{0:T(1024)S(1)}, f32[8256]{0:T(1024)S(1)}, u32[]{:S(2)}, u32[]{:S(2)}) collective-permute-start(f32[8256]{0:T(1024)S(1)} %add.32), channel_id=1, source_target_pairs={{0,8},{1,9},{2,10},{3,11},{4,12},{5,13},{6,14},{7,15},{8,0},{9,1},... | collective-permute-start | bytes 99080 | tf_op jit(solution)/shard_map/ppermute | solution.py:21
  122.7 5.8 %collective-permute-start.8 = (f32[8256]{0:T(1024)S(1)}, f32[8256]{0:T(1024)S(1)}, u32[]{:S(2)}, u32[]{:S(2)}) collective-permute-start(f32[8256]{0:T(1024)S(1)} %add.33), channel_id=1, source_target_pairs={{0,16},{16,0},{32,48},{48,32},{64,80},{80,64},{96,112},{112,96},{1... | collective-permute-start | bytes 99080 | tf_op jit(solution)/shard_map/ppermute | solution.py:21
  128.5 6.7 %collective-permute-start.9 = (f32[8256]{0:T(1024)S(1)}, f32[8256]{0:T(1024)S(1)}, u32[]{:S(2)}, u32[]{:S(2)}) collective-permute-start(f32[8256]{0:T(1024)S(1)} %add.34), channel_id=1, source_target_pairs={{0,32},{16,48},{32,0},{48,16},{64,96},{80,112},{96,64},{112,80},{1... | collective-permute-start | bytes 99080 | tf_op jit(solution)/shard_map/ppermute | solution.py:21
  135.3 10.0 %collective-permute-start.10 = (f32[8256]{0:T(1024)S(1)}, f32[8256]{0:T(1024)S(1)}, u32[]{:S(2)}, u32[]{:S(2)}) collective-permute-start(f32[8256]{0:T(1024)S(1)} %add.35), channel_id=1, source_target_pairs={{0,64},{16,80},{32,96},{48,112},{64,0},{80,16},{96,32},{112,48},{1... | collective-permute-start | bytes 99080 | tf_op jit(solution)/shard_map/ppermute | solution.py:21
  145.2 5.8 %collective-permute-start.11 = (f32[8256]{0:T(1024)S(1)}, f32[8256]{0:T(1024)S(1)}, u32[]{:S(2)}, u32[]{:S(2)}) collective-permute-start(f32[8256]{0:T(1024)S(1)} %add.36), channel_id=1, source_target_pairs={{0,128},{16,144},{32,160},{48,176},{64,192},{80,208},{96,224},{112... | collective-permute-start | bytes 99080 | tf_op jit(solution)/shard_map/ppermute | solution.py:21
  151.1 7.1 %collective-permute-start.12 = (f32[8256]{0:T(1024)S(1)}, f32[8256]{0:T(1024)S(1)}, u32[]{:S(2)}, u32[]{:S(2)}) collective-permute-start(f32[8256]{0:T(1024)S(1)} %add.37), channel_id=1, source_target_pairs={{0,384},{16,400},{32,416},{48,432},{64,448},{80,464},{96,480},{112... | collective-permute-start | bytes 99080 | tf_op jit(solution)/shard_map/ppermute | solution.py:21
  168.7 0.7 copy-start.5

commit v10 on v9

--- a/solution.py
+++ b/solution.py
@@ -1,3 +1,5 @@
+import functools
+
 import jax
 import jax.numpy as jnp
 from jax import lax
@@ -101,11 +103,11 @@
     )(below, own, above, below_pot, own_pot, above_pot)
 
 
-def rayleigh_ritz_kernel(first_ref, margin_ref, subspace_ref, norms_ref, projected_ref, residual_ref,
-                         projected_buf, residual_buf):
-    size = margin_ref.shape[0]
-    work = margin_ref[...]
-    rest = subspace_ref[...]
+def rayleigh_ritz_kernel(scale, first_ref, packed_ref, projected_ref, residual_ref, projected_buf, residual_buf):
+    size = packed_ref.shape[0]
+    work = packed_ref[:, 0:size] * scale
+    rest = packed_ref[:, size : 2 * size] * scale
+    norms = packed_ref[:, 2 * size : 2 * size + 1] * scale
     rows = lax.broadcasted_iota(jnp.int32, (size, size), 0)
     cols = lax.broadcasted_iota(jnp.int32, (size, size), 1)
     row_index = rows[:, :1]
@@ -129,24 +131,24 @@
         rest = rest - columns[i] * row
         projected = jnp.where(rows == i, row, projected)
     projected_buf[...] = projected
-    residual_buf[...] = norms_ref[...] - jnp.sum(coeff_t * coeff_t, axis=1, keepdims=True)
+    residual_buf[...] = norms - jnp.sum(coeff_t * coeff_t, axis=1, keepdims=True)
     first = first_ref[0]
     count = projected_ref.shape[0]
     projected_ref[...] = projected_buf[pl.ds(first, count), :]
     residual_ref[...] = residual_buf[pl.ds(first, count), :]
 
 
-def rayleigh_ritz(first_band, band_count, margin, subspace, image_norms):
-    size = margin.shape[0]
+def rayleigh_ritz(first_band, band_count, packed, scale):
+    size = packed.shape[0]
     return pl.pallas_call(
-        rayleigh_ritz_kernel,
+        functools.partial(rayleigh_ritz_kernel, scale),
         out_shape=(jax.ShapeDtypeStruct((band_count, size), jnp.float32),
                    jax.ShapeDtypeStruct((band_count, 1), jnp.float32)),
-        in_specs=[pl.BlockSpec(memory_space=pltpu.SMEM)] + [pl.BlockSpec(memory_space=pltpu.VMEM)] * 3,
+        in_specs=[pl.BlockSpec(memory_space=pltpu.SMEM), pl.BlockSpec(memory_space=pltpu.VMEM)],
         out_specs=(pl.BlockSpec(memory_space=pltpu.VMEM), pl.BlockSpec(memory_space=pltpu.VMEM)),
         scratch_shapes=[pltpu.VMEM((size, size), jnp.float32), pltpu.VMEM((size, 1), jnp.float32)],
         cost_estimate=pl.CostEstimate(flops=6 * size**3, transcendentals=size, bytes_accessed=4 * 4 * size * size),
-    )(first_band.reshape(1).astype(jnp.int32), margin, subspace, image_norms.reshape(size, 1))
+    )(first_band.reshape(1).astype(jnp.int32), packed)
 
 
 def replica_pairs(direction):
@@ -189,16 +191,11 @@
         image_here, bands_here.T, precision=lax.Precision.HIGHEST, preferred_element_type=jnp.float32
     )
     norm_part = jnp.sum(image_here * image_here, axis=1)
-    packed = jnp.concatenate([margin_part.reshape(-1), image_part.reshape(-1), norm_part])
+    margin_part = (margin_part + margin_part.T) / 2
+    packed = jnp.concatenate([margin_part, image_part, norm_part[:, None]], axis=1)
     packed = butterfly_sum(packed, "grid", [flip(1), flip(2), ring_of_four(0, 2), flip(8)])
     packed = butterfly_sum(packed, "band", [flip(1), flip(2), flip(4), flip(8), ring_of_four(0, 8)])
-    packed = packed * inverse_cells
-    square = total_bands * total_bands
-    margin = packed[:square].reshape(total_bands, total_bands)
-    subspace = packed[square : 2 * square].reshape(total_bands, total_bands)
-    image_norms = packed[2 * square :]
-    margin = (margin + margin.T) / 2
-    projected_rows, residual_rows = rayleigh_ritz(first_band, band_count, margin, subspace, image_norms)
+    projected_rows, residual_rows = rayleigh_ritz(first_band, band_count, packed, inverse_cells)
     residual_rows = residual_rows.reshape(-1)
     return (current, projected_rows, residual_rows)
 

time: 171 us -> 176 us (1.029)
  Pallas kernels: 14.2 us -> 16.8 us
  starting transfers between devices: 57.2 us -> 59.6 us
  waiting for transfers between devices: 55.9 us -> 58.2 us
    pallas_call x1, Pallas kernels: 8.4 us -> 11 us  [rayleigh_ritz(): pl.pallas_call(functools.partial(rayleigh_ritz_kernel, scale), out_shape=...]
    ppermute x9, starting transfers between devices: 36 us -> 38.3 us  [butterfly_sum(): values = values + lax.ppermute(values, axis, pairs)]
    ppermute x9, waiting for transfers between devices: 45.3 us -> 47.6 us  [butterfly_sum(): values = values + lax.ppermute(values, axis, pairs)]
where the time goes in v10:
time: 176 us
  starting transfers between devices  59.6 us (34%)
  waiting for transfers between devices  58.2 us (33%)
  blocking collectives  32.5 us (18%)
  Pallas kernels  16.8 us (10%)
  local copies, waits for them, and re-layouts  5.06 us (3%)
  other arithmetic  2.04 us (1%)
    ppermute x9, waiting for transfers between devices, butterfly_sum(): values = values + lax.ppermute(values, axis, pairs)  47.6 us
    ppermute x9, starting transfers between devices, butterfly_sum(): values = values + lax.ppermute(values, axis, pairs)  38.3 us
    all_to_all x1, blocking collectives, on_device(): moved = lax.all_to_all(both, 'band', 2, 1, tiled=True)  32.5 us
    ppermute x1, starting transfers between devices, on_device(): lax.ppermute(potential[potential.shape[0] - width:], ('band', 'grid'), re...  13.8 us
    pallas_call x1, Pallas kernels, rayleigh_ritz(): pl.pallas_call(functools.partial(rayleigh_ritz_kernel, scale), out_shape=...  11 us
    ppermute x1, waiting for transfers between devices, on_device(): lax.ppermute(potential[:width], ('band', 'grid'), replica_pairs(-1))  10.6 us
    pallas_call x1, Pallas kernels, filter_and_image(): pl.pallas_call(filter_kernel, out_shape=(jax.ShapeDtypeStruct(shape, jnp....  5.78 us
    ppermute x1, starting transfers between devices, on_device(): lax.ppermute(trial_bands[:, :width], 'grid', [((i + 1) % count, i) for i...  3.64 us
  transfers between devices with their start and end apart: 13, of which 10 were waited for; matrix products, arithmetic and copies ran while one was open for 0% of the time, Pallas kernels for 0%

profile of v10, /device:TPU:24, one launch (start us, length us, event | category | flops | bytes accessed | tf_op | source)
XLA Modules:
  0.0 175.8 jit_solution(17600903678337447412)
XLA Ops:
  0.6 1.9 %collective-permute-start = (f32[2,10,32,128]{3,2,1,0:T(8,128)}, f32[2,10,32,128]{3,2,1,0:T(8,128)S(1)}, u32[]{:S(2)}, u32[]{:S(2)}) collective-permute-start(f32[2,10,32,128]{3,2,1,0:T(8,128)} %own_ref.1), channel_id=1, source_target_pairs={{0,1},{1,2},{2,3},{3,4},{4,5},{5,6},{6,7},{7,8},{8,9},{9,10},{10,1... | collective-permute-start | bytes 983048 | tf_op jit(solution)/shard_map/ppermute | solution.py:170
  2.6 3.6 %collective-permute-start.1 = (f32[2,10,32,128]{3,2,1,0:T(8,128)}, f32[2,10,32,128]{3,2,1,0:T(8,128)S(1)}, u32[]{:S(2)}, u32[]{:S(2)}) collective-permute-start(f32[2,10,32,128]{3,2,1,0:T(8,128)} %own_ref.1), channel_id=1, source_target_pairs={{1,0},{2,1},{3,2},{4,3},{5,4},{6,5},{7,6},{8,7},{9,8},{10,9},{11,1... | collective-permute-start | bytes 983048 | tf_op jit(solution)/shard_map/ppermute | solution.py:171
  6.2 13.8 %collective-permute-start.2 = (f32[10,32,128]{2,1,0:T(8,128)}, f32[10,32,128]{2,1,0:T(8,128)S(1)}, u32[]{:S(2)}, u32[]{:S(2)}) collective-permute-start(f32[10,32,128]{2,1,0:T(8,128)} %own_pot.1), channel_id=1, source_target_pairs={{79,0},{95,16},{111,32},{127,48},{15,64},{31,80},{47,96},{63,112},... | collective-permute-start | bytes 491528 | tf_op jit(solution)/shard_map/ppermute | solution.py:172
  20.0 1.9 %collective-permute-start.3 = (f32[10,32,128]{2,1,0:T(8,128)}, f32[10,32,128]{2,1,0:T(8,128)S(1)}, u32[]{:S(2)}, u32[]{:S(2)}) collective-permute-start(f32[10,32,128]{2,1,0:T(8,128)} %own_pot.1), channel_id=1, source_target_pairs={{1,0},{17,16},{33,32},{49,48},{65,64},{81,80},{97,96},{113,112},{1... | collective-permute-start | bytes 491528 | tf_op jit(solution)/shard_map/ppermute | solution.py:173
  21.9 10.6 %collective-permute-done.3.above_pot = f32[10,32,128]{2,1,0:T(8,128)S(1)} collective-permute-done((f32[10,32,128]{2,1,0:T(8,128)}, f32[10,32,128]{2,1,0:T(8,128)S(1)}, u32[]{:S(2)}, u32[]{:S(2)}) %collective-permute-start.3) | collective-permute-done | bytes 163872 | tf_op jit(solution)/shard_map/ppermute | solution.py:173
  32.6 0.7 copy-done.4
  33.3 0.7 copy-done.2
  34.0 5.8 %shard_map.49 = (f32[2,10,32,128]{3,2,1,0:T(8,128)}, f32[2,10,32,128]{3,2,1,0:T(8,128)}) custom-call(f32[2,10,32,128]{3,2,1,0:T(8,128)} %copy-done.1, f32[2,10,32,128]{3,2,1,0:T(8,128)} %own_ref.1, f32[2,10,32,128]{3,2,1,0:T(8,128)} %copy-done.2, f32[10,32,128]{2,1,0:T(8,128)} %copy-done.3, f32[10,32,128]{2,1,0:T(8,128)} %own_pot.1, f32[10,32,128]{2,1,0:T(8,128)} %copy-done.4), custom_call_target="tpu_custom_call" | custom-call | flops 29491200 | bytes 2949120 | tf_op jit(solution)/shard_map/pallas_call | solution.py:95
  39.8 1.0 stack.7
  41.1 0.7 copy-done
  42.4 32.5 %all_to_all.15 = f32[2,2,32,1280]{3,1,0,2:T(2,128)S(1)} all-to-all(f32[2,2,32,1280]{3,1,0,2:T(2,128)S(1)} %pad_maximum_fusion), channel_id=1, replica_groups=mesh['band'=32,'grid'=16] {'band'}, dimensions={2} | all-to-all | bytes 1310720 | tf_op jit(solution)/shard_map/all_to_all | solution.py:184
  76.7 17.2 %collective-permute-start.4 = (f32[64,129]{1,0:T(8,128)S(1)}, f32[64,129]{1,0:T(8,128)S(1)}, u32[]{:S(2)}, u32[]{:S(2)}) collective-permute-start(f32[64,129]{1,0:T(8,128)S(1)} %pad_maximum_fusion.1), channel_id=1, source_target_pairs={{0,1},{1,0},{2,3},{3,2},{4,5},{5,4},{6,7},{7,6},{8,9},{9,8},{10,11... | collective-permute-start | bytes 99080 | tf_op jit(solution)/shard_map/ppermute | solution.py:23
  93.9 0.9 collective-permute-done.4
  94.9 1.9 %collective-permute-start.5 = (f32[64,129]{1,0:T(8,128)S(1)}, f32[64,129]{1,0:T(8,128)S(1)}, u32[]{:S(2)}, u32[]{:S(2)}) collective-permute-start(f32[64,129]{1,0:T(8,128)S(1)} %fusion.8), channel_id=1, source_target_pairs={{0,2},{1,3},{2,0},{3,1},{4,6},{5,7},{6,4},{7,5},{8,10},{9,11},{10,... | collective-permute-start | bytes 99080 | tf_op jit(solution)/shard_map/ppermute | solution.py:23
  96.8 4.3 %collective-permute-done.5 = f32[64,129]{1,0:T(8,128)S(1)} collective-permute-done((f32[64,129]{1,0:T(8,128)S(1)}, f32[64,129]{1,0:T(8,128)S(1)}, u32[]{:S(2)}, u32[]{:S(2)}) %collective-permute-start.5) | collective-permute-done | bytes 33056 | tf_op jit(solution)/shard_map/ppermute | solution.py:23
  101.2 1.9 %collective-permute-start.6 = (f32[64,129]{1,0:T(8,128)S(1)}, f32[64,129]{1,0:T(8,128)S(1)}, u32[]{:S(2)}, u32[]{:S(2)}) collective-permute-start(f32[64,129]{1,0:T(8,128)S(1)} %add.32), channel_id=1, source_target_pairs={{0,6},{1,7},{2,4},{3,5},{4,2},{5,3},{6,0},{7,1},{8,14},{9,15},{10,... | collective-permute-start | bytes 99080 | tf_op jit(solution)/shard_map/ppermute | solution.py:23
  103.1 5.4 %collective-permute-done.6 = f32[64,129]{1,0:T(8,128)S(1)} collective-permute-done((f32[64,129]{1,0:T(8,128)S(1)}, f32[64,129]{1,0:T(8,128)S(1)}, u32[]{:S(2)}, u32[]{:S(2)}) %collective-permute-start.6) | collective-permute-done | bytes 33056 | tf_op jit(solution)/shard_map/ppermute | solution.py:23
  108.5 4.4 %collective-permute-start.7 = (f32[64,129]{1,0:T(8,128)S(1)}, f32[64,129]{1,0:T(8,128)S(1)}, u32[]{:S(2)}, u32[]{:S(2)}) collective-permute-start(f32[64,129]{1,0:T(8,128)S(1)} %add.33), channel_id=1, source_target_pairs={{0,8},{1,9},{2,10},{3,11},{4,12},{5,13},{6,14},{7,15},{8,0},{9,1},... | collective-permute-start | bytes 99080 | tf_op jit(solution)/shard_map/ppermute | solution.py:23
  113.0 11.0 %collective-permute-done.7 = f32[64,129]{1,0:T(8,128)S(1)} collective-permute-done((f32[64,129]{1,0:T(8,128)S(1)}, f32[64,129]{1,0:T(8,128)S(1)}, u32[]{:S(2)}, u32[]{:S(2)}) %collective-permute-start.7) | collective-permute-done | bytes 33056 | tf_op jit(solution)/shard_map/ppermute | solution.py:23
  124.0 3.2 %collective-permute-start.8 = (f32[64,129]{1,0:T(8,128)S(1)}, f32[64,129]{1,0:T(8,128)S(1)}, u32[]{:S(2)}, u32[]{:S(2)}) collective-permute-start(f32[64,129]{1,0:T(8,128)S(1)} %add.34), channel_id=1, source_target_pairs={{0,16},{16,0},{32,48},{48,32},{64,80},{80,64},{96,112},{112,96},{1... | collective-permute-start | bytes 99080 | tf_op jit(solution)/shard_map/ppermute | solution.py:23
  127.2 3.0 %collective-permute-done.8 = f32[64,129]{1,0:T(8,128)S(1)} collective-permute-done((f32[64,129]{1,0:T(8,128)S(1)}, f32[64,129]{1,0:T(8,128)S(1)}, u32[]{:S(2)}, u32[]{:S(2)}) %collective-permute-start.8) | collective-permute-done | bytes 33056 | tf_op jit(solution)/shard_map/ppermute | solution.py:23
  130.1 2.4 %collective-permute-start.9 = (f32[64,129]{1,0:T(8,128)S(1)}, f32[64,129]{1,0:T(8,128)S(1)}, u32[]{:S(2)}, u32[]{:S(2)}) collective-permute-start(f32[64,129]{1,0:T(8,128)S(1)} %add.35), channel_id=1, source_target_pairs={{0,32},{16,48},{32,0},{48,16},{64,96},{80,112},{96,64},{112,80},{1... | collective-permute-start | bytes 99080 | tf_op jit(solution)/shard_map/ppermute | solution.py:23
  132.5 4.7 %collective-permute-done.9 = f32[64,129]{1,0:T(8,128)S(1)} collective-permute-done((f32[64,129]{1,0:T(8,128)S(1)}, f32[64,129]{1,0:T(8,128)S(1)}, u32[]{:S(2)}, u32[]{:S(2)}) %collective-permute-start.9) | collective-permute-done | bytes 33056 | tf_op jit(solution)/shard_map/ppermute | solution.py:23
  137.2 2.5 %collective-permute-start.10 = (f32[64,129]{1,0:T(8,128)S(1)}, f32[64,129]{1,0:T(8,128)S(1)}, u32[]{:S(2)}, u32[]{:S(2)}) collective-permute-start(f32[64,129]{1,0:T(8,128)S(1)} %add.36), channel_id=1, source_target_pairs={{0,64},{16,80},{32,96},{48,112},{64,0},{80,16},{96,32},{112,48},{1... | collective-permute-start | bytes 99080 | tf_op jit(solution)/shard_map/ppermute | solution.py:23
  139.7 9.6 %collective-permute-done.10 = f32[64,129]{1,0:T(8,128)S(1)} collective-permute-done((f32[64,129]{1,0:T(8,128)S(1)}, f32[64,129]{1,0:T(8,128)S(1)}, u32[]{:S(2)}, u32[]{:S(2)}) %collective-permute-start.10) | collective-permute-done | bytes 33056 | tf_op jit(solution)/shard_map/ppermute | solution.py:23
  149.4 1.9 %collective-permute-start.11 = (f32[64,129]{1,0:T(8,128)S(1)}, f32[64,129]{1,0:T(8,128)S(1)}, u32[]{:S(2)}, u32[]{:S(2)}) collective-permute-start(f32[64,129]{1,0:T(8,128)S(1)} %add.37), channel_id=1, source_target_pairs={{0,128},{16,144},{32,160},{48,176},{64,192},{80,208},{96,224},{112... | collective-permute-start | bytes 99080 | tf_op jit(solution)/shard_map/ppermute | solution.py:23
  151.3 4.2 %collective-permute-done.11 = f32[64,129]{1,0:T(8,128)S(1)} collective-permute-done((f32[64,129]{1,0:T(8,128)S(1)}, f32[64,129]{1,0:T(8,128)S(1)}, u32[]{:S(2)}, u32[]{:S(2)}) %collective-permute-start.11) | collective-permute-done | bytes 33056 | tf_op jit(solution)/shard_map/ppermute | solution.py:23
  155.5 2.9 %collective-permute-start.12 = (f32[64,129]{1,0:T(8,128)S(1)}, f32[64,129]{1,0:T(8,128)S(1)}, u32[]{:S(2)}, u32[]{:S(2)}) collective-permute-start(f32[64,129]{1,0:T(8,128)S(1)} %add.38), channel_id=1, source_target_pairs={{0,384},{16,400},{32,416},{48,432},{64,448},{80,464},{96,480},{112... | collective-permute-start | bytes 99080 | tf_op jit(solution)/shard_map/ppermute | solution.py:23
  158.5 4.5 %collective-permute-done.12 = f32[64,129]{1,0:T(8,128)S(1)} collective-permute-done((f32[64,129]{1,0:T(8,128)S(1)}, f32[64,129]{1,0:T(8,128)S(1)}, u32[]{:S(2)}, u32[]{:S(2)}) %collective-permute-start.12) | collective-permute-done | bytes 33056 | tf_op jit(solution)/shard_map/ppermute | solution.py:23
  162.9 0.6 add.39.packed_ref
  163.5 11.0 %shard_map.50 = (f32[2,64]{1,0:T(2,128)}, f32[2,1]{1,0:T(2,128)}) custom-call(s32[1]{0:T(128)} %bitcast.first_ref, f32[64,129]{1,0:T(8,128)} %add.39.packed_ref), custom_call_target="tpu_custom_call" | custom-call | flops 1572864 | bytes 65536 | tf_op jit(solution)/shard_map/pallas_call | solution.py:143
  174.5 0.7 copy-done.5
  (33 shorter events, 3.5 us)
Async XLA Ops:
  0.6 31.9 %collective-permute-start = (f32[2,10,32,128]{3,2,1,0:T(8,128)}, f32[2,10,32,128]{3,2,1,0:T(8,128)S(1)}, u32[]{:S(2)}, u32[]{:S(2)}) collective-permute-start(f32[2,10,32,128]{3,2,1,0:T(8,128)} %own_ref.1), channel_id=1, source_target_pairs={{0,1},{1,2},{2,3},{3,4},{4,5},{5,6},{6,7},{7,8},{8,9},{9,10},{10,1... | collective-permute-start | bytes 983048 | tf_op jit(solution)/shard_map/ppermute | solution.py:170
  2.6 30.0 %collective-permute-start.1 = (f32[2,10,32,128]{3,2,1,0:T(8,128)}, f32[2,10,32,128]{3,2,1,0:T(8,128)S(1)}, u32[]{:S(2)}, u32[]{:S(2)}) collective-permute-start(f32[2,10,32,128]{3,2,1,0:T(8,128)} %own_ref.1), channel_id=1, source_target_pairs={{1,0},{2,1},{3,2},{4,3},{5,4},{6,5},{7,6},{8,7},{9,8},{10,9},{11,1... | collective-permute-start | bytes 983048 | tf_op jit(solution)/shard_map/ppermute | solution.py:171
  6.2 15.7 %collective-permute-start.2 = (f32[10,32,128]{2,1,0:T(8,128)}, f32[10,32,128]{2,1,0:T(8,128)S(1)}, u32[]{:S(2)}, u32[]{:S(2)}) collective-permute-start(f32[10,32,128]{2,1,0:T(8,128)} %own_pot.1), channel_id=1, source_target_pairs={{79,0},{95,16},{111,32},{127,48},{15,64},{31,80},{47,96},{63,112},... | collective-permute-start | bytes 491528 | tf_op jit(solution)/shard_map/ppermute | solution.py:172
  20.0 12.6 %collective-permute-start.3 = (f32[10,32,128]{2,1,0:T(8,128)}, f32[10,32,128]{2,1,0:T(8,128)S(1)}, u32[]{:S(2)}, u32[]{:S(2)}) collective-permute-start(f32[10,32,128]{2,1,0:T(8,128)} %own_pot.1), channel_id=1, source_target_pairs={{1,0},{17,16},{33,32},{49,48},{65,64},{81,80},{97,96},{113,112},{1... | collective-permute-start | bytes 491528 | tf_op jit(solution)/shard_map/ppermute | solution.py:173
  21.9 10.6 %copy-start.3 = (f32[10,32,128]{2,1,0:T(8,128)}, f32[10,32,128]{2,1,0:T(8,128)S(1)}, u32[]{:S(2)}) copy-start(f32[10,32,128]{2,1,0:T(8,128)S(1)} %collective-permute-done.2.below_pot) | copy-start | bytes 491524
  32.5 0.7 copy-start.4
  32.6 0.8 copy-start.1
  33.3 0.7 copy-start.2
  40.9 1.0 copy-start
  76.7 18.1 %collective-permute-start.4 = (f32[64,129]{1,0:T(8,128)S(1)}, f32[64,129]{1,0:T(8,128)S(1)}, u32[]{:S(2)}, u32[]{:S(2)}) collective-permute-start(f32[64,129]{1,0:T(8,128)S(1)} %pad_maximum_fusion.1), channel_id=1, source_target_pairs={{0,1},{1,0},{2,3},{3,2},{4,5},{5,4},{6,7},{7,6},{8,9},{9,8},{10,11... | collective-permute-start | bytes 99080 | tf_op jit(solution)/shard_map/ppermute | solution.py:23
  94.9 6.2 %collective-permute-start.5 = (f32[64,129]{1,0:T(8,128)S(1)}, f32[64,129]{1,0:T(8,128)S(1)}, u32[]{:S(2)}, u32[]{:S(2)}) collective-permute-start(f32[64,129]{1,0:T(8,128)S(1)} %fusion.8), channel_id=1, source_target_pairs={{0,2},{1,3},{2,0},{3,1},{4,6},{5,7},{6,4},{7,5},{8,10},{9,11},{10,... | collective-permute-start | bytes 99080 | tf_op jit(solution)/shard_map/ppermute | solution.py:23
  101.2 7.4 %collective-permute-start.6 = (f32[64,129]{1,0:T(8,128)S(1)}, f32[64,129]{1,0:T(8,128)S(1)}, u32[]{:S(2)}, u32[]{:S(2)}) collective-permute-start(f32[64,129]{1,0:T(8,128)S(1)} %add.32), channel_id=1, source_target_pairs={{0,6},{1,7},{2,4},{3,5},{4,2},{5,3},{6,0},{7,1},{8,14},{9,15},{10,... | collective-permute-start | bytes 99080 | tf_op jit(solution)/shard_map/ppermute | solution.py:23
  108.5 15.4 %collective-permute-start.7 = (f32[64,129]{1,0:T(8,128)S(1)}, f32[64,129]{1,0:T(8,128)S(1)}, u32[]{:S(2)}, u32[]{:S(2)}) collective-permute-start(f32[64,129]{1,0:T(8,128)S(1)} %add.33), channel_id=1, source_target_pairs={{0,8},{1,9},{2,10},{3,11},{4,12},{5,13},{6,14},{7,15},{8,0},{9,1},... | collective-permute-start | bytes 99080 | tf_op jit(solution)/shard_map/ppermute | solution.py:23
  124.0 6.2 %collective-permute-start.8 = (f32[64,129]{1,0:T(8,128)S(1)}, f32[64,129]{1,0:T(8,128)S(1)}, u32[]{:S(2)}, u32[]{:S(2)}) collective-permute-start(f32[64,129]{1,0:T(8,128)S(1)} %add.34), channel_id=1, source_target_pairs={{0,16},{16,0},{32,48},{48,32},{64,80},{80,64},{96,112},{112,96},{1... | collective-permute-start | bytes 99080 | tf_op jit(solution)/shard_map/ppermute | solution.py:23
  130.1 7.1 %collective-permute-start.9 = (f32[64,129]{1,0:T(8,128)S(1)}, f32[64,129]{1,0:T(8,128)S(1)}, u32[]{:S(2)}, u32[]{:S(2)}) collective-permute-start(f32[64,129]{1,0:T(8,128)S(1)} %add.35), channel_id=1, source_target_pairs={{0,32},{16,48},{32,0},{48,16},{64,96},{80,112},{96,64},{112,80},{1... | collective-permute-start | bytes 99080 | tf_op jit(solution)/shard_map/ppermute | solution.py:23
  137.2 12.2 %collective-permute-start.10 = (f32[64,129]{1,0:T(8,128)S(1)}, f32[64,129]{1,0:T(8,128)S(1)}, u32[]{:S(2)}, u32[]{:S(2)}) collective-permute-start(f32[64,129]{1,0:T(8,128)S(1)} %add.36), channel_id=1, source_target_pairs={{0,64},{16,80},{32,96},{48,112},{64,0},{80,16},{96,32},{112,48},{1... | collective-permute-start | bytes 99080 | tf_op jit(solution)/shard_map/ppermute | solution.py:23
  149.4 6.2 %collective-permute-start.11 = (f32[64,129]{1,0:T(8,128)S(1)}, f32[64,129]{1,0:T(8,128)S(1)}, u32[]{:S(2)}, u32[]{:S(2)}) collective-permute-start(f32[64,129]{1,0:T(8,128)S(1)} %add.37), channel_id=1, source_target_pairs={{0,128},{16,144},{32,160},{48,176},{64,192},{80,208},{96,224},{112... | collective-permute-start | bytes 99080 | tf_op jit(solution)/shard_map/ppermute | solution.py:23
  155.5 7.4 %collective-permute-start.12 = (f32[64,129]{1,0:T(8,128)S(1)}, f32[64,129]{1,0:T(8,128)S(1)}, u32[]{:S(2)}, u32[]{:S(2)}) collective-permute-start(f32[64,129]{1,0:T(8,128)S(1)} %add.38), channel_id=1, source_target_pairs={{0,384},{16,400},{32,416},{48,432},{64,448},{80,464},{96,480},{112... | collective-permute-start | bytes 99080 | tf_op jit(solution)/shard_map/ppermute | solution.py:23
  174.5 0.7 copy-start.5

commit v11 on v9

--- a/solution.py
+++ b/solution.py
@@ -190,8 +190,8 @@
     )
     norm_part = jnp.sum(image_here * image_here, axis=1)
     packed = jnp.concatenate([margin_part.reshape(-1), image_part.reshape(-1), norm_part])
+    packed = butterfly_sum(packed, "band", [flip(1), flip(2), flip(4), flip(8), ring_of_four(0, 8)])
     packed = butterfly_sum(packed, "grid", [flip(1), flip(2), ring_of_four(0, 2), flip(8)])
-    packed = butterfly_sum(packed, "band", [flip(1), flip(2), flip(4), flip(8), ring_of_four(0, 8)])
     packed = packed * inverse_cells
     square = total_bands * total_bands
     margin = packed[:square].reshape(total_bands, total_bands)

time: 171 us -> 166 us (0.971)
  waiting for transfers between devices: 55.9 us -> 42.1 us
  starting transfers between devices: 57.2 us -> 65.9 us
    ppermute x9, waiting for transfers between devices: 45.3 us -> 31.5 us  [butterfly_sum(): values = values + lax.ppermute(values, axis, pairs)]
    ppermute x9, starting transfers between devices: 36 us -> 44.7 us  [butterfly_sum(): values = values + lax.ppermute(values, axis, pairs)]
where the time goes in v11:
time: 166 us; the launch traced here: 165 us
  starting transfers between devices  65.9 us (40%)
  waiting for transfers between devices  42.1 us (25%)
  blocking collectives  32.5 us (20%)
  Pallas kernels  14.2 us (9%)
  local copies, waits for them, and re-layouts  6.69 us (4%)
  other arithmetic  1.85 us (1%)
    ppermute x9, starting transfers between devices, butterfly_sum(): values = values + lax.ppermute(values, axis, pairs)  44.7 us
    all_to_all x1, blocking collectives, on_device(): moved = lax.all_to_all(both, 'band', 2, 1, tiled=True)  32.5 us
    ppermute x9, waiting for transfers between devices, butterfly_sum(): values = values + lax.ppermute(values, axis, pairs)  31.5 us
    ppermute x1, starting transfers between devices, on_device(): lax.ppermute(potential[potential.shape[0] - width:], ('band', 'grid'), re...  13.8 us
    ppermute x1, waiting for transfers between devices, on_device(): lax.ppermute(potential[:width], ('band', 'grid'), replica_pairs(-1))  10.6 us
    pallas_call x1, Pallas kernels, rayleigh_ritz(): pl.pallas_call(rayleigh_ritz_kernel, out_shape=(jax.ShapeDtypeStruct((ban...  8.4 us
    pallas_call x1, Pallas kernels, filter_and_image(): pl.pallas_call(filter_kernel, out_shape=(jax.ShapeDtypeStruct(shape, jnp....  5.77 us
    ppermute x1, starting transfers between devices, on_device(): lax.ppermute(trial_bands[:, :width], 'grid', [((i + 1) % count, i) for i...  3.64 us
  transfers between devices with their start and end apart: 13, of which 10 were waited for; matrix products, arithmetic and copies ran while one was open for 0% of the time, Pallas kernels for 0%

profile of v11, /device:TPU:24, one launch (start us, length us, event | category | flops | bytes accessed | tf_op | source)
XLA Modules:
  0.0 165.0 jit_solution(4043988851374392513)
XLA Ops:
  0.6 1.9 %collective-permute-start = (f32[2,10,32,128]{3,2,1,0:T(8,128)}, f32[2,10,32,128]{3,2,1,0:T(8,128)S(1)}, u32[]{:S(2)}, u32[]{:S(2)}) collective-permute-start(f32[2,10,32,128]{3,2,1,0:T(8,128)} %own_ref.1), channel_id=1, source_target_pairs={{0,1},{1,2},{2,3},{3,4},{4,5},{5,6},{6,7},{7,8},{8,9},{9,10},{10,1... | collective-permute-start | bytes 983048 | tf_op jit(solution)/shard_map/ppermute | solution.py:168
  2.6 3.6 %collective-permute-start.1 = (f32[2,10,32,128]{3,2,1,0:T(8,128)}, f32[2,10,32,128]{3,2,1,0:T(8,128)S(1)}, u32[]{:S(2)}, u32[]{:S(2)}) collective-permute-start(f32[2,10,32,128]{3,2,1,0:T(8,128)} %own_ref.1), channel_id=1, source_target_pairs={{1,0},{2,1},{3,2},{4,3},{5,4},{6,5},{7,6},{8,7},{9,8},{10,9},{11,1... | collective-permute-start | bytes 983048 | tf_op jit(solution)/shard_map/ppermute | solution.py:169
  6.2 13.8 %collective-permute-start.2 = (f32[10,32,128]{2,1,0:T(8,128)}, f32[10,32,128]{2,1,0:T(8,128)S(1)}, u32[]{:S(2)}, u32[]{:S(2)}) collective-permute-start(f32[10,32,128]{2,1,0:T(8,128)} %own_pot.1), channel_id=1, source_target_pairs={{79,0},{95,16},{111,32},{127,48},{15,64},{31,80},{47,96},{63,112},... | collective-permute-start | bytes 491528 | tf_op jit(solution)/shard_map/ppermute | solution.py:170
  20.0 1.9 %collective-permute-start.3 = (f32[10,32,128]{2,1,0:T(8,128)}, f32[10,32,128]{2,1,0:T(8,128)S(1)}, u32[]{:S(2)}, u32[]{:S(2)}) collective-permute-start(f32[10,32,128]{2,1,0:T(8,128)} %own_pot.1), channel_id=1, source_target_pairs={{1,0},{17,16},{33,32},{49,48},{65,64},{81,80},{97,96},{113,112},{1... | collective-permute-start | bytes 491528 | tf_op jit(solution)/shard_map/ppermute | solution.py:171
  21.9 10.6 %collective-permute-done.3.above_pot = f32[10,32,128]{2,1,0:T(8,128)S(1)} collective-permute-done((f32[10,32,128]{2,1,0:T(8,128)}, f32[10,32,128]{2,1,0:T(8,128)S(1)}, u32[]{:S(2)}, u32[]{:S(2)}) %collective-permute-start.3) | collective-permute-done | bytes 163872 | tf_op jit(solution)/shard_map/ppermute | solution.py:171
  33.3 0.7 copy-done.2
  34.0 5.8 %shard_map.49 = (f32[2,10,32,128]{3,2,1,0:T(8,128)}, f32[2,10,32,128]{3,2,1,0:T(8,128)}) custom-call(f32[2,10,32,128]{3,2,1,0:T(8,128)} %copy-done.1, f32[2,10,32,128]{3,2,1,0:T(8,128)} %own_ref.1, f32[2,10,32,128]{3,2,1,0:T(8,128)} %copy-done.2, f32[10,32,128]{2,1,0:T(8,128)} %copy-done.3, f32[10,32,128]{2,1,0:T(8,128)} %own_pot.1, f32[10,32,128]{2,1,0:T(8,128)} %copy-done.4), custom_call_target="tpu_custom_call" | custom-call | flops 29491200 | bytes 2949120 | tf_op jit(solution)/shard_map/pallas_call | solution.py:93
  39.8 1.0 stack.7
  41.1 0.7 copy-done
  42.4 32.5 %all_to_all.15 = f32[2,2,32,1280]{3,1,0,2:T(2,128)S(1)} all-to-all(f32[2,2,32,1280]{3,1,0,2:T(2,128)S(1)} %pad_maximum_fusion), channel_id=1, replica_groups=mesh['band'=32,'grid'=16] {'band'}, dimensions={2} | all-to-all | bytes 1310720 | tf_op jit(solution)/shard_map/all_to_all | solution.py:182
  76.8 1.9 %collective-permute-start.4 = (f32[8256]{0:T(1024)S(1)}, f32[8256]{0:T(1024)S(1)}, u32[]{:S(2)}, u32[]{:S(2)}) collective-permute-start(f32[8256]{0:T(1024)S(1)} %constant_dynamic-update-slice_fusion), channel_id=1, source_target_pairs={{0,16},{16,0},{32,48},{48,32},{64,80},{80,64},{96,112},{112,96},{1... | collective-permute-start | bytes 99080 | tf_op jit(solution)/shard_map/ppermute | solution.py:21
  78.7 4.1 %collective-permute-done.4 = f32[8256]{0:T(1024)S(1)} collective-permute-done((f32[8256]{0:T(1024)S(1)}, f32[8256]{0:T(1024)S(1)}, u32[]{:S(2)}, u32[]{:S(2)}) %collective-permute-start.4) | collective-permute-done | bytes 33056 | tf_op jit(solution)/shard_map/ppermute | solution.py:21
  82.8 2.8 %collective-permute-start.5 = (f32[8256]{0:T(1024)S(1)}, f32[8256]{0:T(1024)S(1)}, u32[]{:S(2)}, u32[]{:S(2)}) collective-permute-start(f32[8256]{0:T(1024)S(1)} %add.30), channel_id=1, source_target_pairs={{0,32},{16,48},{32,0},{48,16},{64,96},{80,112},{96,64},{112,80},{1... | collective-permute-start | bytes 99080 | tf_op jit(solution)/shard_map/ppermute | solution.py:21
  85.7 3.9 %collective-permute-done.5 = f32[8256]{0:T(1024)S(1)} collective-permute-done((f32[8256]{0:T(1024)S(1)}, f32[8256]{0:T(1024)S(1)}, u32[]{:S(2)}, u32[]{:S(2)}) %collective-permute-start.5) | collective-permute-done | bytes 33056 | tf_op jit(solution)/shard_map/ppermute | solution.py:21
  89.6 5.2 %collective-permute-start.6 = (f32[8256]{0:T(1024)S(1)}, f32[8256]{0:T(1024)S(1)}, u32[]{:S(2)}, u32[]{:S(2)}) collective-permute-start(f32[8256]{0:T(1024)S(1)} %add.31), channel_id=1, source_target_pairs={{0,64},{16,80},{32,96},{48,112},{64,0},{80,16},{96,32},{112,48},{1... | collective-permute-start | bytes 99080 | tf_op jit(solution)/shard_map/ppermute | solution.py:21
  94.8 4.5 %collective-permute-done.6 = f32[8256]{0:T(1024)S(1)} collective-permute-done((f32[8256]{0:T(1024)S(1)}, f32[8256]{0:T(1024)S(1)}, u32[]{:S(2)}, u32[]{:S(2)}) %collective-permute-start.6) | collective-permute-done | bytes 33056 | tf_op jit(solution)/shard_map/ppermute | solution.py:21
  99.3 1.9 %collective-permute-start.7 = (f32[8256]{0:T(1024)S(1)}, f32[8256]{0:T(1024)S(1)}, u32[]{:S(2)}, u32[]{:S(2)}) collective-permute-start(f32[8256]{0:T(1024)S(1)} %add.32), channel_id=1, source_target_pairs={{0,128},{16,144},{32,160},{48,176},{64,192},{80,208},{96,224},{112... | collective-permute-start | bytes 99080 | tf_op jit(solution)/shard_map/ppermute | solution.py:21
  101.3 3.9 %collective-permute-done.7 = f32[8256]{0:T(1024)S(1)} collective-permute-done((f32[8256]{0:T(1024)S(1)}, f32[8256]{0:T(1024)S(1)}, u32[]{:S(2)}, u32[]{:S(2)}) %collective-permute-start.7) | collective-permute-done | bytes 33056 | tf_op jit(solution)/shard_map/ppermute | solution.py:21
  105.2 3.7 %collective-permute-start.8 = (f32[8256]{0:T(1024)S(1)}, f32[8256]{0:T(1024)S(1)}, u32[]{:S(2)}, u32[]{:S(2)}) collective-permute-start(f32[8256]{0:T(1024)S(1)} %add.33), channel_id=1, source_target_pairs={{0,384},{16,400},{32,416},{48,432},{64,448},{80,464},{96,480},{112... | collective-permute-start | bytes 99080 | tf_op jit(solution)/shard_map/ppermute | solution.py:21
  108.9 3.3 %collective-permute-done.8 = f32[8256]{0:T(1024)S(1)} collective-permute-done((f32[8256]{0:T(1024)S(1)}, f32[8256]{0:T(1024)S(1)}, u32[]{:S(2)}, u32[]{:S(2)}) %collective-permute-start.8) | collective-permute-done | bytes 33056 | tf_op jit(solution)/shard_map/ppermute | solution.py:21
  112.3 12.5 %collective-permute-start.9 = (f32[8256]{0:T(1024)S(1)}, f32[8256]{0:T(1024)S(1)}, u32[]{:S(2)}, u32[]{:S(2)}) collective-permute-start(f32[8256]{0:T(1024)S(1)} %add.34), channel_id=1, source_target_pairs={{0,1},{1,0},{2,3},{3,2},{4,5},{5,4},{6,7},{7,6},{8,9},{9,8},{10,11... | collective-permute-start | bytes 99080 | tf_op jit(solution)/shard_map/ppermute | solution.py:21
  124.8 0.8 collective-permute-done.9
  125.6 1.9 %collective-permute-start.10 = (f32[8256]{0:T(1024)S(1)}, f32[8256]{0:T(1024)S(1)}, u32[]{:S(2)}, u32[]{:S(2)}) collective-permute-start(f32[8256]{0:T(1024)S(1)} %add.35), channel_id=1, source_target_pairs={{0,2},{1,3},{2,0},{3,1},{4,6},{5,7},{6,4},{7,5},{8,10},{9,11},{10,... | collective-permute-start | bytes 99080 | tf_op jit(solution)/shard_map/ppermute | solution.py:21
  127.6 3.9 %collective-permute-done.10 = f32[8256]{0:T(1024)S(1)} collective-permute-done((f32[8256]{0:T(1024)S(1)}, f32[8256]{0:T(1024)S(1)}, u32[]{:S(2)}, u32[]{:S(2)}) %collective-permute-start.10) | collective-permute-done | bytes 33056 | tf_op jit(solution)/shard_map/ppermute | solution.py:21
  131.5 4.6 %collective-permute-start.11 = (f32[8256]{0:T(1024)S(1)}, f32[8256]{0:T(1024)S(1)}, u32[]{:S(2)}, u32[]{:S(2)}) collective-permute-start(f32[8256]{0:T(1024)S(1)} %add.36), channel_id=1, source_target_pairs={{0,6},{1,7},{2,4},{3,5},{4,2},{5,3},{6,0},{7,1},{8,14},{9,15},{10,... | collective-permute-start | bytes 99080 | tf_op jit(solution)/shard_map/ppermute | solution.py:21
  136.1 2.5 %collective-permute-done.11 = f32[8256]{0:T(1024)S(1)} collective-permute-done((f32[8256]{0:T(1024)S(1)}, f32[8256]{0:T(1024)S(1)}, u32[]{:S(2)}, u32[]{:S(2)}) %collective-permute-start.11) | collective-permute-done | bytes 33056 | tf_op jit(solution)/shard_map/ppermute | solution.py:21
  138.5 10.1 %collective-permute-start.12 = (f32[8256]{0:T(1024)S(1)}, f32[8256]{0:T(1024)S(1)}, u32[]{:S(2)}, u32[]{:S(2)}) collective-permute-start(f32[8256]{0:T(1024)S(1)} %add.37), channel_id=1, source_target_pairs={{0,8},{1,9},{2,10},{3,11},{4,12},{5,13},{6,14},{7,15},{8,0},{9,1},... | collective-permute-start | bytes 99080 | tf_op jit(solution)/shard_map/ppermute | solution.py:21
  148.6 4.5 %collective-permute-done.12 = f32[8256]{0:T(1024)S(1)} collective-permute-done((f32[8256]{0:T(1024)S(1)}, f32[8256]{0:T(1024)S(1)}, u32[]{:S(2)}, u32[]{:S(2)}) %collective-permute-start.12) | collective-permute-done | bytes 33056 | tf_op jit(solution)/shard_map/ppermute | solution.py:21
  153.9 0.7 slice.42.subspace_ref
  154.6 0.7 copy.14.norms_ref
  155.3 8.4 %shard_map.50 = (f32[2,64]{1,0:T(2,128)}, f32[2,1]{1,0:T(2,128)}) custom-call(s32[1]{0:T(128)} %bitcast.first_ref, f32[64,64]{1,0:T(8,128)} %fusion.margin_ref, f32[64,64]{1,0:T(8,128)} %slice.42.subspace_ref, f32[64,1]{1,0:T(8,128)} %copy.14.norms_ref), custom_call_target="tpu_custom_call" | custom-call | flops 1572864 | bytes 65536 | tf_op jit(solution)/shard_map/pallas_call | solution.py:141
  163.7 0.7 copy-done.5
  (42 shorter events, 4.9 us)
Async XLA Ops:
  0.6 31.9 %collective-permute-start = (f32[2,10,32,128]{3,2,1,0:T(8,128)}, f32[2,10,32,128]{3,2,1,0:T(8,128)S(1)}, u32[]{:S(2)}, u32[]{:S(2)}) collective-permute-start(f32[2,10,32,128]{3,2,1,0:T(8,128)} %own_ref.1), channel_id=1, source_target_pairs={{0,1},{1,2},{2,3},{3,4},{4,5},{5,6},{6,7},{7,8},{8,9},{9,10},{10,1... | collective-permute-start | bytes 983048 | tf_op jit(solution)/shard_map/ppermute | solution.py:168
  2.6 30.0 %collective-permute-start.1 = (f32[2,10,32,128]{3,2,1,0:T(8,128)}, f32[2,10,32,128]{3,2,1,0:T(8,128)S(1)}, u32[]{:S(2)}, u32[]{:S(2)}) collective-permute-start(f32[2,10,32,128]{3,2,1,0:T(8,128)} %own_ref.1), channel_id=1, source_target_pairs={{1,0},{2,1},{3,2},{4,3},{5,4},{6,5},{7,6},{8,7},{9,8},{10,9},{11,1... | collective-permute-start | bytes 983048 | tf_op jit(solution)/shard_map/ppermute | solution.py:169
  6.2 15.7 %collective-permute-start.2 = (f32[10,32,128]{2,1,0:T(8,128)}, f32[10,32,128]{2,1,0:T(8,128)S(1)}, u32[]{:S(2)}, u32[]{:S(2)}) collective-permute-start(f32[10,32,128]{2,1,0:T(8,128)} %own_pot.1), channel_id=1, source_target_pairs={{79,0},{95,16},{111,32},{127,48},{15,64},{31,80},{47,96},{63,112},... | collective-permute-start | bytes 491528 | tf_op jit(solution)/shard_map/ppermute | solution.py:170
  20.0 12.6 %collective-permute-start.3 = (f32[10,32,128]{2,1,0:T(8,128)}, f32[10,32,128]{2,1,0:T(8,128)S(1)}, u32[]{:S(2)}, u32[]{:S(2)}) collective-permute-start(f32[10,32,128]{2,1,0:T(8,128)} %own_pot.1), channel_id=1, source_target_pairs={{1,0},{17,16},{33,32},{49,48},{65,64},{81,80},{97,96},{113,112},{1... | collective-permute-start | bytes 491528 | tf_op jit(solution)/shard_map/ppermute | solution.py:171
  21.9 10.6 %copy-start.3 = (f32[10,32,128]{2,1,0:T(8,128)}, f32[10,32,128]{2,1,0:T(8,128)S(1)}, u32[]{:S(2)}) copy-start(f32[10,32,128]{2,1,0:T(8,128)S(1)} %collective-permute-done.2.below_pot) | copy-start | bytes 491524
  32.5 0.7 copy-start.4
  32.6 0.8 copy-start.1
  33.3 0.7 copy-start.2
  40.8 1.0 copy-start
  76.8 6.1 %collective-permute-start.4 = (f32[8256]{0:T(1024)S(1)}, f32[8256]{0:T(1024)S(1)}, u32[]{:S(2)}, u32[]{:S(2)}) collective-permute-start(f32[8256]{0:T(1024)S(1)} %constant_dynamic-update-slice_fusion), channel_id=1, source_target_pairs={{0,16},{16,0},{32,48},{48,32},{64,80},{80,64},{96,112},{112,96},{1... | collective-permute-start | bytes 99080 | tf_op jit(solution)/shard_map/ppermute | solution.py:21
  82.8 6.7 %collective-permute-start.5 = (f32[8256]{0:T(1024)S(1)}, f32[8256]{0:T(1024)S(1)}, u32[]{:S(2)}, u32[]{:S(2)}) collective-permute-start(f32[8256]{0:T(1024)S(1)} %add.30), channel_id=1, source_target_pairs={{0,32},{16,48},{32,0},{48,16},{64,96},{80,112},{96,64},{112,80},{1... | collective-permute-start | bytes 99080 | tf_op jit(solution)/shard_map/ppermute | solution.py:21
  89.6 9.8 %collective-permute-start.6 = (f32[8256]{0:T(1024)S(1)}, f32[8256]{0:T(1024)S(1)}, u32[]{:S(2)}, u32[]{:S(2)}) collective-permute-start(f32[8256]{0:T(1024)S(1)} %add.31), channel_id=1, source_target_pairs={{0,64},{16,80},{32,96},{48,112},{64,0},{80,16},{96,32},{112,48},{1... | collective-permute-start | bytes 99080 | tf_op jit(solution)/shard_map/ppermute | solution.py:21
  99.3 5.8 %collective-permute-start.7 = (f32[8256]{0:T(1024)S(1)}, f32[8256]{0:T(1024)S(1)}, u32[]{:S(2)}, u32[]{:S(2)}) collective-permute-start(f32[8256]{0:T(1024)S(1)} %add.32), channel_id=1, source_target_pairs={{0,128},{16,144},{32,160},{48,176},{64,192},{80,208},{96,224},{112... | collective-permute-start | bytes 99080 | tf_op jit(solution)/shard_map/ppermute | solution.py:21
  105.2 7.1 %collective-permute-start.8 = (f32[8256]{0:T(1024)S(1)}, f32[8256]{0:T(1024)S(1)}, u32[]{:S(2)}, u32[]{:S(2)}) collective-permute-start(f32[8256]{0:T(1024)S(1)} %add.33), channel_id=1, source_target_pairs={{0,384},{16,400},{32,416},{48,432},{64,448},{80,464},{96,480},{112... | collective-permute-start | bytes 99080 | tf_op jit(solution)/shard_map/ppermute | solution.py:21
  112.3 13.4 %collective-permute-start.9 = (f32[8256]{0:T(1024)S(1)}, f32[8256]{0:T(1024)S(1)}, u32[]{:S(2)}, u32[]{:S(2)}) collective-permute-start(f32[8256]{0:T(1024)S(1)} %add.34), channel_id=1, source_target_pairs={{0,1},{1,0},{2,3},{3,2},{4,5},{5,4},{6,7},{7,6},{8,9},{9,8},{10,11... | collective-permute-start | bytes 99080 | tf_op jit(solution)/shard_map/ppermute | solution.py:21
  125.6 5.8 %collective-permute-start.10 = (f32[8256]{0:T(1024)S(1)}, f32[8256]{0:T(1024)S(1)}, u32[]{:S(2)}, u32[]{:S(2)}) collective-permute-start(f32[8256]{0:T(1024)S(1)} %add.35), channel_id=1, source_target_pairs={{0,2},{1,3},{2,0},{3,1},{4,6},{5,7},{6,4},{7,5},{8,10},{9,11},{10,... | collective-permute-start | bytes 99080 | tf_op jit(solution)/shard_map/ppermute | solution.py:21
  131.5 7.1 %collective-permute-start.11 = (f32[8256]{0:T(1024)S(1)}, f32[8256]{0:T(1024)S(1)}, u32[]{:S(2)}, u32[]{:S(2)}) collective-permute-start(f32[8256]{0:T(1024)S(1)} %add.36), channel_id=1, source_target_pairs={{0,6},{1,7},{2,4},{3,5},{4,2},{5,3},{6,0},{7,1},{8,14},{9,15},{10,... | collective-permute-start | bytes 99080 | tf_op jit(solution)/shard_map/ppermute | solution.py:21
  138.5 14.6 %collective-permute-start.12 = (f32[8256]{0:T(1024)S(1)}, f32[8256]{0:T(1024)S(1)}, u32[]{:S(2)}, u32[]{:S(2)}) collective-permute-start(f32[8256]{0:T(1024)S(1)} %add.37), channel_id=1, source_target_pairs={{0,8},{1,9},{2,10},{3,11},{4,12},{5,13},{6,14},{7,15},{8,0},{9,1},... | collective-permute-start | bytes 99080 | tf_op jit(solution)/shard_map/ppermute | solution.py:21
  163.7 0.7 copy-start.5

commit v12 on v11

--- a/solution.py
+++ b/solution.py
@@ -191,7 +191,7 @@
     norm_part = jnp.sum(image_here * image_here, axis=1)
     packed = jnp.concatenate([margin_part.reshape(-1), image_part.reshape(-1), norm_part])
     packed = butterfly_sum(packed, "band", [flip(1), flip(2), flip(4), flip(8), ring_of_four(0, 8)])
-    packed = butterfly_sum(packed, "grid", [flip(1), flip(2), ring_of_four(0, 2), flip(8)])
+    packed = butterfly_sum(packed, "grid", [flip(8), flip(2), ring_of_four(0, 2), flip(1)])
     packed = packed * inverse_cells
     square = total_bands * total_bands
     margin = packed[:square].reshape(total_bands, total_bands)

time: 166 us -> 169 us (1.018)
  the two profiles are of different devices: /device:TPU:24 before, /device:TPU:1 now
where the time goes in v12:
time: 169 us
  starting transfers between devices  81.3 us (48%)
  blocking collectives  32.1 us (19%)
  waiting for transfers between devices  30.8 us (18%)
  Pallas kernels  14.2 us (8%)
  local copies, waits for them, and re-layouts  6.69 us (4%)
  other arithmetic  1.85 us (1%)
    ppermute x9, starting transfers between devices, butterfly_sum(): values = values + lax.ppermute(values, axis, pairs)  54.2 us
    all_to_all x1, blocking collectives, on_device(): moved = lax.all_to_all(both, 'band', 2, 1, tiled=True)  32.1 us
    ppermute x9, waiting for transfers between devices, butterfly_sum(): values = values + lax.ppermute(values, axis, pairs)  29.6 us
    ppermute x1, starting transfers between devices, on_device(): lax.ppermute(potential[:width], ('band', 'grid'), replica_pairs(-1))  14.5 us
    pallas_call x1, Pallas kernels, rayleigh_ritz(): pl.pallas_call(rayleigh_ritz_kernel, out_shape=(jax.ShapeDtypeStruct((ban...  8.4 us
    ppermute x1, starting transfers between devices, on_device(): lax.ppermute(trial_bands[:, :width], 'grid', [((i + 1) % count, i) for i...  6.11 us
    pallas_call x1, Pallas kernels, filter_and_image(): pl.pallas_call(filter_kernel, out_shape=(jax.ShapeDtypeStruct(shape, jnp....  5.77 us
    ppermute x1, starting transfers between devices, on_device(): lax.ppermute(trial_bands[:, trial_bands.shape[1] - width:], 'grid', [(i,...  4.59 us
  transfers between devices with their start and end apart: 13, of which 10 were waited for; matrix products, arithmetic and copies ran while one was open for 0% of the time, Pallas kernels for 0%

profile of v12, /device:TPU:1, one launch (start us, length us, event | category | flops | bytes accessed | tf_op | source)
XLA Modules:
  0.0 168.6 jit_solution(5140755131936398360)
XLA Ops:
  0.6 4.6 %collective-permute-start = (f32[2,10,32,128]{3,2,1,0:T(8,128)}, f32[2,10,32,128]{3,2,1,0:T(8,128)S(1)}, u32[]{:S(2)}, u32[]{:S(2)}) collective-permute-start(f32[2,10,32,128]{3,2,1,0:T(8,128)} %own_ref.1), channel_id=1, source_target_pairs={{0,1},{1,2},{2,3},{3,4},{4,5},{5,6},{6,7},{7,8},{8,9},{9,10},{10,1... | collective-permute-start | bytes 983048 | tf_op jit(solution)/shard_map/ppermute | solution.py:168
  5.2 6.1 %collective-permute-start.1 = (f32[2,10,32,128]{3,2,1,0:T(8,128)}, f32[2,10,32,128]{3,2,1,0:T(8,128)S(1)}, u32[]{:S(2)}, u32[]{:S(2)}) collective-permute-start(f32[2,10,32,128]{3,2,1,0:T(8,128)} %own_ref.1), channel_id=1, source_target_pairs={{1,0},{2,1},{3,2},{4,3},{5,4},{6,5},{7,6},{8,7},{9,8},{10,9},{11,1... | collective-permute-start | bytes 983048 | tf_op jit(solution)/shard_map/ppermute | solution.py:169
  11.4 1.9 %collective-permute-start.2 = (f32[10,32,128]{2,1,0:T(8,128)}, f32[10,32,128]{2,1,0:T(8,128)S(1)}, u32[]{:S(2)}, u32[]{:S(2)}) collective-permute-start(f32[10,32,128]{2,1,0:T(8,128)} %own_pot.1), channel_id=1, source_target_pairs={{79,0},{95,16},{111,32},{127,48},{15,64},{31,80},{47,96},{63,112},... | collective-permute-start | bytes 491528 | tf_op jit(solution)/shard_map/ppermute | solution.py:170
  13.3 14.5 %collective-permute-start.3 = (f32[10,32,128]{2,1,0:T(8,128)}, f32[10,32,128]{2,1,0:T(8,128)S(1)}, u32[]{:S(2)}, u32[]{:S(2)}) collective-permute-start(f32[10,32,128]{2,1,0:T(8,128)} %own_pot.1), channel_id=1, source_target_pairs={{1,0},{17,16},{33,32},{49,48},{65,64},{81,80},{97,96},{113,112},{1... | collective-permute-start | bytes 491528 | tf_op jit(solution)/shard_map/ppermute | solution.py:171
  27.8 1.2 collective-permute-done.3.above_pot
  29.7 0.7 copy-done.2
  30.5 5.8 %shard_map.49 = (f32[2,10,32,128]{3,2,1,0:T(8,128)}, f32[2,10,32,128]{3,2,1,0:T(8,128)}) custom-call(f32[2,10,32,128]{3,2,1,0:T(8,128)} %copy-done.1, f32[2,10,32,128]{3,2,1,0:T(8,128)} %own_ref.1, f32[2,10,32,128]{3,2,1,0:T(8,128)} %copy-done.2, f32[10,32,128]{2,1,0:T(8,128)} %copy-done.3, f32[10,32,128]{2,1,0:T(8,128)} %own_pot.1, f32[10,32,128]{2,1,0:T(8,128)} %copy-done.4), custom_call_target="tpu_custom_call" | custom-call | flops 29491200 | bytes 2949120 | tf_op jit(solution)/shard_map/pallas_call | solution.py:93
  36.2 1.0 stack.7
  37.5 0.7 copy-done
  38.9 32.1 %all_to_all.15 = f32[2,2,32,1280]{3,1,0,2:T(2,128)S(1)} all-to-all(f32[2,2,32,1280]{3,1,0,2:T(2,128)S(1)} %pad_maximum_fusion), channel_id=1, replica_groups=mesh['band'=32,'grid'=16] {'band'}, dimensions={2} | all-to-all | bytes 1310720 | tf_op jit(solution)/shard_map/all_to_all | solution.py:182
  72.8 1.9 %collective-permute-start.4 = (f32[8256]{0:T(1024)S(1)}, f32[8256]{0:T(1024)S(1)}, u32[]{:S(2)}, u32[]{:S(2)}) collective-permute-start(f32[8256]{0:T(1024)S(1)} %constant_dynamic-update-slice_fusion), channel_id=1, source_target_pairs={{0,16},{16,0},{32,48},{48,32},{64,80},{80,64},{96,112},{112,96},{1... | collective-permute-start | bytes 99080 | tf_op jit(solution)/shard_map/ppermute | solution.py:21
  74.7 3.3 %collective-permute-done.4 = f32[8256]{0:T(1024)S(1)} collective-permute-done((f32[8256]{0:T(1024)S(1)}, f32[8256]{0:T(1024)S(1)}, u32[]{:S(2)}, u32[]{:S(2)}) %collective-permute-start.4) | collective-permute-done | bytes 33056 | tf_op jit(solution)/shard_map/ppermute | solution.py:21
  78.1 2.5 %collective-permute-start.5 = (f32[8256]{0:T(1024)S(1)}, f32[8256]{0:T(1024)S(1)}, u32[]{:S(2)}, u32[]{:S(2)}) collective-permute-start(f32[8256]{0:T(1024)S(1)} %add.30), channel_id=1, source_target_pairs={{0,32},{16,48},{32,0},{48,16},{64,96},{80,112},{96,64},{112,80},{1... | collective-permute-start | bytes 99080 | tf_op jit(solution)/shard_map/ppermute | solution.py:21
  80.5 4.8 %collective-permute-done.5 = f32[8256]{0:T(1024)S(1)} collective-permute-done((f32[8256]{0:T(1024)S(1)}, f32[8256]{0:T(1024)S(1)}, u32[]{:S(2)}, u32[]{:S(2)}) %collective-permute-start.5) | collective-permute-done | bytes 33056 | tf_op jit(solution)/shard_map/ppermute | solution.py:21
  85.4 5.4 %collective-permute-start.6 = (f32[8256]{0:T(1024)S(1)}, f32[8256]{0:T(1024)S(1)}, u32[]{:S(2)}, u32[]{:S(2)}) collective-permute-start(f32[8256]{0:T(1024)S(1)} %add.31), channel_id=1, source_target_pairs={{0,64},{16,80},{32,96},{48,112},{64,0},{80,16},{96,32},{112,48},{1... | collective-permute-start | bytes 99080 | tf_op jit(solution)/shard_map/ppermute | solution.py:21
  90.8 3.9 %collective-permute-done.6 = f32[8256]{0:T(1024)S(1)} collective-permute-done((f32[8256]{0:T(1024)S(1)}, f32[8256]{0:T(1024)S(1)}, u32[]{:S(2)}, u32[]{:S(2)}) %collective-permute-start.6) | collective-permute-done | bytes 33056 | tf_op jit(solution)/shard_map/ppermute | solution.py:21
  94.7 1.9 %collective-permute-start.7 = (f32[8256]{0:T(1024)S(1)}, f32[8256]{0:T(1024)S(1)}, u32[]{:S(2)}, u32[]{:S(2)}) collective-permute-start(f32[8256]{0:T(1024)S(1)} %add.32), channel_id=1, source_target_pairs={{0,128},{16,144},{32,160},{48,176},{64,192},{80,208},{96,224},{112... | collective-permute-start | bytes 99080 | tf_op jit(solution)/shard_map/ppermute | solution.py:21
  96.6 2.8 %collective-permute-done.7 = f32[8256]{0:T(1024)S(1)} collective-permute-done((f32[8256]{0:T(1024)S(1)}, f32[8256]{0:T(1024)S(1)}, u32[]{:S(2)}, u32[]{:S(2)}) %collective-permute-start.7) | collective-permute-done | bytes 33056 | tf_op jit(solution)/shard_map/ppermute | solution.py:21
  99.4 1.9 %collective-permute-start.8 = (f32[8256]{0:T(1024)S(1)}, f32[8256]{0:T(1024)S(1)}, u32[]{:S(2)}, u32[]{:S(2)}) collective-permute-start(f32[8256]{0:T(1024)S(1)} %add.33), channel_id=1, source_target_pairs={{0,384},{16,400},{32,416},{48,432},{64,448},{80,464},{96,480},{112... | collective-permute-start | bytes 99080 | tf_op jit(solution)/shard_map/ppermute | solution.py:21
  101.3 4.0 %collective-permute-done.8 = f32[8256]{0:T(1024)S(1)} collective-permute-done((f32[8256]{0:T(1024)S(1)}, f32[8256]{0:T(1024)S(1)}, u32[]{:S(2)}, u32[]{:S(2)}) %collective-permute-start.8) | collective-permute-done | bytes 33056 | tf_op jit(solution)/shard_map/ppermute | solution.py:21
  105.3 6.1 %collective-permute-start.9 = (f32[8256]{0:T(1024)S(1)}, f32[8256]{0:T(1024)S(1)}, u32[]{:S(2)}, u32[]{:S(2)}) collective-permute-start(f32[8256]{0:T(1024)S(1)} %add.34), channel_id=1, source_target_pairs={{0,8},{1,9},{2,10},{3,11},{4,12},{5,13},{6,14},{7,15},{8,0},{9,1},... | collective-permute-start | bytes 99080 | tf_op jit(solution)/shard_map/ppermute | solution.py:21
  111.4 7.3 %collective-permute-done.9 = f32[8256]{0:T(1024)S(1)} collective-permute-done((f32[8256]{0:T(1024)S(1)}, f32[8256]{0:T(1024)S(1)}, u32[]{:S(2)}, u32[]{:S(2)}) %collective-permute-start.9) | collective-permute-done | bytes 33056 | tf_op jit(solution)/shard_map/ppermute | solution.py:21
  118.7 8.3 %collective-permute-start.10 = (f32[8256]{0:T(1024)S(1)}, f32[8256]{0:T(1024)S(1)}, u32[]{:S(2)}, u32[]{:S(2)}) collective-permute-start(f32[8256]{0:T(1024)S(1)} %add.35), channel_id=1, source_target_pairs={{0,2},{1,3},{2,0},{3,1},{4,6},{5,7},{6,4},{7,5},{8,10},{9,11},{10,... | collective-permute-start | bytes 99080 | tf_op jit(solution)/shard_map/ppermute | solution.py:21
  127.0 1.3 collective-permute-done.10
  128.4 18.3 %collective-permute-start.11 = (f32[8256]{0:T(1024)S(1)}, f32[8256]{0:T(1024)S(1)}, u32[]{:S(2)}, u32[]{:S(2)}) collective-permute-start(f32[8256]{0:T(1024)S(1)} %add.36), channel_id=1, source_target_pairs={{0,6},{1,7},{2,4},{3,5},{4,2},{5,3},{6,0},{7,1},{8,14},{9,15},{10,... | collective-permute-start | bytes 99080 | tf_op jit(solution)/shard_map/ppermute | solution.py:21
  146.6 1.3 collective-permute-done.11
  148.0 7.9 %collective-permute-start.12 = (f32[8256]{0:T(1024)S(1)}, f32[8256]{0:T(1024)S(1)}, u32[]{:S(2)}, u32[]{:S(2)}) collective-permute-start(f32[8256]{0:T(1024)S(1)} %add.37), channel_id=1, source_target_pairs={{0,1},{1,0},{2,3},{3,2},{4,5},{5,4},{6,7},{7,6},{8,9},{9,8},{10,11... | collective-permute-start | bytes 99080 | tf_op jit(solution)/shard_map/ppermute | solution.py:21
  155.9 0.8 collective-permute-done.12
  157.5 0.7 slice.42.subspace_ref
  158.2 0.7 copy.14.norms_ref
  158.9 8.4 %shard_map.50 = (f32[2,64]{1,0:T(2,128)}, f32[2,1]{1,0:T(2,128)}) custom-call(s32[1]{0:T(128)} %bitcast.first_ref, f32[64,64]{1,0:T(8,128)} %fusion.margin_ref, f32[64,64]{1,0:T(8,128)} %slice.42.subspace_ref, f32[64,1]{1,0:T(8,128)} %copy.14.norms_ref), custom_call_target="tpu_custom_call" | custom-call | flops 1572864 | bytes 65536 | tf_op jit(solution)/shard_map/pallas_call | solution.py:141
  167.3 0.7 copy-done.5
  (42 shorter events, 4.9 us)
Async XLA Ops:
  0.6 28.3 %collective-permute-start = (f32[2,10,32,128]{3,2,1,0:T(8,128)}, f32[2,10,32,128]{3,2,1,0:T(8,128)S(1)}, u32[]{:S(2)}, u32[]{:S(2)}) collective-permute-start(f32[2,10,32,128]{3,2,1,0:T(8,128)} %own_ref.1), channel_id=1, source_target_pairs={{0,1},{1,2},{2,3},{3,4},{4,5},{5,6},{6,7},{7,8},{8,9},{9,10},{10,1... | collective-permute-start | bytes 983048 | tf_op jit(solution)/shard_map/ppermute | solution.py:168
  5.2 23.7 %collective-permute-start.1 = (f32[2,10,32,128]{3,2,1,0:T(8,128)}, f32[2,10,32,128]{3,2,1,0:T(8,128)S(1)}, u32[]{:S(2)}, u32[]{:S(2)}) collective-permute-start(f32[2,10,32,128]{3,2,1,0:T(8,128)} %own_ref.1), channel_id=1, source_target_pairs={{1,0},{2,1},{3,2},{4,3},{5,4},{6,5},{7,6},{8,7},{9,8},{10,9},{11,1... | collective-permute-start | bytes 983048 | tf_op jit(solution)/shard_map/ppermute | solution.py:169
  11.4 16.4 %collective-permute-start.2 = (f32[10,32,128]{2,1,0:T(8,128)}, f32[10,32,128]{2,1,0:T(8,128)S(1)}, u32[]{:S(2)}, u32[]{:S(2)}) collective-permute-start(f32[10,32,128]{2,1,0:T(8,128)} %own_pot.1), channel_id=1, source_target_pairs={{79,0},{95,16},{111,32},{127,48},{15,64},{31,80},{47,96},{63,112},... | collective-permute-start | bytes 491528 | tf_op jit(solution)/shard_map/ppermute | solution.py:170
  13.3 15.7 %collective-permute-start.3 = (f32[10,32,128]{2,1,0:T(8,128)}, f32[10,32,128]{2,1,0:T(8,128)S(1)}, u32[]{:S(2)}, u32[]{:S(2)}) collective-permute-start(f32[10,32,128]{2,1,0:T(8,128)} %own_pot.1), channel_id=1, source_target_pairs={{1,0},{17,16},{33,32},{49,48},{65,64},{81,80},{97,96},{113,112},{1... | collective-permute-start | bytes 491528 | tf_op jit(solution)/shard_map/ppermute | solution.py:171
  27.8 1.2 copy-start.3
  29.0 0.7 copy-start.4
  29.0 0.8 copy-start.1
  29.7 0.7 copy-start.2
  37.3 1.0 copy-start
  72.8 5.2 %collective-permute-start.4 = (f32[8256]{0:T(1024)S(1)}, f32[8256]{0:T(1024)S(1)}, u32[]{:S(2)}, u32[]{:S(2)}) collective-permute-start(f32[8256]{0:T(1024)S(1)} %constant_dynamic-update-slice_fusion), channel_id=1, source_target_pairs={{0,16},{16,0},{32,48},{48,32},{64,80},{80,64},{96,112},{112,96},{1... | collective-permute-start | bytes 99080 | tf_op jit(solution)/shard_map/ppermute | solution.py:21
  78.1 7.3 %collective-permute-start.5 = (f32[8256]{0:T(1024)S(1)}, f32[8256]{0:T(1024)S(1)}, u32[]{:S(2)}, u32[]{:S(2)}) collective-permute-start(f32[8256]{0:T(1024)S(1)} %add.30), channel_id=1, source_target_pairs={{0,32},{16,48},{32,0},{48,16},{64,96},{80,112},{96,64},{112,80},{1... | collective-permute-start | bytes 99080 | tf_op jit(solution)/shard_map/ppermute | solution.py:21
  85.4 9.3 %collective-permute-start.6 = (f32[8256]{0:T(1024)S(1)}, f32[8256]{0:T(1024)S(1)}, u32[]{:S(2)}, u32[]{:S(2)}) collective-permute-start(f32[8256]{0:T(1024)S(1)} %add.31), channel_id=1, source_target_pairs={{0,64},{16,80},{32,96},{48,112},{64,0},{80,16},{96,32},{112,48},{1... | collective-permute-start | bytes 99080 | tf_op jit(solution)/shard_map/ppermute | solution.py:21
  94.7 4.7 %collective-permute-start.7 = (f32[8256]{0:T(1024)S(1)}, f32[8256]{0:T(1024)S(1)}, u32[]{:S(2)}, u32[]{:S(2)}) collective-permute-start(f32[8256]{0:T(1024)S(1)} %add.32), channel_id=1, source_target_pairs={{0,128},{16,144},{32,160},{48,176},{64,192},{80,208},{96,224},{112... | collective-permute-start | bytes 99080 | tf_op jit(solution)/shard_map/ppermute | solution.py:21
  99.4 5.9 %collective-permute-start.8 = (f32[8256]{0:T(1024)S(1)}, f32[8256]{0:T(1024)S(1)}, u32[]{:S(2)}, u32[]{:S(2)}) collective-permute-start(f32[8256]{0:T(1024)S(1)} %add.33), channel_id=1, source_target_pairs={{0,384},{16,400},{32,416},{48,432},{64,448},{80,464},{96,480},{112... | collective-permute-start | bytes 99080 | tf_op jit(solution)/shard_map/ppermute | solution.py:21
  105.3 13.4 %collective-permute-start.9 = (f32[8256]{0:T(1024)S(1)}, f32[8256]{0:T(1024)S(1)}, u32[]{:S(2)}, u32[]{:S(2)}) collective-permute-start(f32[8256]{0:T(1024)S(1)} %add.34), channel_id=1, source_target_pairs={{0,8},{1,9},{2,10},{3,11},{4,12},{5,13},{6,14},{7,15},{8,0},{9,1},... | collective-permute-start | bytes 99080 | tf_op jit(solution)/shard_map/ppermute | solution.py:21
  118.7 9.6 %collective-permute-start.10 = (f32[8256]{0:T(1024)S(1)}, f32[8256]{0:T(1024)S(1)}, u32[]{:S(2)}, u32[]{:S(2)}) collective-permute-start(f32[8256]{0:T(1024)S(1)} %add.35), channel_id=1, source_target_pairs={{0,2},{1,3},{2,0},{3,1},{4,6},{5,7},{6,4},{7,5},{8,10},{9,11},{10,... | collective-permute-start | bytes 99080 | tf_op jit(solution)/shard_map/ppermute | solution.py:21
  128.4 19.6 %collective-permute-start.11 = (f32[8256]{0:T(1024)S(1)}, f32[8256]{0:T(1024)S(1)}, u32[]{:S(2)}, u32[]{:S(2)}) collective-permute-start(f32[8256]{0:T(1024)S(1)} %add.36), channel_id=1, source_target_pairs={{0,6},{1,7},{2,4},{3,5},{4,2},{5,3},{6,0},{7,1},{8,14},{9,15},{10,... | collective-permute-start | bytes 99080 | tf_op jit(solution)/shard_map/ppermute | solution.py:21
  148.0 8.7 %collective-permute-start.12 = (f32[8256]{0:T(1024)S(1)}, f32[8256]{0:T(1024)S(1)}, u32[]{:S(2)}, u32[]{:S(2)}) collective-permute-start(f32[8256]{0:T(1024)S(1)} %add.37), channel_id=1, source_target_pairs={{0,1},{1,0},{2,3},{3,2},{4,5},{5,4},{6,7},{7,6},{8,9},{9,8},{10,11... | collective-permute-start | bytes 99080 | tf_op jit(solution)/shard_map/ppermute | solution.py:21
  167.3 0.7 copy-start.5

commit v13 on v10

--- a/solution.py
+++ b/solution.py
@@ -104,10 +104,9 @@
 
 
 def rayleigh_ritz_kernel(scale, first_ref, packed_ref, projected_ref, residual_ref, projected_buf, residual_buf):
-    size = packed_ref.shape[0]
-    work = packed_ref[:, 0:size] * scale
-    rest = packed_ref[:, size : 2 * size] * scale
-    norms = packed_ref[:, 2 * size : 2 * size + 1] * scale
+    size = packed_ref.shape[1]
+    work = packed_ref[0:size, :] * scale
+    rest = packed_ref[size : 2 * size, :] * scale
     rows = lax.broadcasted_iota(jnp.int32, (size, size), 0)
     cols = lax.broadcasted_iota(jnp.int32, (size, size), 1)
     row_index = rows[:, :1]
@@ -131,6 +130,7 @@
         rest = rest - columns[i] * row
         projected = jnp.where(rows == i, row, projected)
     projected_buf[...] = projected
+    norms = jnp.sum(jnp.where(rows == cols, packed_ref[2 * size : 2 * size + 1, :] * scale, 0.0), axis=1, keepdims=True)
     residual_buf[...] = norms - jnp.sum(coeff_t * coeff_t, axis=1, keepdims=True)
     first = first_ref[0]
     count = projected_ref.shape[0]
@@ -139,7 +139,7 @@
 
 
 def rayleigh_ritz(first_band, band_count, packed, scale):
-    size = packed.shape[0]
+    size = packed.shape[1]
     return pl.pallas_call(
         functools.partial(rayleigh_ritz_kernel, scale),
         out_shape=(jax.ShapeDtypeStruct((band_count, size), jnp.float32),
@@ -192,9 +192,9 @@
     )
     norm_part = jnp.sum(image_here * image_here, axis=1)
     margin_part = (margin_part + margin_part.T) / 2
-    packed = jnp.concatenate([margin_part, image_part, norm_part[:, None]], axis=1)
+    packed = jnp.concatenate([margin_part, image_part, norm_part[None, :]], axis=0)
+    packed = butterfly_sum(packed, "band", [flip(1), flip(2), flip(4), flip(8), ring_of_four(0, 8)])
     packed = butterfly_sum(packed, "grid", [flip(1), flip(2), ring_of_four(0, 2), flip(8)])
-    packed = butterfly_sum(packed, "band", [flip(1), flip(2), flip(4), flip(8), ring_of_four(0, 8)])
     projected_rows, residual_rows = rayleigh_ritz(first_band, band_count, packed, inverse_cells)
     residual_rows = residual_rows.reshape(-1)
     return (current, projected_rows, residual_rows)

time: 176 us -> 170 us (0.966)
  waiting for transfers between devices: 58.2 us -> 44.1 us
  starting transfers between devices: 59.6 us -> 68.8 us
  Pallas kernels: 16.8 us -> 14.2 us
    ppermute x9, waiting for transfers between devices: 47.6 us -> 33.5 us  [butterfly_sum(): values = values + lax.ppermute(values, axis, pairs)]
    ppermute x9, starting transfers between devices: 38.3 us -> 47.6 us  [butterfly_sum(): values = values + lax.ppermute(values, axis, pairs)]
    pallas_call x1, Pallas kernels: 11 us -> 8.47 us  [rayleigh_ritz(): pl.pallas_call(functools.partial(rayleigh_ritz_kernel, scale), out_shape=...]
where the time goes in v13:
time: 170 us; the launch traced here: 168 us
  starting transfers between devices  68.8 us (40%)
  waiting for transfers between devices  44.1 us (26%)
  blocking collectives  32.5 us (19%)
  Pallas kernels  14.2 us (8%)
  local copies, waits for them, and re-layouts  5.04 us (3%)
  other arithmetic  1.92 us (1%)
    ppermute x9, starting transfers between devices, butterfly_sum(): values = values + lax.ppermute(values, axis, pairs)  47.6 us
    ppermute x9, waiting for transfers between devices, butterfly_sum(): values = values + lax.ppermute(values, axis, pairs)  33.5 us
    all_to_all x1, blocking collectives, on_device(): moved = lax.all_to_all(both, 'band', 2, 1, tiled=True)  32.5 us
    ppermute x1, starting transfers between devices, on_device(): lax.ppermute(potential[potential.shape[0] - width:], ('band', 'grid'), re...  13.8 us
    ppermute x1, waiting for transfers between devices, on_device(): lax.ppermute(potential[:width], ('band', 'grid'), replica_pairs(-1))  10.6 us
    pallas_call x1, Pallas kernels, rayleigh_ritz(): pl.pallas_call(functools.partial(rayleigh_ritz_kernel, scale), out_shape=...  8.47 us
    pallas_call x1, Pallas kernels, filter_and_image(): pl.pallas_call(filter_kernel, out_shape=(jax.ShapeDtypeStruct(shape, jnp....  5.78 us
    ppermute x1, starting transfers between devices, on_device(): lax.ppermute(trial_bands[:, :width], 'grid', [((i + 1) % count, i) for i...  3.64 us
  transfers between devices with their start and end apart: 13, of which 10 were waited for; matrix products, arithmetic and copies ran while one was open for 0% of the time, Pallas kernels for 0%

profile of v13, /device:TPU:24, one launch (start us, length us, event | category | flops | bytes accessed | tf_op | source)
XLA Modules:
  0.0 168.3 jit_solution(13112924434388792420)
XLA Ops:
  0.6 1.9 %collective-permute-start = (f32[2,10,32,128]{3,2,1,0:T(8,128)}, f32[2,10,32,128]{3,2,1,0:T(8,128)S(1)}, u32[]{:S(2)}, u32[]{:S(2)}) collective-permute-start(f32[2,10,32,128]{3,2,1,0:T(8,128)} %own_ref.1), channel_id=1, source_target_pairs={{0,1},{1,2},{2,3},{3,4},{4,5},{5,6},{6,7},{7,8},{8,9},{9,10},{10,1... | collective-permute-start | bytes 983048 | tf_op jit(solution)/shard_map/ppermute | solution.py:170
  2.6 3.6 %collective-permute-start.1 = (f32[2,10,32,128]{3,2,1,0:T(8,128)}, f32[2,10,32,128]{3,2,1,0:T(8,128)S(1)}, u32[]{:S(2)}, u32[]{:S(2)}) collective-permute-start(f32[2,10,32,128]{3,2,1,0:T(8,128)} %own_ref.1), channel_id=1, source_target_pairs={{1,0},{2,1},{3,2},{4,3},{5,4},{6,5},{7,6},{8,7},{9,8},{10,9},{11,1... | collective-permute-start | bytes 983048 | tf_op jit(solution)/shard_map/ppermute | solution.py:171
  6.2 13.8 %collective-permute-start.2 = (f32[10,32,128]{2,1,0:T(8,128)}, f32[10,32,128]{2,1,0:T(8,128)S(1)}, u32[]{:S(2)}, u32[]{:S(2)}) collective-permute-start(f32[10,32,128]{2,1,0:T(8,128)} %own_pot.1), channel_id=1, source_target_pairs={{79,0},{95,16},{111,32},{127,48},{15,64},{31,80},{47,96},{63,112},... | collective-permute-start | bytes 491528 | tf_op jit(solution)/shard_map/ppermute | solution.py:172
  20.0 1.9 %collective-permute-start.3 = (f32[10,32,128]{2,1,0:T(8,128)}, f32[10,32,128]{2,1,0:T(8,128)S(1)}, u32[]{:S(2)}, u32[]{:S(2)}) collective-permute-start(f32[10,32,128]{2,1,0:T(8,128)} %own_pot.1), channel_id=1, source_target_pairs={{1,0},{17,16},{33,32},{49,48},{65,64},{81,80},{97,96},{113,112},{1... | collective-permute-start | bytes 491528 | tf_op jit(solution)/shard_map/ppermute | solution.py:173
  21.9 10.6 %collective-permute-done.3.above_pot = f32[10,32,128]{2,1,0:T(8,128)S(1)} collective-permute-done((f32[10,32,128]{2,1,0:T(8,128)}, f32[10,32,128]{2,1,0:T(8,128)S(1)}, u32[]{:S(2)}, u32[]{:S(2)}) %collective-permute-start.3) | collective-permute-done | bytes 163872 | tf_op jit(solution)/shard_map/ppermute | solution.py:173
  32.6 0.7 copy-done.4
  33.3 0.7 copy-done.2
  34.0 5.8 %shard_map.49 = (f32[2,10,32,128]{3,2,1,0:T(8,128)}, f32[2,10,32,128]{3,2,1,0:T(8,128)}) custom-call(f32[2,10,32,128]{3,2,1,0:T(8,128)} %copy-done.1, f32[2,10,32,128]{3,2,1,0:T(8,128)} %own_ref.1, f32[2,10,32,128]{3,2,1,0:T(8,128)} %copy-done.2, f32[10,32,128]{2,1,0:T(8,128)} %copy-done.3, f32[10,32,128]{2,1,0:T(8,128)} %own_pot.1, f32[10,32,128]{2,1,0:T(8,128)} %copy-done.4), custom_call_target="tpu_custom_call" | custom-call | flops 29491200 | bytes 2949120 | tf_op jit(solution)/shard_map/pallas_call | solution.py:95
  39.8 1.0 stack.7
  41.1 0.7 copy-done
  42.4 32.5 %all_to_all.15 = f32[2,2,32,1280]{3,1,0,2:T(2,128)S(1)} all-to-all(f32[2,2,32,1280]{3,1,0,2:T(2,128)S(1)} %pad_maximum_fusion), channel_id=1, replica_groups=mesh['band'=32,'grid'=16] {'band'}, dimensions={2} | all-to-all | bytes 1310720 | tf_op jit(solution)/shard_map/all_to_all | solution.py:184
  76.7 1.9 %collective-permute-start.4 = (f32[129,64]{1,0:T(8,128)S(1)}, f32[129,64]{1,0:T(8,128)S(1)}, u32[]{:S(2)}, u32[]{:S(2)}) collective-permute-start(f32[129,64]{1,0:T(8,128)S(1)} %pad_maximum_fusion.1), channel_id=1, source_target_pairs={{0,16},{16,0},{32,48},{48,32},{64,80},{80,64},{96,112},{112,96},{1... | collective-permute-start | bytes 99080 | tf_op jit(solution)/shard_map/ppermute | solution.py:23
  78.6 4.5 %collective-permute-done.4 = f32[129,64]{1,0:T(8,128)S(1)} collective-permute-done((f32[129,64]{1,0:T(8,128)S(1)}, f32[129,64]{1,0:T(8,128)S(1)}, u32[]{:S(2)}, u32[]{:S(2)}) %collective-permute-start.4) | collective-permute-done | bytes 33056 | tf_op jit(solution)/shard_map/ppermute | solution.py:23
  83.1 4.4 %collective-permute-start.5 = (f32[129,64]{1,0:T(8,128)S(1)}, f32[129,64]{1,0:T(8,128)S(1)}, u32[]{:S(2)}, u32[]{:S(2)}) collective-permute-start(f32[129,64]{1,0:T(8,128)S(1)} %fusion.1), channel_id=1, source_target_pairs={{0,32},{16,48},{32,0},{48,16},{64,96},{80,112},{96,64},{112,80},{1... | collective-permute-start | bytes 99080 | tf_op jit(solution)/shard_map/ppermute | solution.py:23
  87.5 2.9 %collective-permute-done.5 = f32[129,64]{1,0:T(8,128)S(1)} collective-permute-done((f32[129,64]{1,0:T(8,128)S(1)}, f32[129,64]{1,0:T(8,128)S(1)}, u32[]{:S(2)}, u32[]{:S(2)}) %collective-permute-start.5) | collective-permute-done | bytes 33056 | tf_op jit(solution)/shard_map/ppermute | solution.py:23
  90.4 6.3 %collective-permute-start.6 = (f32[129,64]{1,0:T(8,128)S(1)}, f32[129,64]{1,0:T(8,128)S(1)}, u32[]{:S(2)}, u32[]{:S(2)}) collective-permute-start(f32[129,64]{1,0:T(8,128)S(1)} %add.32), channel_id=1, source_target_pairs={{0,64},{16,80},{32,96},{48,112},{64,0},{80,16},{96,32},{112,48},{1... | collective-permute-start | bytes 99080 | tf_op jit(solution)/shard_map/ppermute | solution.py:23
  96.8 5.1 %collective-permute-done.6 = f32[129,64]{1,0:T(8,128)S(1)} collective-permute-done((f32[129,64]{1,0:T(8,128)S(1)}, f32[129,64]{1,0:T(8,128)S(1)}, u32[]{:S(2)}, u32[]{:S(2)}) %collective-permute-start.6) | collective-permute-done | bytes 33056 | tf_op jit(solution)/shard_map/ppermute | solution.py:23
  101.9 3.3 %collective-permute-start.7 = (f32[129,64]{1,0:T(8,128)S(1)}, f32[129,64]{1,0:T(8,128)S(1)}, u32[]{:S(2)}, u32[]{:S(2)}) collective-permute-start(f32[129,64]{1,0:T(8,128)S(1)} %add.33), channel_id=1, source_target_pairs={{0,128},{16,144},{32,160},{48,176},{64,192},{80,208},{96,224},{112... | collective-permute-start | bytes 99080 | tf_op jit(solution)/shard_map/ppermute | solution.py:23
  105.3 2.9 %collective-permute-done.7 = f32[129,64]{1,0:T(8,128)S(1)} collective-permute-done((f32[129,64]{1,0:T(8,128)S(1)}, f32[129,64]{1,0:T(8,128)S(1)}, u32[]{:S(2)}, u32[]{:S(2)}) %collective-permute-start.7) | collective-permute-done | bytes 33056 | tf_op jit(solution)/shard_map/ppermute | solution.py:23
  108.2 1.9 %collective-permute-start.8 = (f32[129,64]{1,0:T(8,128)S(1)}, f32[129,64]{1,0:T(8,128)S(1)}, u32[]{:S(2)}, u32[]{:S(2)}) collective-permute-start(f32[129,64]{1,0:T(8,128)S(1)} %add.34), channel_id=1, source_target_pairs={{0,384},{16,400},{32,416},{48,432},{64,448},{80,464},{96,480},{112... | collective-permute-start | bytes 99080 | tf_op jit(solution)/shard_map/ppermute | solution.py:23
  110.1 5.5 %collective-permute-done.8 = f32[129,64]{1,0:T(8,128)S(1)} collective-permute-done((f32[129,64]{1,0:T(8,128)S(1)}, f32[129,64]{1,0:T(8,128)S(1)}, u32[]{:S(2)}, u32[]{:S(2)}) %collective-permute-start.8) | collective-permute-done | bytes 33056 | tf_op jit(solution)/shard_map/ppermute | solution.py:23
  115.6 12.4 %collective-permute-start.9 = (f32[129,64]{1,0:T(8,128)S(1)}, f32[129,64]{1,0:T(8,128)S(1)}, u32[]{:S(2)}, u32[]{:S(2)}) collective-permute-start(f32[129,64]{1,0:T(8,128)S(1)} %add.35), channel_id=1, source_target_pairs={{0,1},{1,0},{2,3},{3,2},{4,5},{5,4},{6,7},{7,6},{8,9},{9,8},{10,11... | collective-permute-start | bytes 99080 | tf_op jit(solution)/shard_map/ppermute | solution.py:23
  128.0 0.9 collective-permute-done.9
  128.9 1.9 %collective-permute-start.10 = (f32[129,64]{1,0:T(8,128)S(1)}, f32[129,64]{1,0:T(8,128)S(1)}, u32[]{:S(2)}, u32[]{:S(2)}) collective-permute-start(f32[129,64]{1,0:T(8,128)S(1)} %add.36), channel_id=1, source_target_pairs={{0,2},{1,3},{2,0},{3,1},{4,6},{5,7},{6,4},{7,5},{8,10},{9,11},{10,... | collective-permute-start | bytes 99080 | tf_op jit(solution)/shard_map/ppermute | solution.py:23
  130.8 4.4 %collective-permute-done.10 = f32[129,64]{1,0:T(8,128)S(1)} collective-permute-done((f32[129,64]{1,0:T(8,128)S(1)}, f32[129,64]{1,0:T(8,128)S(1)}, u32[]{:S(2)}, u32[]{:S(2)}) %collective-permute-start.10) | collective-permute-done | bytes 33056 | tf_op jit(solution)/shard_map/ppermute | solution.py:23
  135.3 4.8 %collective-permute-start.11 = (f32[129,64]{1,0:T(8,128)S(1)}, f32[129,64]{1,0:T(8,128)S(1)}, u32[]{:S(2)}, u32[]{:S(2)}) collective-permute-start(f32[129,64]{1,0:T(8,128)S(1)} %add.37), channel_id=1, source_target_pairs={{0,6},{1,7},{2,4},{3,5},{4,2},{5,3},{6,0},{7,1},{8,14},{9,15},{10,... | collective-permute-start | bytes 99080 | tf_op jit(solution)/shard_map/ppermute | solution.py:23
  140.1 2.6 %collective-permute-done.11 = f32[129,64]{1,0:T(8,128)S(1)} collective-permute-done((f32[129,64]{1,0:T(8,128)S(1)}, f32[129,64]{1,0:T(8,128)S(1)}, u32[]{:S(2)}, u32[]{:S(2)}) %collective-permute-start.11) | collective-permute-done | bytes 33056 | tf_op jit(solution)/shard_map/ppermute | solution.py:23
  142.7 10.5 %collective-permute-start.12 = (f32[129,64]{1,0:T(8,128)S(1)}, f32[129,64]{1,0:T(8,128)S(1)}, u32[]{:S(2)}, u32[]{:S(2)}) collective-permute-start(f32[129,64]{1,0:T(8,128)S(1)} %add.38), channel_id=1, source_target_pairs={{0,8},{1,9},{2,10},{3,11},{4,12},{5,13},{6,14},{7,15},{8,0},{9,1},... | collective-permute-start | bytes 99080 | tf_op jit(solution)/shard_map/ppermute | solution.py:23
  153.2 4.7 %collective-permute-done.12 = f32[129,64]{1,0:T(8,128)S(1)} collective-permute-done((f32[129,64]{1,0:T(8,128)S(1)}, f32[129,64]{1,0:T(8,128)S(1)}, u32[]{:S(2)}, u32[]{:S(2)}) %collective-permute-start.12) | collective-permute-done | bytes 33056 | tf_op jit(solution)/shard_map/ppermute | solution.py:23
  157.9 0.6 add.39.packed_ref
  158.6 8.5 %shard_map.50 = (f32[2,64]{1,0:T(2,128)}, f32[2,1]{1,0:T(2,128)}) custom-call(s32[1]{0:T(128)} %bitcast.first_ref, f32[129,64]{1,0:T(8,128)} %add.39.packed_ref), custom_call_target="tpu_custom_call" | custom-call | flops 1572864 | bytes 65536 | tf_op jit(solution)/shard_map/pallas_call | solution.py:143
  167.1 0.6 copy-done.5
  (33 shorter events, 3.4 us)
Async XLA Ops:
  0.6 31.9 %collective-permute-start = (f32[2,10,32,128]{3,2,1,0:T(8,128)}, f32[2,10,32,128]{3,2,1,0:T(8,128)S(1)}, u32[]{:S(2)}, u32[]{:S(2)}) collective-permute-start(f32[2,10,32,128]{3,2,1,0:T(8,128)} %own_ref.1), channel_id=1, source_target_pairs={{0,1},{1,2},{2,3},{3,4},{4,5},{5,6},{6,7},{7,8},{8,9},{9,10},{10,1... | collective-permute-start | bytes 983048 | tf_op jit(solution)/shard_map/ppermute | solution.py:170
  2.6 30.0 %collective-permute-start.1 = (f32[2,10,32,128]{3,2,1,0:T(8,128)}, f32[2,10,32,128]{3,2,1,0:T(8,128)S(1)}, u32[]{:S(2)}, u32[]{:S(2)}) collective-permute-start(f32[2,10,32,128]{3,2,1,0:T(8,128)} %own_ref.1), channel_id=1, source_target_pairs={{1,0},{2,1},{3,2},{4,3},{5,4},{6,5},{7,6},{8,7},{9,8},{10,9},{11,1... | collective-permute-start | bytes 983048 | tf_op jit(solution)/shard_map/ppermute | solution.py:171
  6.2 15.7 %collective-permute-start.2 = (f32[10,32,128]{2,1,0:T(8,128)}, f32[10,32,128]{2,1,0:T(8,128)S(1)}, u32[]{:S(2)}, u32[]{:S(2)}) collective-permute-start(f32[10,32,128]{2,1,0:T(8,128)} %own_pot.1), channel_id=1, source_target_pairs={{79,0},{95,16},{111,32},{127,48},{15,64},{31,80},{47,96},{63,112},... | collective-permute-start | bytes 491528 | tf_op jit(solution)/shard_map/ppermute | solution.py:172
  20.0 12.6 %collective-permute-start.3 = (f32[10,32,128]{2,1,0:T(8,128)}, f32[10,32,128]{2,1,0:T(8,128)S(1)}, u32[]{:S(2)}, u32[]{:S(2)}) collective-permute-start(f32[10,32,128]{2,1,0:T(8,128)} %own_pot.1), channel_id=1, source_target_pairs={{1,0},{17,16},{33,32},{49,48},{65,64},{81,80},{97,96},{113,112},{1... | collective-permute-start | bytes 491528 | tf_op jit(solution)/shard_map/ppermute | solution.py:173
  21.9 10.6 %copy-start.3 = (f32[10,32,128]{2,1,0:T(8,128)}, f32[10,32,128]{2,1,0:T(8,128)S(1)}, u32[]{:S(2)}) copy-start(f32[10,32,128]{2,1,0:T(8,128)S(1)} %collective-permute-done.2.below_pot) | copy-start | bytes 491524
  32.5 0.7 copy-start.4
  32.6 0.8 copy-start.1
  33.3 0.7 copy-start.2
  40.9 1.0 copy-start
  76.7 6.4 %collective-permute-start.4 = (f32[129,64]{1,0:T(8,128)S(1)}, f32[129,64]{1,0:T(8,128)S(1)}, u32[]{:S(2)}, u32[]{:S(2)}) collective-permute-start(f32[129,64]{1,0:T(8,128)S(1)} %pad_maximum_fusion.1), channel_id=1, source_target_pairs={{0,16},{16,0},{32,48},{48,32},{64,80},{80,64},{96,112},{112,96},{1... | collective-permute-start | bytes 99080 | tf_op jit(solution)/shard_map/ppermute | solution.py:23
  83.1 7.3 %collective-permute-start.5 = (f32[129,64]{1,0:T(8,128)S(1)}, f32[129,64]{1,0:T(8,128)S(1)}, u32[]{:S(2)}, u32[]{:S(2)}) collective-permute-start(f32[129,64]{1,0:T(8,128)S(1)} %fusion.1), channel_id=1, source_target_pairs={{0,32},{16,48},{32,0},{48,16},{64,96},{80,112},{96,64},{112,80},{1... | collective-permute-start | bytes 99080 | tf_op jit(solution)/shard_map/ppermute | solution.py:23
  90.4 11.5 %collective-permute-start.6 = (f32[129,64]{1,0:T(8,128)S(1)}, f32[129,64]{1,0:T(8,128)S(1)}, u32[]{:S(2)}, u32[]{:S(2)}) collective-permute-start(f32[129,64]{1,0:T(8,128)S(1)} %add.32), channel_id=1, source_target_pairs={{0,64},{16,80},{32,96},{48,112},{64,0},{80,16},{96,32},{112,48},{1... | collective-permute-start | bytes 99080 | tf_op jit(solution)/shard_map/ppermute | solution.py:23
  101.9 6.2 %collective-permute-start.7 = (f32[129,64]{1,0:T(8,128)S(1)}, f32[129,64]{1,0:T(8,128)S(1)}, u32[]{:S(2)}, u32[]{:S(2)}) collective-permute-start(f32[129,64]{1,0:T(8,128)S(1)} %add.33), channel_id=1, source_target_pairs={{0,128},{16,144},{32,160},{48,176},{64,192},{80,208},{96,224},{112... | collective-permute-start | bytes 99080 | tf_op jit(solution)/shard_map/ppermute | solution.py:23
  108.2 7.4 %collective-permute-start.8 = (f32[129,64]{1,0:T(8,128)S(1)}, f32[129,64]{1,0:T(8,128)S(1)}, u32[]{:S(2)}, u32[]{:S(2)}) collective-permute-start(f32[129,64]{1,0:T(8,128)S(1)} %add.34), channel_id=1, source_target_pairs={{0,384},{16,400},{32,416},{48,432},{64,448},{80,464},{96,480},{112... | collective-permute-start | bytes 99080 | tf_op jit(solution)/shard_map/ppermute | solution.py:23
  115.6 13.3 %collective-permute-start.9 = (f32[129,64]{1,0:T(8,128)S(1)}, f32[129,64]{1,0:T(8,128)S(1)}, u32[]{:S(2)}, u32[]{:S(2)}) collective-permute-start(f32[129,64]{1,0:T(8,128)S(1)} %add.35), channel_id=1, source_target_pairs={{0,1},{1,0},{2,3},{3,2},{4,5},{5,4},{6,7},{7,6},{8,9},{9,8},{10,11... | collective-permute-start | bytes 99080 | tf_op jit(solution)/shard_map/ppermute | solution.py:23
  128.9 6.3 %collective-permute-start.10 = (f32[129,64]{1,0:T(8,128)S(1)}, f32[129,64]{1,0:T(8,128)S(1)}, u32[]{:S(2)}, u32[]{:S(2)}) collective-permute-start(f32[129,64]{1,0:T(8,128)S(1)} %add.36), channel_id=1, source_target_pairs={{0,2},{1,3},{2,0},{3,1},{4,6},{5,7},{6,4},{7,5},{8,10},{9,11},{10,... | collective-permute-start | bytes 99080 | tf_op jit(solution)/shard_map/ppermute | solution.py:23
  135.3 7.4 %collective-permute-start.11 = (f32[129,64]{1,0:T(8,128)S(1)}, f32[129,64]{1,0:T(8,128)S(1)}, u32[]{:S(2)}, u32[]{:S(2)}) collective-permute-start(f32[129,64]{1,0:T(8,128)S(1)} %add.37), channel_id=1, source_target_pairs={{0,6},{1,7},{2,4},{3,5},{4,2},{5,3},{6,0},{7,1},{8,14},{9,15},{10,... | collective-permute-start | bytes 99080 | tf_op jit(solution)/shard_map/ppermute | solution.py:23
  142.7 15.3 %collective-permute-start.12 = (f32[129,64]{1,0:T(8,128)S(1)}, f32[129,64]{1,0:T(8,128)S(1)}, u32[]{:S(2)}, u32[]{:S(2)}) collective-permute-start(f32[129,64]{1,0:T(8,128)S(1)} %add.38), channel_id=1, source_target_pairs={{0,8},{1,9},{2,10},{3,11},{4,12},{5,13},{6,14},{7,15},{8,0},{9,1},... | collective-permute-start | bytes 99080 | tf_op jit(solution)/shard_map/ppermute | solution.py:23
  167.1 0.6 copy-start.5

commit v14 on v11

--- a/solution.py
+++ b/solution.py
@@ -190,7 +190,7 @@
     )
     norm_part = jnp.sum(image_here * image_here, axis=1)
     packed = jnp.concatenate([margin_part.reshape(-1), image_part.reshape(-1), norm_part])
-    packed = butterfly_sum(packed, "band", [flip(1), flip(2), flip(4), flip(8), ring_of_four(0, 8)])
+    packed = butterfly_sum(packed, "band", [flip(8), ring_of_four(0, 8), flip(1), flip(2), flip(4)])
     packed = butterfly_sum(packed, "grid", [flip(1), flip(2), ring_of_four(0, 2), flip(8)])
     packed = packed * inverse_cells
     square = total_bands * total_bands

time: 166 us -> 166 us (level)
  starting transfers between devices: 65.9 us -> 60.1 us
  waiting for transfers between devices: 42.1 us -> 47.3 us
    ppermute x9, starting transfers between devices: 44.7 us -> 38.9 us  [butterfly_sum(): values = values + lax.ppermute(values, axis, pairs)]
    ppermute x9, waiting for transfers between devices: 31.5 us -> 36.7 us  [butterfly_sum(): values = values + lax.ppermute(values, axis, pairs)]
where the time goes in v14:
time: 166 us; the launch traced here: 164 us
  starting transfers between devices  60.1 us (36%)
  waiting for transfers between devices  47.3 us (28%)
  blocking collectives  32.5 us (20%)
  Pallas kernels  14.2 us (9%)
  local copies, waits for them, and re-layouts  6.69 us (4%)
  other arithmetic  1.85 us (1%)
    ppermute x9, starting transfers between devices, butterfly_sum(): values = values + lax.ppermute(values, axis, pairs)  38.9 us
    ppermute x9, waiting for transfers between devices, butterfly_sum(): values = values + lax.ppermute(values, axis, pairs)  36.7 us
    all_to_all x1, blocking collectives, on_device(): moved = lax.all_to_all(both, 'band', 2, 1, tiled=True)  32.5 us
    ppermute x1, starting transfers between devices, on_device(): lax.ppermute(potential[potential.shape[0] - width:], ('band', 'grid'), re...  13.8 us
    ppermute x1, waiting for transfers between devices, on_device(): lax.ppermute(potential[:width], ('band', 'grid'), replica_pairs(-1))  10.6 us
    pallas_call x1, Pallas kernels, rayleigh_ritz(): pl.pallas_call(rayleigh_ritz_kernel, out_shape=(jax.ShapeDtypeStruct((ban...  8.4 us
    pallas_call x1, Pallas kernels, filter_and_image(): pl.pallas_call(filter_kernel, out_shape=(jax.ShapeDtypeStruct(shape, jnp....  5.77 us
    ppermute x1, starting transfers between devices, on_device(): lax.ppermute(trial_bands[:, :width], 'grid', [((i + 1) % count, i) for i...  3.64 us
  transfers between devices with their start and end apart: 13, of which 10 were waited for; matrix products, arithmetic and copies ran while one was open for 0% of the time, Pallas kernels for 0%

profile of v14, /device:TPU:24, one launch (start us, length us, event | category | flops | bytes accessed | tf_op | source)
XLA Modules:
  0.0 164.4 jit_solution(9447187018296327505)
XLA Ops:
  0.6 1.9 %collective-permute-start = (f32[2,10,32,128]{3,2,1,0:T(8,128)}, f32[2,10,32,128]{3,2,1,0:T(8,128)S(1)}, u32[]{:S(2)}, u32[]{:S(2)}) collective-permute-start(f32[2,10,32,128]{3,2,1,0:T(8,128)} %own_ref.1), channel_id=1, source_target_pairs={{0,1},{1,2},{2,3},{3,4},{4,5},{5,6},{6,7},{7,8},{8,9},{9,10},{10,1... | collective-permute-start | bytes 983048 | tf_op jit(solution)/shard_map/ppermute | solution.py:168
  2.6 3.6 %collective-permute-start.1 = (f32[2,10,32,128]{3,2,1,0:T(8,128)}, f32[2,10,32,128]{3,2,1,0:T(8,128)S(1)}, u32[]{:S(2)}, u32[]{:S(2)}) collective-permute-start(f32[2,10,32,128]{3,2,1,0:T(8,128)} %own_ref.1), channel_id=1, source_target_pairs={{1,0},{2,1},{3,2},{4,3},{5,4},{6,5},{7,6},{8,7},{9,8},{10,9},{11,1... | collective-permute-start | bytes 983048 | tf_op jit(solution)/shard_map/ppermute | solution.py:169
  6.2 13.8 %collective-permute-start.2 = (f32[10,32,128]{2,1,0:T(8,128)}, f32[10,32,128]{2,1,0:T(8,128)S(1)}, u32[]{:S(2)}, u32[]{:S(2)}) collective-permute-start(f32[10,32,128]{2,1,0:T(8,128)} %own_pot.1), channel_id=1, source_target_pairs={{79,0},{95,16},{111,32},{127,48},{15,64},{31,80},{47,96},{63,112},... | collective-permute-start | bytes 491528 | tf_op jit(solution)/shard_map/ppermute | solution.py:170
  20.0 1.9 %collective-permute-start.3 = (f32[10,32,128]{2,1,0:T(8,128)}, f32[10,32,128]{2,1,0:T(8,128)S(1)}, u32[]{:S(2)}, u32[]{:S(2)}) collective-permute-start(f32[10,32,128]{2,1,0:T(8,128)} %own_pot.1), channel_id=1, source_target_pairs={{1,0},{17,16},{33,32},{49,48},{65,64},{81,80},{97,96},{113,112},{1... | collective-permute-start | bytes 491528 | tf_op jit(solution)/shard_map/ppermute | solution.py:171
  21.9 10.6 %collective-permute-done.3.above_pot = f32[10,32,128]{2,1,0:T(8,128)S(1)} collective-permute-done((f32[10,32,128]{2,1,0:T(8,128)}, f32[10,32,128]{2,1,0:T(8,128)S(1)}, u32[]{:S(2)}, u32[]{:S(2)}) %collective-permute-start.3) | collective-permute-done | bytes 163872 | tf_op jit(solution)/shard_map/ppermute | solution.py:171
  33.3 0.7 copy-done.2
  34.0 5.8 %shard_map.49 = (f32[2,10,32,128]{3,2,1,0:T(8,128)}, f32[2,10,32,128]{3,2,1,0:T(8,128)}) custom-call(f32[2,10,32,128]{3,2,1,0:T(8,128)} %copy-done.1, f32[2,10,32,128]{3,2,1,0:T(8,128)} %own_ref.1, f32[2,10,32,128]{3,2,1,0:T(8,128)} %copy-done.2, f32[10,32,128]{2,1,0:T(8,128)} %copy-done.3, f32[10,32,128]{2,1,0:T(8,128)} %own_pot.1, f32[10,32,128]{2,1,0:T(8,128)} %copy-done.4), custom_call_target="tpu_custom_call" | custom-call | flops 29491200 | bytes 2949120 | tf_op jit(solution)/shard_map/pallas_call | solution.py:93
  39.8 1.0 stack.7
  41.1 0.7 copy-done
  42.4 32.5 %all_to_all.15 = f32[2,2,32,1280]{3,1,0,2:T(2,128)S(1)} all-to-all(f32[2,2,32,1280]{3,1,0,2:T(2,128)S(1)} %pad_maximum_fusion), channel_id=1, replica_groups=mesh['band'=32,'grid'=16] {'band'}, dimensions={2} | all-to-all | bytes 1310720 | tf_op jit(solution)/shard_map/all_to_all | solution.py:182
  76.8 1.9 %collective-permute-start.4 = (f32[8256]{0:T(1024)S(1)}, f32[8256]{0:T(1024)S(1)}, u32[]{:S(2)}, u32[]{:S(2)}) collective-permute-start(f32[8256]{0:T(1024)S(1)} %constant_dynamic-update-slice_fusion), channel_id=1, source_target_pairs={{0,128},{16,144},{32,160},{48,176},{64,192},{80,208},{96,224},{112... | collective-permute-start | bytes 99080 | tf_op jit(solution)/shard_map/ppermute | solution.py:21
  78.7 4.1 %collective-permute-done.4 = f32[8256]{0:T(1024)S(1)} collective-permute-done((f32[8256]{0:T(1024)S(1)}, f32[8256]{0:T(1024)S(1)}, u32[]{:S(2)}, u32[]{:S(2)}) %collective-permute-start.4) | collective-permute-done | bytes 33056 | tf_op jit(solution)/shard_map/ppermute | solution.py:21
  82.8 2.5 %collective-permute-start.5 = (f32[8256]{0:T(1024)S(1)}, f32[8256]{0:T(1024)S(1)}, u32[]{:S(2)}, u32[]{:S(2)}) collective-permute-start(f32[8256]{0:T(1024)S(1)} %add.30), channel_id=1, source_target_pairs={{0,384},{16,400},{32,416},{48,432},{64,448},{80,464},{96,480},{112... | collective-permute-start | bytes 99080 | tf_op jit(solution)/shard_map/ppermute | solution.py:21
  85.3 4.6 %collective-permute-done.5 = f32[8256]{0:T(1024)S(1)} collective-permute-done((f32[8256]{0:T(1024)S(1)}, f32[8256]{0:T(1024)S(1)}, u32[]{:S(2)}, u32[]{:S(2)}) %collective-permute-start.5) | collective-permute-done | bytes 33056 | tf_op jit(solution)/shard_map/ppermute | solution.py:21
  89.9 1.9 %collective-permute-start.6 = (f32[8256]{0:T(1024)S(1)}, f32[8256]{0:T(1024)S(1)}, u32[]{:S(2)}, u32[]{:S(2)}) collective-permute-start(f32[8256]{0:T(1024)S(1)} %add.31), channel_id=1, source_target_pairs={{0,16},{16,0},{32,48},{48,32},{64,80},{80,64},{96,112},{112,96},{1... | collective-permute-start | bytes 99080 | tf_op jit(solution)/shard_map/ppermute | solution.py:21
  91.8 3.9 %collective-permute-done.6 = f32[8256]{0:T(1024)S(1)} collective-permute-done((f32[8256]{0:T(1024)S(1)}, f32[8256]{0:T(1024)S(1)}, u32[]{:S(2)}, u32[]{:S(2)}) %collective-permute-start.6) | collective-permute-done | bytes 33056 | tf_op jit(solution)/shard_map/ppermute | solution.py:21
  95.7 2.3 %collective-permute-start.7 = (f32[8256]{0:T(1024)S(1)}, f32[8256]{0:T(1024)S(1)}, u32[]{:S(2)}, u32[]{:S(2)}) collective-permute-start(f32[8256]{0:T(1024)S(1)} %add.32), channel_id=1, source_target_pairs={{0,32},{16,48},{32,0},{48,16},{64,96},{80,112},{96,64},{112,80},{1... | collective-permute-start | bytes 99080 | tf_op jit(solution)/shard_map/ppermute | solution.py:21
  98.0 4.5 %collective-permute-done.7 = f32[8256]{0:T(1024)S(1)} collective-permute-done((f32[8256]{0:T(1024)S(1)}, f32[8256]{0:T(1024)S(1)}, u32[]{:S(2)}, u32[]{:S(2)}) %collective-permute-start.7) | collective-permute-done | bytes 33056 | tf_op jit(solution)/shard_map/ppermute | solution.py:21
  102.5 1.9 %collective-permute-start.8 = (f32[8256]{0:T(1024)S(1)}, f32[8256]{0:T(1024)S(1)}, u32[]{:S(2)}, u32[]{:S(2)}) collective-permute-start(f32[8256]{0:T(1024)S(1)} %add.33), channel_id=1, source_target_pairs={{0,64},{16,80},{32,96},{48,112},{64,0},{80,16},{96,32},{112,48},{1... | collective-permute-start | bytes 99080 | tf_op jit(solution)/shard_map/ppermute | solution.py:21
  104.4 8.2 %collective-permute-done.8 = f32[8256]{0:T(1024)S(1)} collective-permute-done((f32[8256]{0:T(1024)S(1)}, f32[8256]{0:T(1024)S(1)}, u32[]{:S(2)}, u32[]{:S(2)}) %collective-permute-start.8) | collective-permute-done | bytes 33056 | tf_op jit(solution)/shard_map/ppermute | solution.py:21
  112.6 11.6 %collective-permute-start.9 = (f32[8256]{0:T(1024)S(1)}, f32[8256]{0:T(1024)S(1)}, u32[]{:S(2)}, u32[]{:S(2)}) collective-permute-start(f32[8256]{0:T(1024)S(1)} %add.34), channel_id=1, source_target_pairs={{0,1},{1,0},{2,3},{3,2},{4,5},{5,4},{6,7},{7,6},{8,9},{9,8},{10,11... | collective-permute-start | bytes 99080 | tf_op jit(solution)/shard_map/ppermute | solution.py:21
  124.2 0.8 collective-permute-done.9
  125.0 1.9 %collective-permute-start.10 = (f32[8256]{0:T(1024)S(1)}, f32[8256]{0:T(1024)S(1)}, u32[]{:S(2)}, u32[]{:S(2)}) collective-permute-start(f32[8256]{0:T(1024)S(1)} %add.35), channel_id=1, source_target_pairs={{0,2},{1,3},{2,0},{3,1},{4,6},{5,7},{6,4},{7,5},{8,10},{9,11},{10,... | collective-permute-start | bytes 99080 | tf_op jit(solution)/shard_map/ppermute | solution.py:21
  126.9 3.9 %collective-permute-done.10 = f32[8256]{0:T(1024)S(1)} collective-permute-done((f32[8256]{0:T(1024)S(1)}, f32[8256]{0:T(1024)S(1)}, u32[]{:S(2)}, u32[]{:S(2)}) %collective-permute-start.10) | collective-permute-done | bytes 33056 | tf_op jit(solution)/shard_map/ppermute | solution.py:21
  130.9 4.6 %collective-permute-start.11 = (f32[8256]{0:T(1024)S(1)}, f32[8256]{0:T(1024)S(1)}, u32[]{:S(2)}, u32[]{:S(2)}) collective-permute-start(f32[8256]{0:T(1024)S(1)} %add.36), channel_id=1, source_target_pairs={{0,6},{1,7},{2,4},{3,5},{4,2},{5,3},{6,0},{7,1},{8,14},{9,15},{10,... | collective-permute-start | bytes 99080 | tf_op jit(solution)/shard_map/ppermute | solution.py:21
  135.5 2.5 %collective-permute-done.11 = f32[8256]{0:T(1024)S(1)} collective-permute-done((f32[8256]{0:T(1024)S(1)}, f32[8256]{0:T(1024)S(1)}, u32[]{:S(2)}, u32[]{:S(2)}) %collective-permute-start.11) | collective-permute-done | bytes 33056 | tf_op jit(solution)/shard_map/ppermute | solution.py:21
  137.9 10.3 %collective-permute-start.12 = (f32[8256]{0:T(1024)S(1)}, f32[8256]{0:T(1024)S(1)}, u32[]{:S(2)}, u32[]{:S(2)}) collective-permute-start(f32[8256]{0:T(1024)S(1)} %add.37), channel_id=1, source_target_pairs={{0,8},{1,9},{2,10},{3,11},{4,12},{5,13},{6,14},{7,15},{8,0},{9,1},... | collective-permute-start | bytes 99080 | tf_op jit(solution)/shard_map/ppermute | solution.py:21
  148.3 4.2 %collective-permute-done.12 = f32[8256]{0:T(1024)S(1)} collective-permute-done((f32[8256]{0:T(1024)S(1)}, f32[8256]{0:T(1024)S(1)}, u32[]{:S(2)}, u32[]{:S(2)}) %collective-permute-start.12) | collective-permute-done | bytes 33056 | tf_op jit(solution)/shard_map/ppermute | solution.py:21
  153.3 0.7 slice.42.subspace_ref
  154.0 0.7 copy.14.norms_ref
  154.7 8.4 %shard_map.50 = (f32[2,64]{1,0:T(2,128)}, f32[2,1]{1,0:T(2,128)}) custom-call(s32[1]{0:T(128)} %bitcast.first_ref, f32[64,64]{1,0:T(8,128)} %fusion.margin_ref, f32[64,64]{1,0:T(8,128)} %slice.42.subspace_ref, f32[64,1]{1,0:T(8,128)} %copy.14.norms_ref), custom_call_target="tpu_custom_call" | custom-call | flops 1572864 | bytes 65536 | tf_op jit(solution)/shard_map/pallas_call | solution.py:141
  163.1 0.7 copy-done.5
  (42 shorter events, 4.9 us)
Async XLA Ops:
  0.6 31.9 %collective-permute-start = (f32[2,10,32,128]{3,2,1,0:T(8,128)}, f32[2,10,32,128]{3,2,1,0:T(8,128)S(1)}, u32[]{:S(2)}, u32[]{:S(2)}) collective-permute-start(f32[2,10,32,128]{3,2,1,0:T(8,128)} %own_ref.1), channel_id=1, source_target_pairs={{0,1},{1,2},{2,3},{3,4},{4,5},{5,6},{6,7},{7,8},{8,9},{9,10},{10,1... | collective-permute-start | bytes 983048 | tf_op jit(solution)/shard_map/ppermute | solution.py:168
  2.6 30.0 %collective-permute-start.1 = (f32[2,10,32,128]{3,2,1,0:T(8,128)}, f32[2,10,32,128]{3,2,1,0:T(8,128)S(1)}, u32[]{:S(2)}, u32[]{:S(2)}) collective-permute-start(f32[2,10,32,128]{3,2,1,0:T(8,128)} %own_ref.1), channel_id=1, source_target_pairs={{1,0},{2,1},{3,2},{4,3},{5,4},{6,5},{7,6},{8,7},{9,8},{10,9},{11,1... | collective-permute-start | bytes 983048 | tf_op jit(solution)/shard_map/ppermute | solution.py:169
  6.2 15.7 %collective-permute-start.2 = (f32[10,32,128]{2,1,0:T(8,128)}, f32[10,32,128]{2,1,0:T(8,128)S(1)}, u32[]{:S(2)}, u32[]{:S(2)}) collective-permute-start(f32[10,32,128]{2,1,0:T(8,128)} %own_pot.1), channel_id=1, source_target_pairs={{79,0},{95,16},{111,32},{127,48},{15,64},{31,80},{47,96},{63,112},... | collective-permute-start | bytes 491528 | tf_op jit(solution)/shard_map/ppermute | solution.py:170
  20.0 12.6 %collective-permute-start.3 = (f32[10,32,128]{2,1,0:T(8,128)}, f32[10,32,128]{2,1,0:T(8,128)S(1)}, u32[]{:S(2)}, u32[]{:S(2)}) collective-permute-start(f32[10,32,128]{2,1,0:T(8,128)} %own_pot.1), channel_id=1, source_target_pairs={{1,0},{17,16},{33,32},{49,48},{65,64},{81,80},{97,96},{113,112},{1... | collective-permute-start | bytes 491528 | tf_op jit(solution)/shard_map/ppermute | solution.py:171
  21.9 10.6 %copy-start.3 = (f32[10,32,128]{2,1,0:T(8,128)}, f32[10,32,128]{2,1,0:T(8,128)S(1)}, u32[]{:S(2)}) copy-start(f32[10,32,128]{2,1,0:T(8,128)S(1)} %collective-permute-done.2.below_pot) | copy-start | bytes 491524
  32.5 0.7 copy-start.4
  32.6 0.8 copy-start.1
  33.3 0.7 copy-start.2
  40.8 1.0 copy-start
  76.8 6.1 %collective-permute-start.4 = (f32[8256]{0:T(1024)S(1)}, f32[8256]{0:T(1024)S(1)}, u32[]{:S(2)}, u32[]{:S(2)}) collective-permute-start(f32[8256]{0:T(1024)S(1)} %constant_dynamic-update-slice_fusion), channel_id=1, source_target_pairs={{0,128},{16,144},{32,160},{48,176},{64,192},{80,208},{96,224},{112... | collective-permute-start | bytes 99080 | tf_op jit(solution)/shard_map/ppermute | solution.py:21
  82.8 7.1 %collective-permute-start.5 = (f32[8256]{0:T(1024)S(1)}, f32[8256]{0:T(1024)S(1)}, u32[]{:S(2)}, u32[]{:S(2)}) collective-permute-start(f32[8256]{0:T(1024)S(1)} %add.30), channel_id=1, source_target_pairs={{0,384},{16,400},{32,416},{48,432},{64,448},{80,464},{96,480},{112... | collective-permute-start | bytes 99080 | tf_op jit(solution)/shard_map/ppermute | solution.py:21
  89.9 5.8 %collective-permute-start.6 = (f32[8256]{0:T(1024)S(1)}, f32[8256]{0:T(1024)S(1)}, u32[]{:S(2)}, u32[]{:S(2)}) collective-permute-start(f32[8256]{0:T(1024)S(1)} %add.31), channel_id=1, source_target_pairs={{0,16},{16,0},{32,48},{48,32},{64,80},{80,64},{96,112},{112,96},{1... | collective-permute-start | bytes 99080 | tf_op jit(solution)/shard_map/ppermute | solution.py:21
  95.7 6.7 %collective-permute-start.7 = (f32[8256]{0:T(1024)S(1)}, f32[8256]{0:T(1024)S(1)}, u32[]{:S(2)}, u32[]{:S(2)}) collective-permute-start(f32[8256]{0:T(1024)S(1)} %add.32), channel_id=1, source_target_pairs={{0,32},{16,48},{32,0},{48,16},{64,96},{80,112},{96,64},{112,80},{1... | collective-permute-start | bytes 99080 | tf_op jit(solution)/shard_map/ppermute | solution.py:21
  102.5 10.1 %collective-permute-start.8 = (f32[8256]{0:T(1024)S(1)}, f32[8256]{0:T(1024)S(1)}, u32[]{:S(2)}, u32[]{:S(2)}) collective-permute-start(f32[8256]{0:T(1024)S(1)} %add.33), channel_id=1, source_target_pairs={{0,64},{16,80},{32,96},{48,112},{64,0},{80,16},{96,32},{112,48},{1... | collective-permute-start | bytes 99080 | tf_op jit(solution)/shard_map/ppermute | solution.py:21
  112.6 12.4 %collective-permute-start.9 = (f32[8256]{0:T(1024)S(1)}, f32[8256]{0:T(1024)S(1)}, u32[]{:S(2)}, u32[]{:S(2)}) collective-permute-start(f32[8256]{0:T(1024)S(1)} %add.34), channel_id=1, source_target_pairs={{0,1},{1,0},{2,3},{3,2},{4,5},{5,4},{6,7},{7,6},{8,9},{9,8},{10,11... | collective-permute-start | bytes 99080 | tf_op jit(solution)/shard_map/ppermute | solution.py:21
  125.0 5.8 %collective-permute-start.10 = (f32[8256]{0:T(1024)S(1)}, f32[8256]{0:T(1024)S(1)}, u32[]{:S(2)}, u32[]{:S(2)}) collective-permute-start(f32[8256]{0:T(1024)S(1)} %add.35), channel_id=1, source_target_pairs={{0,2},{1,3},{2,0},{3,1},{4,6},{5,7},{6,4},{7,5},{8,10},{9,11},{10,... | collective-permute-start | bytes 99080 | tf_op jit(solution)/shard_map/ppermute | solution.py:21
  130.9 7.1 %collective-permute-start.11 = (f32[8256]{0:T(1024)S(1)}, f32[8256]{0:T(1024)S(1)}, u32[]{:S(2)}, u32[]{:S(2)}) collective-permute-start(f32[8256]{0:T(1024)S(1)} %add.36), channel_id=1, source_target_pairs={{0,6},{1,7},{2,4},{3,5},{4,2},{5,3},{6,0},{7,1},{8,14},{9,15},{10,... | collective-permute-start | bytes 99080 | tf_op jit(solution)/shard_map/ppermute | solution.py:21
  137.9 14.6 %collective-permute-start.12 = (f32[8256]{0:T(1024)S(1)}, f32[8256]{0:T(1024)S(1)}, u32[]{:S(2)}, u32[]{:S(2)}) collective-permute-start(f32[8256]{0:T(1024)S(1)} %add.37), channel_id=1, source_target_pairs={{0,8},{1,9},{2,10},{3,11},{4,12},{5,13},{6,14},{7,15},{8,0},{9,1},... | collective-permute-start | bytes 99080 | tf_op jit(solution)/shard_map/ppermute | solution.py:21
  163.1 0.7 copy-start.5

commit v15 on v11

--- a/solution.py
+++ b/solution.py
@@ -40,8 +40,8 @@
     width = below_ref.shape[1]
     for at, source, pot in ((0, below_ref, below_pot), (width, own_ref, own_pot),
                             (width + own_planes, above_ref, above_pot)):
-        first_buf[:, at : at + source.shape[1]] = source[...]
-        wide_pot[at : at + source.shape[1]] = pot[...]
+        pltpu.sync_copy(source, first_buf.at[:, at : at + source.shape[1]])
+        pltpu.sync_copy(pot, wide_pot.at[at : at + pot.shape[0]])
     rows, lanes = first_buf.shape[2], first_buf.shape[3]
 
     def apply(field, band, plane):
@@ -93,7 +93,7 @@
     return pl.pallas_call(
         filter_kernel,
         out_shape=(jax.ShapeDtypeStruct(shape, jnp.float32), jax.ShapeDtypeStruct(shape, jnp.float32)),
-        in_specs=[pl.BlockSpec(memory_space=pltpu.VMEM)] * 6,
+        in_specs=[pl.BlockSpec(memory_space=pl.ANY)] * 6,
         out_specs=(pl.BlockSpec(memory_space=pltpu.VMEM), pl.BlockSpec(memory_space=pltpu.VMEM)),
         scratch_shapes=[pltpu.VMEM((band_count, total, rows, lanes), jnp.float32)] * 3
         + [pltpu.VMEM((total, rows, lanes), jnp.float32)],

time: 166 us -> 171 us (1.030)
  Pallas kernels: 14.2 us -> 18.1 us
    pallas_call x1, Pallas kernels: 5.77 us -> 9.75 us  [filter_and_image(): pl.pallas_call(filter_kernel, out_shape=(jax.ShapeDtypeStruct(shape, jnp....]
where the time goes in v15:
time: 171 us; the launch traced here: 169 us
  starting transfers between devices  65.7 us (38%)
  waiting for transfers between devices  42.3 us (25%)
  blocking collectives  32.5 us (19%)
  Pallas kernels  18.1 us (11%)
  local copies, waits for them, and re-layouts  6.69 us (4%)
  other arithmetic  1.85 us (1%)
    ppermute x9, starting transfers between devices, butterfly_sum(): values = values + lax.ppermute(values, axis, pairs)  44.5 us
    all_to_all x1, blocking collectives, on_device(): moved = lax.all_to_all(both, 'band', 2, 1, tiled=True)  32.5 us
    ppermute x9, waiting for transfers between devices, butterfly_sum(): values = values + lax.ppermute(values, axis, pairs)  31.7 us
    ppermute x1, starting transfers between devices, on_device(): lax.ppermute(potential[potential.shape[0] - width:], ('band', 'grid'), re...  13.8 us
    ppermute x1, waiting for transfers between devices, on_device(): lax.ppermute(potential[:width], ('band', 'grid'), replica_pairs(-1))  10.6 us
    pallas_call x1, Pallas kernels, filter_and_image(): pl.pallas_call(filter_kernel, out_shape=(jax.ShapeDtypeStruct(shape, jnp....  9.75 us
    pallas_call x1, Pallas kernels, rayleigh_ritz(): pl.pallas_call(rayleigh_ritz_kernel, out_shape=(jax.ShapeDtypeStruct((ban...  8.4 us
    ppermute x1, starting transfers between devices, on_device(): lax.ppermute(trial_bands[:, :width], 'grid', [((i + 1) % count, i) for i...  3.64 us
  transfers between devices with their start and end apart: 13, of which 10 were waited for; matrix products, arithmetic and copies ran while one was open for 0% of the time, Pallas kernels for 0%

profile of v15, /device:TPU:24, one launch (start us, length us, event | category | flops | bytes accessed | tf_op | source)
XLA Modules:
  0.0 169.0 jit_solution(8895364457387887562)
XLA Ops:
  0.6 1.9 %collective-permute-start = (f32[2,10,32,128]{3,2,1,0:T(8,128)}, f32[2,10,32,128]{3,2,1,0:T(8,128)S(1)}, u32[]{:S(2)}, u32[]{:S(2)}) collective-permute-start(f32[2,10,32,128]{3,2,1,0:T(8,128)} %own_ref.1), channel_id=1, source_target_pairs={{0,1},{1,2},{2,3},{3,4},{4,5},{5,6},{6,7},{7,8},{8,9},{9,10},{10,1... | collective-permute-start | bytes 983048 | tf_op jit(solution)/shard_map/ppermute | solution.py:168
  2.6 3.6 %collective-permute-start.1 = (f32[2,10,32,128]{3,2,1,0:T(8,128)}, f32[2,10,32,128]{3,2,1,0:T(8,128)S(1)}, u32[]{:S(2)}, u32[]{:S(2)}) collective-permute-start(f32[2,10,32,128]{3,2,1,0:T(8,128)} %own_ref.1), channel_id=1, source_target_pairs={{1,0},{2,1},{3,2},{4,3},{5,4},{6,5},{7,6},{8,7},{9,8},{10,9},{11,1... | collective-permute-start | bytes 983048 | tf_op jit(solution)/shard_map/ppermute | solution.py:169
  6.2 13.8 %collective-permute-start.2 = (f32[10,32,128]{2,1,0:T(8,128)}, f32[10,32,128]{2,1,0:T(8,128)S(1)}, u32[]{:S(2)}, u32[]{:S(2)}) collective-permute-start(f32[10,32,128]{2,1,0:T(8,128)} %own_pot.1), channel_id=1, source_target_pairs={{79,0},{95,16},{111,32},{127,48},{15,64},{31,80},{47,96},{63,112},... | collective-permute-start | bytes 491528 | tf_op jit(solution)/shard_map/ppermute | solution.py:170
  20.0 1.9 %collective-permute-start.3 = (f32[10,32,128]{2,1,0:T(8,128)}, f32[10,32,128]{2,1,0:T(8,128)S(1)}, u32[]{:S(2)}, u32[]{:S(2)}) collective-permute-start(f32[10,32,128]{2,1,0:T(8,128)} %own_pot.1), channel_id=1, source_target_pairs={{1,0},{17,16},{33,32},{49,48},{65,64},{81,80},{97,96},{113,112},{1... | collective-permute-start | bytes 491528 | tf_op jit(solution)/shard_map/ppermute | solution.py:171
  21.9 10.6 %collective-permute-done.3.above_pot = f32[10,32,128]{2,1,0:T(8,128)S(1)} collective-permute-done((f32[10,32,128]{2,1,0:T(8,128)}, f32[10,32,128]{2,1,0:T(8,128)S(1)}, u32[]{:S(2)}, u32[]{:S(2)}) %collective-permute-start.3) | collective-permute-done | bytes 163872 | tf_op jit(solution)/shard_map/ppermute | solution.py:171
  33.3 0.7 copy-done.2
  34.0 9.7 %shard_map.49 = (f32[2,10,32,128]{3,2,1,0:T(8,128)}, f32[2,10,32,128]{3,2,1,0:T(8,128)}) custom-call(f32[2,10,32,128]{3,2,1,0:T(8,128)} %copy-done.1, f32[2,10,32,128]{3,2,1,0:T(8,128)} %own_ref.1, f32[2,10,32,128]{3,2,1,0:T(8,128)} %copy-done.2, f32[10,32,128]{2,1,0:T(8,128)} %copy-done.3, f32[10,32,128]{2,1,0:T(8,128)} %own_pot.1, f32[10,32,128]{2,1,0:T(8,128)} %copy-done.4), custom_call_target="tpu_custom_call" | custom-call | flops 29491200 | bytes 2949120 | tf_op jit(solution)/shard_map/pallas_call | solution.py:93
  43.8 1.0 stack.7
  45.1 0.7 copy-done
  46.4 32.5 %all_to_all.15 = f32[2,2,32,1280]{3,1,0,2:T(2,128)S(1)} all-to-all(f32[2,2,32,1280]{3,1,0,2:T(2,128)S(1)} %pad_maximum_fusion), channel_id=1, replica_groups=mesh['band'=32,'grid'=16] {'band'}, dimensions={2} | all-to-all | bytes 1310720 | tf_op jit(solution)/shard_map/all_to_all | solution.py:182
  80.7 1.9 %collective-permute-start.4 = (f32[8256]{0:T(1024)S(1)}, f32[8256]{0:T(1024)S(1)}, u32[]{:S(2)}, u32[]{:S(2)}) collective-permute-start(f32[8256]{0:T(1024)S(1)} %constant_dynamic-update-slice_fusion), channel_id=1, source_target_pairs={{0,16},{16,0},{32,48},{48,32},{64,80},{80,64},{96,112},{112,96},{1... | collective-permute-start | bytes 99080 | tf_op jit(solution)/shard_map/ppermute | solution.py:21
  82.7 4.1 %collective-permute-done.4 = f32[8256]{0:T(1024)S(1)} collective-permute-done((f32[8256]{0:T(1024)S(1)}, f32[8256]{0:T(1024)S(1)}, u32[]{:S(2)}, u32[]{:S(2)}) %collective-permute-start.4) | collective-permute-done | bytes 33056 | tf_op jit(solution)/shard_map/ppermute | solution.py:21
  86.8 2.8 %collective-permute-start.5 = (f32[8256]{0:T(1024)S(1)}, f32[8256]{0:T(1024)S(1)}, u32[]{:S(2)}, u32[]{:S(2)}) collective-permute-start(f32[8256]{0:T(1024)S(1)} %add.30), channel_id=1, source_target_pairs={{0,32},{16,48},{32,0},{48,16},{64,96},{80,112},{96,64},{112,80},{1... | collective-permute-start | bytes 99080 | tf_op jit(solution)/shard_map/ppermute | solution.py:21
  89.6 3.9 %collective-permute-done.5 = f32[8256]{0:T(1024)S(1)} collective-permute-done((f32[8256]{0:T(1024)S(1)}, f32[8256]{0:T(1024)S(1)}, u32[]{:S(2)}, u32[]{:S(2)}) %collective-permute-start.5) | collective-permute-done | bytes 33056 | tf_op jit(solution)/shard_map/ppermute | solution.py:21
  93.6 5.2 %collective-permute-start.6 = (f32[8256]{0:T(1024)S(1)}, f32[8256]{0:T(1024)S(1)}, u32[]{:S(2)}, u32[]{:S(2)}) collective-permute-start(f32[8256]{0:T(1024)S(1)} %add.31), channel_id=1, source_target_pairs={{0,64},{16,80},{32,96},{48,112},{64,0},{80,16},{96,32},{112,48},{1... | collective-permute-start | bytes 99080 | tf_op jit(solution)/shard_map/ppermute | solution.py:21
  98.8 4.5 %collective-permute-done.6 = f32[8256]{0:T(1024)S(1)} collective-permute-done((f32[8256]{0:T(1024)S(1)}, f32[8256]{0:T(1024)S(1)}, u32[]{:S(2)}, u32[]{:S(2)}) %collective-permute-start.6) | collective-permute-done | bytes 33056 | tf_op jit(solution)/shard_map/ppermute | solution.py:21
  103.3 1.9 %collective-permute-start.7 = (f32[8256]{0:T(1024)S(1)}, f32[8256]{0:T(1024)S(1)}, u32[]{:S(2)}, u32[]{:S(2)}) collective-permute-start(f32[8256]{0:T(1024)S(1)} %add.32), channel_id=1, source_target_pairs={{0,128},{16,144},{32,160},{48,176},{64,192},{80,208},{96,224},{112... | collective-permute-start | bytes 99080 | tf_op jit(solution)/shard_map/ppermute | solution.py:21
  105.2 3.9 %collective-permute-done.7 = f32[8256]{0:T(1024)S(1)} collective-permute-done((f32[8256]{0:T(1024)S(1)}, f32[8256]{0:T(1024)S(1)}, u32[]{:S(2)}, u32[]{:S(2)}) %collective-permute-start.7) | collective-permute-done | bytes 33056 | tf_op jit(solution)/shard_map/ppermute | solution.py:21
  109.2 3.7 %collective-permute-start.8 = (f32[8256]{0:T(1024)S(1)}, f32[8256]{0:T(1024)S(1)}, u32[]{:S(2)}, u32[]{:S(2)}) collective-permute-start(f32[8256]{0:T(1024)S(1)} %add.33), channel_id=1, source_target_pairs={{0,384},{16,400},{32,416},{48,432},{64,448},{80,464},{96,480},{112... | collective-permute-start | bytes 99080 | tf_op jit(solution)/shard_map/ppermute | solution.py:21
  112.9 3.3 %collective-permute-done.8 = f32[8256]{0:T(1024)S(1)} collective-permute-done((f32[8256]{0:T(1024)S(1)}, f32[8256]{0:T(1024)S(1)}, u32[]{:S(2)}, u32[]{:S(2)}) %collective-permute-start.8) | collective-permute-done | bytes 33056 | tf_op jit(solution)/shard_map/ppermute | solution.py:21
  116.2 12.5 %collective-permute-start.9 = (f32[8256]{0:T(1024)S(1)}, f32[8256]{0:T(1024)S(1)}, u32[]{:S(2)}, u32[]{:S(2)}) collective-permute-start(f32[8256]{0:T(1024)S(1)} %add.34), channel_id=1, source_target_pairs={{0,1},{1,0},{2,3},{3,2},{4,5},{5,4},{6,7},{7,6},{8,9},{9,8},{10,11... | collective-permute-start | bytes 99080 | tf_op jit(solution)/shard_map/ppermute | solution.py:21
  128.8 0.8 collective-permute-done.9
  129.6 1.9 %collective-permute-start.10 = (f32[8256]{0:T(1024)S(1)}, f32[8256]{0:T(1024)S(1)}, u32[]{:S(2)}, u32[]{:S(2)}) collective-permute-start(f32[8256]{0:T(1024)S(1)} %add.35), channel_id=1, source_target_pairs={{0,2},{1,3},{2,0},{3,1},{4,6},{5,7},{6,4},{7,5},{8,10},{9,11},{10,... | collective-permute-start | bytes 99080 | tf_op jit(solution)/shard_map/ppermute | solution.py:21
  131.5 3.9 %collective-permute-done.10 = f32[8256]{0:T(1024)S(1)} collective-permute-done((f32[8256]{0:T(1024)S(1)}, f32[8256]{0:T(1024)S(1)}, u32[]{:S(2)}, u32[]{:S(2)}) %collective-permute-start.10) | collective-permute-done | bytes 33056 | tf_op jit(solution)/shard_map/ppermute | solution.py:21
  135.5 4.4 %collective-permute-start.11 = (f32[8256]{0:T(1024)S(1)}, f32[8256]{0:T(1024)S(1)}, u32[]{:S(2)}, u32[]{:S(2)}) collective-permute-start(f32[8256]{0:T(1024)S(1)} %add.36), channel_id=1, source_target_pairs={{0,6},{1,7},{2,4},{3,5},{4,2},{5,3},{6,0},{7,1},{8,14},{9,15},{10,... | collective-permute-start | bytes 99080 | tf_op jit(solution)/shard_map/ppermute | solution.py:21
  139.8 2.7 %collective-permute-done.11 = f32[8256]{0:T(1024)S(1)} collective-permute-done((f32[8256]{0:T(1024)S(1)}, f32[8256]{0:T(1024)S(1)}, u32[]{:S(2)}, u32[]{:S(2)}) %collective-permute-start.11) | collective-permute-done | bytes 33056 | tf_op jit(solution)/shard_map/ppermute | solution.py:21
  142.5 10.1 %collective-permute-start.12 = (f32[8256]{0:T(1024)S(1)}, f32[8256]{0:T(1024)S(1)}, u32[]{:S(2)}, u32[]{:S(2)}) collective-permute-start(f32[8256]{0:T(1024)S(1)} %add.37), channel_id=1, source_target_pairs={{0,8},{1,9},{2,10},{3,11},{4,12},{5,13},{6,14},{7,15},{8,0},{9,1},... | collective-permute-start | bytes 99080 | tf_op jit(solution)/shard_map/ppermute | solution.py:21
  152.6 4.5 %collective-permute-done.12 = f32[8256]{0:T(1024)S(1)} collective-permute-done((f32[8256]{0:T(1024)S(1)}, f32[8256]{0:T(1024)S(1)}, u32[]{:S(2)}, u32[]{:S(2)}) %collective-permute-start.12) | collective-permute-done | bytes 33056 | tf_op jit(solution)/shard_map/ppermute | solution.py:21
  157.9 0.7 slice.42.subspace_ref
  158.6 0.7 copy.14.norms_ref
  159.3 8.4 %shard_map.50 = (f32[2,64]{1,0:T(2,128)}, f32[2,1]{1,0:T(2,128)}) custom-call(s32[1]{0:T(128)} %bitcast.first_ref, f32[64,64]{1,0:T(8,128)} %fusion.margin_ref, f32[64,64]{1,0:T(8,128)} %slice.42.subspace_ref, f32[64,1]{1,0:T(8,128)} %copy.14.norms_ref), custom_call_target="tpu_custom_call" | custom-call | flops 1572864 | bytes 65536 | tf_op jit(solution)/shard_map/pallas_call | solution.py:141
  167.7 0.7 copy-done.5
  (42 shorter events, 4.9 us)
Async XLA Ops:
  0.6 31.9 %collective-permute-start = (f32[2,10,32,128]{3,2,1,0:T(8,128)}, f32[2,10,32,128]{3,2,1,0:T(8,128)S(1)}, u32[]{:S(2)}, u32[]{:S(2)}) collective-permute-start(f32[2,10,32,128]{3,2,1,0:T(8,128)} %own_ref.1), channel_id=1, source_target_pairs={{0,1},{1,2},{2,3},{3,4},{4,5},{5,6},{6,7},{7,8},{8,9},{9,10},{10,1... | collective-permute-start | bytes 983048 | tf_op jit(solution)/shard_map/ppermute | solution.py:168
  2.6 30.0 %collective-permute-start.1 = (f32[2,10,32,128]{3,2,1,0:T(8,128)}, f32[2,10,32,128]{3,2,1,0:T(8,128)S(1)}, u32[]{:S(2)}, u32[]{:S(2)}) collective-permute-start(f32[2,10,32,128]{3,2,1,0:T(8,128)} %own_ref.1), channel_id=1, source_target_pairs={{1,0},{2,1},{3,2},{4,3},{5,4},{6,5},{7,6},{8,7},{9,8},{10,9},{11,1... | collective-permute-start | bytes 983048 | tf_op jit(solution)/shard_map/ppermute | solution.py:169
  6.2 15.7 %collective-permute-start.2 = (f32[10,32,128]{2,1,0:T(8,128)}, f32[10,32,128]{2,1,0:T(8,128)S(1)}, u32[]{:S(2)}, u32[]{:S(2)}) collective-permute-start(f32[10,32,128]{2,1,0:T(8,128)} %own_pot.1), channel_id=1, source_target_pairs={{79,0},{95,16},{111,32},{127,48},{15,64},{31,80},{47,96},{63,112},... | collective-permute-start | bytes 491528 | tf_op jit(solution)/shard_map/ppermute | solution.py:170
  20.0 12.6 %collective-permute-start.3 = (f32[10,32,128]{2,1,0:T(8,128)}, f32[10,32,128]{2,1,0:T(8,128)S(1)}, u32[]{:S(2)}, u32[]{:S(2)}) collective-permute-start(f32[10,32,128]{2,1,0:T(8,128)} %own_pot.1), channel_id=1, source_target_pairs={{1,0},{17,16},{33,32},{49,48},{65,64},{81,80},{97,96},{113,112},{1... | collective-permute-start | bytes 491528 | tf_op jit(solution)/shard_map/ppermute | solution.py:171
  21.9 10.6 %copy-start.3 = (f32[10,32,128]{2,1,0:T(8,128)}, f32[10,32,128]{2,1,0:T(8,128)S(1)}, u32[]{:S(2)}) copy-start(f32[10,32,128]{2,1,0:T(8,128)S(1)} %collective-permute-done.2.below_pot) | copy-start | bytes 491524
  32.5 0.7 copy-start.4
  32.6 0.8 copy-start.1
  33.3 0.7 copy-start.2
  44.8 1.0 copy-start
  80.7 6.1 %collective-permute-start.4 = (f32[8256]{0:T(1024)S(1)}, f32[8256]{0:T(1024)S(1)}, u32[]{:S(2)}, u32[]{:S(2)}) collective-permute-start(f32[8256]{0:T(1024)S(1)} %constant_dynamic-update-slice_fusion), channel_id=1, source_target_pairs={{0,16},{16,0},{32,48},{48,32},{64,80},{80,64},{96,112},{112,96},{1... | collective-permute-start | bytes 99080 | tf_op jit(solution)/shard_map/ppermute | solution.py:21
  86.8 6.7 %collective-permute-start.5 = (f32[8256]{0:T(1024)S(1)}, f32[8256]{0:T(1024)S(1)}, u32[]{:S(2)}, u32[]{:S(2)}) collective-permute-start(f32[8256]{0:T(1024)S(1)} %add.30), channel_id=1, source_target_pairs={{0,32},{16,48},{32,0},{48,16},{64,96},{80,112},{96,64},{112,80},{1... | collective-permute-start | bytes 99080 | tf_op jit(solution)/shard_map/ppermute | solution.py:21
  93.6 9.8 %collective-permute-start.6 = (f32[8256]{0:T(1024)S(1)}, f32[8256]{0:T(1024)S(1)}, u32[]{:S(2)}, u32[]{:S(2)}) collective-permute-start(f32[8256]{0:T(1024)S(1)} %add.31), channel_id=1, source_target_pairs={{0,64},{16,80},{32,96},{48,112},{64,0},{80,16},{96,32},{112,48},{1... | collective-permute-start | bytes 99080 | tf_op jit(solution)/shard_map/ppermute | solution.py:21
  103.3 5.8 %collective-permute-start.7 = (f32[8256]{0:T(1024)S(1)}, f32[8256]{0:T(1024)S(1)}, u32[]{:S(2)}, u32[]{:S(2)}) collective-permute-start(f32[8256]{0:T(1024)S(1)} %add.32), channel_id=1, source_target_pairs={{0,128},{16,144},{32,160},{48,176},{64,192},{80,208},{96,224},{112... | collective-permute-start | bytes 99080 | tf_op jit(solution)/shard_map/ppermute | solution.py:21
  109.2 7.1 %collective-permute-start.8 = (f32[8256]{0:T(1024)S(1)}, f32[8256]{0:T(1024)S(1)}, u32[]{:S(2)}, u32[]{:S(2)}) collective-permute-start(f32[8256]{0:T(1024)S(1)} %add.33), channel_id=1, source_target_pairs={{0,384},{16,400},{32,416},{48,432},{64,448},{80,464},{96,480},{112... | collective-permute-start | bytes 99080 | tf_op jit(solution)/shard_map/ppermute | solution.py:21
  116.2 13.4 %collective-permute-start.9 = (f32[8256]{0:T(1024)S(1)}, f32[8256]{0:T(1024)S(1)}, u32[]{:S(2)}, u32[]{:S(2)}) collective-permute-start(f32[8256]{0:T(1024)S(1)} %add.34), channel_id=1, source_target_pairs={{0,1},{1,0},{2,3},{3,2},{4,5},{5,4},{6,7},{7,6},{8,9},{9,8},{10,11... | collective-permute-start | bytes 99080 | tf_op jit(solution)/shard_map/ppermute | solution.py:21
  129.6 5.8 %collective-permute-start.10 = (f32[8256]{0:T(1024)S(1)}, f32[8256]{0:T(1024)S(1)}, u32[]{:S(2)}, u32[]{:S(2)}) collective-permute-start(f32[8256]{0:T(1024)S(1)} %add.35), channel_id=1, source_target_pairs={{0,2},{1,3},{2,0},{3,1},{4,6},{5,7},{6,4},{7,5},{8,10},{9,11},{10,... | collective-permute-start | bytes 99080 | tf_op jit(solution)/shard_map/ppermute | solution.py:21
  135.5 7.1 %collective-permute-start.11 = (f32[8256]{0:T(1024)S(1)}, f32[8256]{0:T(1024)S(1)}, u32[]{:S(2)}, u32[]{:S(2)}) collective-permute-start(f32[8256]{0:T(1024)S(1)} %add.36), channel_id=1, source_target_pairs={{0,6},{1,7},{2,4},{3,5},{4,2},{5,3},{6,0},{7,1},{8,14},{9,15},{10,... | collective-permute-start | bytes 99080 | tf_op jit(solution)/shard_map/ppermute | solution.py:21
  142.5 14.6 %collective-permute-start.12 = (f32[8256]{0:T(1024)S(1)}, f32[8256]{0:T(1024)S(1)}, u32[]{:S(2)}, u32[]{:S(2)}) collective-permute-start(f32[8256]{0:T(1024)S(1)} %add.37), channel_id=1, source_target_pairs={{0,8},{1,9},{2,10},{3,11},{4,12},{5,13},{6,14},{7,15},{8,0},{9,1},... | collective-permute-start | bytes 99080 | tf_op jit(solution)/shard_map/ppermute | solution.py:21
  167.7 0.7 copy-start.5

commit v16 on v11

--- a/solution.py
+++ b/solution.py
@@ -133,7 +133,9 @@
     first = first_ref[0]
     count = projected_ref.shape[0]
     projected_ref[...] = projected_buf[pl.ds(first, count), :]
-    residual_ref[...] = residual_buf[pl.ds(first, count), :]
+    picked = jnp.broadcast_to(residual_buf[pl.ds(first, count), :], (count, count))
+    diagonal = lax.broadcasted_iota(jnp.int32, (count, count), 0) == lax.broadcasted_iota(jnp.int32, (count, count), 1)
+    residual_ref[...] = jnp.sum(jnp.where(diagonal, picked, 0.0), axis=0, keepdims=True)
 
 
 def rayleigh_ritz(first_band, band_count, margin, subspace, image_norms):
@@ -141,7 +143,7 @@
     return pl.pallas_call(
         rayleigh_ritz_kernel,
         out_shape=(jax.ShapeDtypeStruct((band_count, size), jnp.float32),
-                   jax.ShapeDtypeStruct((band_count, 1), jnp.float32)),
+                   jax.ShapeDtypeStruct((1, band_count), jnp.float32)),
         in_specs=[pl.BlockSpec(memory_space=pltpu.SMEM)] + [pl.BlockSpec(memory_space=pltpu.VMEM)] * 3,
         out_specs=(pl.BlockSpec(memory_space=pltpu.VMEM), pl.BlockSpec(memory_space=pltpu.VMEM)),
         scratch_shapes=[pltpu.VMEM((size, size), jnp.float32), pltpu.VMEM((size, 1), jnp.float32)],

time: 166 us -> 165 us (level)
  no operation moved by 1% of the time
where the time goes in v16:
time: 165 us; the launch traced here: 164 us
  starting transfers between devices  65.9 us (40%)
  waiting for transfers between devices  42.2 us (26%)
  blocking collectives  32.5 us (20%)
  Pallas kernels  14.1 us (9%)
  local copies, waits for them, and re-layouts  6.02 us (4%)
    ppermute x9, starting transfers between devices, butterfly_sum(): values = values + lax.ppermute(values, axis, pairs)  44.7 us
    all_to_all x1, blocking collectives, on_device(): moved = lax.all_to_all(both, 'band', 2, 1, tiled=True)  32.5 us
    ppermute x9, waiting for transfers between devices, butterfly_sum(): values = values + lax.ppermute(values, axis, pairs)  31.5 us
    ppermute x1, starting transfers between devices, on_device(): lax.ppermute(potential[potential.shape[0] - width:], ('band', 'grid'), re...  13.8 us
    ppermute x1, waiting for transfers between devices, on_device(): lax.ppermute(potential[:width], ('band', 'grid'), replica_pairs(-1))  10.6 us
    pallas_call x1, Pallas kernels, rayleigh_ritz(): pl.pallas_call(rayleigh_ritz_kernel, out_shape=(jax.ShapeDtypeStruct((ban...  8.36 us
    pallas_call x1, Pallas kernels, filter_and_image(): pl.pallas_call(filter_kernel, out_shape=(jax.ShapeDtypeStruct(shape, jnp....  5.78 us
    ppermute x1, starting transfers between devices, on_device(): lax.ppermute(trial_bands[:, :width], 'grid', [((i + 1) % count, i) for i...  3.64 us
  transfers between devices with their start and end apart: 13, of which 10 were waited for; matrix products, arithmetic and copies ran while one was open for 0% of the time, Pallas kernels for 0%

profile of v16, /device:TPU:24, one launch (start us, length us, event | category | flops | bytes accessed | tf_op | source)
XLA Modules:
  0.0 163.7 jit_solution(15056076780397488875)
XLA Ops:
  0.6 1.9 %collective-permute-start = (f32[2,10,32,128]{3,2,1,0:T(8,128)}, f32[2,10,32,128]{3,2,1,0:T(8,128)S(1)}, u32[]{:S(2)}, u32[]{:S(2)}) collective-permute-start(f32[2,10,32,128]{3,2,1,0:T(8,128)} %own_ref.1), channel_id=1, source_target_pairs={{0,1},{1,2},{2,3},{3,4},{4,5},{5,6},{6,7},{7,8},{8,9},{9,10},{10,1... | collective-permute-start | bytes 983048 | tf_op jit(solution)/shard_map/ppermute | solution.py:170
  2.6 3.6 %collective-permute-start.1 = (f32[2,10,32,128]{3,2,1,0:T(8,128)}, f32[2,10,32,128]{3,2,1,0:T(8,128)S(1)}, u32[]{:S(2)}, u32[]{:S(2)}) collective-permute-start(f32[2,10,32,128]{3,2,1,0:T(8,128)} %own_ref.1), channel_id=1, source_target_pairs={{1,0},{2,1},{3,2},{4,3},{5,4},{6,5},{7,6},{8,7},{9,8},{10,9},{11,1... | collective-permute-start | bytes 983048 | tf_op jit(solution)/shard_map/ppermute | solution.py:171
  6.2 13.8 %collective-permute-start.2 = (f32[10,32,128]{2,1,0:T(8,128)}, f32[10,32,128]{2,1,0:T(8,128)S(1)}, u32[]{:S(2)}, u32[]{:S(2)}) collective-permute-start(f32[10,32,128]{2,1,0:T(8,128)} %own_pot.1), channel_id=1, source_target_pairs={{79,0},{95,16},{111,32},{127,48},{15,64},{31,80},{47,96},{63,112},... | collective-permute-start | bytes 491528 | tf_op jit(solution)/shard_map/ppermute | solution.py:172
  20.0 1.9 %collective-permute-start.3 = (f32[10,32,128]{2,1,0:T(8,128)}, f32[10,32,128]{2,1,0:T(8,128)S(1)}, u32[]{:S(2)}, u32[]{:S(2)}) collective-permute-start(f32[10,32,128]{2,1,0:T(8,128)} %own_pot.1), channel_id=1, source_target_pairs={{1,0},{17,16},{33,32},{49,48},{65,64},{81,80},{97,96},{113,112},{1... | collective-permute-start | bytes 491528 | tf_op jit(solution)/shard_map/ppermute | solution.py:173
  21.9 10.6 %collective-permute-done.3.above_pot = f32[10,32,128]{2,1,0:T(8,128)S(1)} collective-permute-done((f32[10,32,128]{2,1,0:T(8,128)}, f32[10,32,128]{2,1,0:T(8,128)S(1)}, u32[]{:S(2)}, u32[]{:S(2)}) %collective-permute-start.3) | collective-permute-done | bytes 163872 | tf_op jit(solution)/shard_map/ppermute | solution.py:173
  32.6 0.6 copy-done.4
  33.3 0.7 copy-done.2
  34.1 5.8 %shard_map.49 = (f32[2,10,32,128]{3,2,1,0:T(8,128)}, f32[2,10,32,128]{3,2,1,0:T(8,128)}) custom-call(f32[2,10,32,128]{3,2,1,0:T(8,128)} %copy-done.1, f32[2,10,32,128]{3,2,1,0:T(8,128)} %own_ref.1, f32[2,10,32,128]{3,2,1,0:T(8,128)} %copy-done.2, f32[10,32,128]{2,1,0:T(8,128)} %copy-done.3, f32[10,32,128]{2,1,0:T(8,128)} %own_pot.1, f32[10,32,128]{2,1,0:T(8,128)} %copy-done.4), custom_call_target="tpu_custom_call" | custom-call | flops 29491200 | bytes 2949120 | tf_op jit(solution)/shard_map/pallas_call | solution.py:93
  39.8 1.0 stack.7
  41.1 0.7 copy-done
  42.5 32.5 %all_to_all.15 = f32[2,2,32,1280]{3,1,0,2:T(2,128)S(1)} all-to-all(f32[2,2,32,1280]{3,1,0,2:T(2,128)S(1)} %pad_maximum_fusion), channel_id=1, replica_groups=mesh['band'=32,'grid'=16] {'band'}, dimensions={2} | all-to-all | bytes 1310720 | tf_op jit(solution)/shard_map/all_to_all | solution.py:184
  76.8 1.9 %collective-permute-start.4 = (f32[8256]{0:T(1024)S(1)}, f32[8256]{0:T(1024)S(1)}, u32[]{:S(2)}, u32[]{:S(2)}) collective-permute-start(f32[8256]{0:T(1024)S(1)} %constant_dynamic-update-slice_fusion), channel_id=1, source_target_pairs={{0,16},{16,0},{32,48},{48,32},{64,80},{80,64},{96,112},{112,96},{1... | collective-permute-start | bytes 99080 | tf_op jit(solution)/shard_map/ppermute | solution.py:21
  78.7 4.1 %collective-permute-done.4 = f32[8256]{0:T(1024)S(1)} collective-permute-done((f32[8256]{0:T(1024)S(1)}, f32[8256]{0:T(1024)S(1)}, u32[]{:S(2)}, u32[]{:S(2)}) %collective-permute-start.4) | collective-permute-done | bytes 33056 | tf_op jit(solution)/shard_map/ppermute | solution.py:21
  82.8 2.8 %collective-permute-start.5 = (f32[8256]{0:T(1024)S(1)}, f32[8256]{0:T(1024)S(1)}, u32[]{:S(2)}, u32[]{:S(2)}) collective-permute-start(f32[8256]{0:T(1024)S(1)} %add.30), channel_id=1, source_target_pairs={{0,32},{16,48},{32,0},{48,16},{64,96},{80,112},{96,64},{112,80},{1... | collective-permute-start | bytes 99080 | tf_op jit(solution)/shard_map/ppermute | solution.py:21
  85.7 3.9 %collective-permute-done.5 = f32[8256]{0:T(1024)S(1)} collective-permute-done((f32[8256]{0:T(1024)S(1)}, f32[8256]{0:T(1024)S(1)}, u32[]{:S(2)}, u32[]{:S(2)}) %collective-permute-start.5) | collective-permute-done | bytes 33056 | tf_op jit(solution)/shard_map/ppermute | solution.py:21
  89.6 5.2 %collective-permute-start.6 = (f32[8256]{0:T(1024)S(1)}, f32[8256]{0:T(1024)S(1)}, u32[]{:S(2)}, u32[]{:S(2)}) collective-permute-start(f32[8256]{0:T(1024)S(1)} %add.31), channel_id=1, source_target_pairs={{0,64},{16,80},{32,96},{48,112},{64,0},{80,16},{96,32},{112,48},{1... | collective-permute-start | bytes 99080 | tf_op jit(solution)/shard_map/ppermute | solution.py:21
  94.8 4.5 %collective-permute-done.6 = f32[8256]{0:T(1024)S(1)} collective-permute-done((f32[8256]{0:T(1024)S(1)}, f32[8256]{0:T(1024)S(1)}, u32[]{:S(2)}, u32[]{:S(2)}) %collective-permute-start.6) | collective-permute-done | bytes 33056 | tf_op jit(solution)/shard_map/ppermute | solution.py:21
  99.4 1.9 %collective-permute-start.7 = (f32[8256]{0:T(1024)S(1)}, f32[8256]{0:T(1024)S(1)}, u32[]{:S(2)}, u32[]{:S(2)}) collective-permute-start(f32[8256]{0:T(1024)S(1)} %add.32), channel_id=1, source_target_pairs={{0,128},{16,144},{32,160},{48,176},{64,192},{80,208},{96,224},{112... | collective-permute-start | bytes 99080 | tf_op jit(solution)/shard_map/ppermute | solution.py:21
  101.3 3.9 %collective-permute-done.7 = f32[8256]{0:T(1024)S(1)} collective-permute-done((f32[8256]{0:T(1024)S(1)}, f32[8256]{0:T(1024)S(1)}, u32[]{:S(2)}, u32[]{:S(2)}) %collective-permute-start.7) | collective-permute-done | bytes 33056 | tf_op jit(solution)/shard_map/ppermute | solution.py:21
  105.2 3.7 %collective-permute-start.8 = (f32[8256]{0:T(1024)S(1)}, f32[8256]{0:T(1024)S(1)}, u32[]{:S(2)}, u32[]{:S(2)}) collective-permute-start(f32[8256]{0:T(1024)S(1)} %add.33), channel_id=1, source_target_pairs={{0,384},{16,400},{32,416},{48,432},{64,448},{80,464},{96,480},{112... | collective-permute-start | bytes 99080 | tf_op jit(solution)/shard_map/ppermute | solution.py:21
  109.0 3.3 %collective-permute-done.8 = f32[8256]{0:T(1024)S(1)} collective-permute-done((f32[8256]{0:T(1024)S(1)}, f32[8256]{0:T(1024)S(1)}, u32[]{:S(2)}, u32[]{:S(2)}) %collective-permute-start.8) | collective-permute-done | bytes 33056 | tf_op jit(solution)/shard_map/ppermute | solution.py:21
  112.3 12.5 %collective-permute-start.9 = (f32[8256]{0:T(1024)S(1)}, f32[8256]{0:T(1024)S(1)}, u32[]{:S(2)}, u32[]{:S(2)}) collective-permute-start(f32[8256]{0:T(1024)S(1)} %add.34), channel_id=1, source_target_pairs={{0,1},{1,0},{2,3},{3,2},{4,5},{5,4},{6,7},{7,6},{8,9},{9,8},{10,11... | collective-permute-start | bytes 99080 | tf_op jit(solution)/shard_map/ppermute | solution.py:21
  124.8 0.8 collective-permute-done.9
  125.7 1.9 %collective-permute-start.10 = (f32[8256]{0:T(1024)S(1)}, f32[8256]{0:T(1024)S(1)}, u32[]{:S(2)}, u32[]{:S(2)}) collective-permute-start(f32[8256]{0:T(1024)S(1)} %add.35), channel_id=1, source_target_pairs={{0,2},{1,3},{2,0},{3,1},{4,6},{5,7},{6,4},{7,5},{8,10},{9,11},{10,... | collective-permute-start | bytes 99080 | tf_op jit(solution)/shard_map/ppermute | solution.py:21
  127.6 3.9 %collective-permute-done.10 = f32[8256]{0:T(1024)S(1)} collective-permute-done((f32[8256]{0:T(1024)S(1)}, f32[8256]{0:T(1024)S(1)}, u32[]{:S(2)}, u32[]{:S(2)}) %collective-permute-start.10) | collective-permute-done | bytes 33056 | tf_op jit(solution)/shard_map/ppermute | solution.py:21
  131.5 4.6 %collective-permute-start.11 = (f32[8256]{0:T(1024)S(1)}, f32[8256]{0:T(1024)S(1)}, u32[]{:S(2)}, u32[]{:S(2)}) collective-permute-start(f32[8256]{0:T(1024)S(1)} %add.36), channel_id=1, source_target_pairs={{0,6},{1,7},{2,4},{3,5},{4,2},{5,3},{6,0},{7,1},{8,14},{9,15},{10,... | collective-permute-start | bytes 99080 | tf_op jit(solution)/shard_map/ppermute | solution.py:21
  136.1 2.5 %collective-permute-done.11 = f32[8256]{0:T(1024)S(1)} collective-permute-done((f32[8256]{0:T(1024)S(1)}, f32[8256]{0:T(1024)S(1)}, u32[]{:S(2)}, u32[]{:S(2)}) %collective-permute-start.11) | collective-permute-done | bytes 33056 | tf_op jit(solution)/shard_map/ppermute | solution.py:21
  138.6 10.1 %collective-permute-start.12 = (f32[8256]{0:T(1024)S(1)}, f32[8256]{0:T(1024)S(1)}, u32[]{:S(2)}, u32[]{:S(2)}) collective-permute-start(f32[8256]{0:T(1024)S(1)} %add.37), channel_id=1, source_target_pairs={{0,8},{1,9},{2,10},{3,11},{4,12},{5,13},{6,14},{7,15},{8,0},{9,1},... | collective-permute-start | bytes 99080 | tf_op jit(solution)/shard_map/ppermute | solution.py:21
  148.7 4.5 %collective-permute-done.12 = f32[8256]{0:T(1024)S(1)} collective-permute-done((f32[8256]{0:T(1024)S(1)}, f32[8256]{0:T(1024)S(1)}, u32[]{:S(2)}, u32[]{:S(2)}) %collective-permute-start.12) | collective-permute-done | bytes 33056 | tf_op jit(solution)/shard_map/ppermute | solution.py:21
  153.9 0.7 slice.42.subspace_ref
  154.6 0.7 copy.14.norms_ref
  155.3 8.4 %shard_map.50 = (f32[2,64]{1,0:T(2,128)}, f32[1,2]{1,0:T(1,128)}) custom-call(s32[1]{0:T(128)} %bitcast.first_ref, f32[64,64]{1,0:T(8,128)} %fusion.margin_ref, f32[64,64]{1,0:T(8,128)} %slice.42.subspace_ref, f32[64,1]{1,0:T(8,128)} %copy.14.norms_ref), custom_call_target="tpu_custom_call" | custom-call | flops 1572864 | bytes 65536 | tf_op jit(solution)/shard_map/pallas_call | solution.py:143
  (39 shorter events, 3.6 us)
Async XLA Ops:
  0.6 31.9 %collective-permute-start = (f32[2,10,32,128]{3,2,1,0:T(8,128)}, f32[2,10,32,128]{3,2,1,0:T(8,128)S(1)}, u32[]{:S(2)}, u32[]{:S(2)}) collective-permute-start(f32[2,10,32,128]{3,2,1,0:T(8,128)} %own_ref.1), channel_id=1, source_target_pairs={{0,1},{1,2},{2,3},{3,4},{4,5},{5,6},{6,7},{7,8},{8,9},{9,10},{10,1... | collective-permute-start | bytes 983048 | tf_op jit(solution)/shard_map/ppermute | solution.py:170
  2.6 30.0 %collective-permute-start.1 = (f32[2,10,32,128]{3,2,1,0:T(8,128)}, f32[2,10,32,128]{3,2,1,0:T(8,128)S(1)}, u32[]{:S(2)}, u32[]{:S(2)}) collective-permute-start(f32[2,10,32,128]{3,2,1,0:T(8,128)} %own_ref.1), channel_id=1, source_target_pairs={{1,0},{2,1},{3,2},{4,3},{5,4},{6,5},{7,6},{8,7},{9,8},{10,9},{11,1... | collective-permute-start | bytes 983048 | tf_op jit(solution)/shard_map/ppermute | solution.py:171
  6.2 15.7 %collective-permute-start.2 = (f32[10,32,128]{2,1,0:T(8,128)}, f32[10,32,128]{2,1,0:T(8,128)S(1)}, u32[]{:S(2)}, u32[]{:S(2)}) collective-permute-start(f32[10,32,128]{2,1,0:T(8,128)} %own_pot.1), channel_id=1, source_target_pairs={{79,0},{95,16},{111,32},{127,48},{15,64},{31,80},{47,96},{63,112},... | collective-permute-start | bytes 491528 | tf_op jit(solution)/shard_map/ppermute | solution.py:172
  20.0 12.6 %collective-permute-start.3 = (f32[10,32,128]{2,1,0:T(8,128)}, f32[10,32,128]{2,1,0:T(8,128)S(1)}, u32[]{:S(2)}, u32[]{:S(2)}) collective-permute-start(f32[10,32,128]{2,1,0:T(8,128)} %own_pot.1), channel_id=1, source_target_pairs={{1,0},{17,16},{33,32},{49,48},{65,64},{81,80},{97,96},{113,112},{1... | collective-permute-start | bytes 491528 | tf_op jit(solution)/shard_map/ppermute | solution.py:173
  21.9 10.6 %copy-start.3 = (f32[10,32,128]{2,1,0:T(8,128)}, f32[10,32,128]{2,1,0:T(8,128)S(1)}, u32[]{:S(2)}) copy-start(f32[10,32,128]{2,1,0:T(8,128)S(1)} %collective-permute-done.2.below_pot) | copy-start | bytes 491524
  32.5 0.7 copy-start.4
  32.6 0.8 copy-start.1
  33.3 0.7 copy-start.2
  40.9 1.0 copy-start
  76.8 6.1 %collective-permute-start.4 = (f32[8256]{0:T(1024)S(1)}, f32[8256]{0:T(1024)S(1)}, u32[]{:S(2)}, u32[]{:S(2)}) collective-permute-start(f32[8256]{0:T(1024)S(1)} %constant_dynamic-update-slice_fusion), channel_id=1, source_target_pairs={{0,16},{16,0},{32,48},{48,32},{64,80},{80,64},{96,112},{112,96},{1... | collective-permute-start | bytes 99080 | tf_op jit(solution)/shard_map/ppermute | solution.py:21
  82.8 6.7 %collective-permute-start.5 = (f32[8256]{0:T(1024)S(1)}, f32[8256]{0:T(1024)S(1)}, u32[]{:S(2)}, u32[]{:S(2)}) collective-permute-start(f32[8256]{0:T(1024)S(1)} %add.30), channel_id=1, source_target_pairs={{0,32},{16,48},{32,0},{48,16},{64,96},{80,112},{96,64},{112,80},{1... | collective-permute-start | bytes 99080 | tf_op jit(solution)/shard_map/ppermute | solution.py:21
  89.6 9.8 %collective-permute-start.6 = (f32[8256]{0:T(1024)S(1)}, f32[8256]{0:T(1024)S(1)}, u32[]{:S(2)}, u32[]{:S(2)}) collective-permute-start(f32[8256]{0:T(1024)S(1)} %add.31), channel_id=1, source_target_pairs={{0,64},{16,80},{32,96},{48,112},{64,0},{80,16},{96,32},{112,48},{1... | collective-permute-start | bytes 99080 | tf_op jit(solution)/shard_map/ppermute | solution.py:21
  99.4 5.8 %collective-permute-start.7 = (f32[8256]{0:T(1024)S(1)}, f32[8256]{0:T(1024)S(1)}, u32[]{:S(2)}, u32[]{:S(2)}) collective-permute-start(f32[8256]{0:T(1024)S(1)} %add.32), channel_id=1, source_target_pairs={{0,128},{16,144},{32,160},{48,176},{64,192},{80,208},{96,224},{112... | collective-permute-start | bytes 99080 | tf_op jit(solution)/shard_map/ppermute | solution.py:21
  105.2 7.1 %collective-permute-start.8 = (f32[8256]{0:T(1024)S(1)}, f32[8256]{0:T(1024)S(1)}, u32[]{:S(2)}, u32[]{:S(2)}) collective-permute-start(f32[8256]{0:T(1024)S(1)} %add.33), channel_id=1, source_target_pairs={{0,384},{16,400},{32,416},{48,432},{64,448},{80,464},{96,480},{112... | collective-permute-start | bytes 99080 | tf_op jit(solution)/shard_map/ppermute | solution.py:21
  112.3 13.4 %collective-permute-start.9 = (f32[8256]{0:T(1024)S(1)}, f32[8256]{0:T(1024)S(1)}, u32[]{:S(2)}, u32[]{:S(2)}) collective-permute-start(f32[8256]{0:T(1024)S(1)} %add.34), channel_id=1, source_target_pairs={{0,1},{1,0},{2,3},{3,2},{4,5},{5,4},{6,7},{7,6},{8,9},{9,8},{10,11... | collective-permute-start | bytes 99080 | tf_op jit(solution)/shard_map/ppermute | solution.py:21
  125.7 5.8 %collective-permute-start.10 = (f32[8256]{0:T(1024)S(1)}, f32[8256]{0:T(1024)S(1)}, u32[]{:S(2)}, u32[]{:S(2)}) collective-permute-start(f32[8256]{0:T(1024)S(1)} %add.35), channel_id=1, source_target_pairs={{0,2},{1,3},{2,0},{3,1},{4,6},{5,7},{6,4},{7,5},{8,10},{9,11},{10,... | collective-permute-start | bytes 99080 | tf_op jit(solution)/shard_map/ppermute | solution.py:21
  131.5 7.1 %collective-permute-start.11 = (f32[8256]{0:T(1024)S(1)}, f32[8256]{0:T(1024)S(1)}, u32[]{:S(2)}, u32[]{:S(2)}) collective-permute-start(f32[8256]{0:T(1024)S(1)} %add.36), channel_id=1, source_target_pairs={{0,6},{1,7},{2,4},{3,5},{4,2},{5,3},{6,0},{7,1},{8,14},{9,15},{10,... | collective-permute-start | bytes 99080 | tf_op jit(solution)/shard_map/ppermute | solution.py:21
  138.6 14.6 %collective-permute-start.12 = (f32[8256]{0:T(1024)S(1)}, f32[8256]{0:T(1024)S(1)}, u32[]{:S(2)}, u32[]{:S(2)}) collective-permute-start(f32[8256]{0:T(1024)S(1)} %add.37), channel_id=1, source_target_pairs={{0,8},{1,9},{2,10},{3,11},{4,12},{5,13},{6,14},{7,15},{8,0},{9,1},... | collective-permute-start | bytes 99080 | tf_op jit(solution)/shard_map/ppermute | solution.py:21

commit v17 on v16

--- a/solution.py
+++ b/solution.py
@@ -34,9 +34,9 @@
     return partner
 
 
-def filter_kernel(below_ref, own_ref, above_ref, below_pot, own_pot, above_pot, filtered_ref, image_ref,
+def filter_kernel(below_ref, own_ref, above_ref, below_pot, own_pot, above_pot, both_ref,
                   first_buf, second_buf, third_buf, wide_pot):
-    band_count, own_planes = filtered_ref.shape[0], filtered_ref.shape[1]
+    band_count, own_planes = both_ref.shape[1], both_ref.shape[2]
     width = below_ref.shape[1]
     for at, source, pot in ((0, below_ref, below_pot), (width, own_ref, own_pot),
                             (width + own_planes, above_ref, above_pot)):
@@ -77,11 +77,11 @@
         older, field, spare = field, spare, older
         sigma_now = sigma_next
     final = bufs[field]
-    filtered_ref[...] = final[:, width : width + own_planes]
+    both_ref[0] = final[:, width : width + own_planes]
 
     for plane in range(width, width + own_planes):
         for band in range(band_count):
-            image_ref[band, plane - width], _ = apply(final, band, plane)
+            both_ref[1, band, plane - width], _ = apply(final, band, plane)
 
 
 def filter_and_image(below, own, above, below_pot, own_pot, above_pot):
@@ -92,9 +92,9 @@
     cells = band_count * total * rows * lanes
     return pl.pallas_call(
         filter_kernel,
-        out_shape=(jax.ShapeDtypeStruct(shape, jnp.float32), jax.ShapeDtypeStruct(shape, jnp.float32)),
+        out_shape=jax.ShapeDtypeStruct((2, *shape), jnp.float32),
         in_specs=[pl.BlockSpec(memory_space=pltpu.VMEM)] * 6,
-        out_specs=(pl.BlockSpec(memory_space=pltpu.VMEM), pl.BlockSpec(memory_space=pltpu.VMEM)),
+        out_specs=pl.BlockSpec(memory_space=pltpu.VMEM),
         scratch_shapes=[pltpu.VMEM((band_count, total, rows, lanes), jnp.float32)] * 3
         + [pltpu.VMEM((total, rows, lanes), jnp.float32)],
         cost_estimate=pl.CostEstimate(flops=30 * cells * 4, transcendentals=0, bytes_accessed=4 * cells * 3),
@@ -171,16 +171,15 @@
     above = lax.ppermute(trial_bands[:, :width], "grid", [((i + 1) % count, i) for i in range(count)])
     below_pot = lax.ppermute(potential[potential.shape[0] - width :], ("band", "grid"), replica_pairs(1))
     above_pot = lax.ppermute(potential[:width], ("band", "grid"), replica_pairs(-1))
-    current, applied = filter_and_image(below, trial_bands, above, below_pot, potential, above_pot)
+    stacked = filter_and_image(below, trial_bands, above, below_pot, potential, above_pot)
+    current = stacked[0]
     band_devices = lax.axis_size("band")
     total_bands = band_count * band_devices
     cell_count = current.shape[1] * current.shape[2] * current.shape[3]
     cell_total = cell_count * lax.axis_size("grid")
     inverse_cells = 1.0 / cell_total
     first_band = lax.axis_index("band") * band_count
-    both = jnp.stack(
-        [current.reshape(band_count, cell_count), applied.reshape(band_count, cell_count)]
-    ).reshape(2, band_count, band_devices, cell_count // band_devices)
+    both = stacked.reshape(2, band_count, band_devices, cell_count // band_devices)
     moved = lax.all_to_all(both, "band", 2, 1, tiled=True)
     bands_here = moved[0].reshape(total_bands, -1)
     image_here = moved[1].reshape(total_bands, -1)

time: 165 us -> 164 us (level)
    reshape x0 -> x2, local copies, waits for them, and re-layouts: none -> 1.71 us  [on_device(): stacked.reshape(2, band_count, band_devices, cell_count // band_devices)]
where the time goes in v17:
time: 164 us; the launch traced here: 163 us
  starting transfers between devices  64.3 us (39%)
  waiting for transfers between devices  43.2 us (26%)
  blocking collectives  32.5 us (20%)
  Pallas kernels  14.2 us (9%)
  local copies, waits for them, and re-layouts  6.21 us (4%)
    ppermute x9, starting transfers between devices, butterfly_sum(): values = values + lax.ppermute(values, axis, pairs)  43.1 us
    ppermute x9, waiting for transfers between devices, butterfly_sum(): values = values + lax.ppermute(values, axis, pairs)  32.5 us
    all_to_all x1, blocking collectives, on_device(): moved = lax.all_to_all(both, 'band', 2, 1, tiled=True)  32.5 us
    ppermute x1, starting transfers between devices, on_device(): lax.ppermute(potential[potential.shape[0] - width:], ('band', 'grid'), re...  13.8 us
    ppermute x1, waiting for transfers between devices, on_device(): lax.ppermute(potential[:width], ('band', 'grid'), replica_pairs(-1))  10.6 us
    pallas_call x1, Pallas kernels, rayleigh_ritz(): pl.pallas_call(rayleigh_ritz_kernel, out_shape=(jax.ShapeDtypeStruct((ban...  8.36 us
    pallas_call x1, Pallas kernels, filter_and_image(): pl.pallas_call(filter_kernel, out_shape=jax.ShapeDtypeStruct((2, *shape),...  5.88 us
    ppermute x1, starting transfers between devices, on_device(): lax.ppermute(trial_bands[:, :width], 'grid', [((i + 1) % count, i) for i...  3.64 us
  transfers between devices with their start and end apart: 13, of which 10 were waited for; matrix products, arithmetic and copies ran while one was open for 0% of the time, Pallas kernels for 0%

profile of v17, /device:TPU:24, one launch (start us, length us, event | category | flops | bytes accessed | tf_op | source)
XLA Modules:
  0.0 163.0 jit_solution(13992092869531176482)
XLA Ops:
  0.6 1.9 %collective-permute-start = (f32[2,10,32,128]{3,2,1,0:T(8,128)}, f32[2,10,32,128]{3,2,1,0:T(8,128)S(1)}, u32[]{:S(2)}, u32[]{:S(2)}) collective-permute-start(f32[2,10,32,128]{3,2,1,0:T(8,128)} %own_ref.1), channel_id=1, source_target_pairs={{0,1},{1,2},{2,3},{3,4},{4,5},{5,6},{6,7},{7,8},{8,9},{9,10},{10,1... | collective-permute-start | bytes 983048 | tf_op jit(solution)/shard_map/ppermute | solution.py:170
  2.6 3.6 %collective-permute-start.1 = (f32[2,10,32,128]{3,2,1,0:T(8,128)}, f32[2,10,32,128]{3,2,1,0:T(8,128)S(1)}, u32[]{:S(2)}, u32[]{:S(2)}) collective-permute-start(f32[2,10,32,128]{3,2,1,0:T(8,128)} %own_ref.1), channel_id=1, source_target_pairs={{1,0},{2,1},{3,2},{4,3},{5,4},{6,5},{7,6},{8,7},{9,8},{10,9},{11,1... | collective-permute-start | bytes 983048 | tf_op jit(solution)/shard_map/ppermute | solution.py:171
  6.2 13.8 %collective-permute-start.2 = (f32[10,32,128]{2,1,0:T(8,128)}, f32[10,32,128]{2,1,0:T(8,128)S(1)}, u32[]{:S(2)}, u32[]{:S(2)}) collective-permute-start(f32[10,32,128]{2,1,0:T(8,128)} %own_pot.1), channel_id=1, source_target_pairs={{79,0},{95,16},{111,32},{127,48},{15,64},{31,80},{47,96},{63,112},... | collective-permute-start | bytes 491528 | tf_op jit(solution)/shard_map/ppermute | solution.py:172
  20.0 1.9 %collective-permute-start.3 = (f32[10,32,128]{2,1,0:T(8,128)}, f32[10,32,128]{2,1,0:T(8,128)S(1)}, u32[]{:S(2)}, u32[]{:S(2)}) collective-permute-start(f32[10,32,128]{2,1,0:T(8,128)} %own_pot.1), channel_id=1, source_target_pairs={{1,0},{17,16},{33,32},{49,48},{65,64},{81,80},{97,96},{113,112},{1... | collective-permute-start | bytes 491528 | tf_op jit(solution)/shard_map/ppermute | solution.py:173
  21.9 10.6 %collective-permute-done.3.above_pot = f32[10,32,128]{2,1,0:T(8,128)S(1)} collective-permute-done((f32[10,32,128]{2,1,0:T(8,128)}, f32[10,32,128]{2,1,0:T(8,128)S(1)}, u32[]{:S(2)}, u32[]{:S(2)}) %collective-permute-start.3) | collective-permute-done | bytes 163872 | tf_op jit(solution)/shard_map/ppermute | solution.py:173
  32.6 0.6 copy-done.4
  33.3 0.7 copy-done.2
  34.1 5.9 %shard_map.49 = f32[2,2,10,32,128]{4,3,2,1,0:T(8,128)} custom-call(f32[2,10,32,128]{3,2,1,0:T(8,128)} %copy-done.1, f32[2,10,32,128]{3,2,1,0:T(8,128)} %own_ref.1, f32[2,10,32,128]{3,2,1,0:T(8,128)} %copy-done.2, f32[10,32,128]{2,1,0:T(8,128)} %copy-done.3, f32[10,32,128]{2,1,0:T(8,128)} %own_pot.1, f32[10,32,128]{2,1,0:T(8,128)} %copy-done.4), custom_call_target="tpu_custom_call" | custom-call | flops 29491200 | bytes 2949120 | tf_op jit(solution)/shard_map/pallas_call | solution.py:93
  39.9 1.2 reshape.48
  41.7 32.5 %all_to_all.15 = f32[2,2,32,1280]{3,1,0,2:T(2,128)S(1)} all-to-all(f32[2,2,32,1280]{3,1,0,2:T(2,128)S(1)} %copy.10), channel_id=1, replica_groups=mesh['band'=32,'grid'=16] {'band'}, dimensions={2} | all-to-all | bytes 1310720 | tf_op jit(solution)/shard_map/all_to_all | solution.py:183
  76.0 2.0 %collective-permute-start.4 = (f32[8256]{0:T(1024)S(1)}, f32[8256]{0:T(1024)S(1)}, u32[]{:S(2)}, u32[]{:S(2)}) collective-permute-start(f32[8256]{0:T(1024)S(1)} %constant_dynamic-update-slice_fusion), channel_id=1, source_target_pairs={{0,16},{16,0},{32,48},{48,32},{64,80},{80,64},{96,112},{112,96},{1... | collective-permute-start | bytes 99080 | tf_op jit(solution)/shard_map/ppermute | solution.py:21
  78.0 4.1 %collective-permute-done.4 = f32[8256]{0:T(1024)S(1)} collective-permute-done((f32[8256]{0:T(1024)S(1)}, f32[8256]{0:T(1024)S(1)}, u32[]{:S(2)}, u32[]{:S(2)}) %collective-permute-start.4) | collective-permute-done | bytes 33056 | tf_op jit(solution)/shard_map/ppermute | solution.py:21
  82.1 2.7 %collective-permute-start.5 = (f32[8256]{0:T(1024)S(1)}, f32[8256]{0:T(1024)S(1)}, u32[]{:S(2)}, u32[]{:S(2)}) collective-permute-start(f32[8256]{0:T(1024)S(1)} %add.30), channel_id=1, source_target_pairs={{0,32},{16,48},{32,0},{48,16},{64,96},{80,112},{96,64},{112,80},{1... | collective-permute-start | bytes 99080 | tf_op jit(solution)/shard_map/ppermute | solution.py:21
  84.9 4.0 %collective-permute-done.5 = f32[8256]{0:T(1024)S(1)} collective-permute-done((f32[8256]{0:T(1024)S(1)}, f32[8256]{0:T(1024)S(1)}, u32[]{:S(2)}, u32[]{:S(2)}) %collective-permute-start.5) | collective-permute-done | bytes 33056 | tf_op jit(solution)/shard_map/ppermute | solution.py:21
  88.9 5.2 %collective-permute-start.6 = (f32[8256]{0:T(1024)S(1)}, f32[8256]{0:T(1024)S(1)}, u32[]{:S(2)}, u32[]{:S(2)}) collective-permute-start(f32[8256]{0:T(1024)S(1)} %add.31), channel_id=1, source_target_pairs={{0,64},{16,80},{32,96},{48,112},{64,0},{80,16},{96,32},{112,48},{1... | collective-permute-start | bytes 99080 | tf_op jit(solution)/shard_map/ppermute | solution.py:21
  94.1 5.4 %collective-permute-done.6 = f32[8256]{0:T(1024)S(1)} collective-permute-done((f32[8256]{0:T(1024)S(1)}, f32[8256]{0:T(1024)S(1)}, u32[]{:S(2)}, u32[]{:S(2)}) %collective-permute-start.6) | collective-permute-done | bytes 33056 | tf_op jit(solution)/shard_map/ppermute | solution.py:21
  99.4 1.9 %collective-permute-start.7 = (f32[8256]{0:T(1024)S(1)}, f32[8256]{0:T(1024)S(1)}, u32[]{:S(2)}, u32[]{:S(2)}) collective-permute-start(f32[8256]{0:T(1024)S(1)} %add.32), channel_id=1, source_target_pairs={{0,128},{16,144},{32,160},{48,176},{64,192},{80,208},{96,224},{112... | collective-permute-start | bytes 99080 | tf_op jit(solution)/shard_map/ppermute | solution.py:21
  101.3 3.9 %collective-permute-done.7 = f32[8256]{0:T(1024)S(1)} collective-permute-done((f32[8256]{0:T(1024)S(1)}, f32[8256]{0:T(1024)S(1)}, u32[]{:S(2)}, u32[]{:S(2)}) %collective-permute-start.7) | collective-permute-done | bytes 33056 | tf_op jit(solution)/shard_map/ppermute | solution.py:21
  105.3 2.9 %collective-permute-start.8 = (f32[8256]{0:T(1024)S(1)}, f32[8256]{0:T(1024)S(1)}, u32[]{:S(2)}, u32[]{:S(2)}) collective-permute-start(f32[8256]{0:T(1024)S(1)} %add.33), channel_id=1, source_target_pairs={{0,384},{16,400},{32,416},{48,432},{64,448},{80,464},{96,480},{112... | collective-permute-start | bytes 99080 | tf_op jit(solution)/shard_map/ppermute | solution.py:21
  108.2 4.1 %collective-permute-done.8 = f32[8256]{0:T(1024)S(1)} collective-permute-done((f32[8256]{0:T(1024)S(1)}, f32[8256]{0:T(1024)S(1)}, u32[]{:S(2)}, u32[]{:S(2)}) %collective-permute-start.8) | collective-permute-done | bytes 33056 | tf_op jit(solution)/shard_map/ppermute | solution.py:21
  112.3 11.8 %collective-permute-start.9 = (f32[8256]{0:T(1024)S(1)}, f32[8256]{0:T(1024)S(1)}, u32[]{:S(2)}, u32[]{:S(2)}) collective-permute-start(f32[8256]{0:T(1024)S(1)} %add.34), channel_id=1, source_target_pairs={{0,1},{1,0},{2,3},{3,2},{4,5},{5,4},{6,7},{7,6},{8,9},{9,8},{10,11... | collective-permute-start | bytes 99080 | tf_op jit(solution)/shard_map/ppermute | solution.py:21
  124.2 0.8 collective-permute-done.9
  125.0 1.9 %collective-permute-start.10 = (f32[8256]{0:T(1024)S(1)}, f32[8256]{0:T(1024)S(1)}, u32[]{:S(2)}, u32[]{:S(2)}) collective-permute-start(f32[8256]{0:T(1024)S(1)} %add.35), channel_id=1, source_target_pairs={{0,2},{1,3},{2,0},{3,1},{4,6},{5,7},{6,4},{7,5},{8,10},{9,11},{10,... | collective-permute-start | bytes 99080 | tf_op jit(solution)/shard_map/ppermute | solution.py:21
  126.9 3.9 %collective-permute-done.10 = f32[8256]{0:T(1024)S(1)} collective-permute-done((f32[8256]{0:T(1024)S(1)}, f32[8256]{0:T(1024)S(1)}, u32[]{:S(2)}, u32[]{:S(2)}) %collective-permute-start.10) | collective-permute-done | bytes 33056 | tf_op jit(solution)/shard_map/ppermute | solution.py:21
  130.9 4.5 %collective-permute-start.11 = (f32[8256]{0:T(1024)S(1)}, f32[8256]{0:T(1024)S(1)}, u32[]{:S(2)}, u32[]{:S(2)}) collective-permute-start(f32[8256]{0:T(1024)S(1)} %add.36), channel_id=1, source_target_pairs={{0,6},{1,7},{2,4},{3,5},{4,2},{5,3},{6,0},{7,1},{8,14},{9,15},{10,... | collective-permute-start | bytes 99080 | tf_op jit(solution)/shard_map/ppermute | solution.py:21
  135.4 2.5 %collective-permute-done.11 = f32[8256]{0:T(1024)S(1)} collective-permute-done((f32[8256]{0:T(1024)S(1)}, f32[8256]{0:T(1024)S(1)}, u32[]{:S(2)}, u32[]{:S(2)}) %collective-permute-start.11) | collective-permute-done | bytes 33056 | tf_op jit(solution)/shard_map/ppermute | solution.py:21
  137.9 10.1 %collective-permute-start.12 = (f32[8256]{0:T(1024)S(1)}, f32[8256]{0:T(1024)S(1)}, u32[]{:S(2)}, u32[]{:S(2)}) collective-permute-start(f32[8256]{0:T(1024)S(1)} %add.37), channel_id=1, source_target_pairs={{0,8},{1,9},{2,10},{3,11},{4,12},{5,13},{6,14},{7,15},{8,0},{9,1},... | collective-permute-start | bytes 99080 | tf_op jit(solution)/shard_map/ppermute | solution.py:21
  148.0 0.7 slice_bitcast_fusion
  148.7 3.7 %collective-permute-done.12 = f32[8256]{0:T(1024)S(1)} collective-permute-done((f32[8256]{0:T(1024)S(1)}, f32[8256]{0:T(1024)S(1)}, u32[]{:S(2)}, u32[]{:S(2)}) %collective-permute-start.12) | collective-permute-done | bytes 33056 | tf_op jit(solution)/shard_map/ppermute | solution.py:21
  152.5 0.7 slice.46.subspace_ref
  153.2 0.7 copy.12.norms_ref
  154.7 8.4 %shard_map.50 = (f32[2,64]{1,0:T(2,128)}, f32[1,2]{1,0:T(1,128)}) custom-call(s32[1]{0:T(128)} %bitcast.1.first_ref, f32[64,64]{1,0:T(8,128)} %fusion.margin_ref, f32[64,64]{1,0:T(8,128)} %slice.46.subspace_ref, f32[64,1]{1,0:T(8,128)} %copy.12.norms_ref), custom_call_target="tpu_custom_call" | custom-call | flops 1572864 | bytes 65536 | tf_op jit(solution)/shard_map/pallas_call | solution.py:143
  (37 shorter events, 3.3 us)
Async XLA Ops:
  0.6 31.9 %collective-permute-start = (f32[2,10,32,128]{3,2,1,0:T(8,128)}, f32[2,10,32,128]{3,2,1,0:T(8,128)S(1)}, u32[]{:S(2)}, u32[]{:S(2)}) collective-permute-start(f32[2,10,32,128]{3,2,1,0:T(8,128)} %own_ref.1), channel_id=1, source_target_pairs={{0,1},{1,2},{2,3},{3,4},{4,5},{5,6},{6,7},{7,8},{8,9},{9,10},{10,1... | collective-permute-start | bytes 983048 | tf_op jit(solution)/shard_map/ppermute | solution.py:170
  2.6 30.0 %collective-permute-start.1 = (f32[2,10,32,128]{3,2,1,0:T(8,128)}, f32[2,10,32,128]{3,2,1,0:T(8,128)S(1)}, u32[]{:S(2)}, u32[]{:S(2)}) collective-permute-start(f32[2,10,32,128]{3,2,1,0:T(8,128)} %own_ref.1), channel_id=1, source_target_pairs={{1,0},{2,1},{3,2},{4,3},{5,4},{6,5},{7,6},{8,7},{9,8},{10,9},{11,1... | collective-permute-start | bytes 983048 | tf_op jit(solution)/shard_map/ppermute | solution.py:171
  6.2 15.7 %collective-permute-start.2 = (f32[10,32,128]{2,1,0:T(8,128)}, f32[10,32,128]{2,1,0:T(8,128)S(1)}, u32[]{:S(2)}, u32[]{:S(2)}) collective-permute-start(f32[10,32,128]{2,1,0:T(8,128)} %own_pot.1), channel_id=1, source_target_pairs={{79,0},{95,16},{111,32},{127,48},{15,64},{31,80},{47,96},{63,112},... | collective-permute-start | bytes 491528 | tf_op jit(solution)/shard_map/ppermute | solution.py:172
  20.0 12.6 %collective-permute-start.3 = (f32[10,32,128]{2,1,0:T(8,128)}, f32[10,32,128]{2,1,0:T(8,128)S(1)}, u32[]{:S(2)}, u32[]{:S(2)}) collective-permute-start(f32[10,32,128]{2,1,0:T(8,128)} %own_pot.1), channel_id=1, source_target_pairs={{1,0},{17,16},{33,32},{49,48},{65,64},{81,80},{97,96},{113,112},{1... | collective-permute-start | bytes 491528 | tf_op jit(solution)/shard_map/ppermute | solution.py:173
  21.9 10.6 %copy-start.3 = (f32[10,32,128]{2,1,0:T(8,128)}, f32[10,32,128]{2,1,0:T(8,128)S(1)}, u32[]{:S(2)}) copy-start(f32[10,32,128]{2,1,0:T(8,128)S(1)} %collective-permute-done.2.below_pot) | copy-start | bytes 491524
  32.5 0.7 copy-start.4
  32.6 0.8 copy-start.1
  33.3 0.7 copy-start.2
  75.9 72.1 %copy-start = (f32[2,2,10,32,128]{4,3,2,1,0:T(8,128)S(1)}, f32[2,2,10,32,128]{4,3,2,1,0:T(8,128)}, u32[]{:S(2)}) copy-start(f32[2,2,10,32,128]{4,3,2,1,0:T(8,128)} %shard_map.49) | copy-start | bytes 1966084
  76.0 6.2 %collective-permute-start.4 = (f32[8256]{0:T(1024)S(1)}, f32[8256]{0:T(1024)S(1)}, u32[]{:S(2)}, u32[]{:S(2)}) collective-permute-start(f32[8256]{0:T(1024)S(1)} %constant_dynamic-update-slice_fusion), channel_id=1, source_target_pairs={{0,16},{16,0},{32,48},{48,32},{64,80},{80,64},{96,112},{112,96},{1... | collective-permute-start | bytes 99080 | tf_op jit(solution)/shard_map/ppermute | solution.py:21
  82.1 6.7 %collective-permute-start.5 = (f32[8256]{0:T(1024)S(1)}, f32[8256]{0:T(1024)S(1)}, u32[]{:S(2)}, u32[]{:S(2)}) collective-permute-start(f32[8256]{0:T(1024)S(1)} %add.30), channel_id=1, source_target_pairs={{0,32},{16,48},{32,0},{48,16},{64,96},{80,112},{96,64},{112,80},{1... | collective-permute-start | bytes 99080 | tf_op jit(solution)/shard_map/ppermute | solution.py:21
  88.9 10.5 %collective-permute-start.6 = (f32[8256]{0:T(1024)S(1)}, f32[8256]{0:T(1024)S(1)}, u32[]{:S(2)}, u32[]{:S(2)}) collective-permute-start(f32[8256]{0:T(1024)S(1)} %add.31), channel_id=1, source_target_pairs={{0,64},{16,80},{32,96},{48,112},{64,0},{80,16},{96,32},{112,48},{1... | collective-permute-start | bytes 99080 | tf_op jit(solution)/shard_map/ppermute | solution.py:21
  99.4 5.8 %collective-permute-start.7 = (f32[8256]{0:T(1024)S(1)}, f32[8256]{0:T(1024)S(1)}, u32[]{:S(2)}, u32[]{:S(2)}) collective-permute-start(f32[8256]{0:T(1024)S(1)} %add.32), channel_id=1, source_target_pairs={{0,128},{16,144},{32,160},{48,176},{64,192},{80,208},{96,224},{112... | collective-permute-start | bytes 99080 | tf_op jit(solution)/shard_map/ppermute | solution.py:21
  105.3 7.1 %collective-permute-start.8 = (f32[8256]{0:T(1024)S(1)}, f32[8256]{0:T(1024)S(1)}, u32[]{:S(2)}, u32[]{:S(2)}) collective-permute-start(f32[8256]{0:T(1024)S(1)} %add.33), channel_id=1, source_target_pairs={{0,384},{16,400},{32,416},{48,432},{64,448},{80,464},{96,480},{112... | collective-permute-start | bytes 99080 | tf_op jit(solution)/shard_map/ppermute | solution.py:21
  112.3 12.7 %collective-permute-start.9 = (f32[8256]{0:T(1024)S(1)}, f32[8256]{0:T(1024)S(1)}, u32[]{:S(2)}, u32[]{:S(2)}) collective-permute-start(f32[8256]{0:T(1024)S(1)} %add.34), channel_id=1, source_target_pairs={{0,1},{1,0},{2,3},{3,2},{4,5},{5,4},{6,7},{7,6},{8,9},{9,8},{10,11... | collective-permute-start | bytes 99080 | tf_op jit(solution)/shard_map/ppermute | solution.py:21
  125.0 5.8 %collective-permute-start.10 = (f32[8256]{0:T(1024)S(1)}, f32[8256]{0:T(1024)S(1)}, u32[]{:S(2)}, u32[]{:S(2)}) collective-permute-start(f32[8256]{0:T(1024)S(1)} %add.35), channel_id=1, source_target_pairs={{0,2},{1,3},{2,0},{3,1},{4,6},{5,7},{6,4},{7,5},{8,10},{9,11},{10,... | collective-permute-start | bytes 99080 | tf_op jit(solution)/shard_map/ppermute | solution.py:21
  130.9 7.1 %collective-permute-start.11 = (f32[8256]{0:T(1024)S(1)}, f32[8256]{0:T(1024)S(1)}, u32[]{:S(2)}, u32[]{:S(2)}) collective-permute-start(f32[8256]{0:T(1024)S(1)} %add.36), channel_id=1, source_target_pairs={{0,6},{1,7},{2,4},{3,5},{4,2},{5,3},{6,0},{7,1},{8,14},{9,15},{10,... | collective-permute-start | bytes 99080 | tf_op jit(solution)/shard_map/ppermute | solution.py:21
  137.9 14.6 %collective-permute-start.12 = (f32[8256]{0:T(1024)S(1)}, f32[8256]{0:T(1024)S(1)}, u32[]{:S(2)}, u32[]{:S(2)}) collective-permute-start(f32[8256]{0:T(1024)S(1)} %add.37), channel_id=1, source_target_pairs={{0,8},{1,9},{2,10},{3,11},{4,12},{5,13},{6,14},{7,15},{8,0},{9,1},... | collective-permute-start | bytes 99080 | tf_op jit(solution)/shard_map/ppermute | solution.py:21

commit v18 on v10

--- a/solution.py
+++ b/solution.py
@@ -36,9 +36,9 @@
     return partner
 
 
-def filter_kernel(below_ref, own_ref, above_ref, below_pot, own_pot, above_pot, filtered_ref, image_ref,
+def filter_kernel(below_ref, own_ref, above_ref, below_pot, own_pot, above_pot, both_ref,
                   first_buf, second_buf, third_buf, wide_pot):
-    band_count, own_planes = filtered_ref.shape[0], filtered_ref.shape[1]
+    band_count, own_planes = both_ref.shape[1], both_ref.shape[2]
     width = below_ref.shape[1]
     for at, source, pot in ((0, below_ref, below_pot), (width, own_ref, own_pot),
                             (width + own_planes, above_ref, above_pot)):
@@ -79,11 +79,11 @@
         older, field, spare = field, spare, older
         sigma_now = sigma_next
     final = bufs[field]
-    filtered_ref[...] = final[:, width : width + own_planes]
+    both_ref[0] = final[:, width : width + own_planes]
 
     for plane in range(width, width + own_planes):
         for band in range(band_count):
-            image_ref[band, plane - width], _ = apply(final, band, plane)
+            both_ref[1, band, plane - width], _ = apply(final, band, plane)
 
 
 def filter_and_image(below, own, above, below_pot, own_pot, above_pot):
@@ -94,9 +94,9 @@
     cells = band_count * total * rows * lanes
     return pl.pallas_call(
         filter_kernel,
-        out_shape=(jax.ShapeDtypeStruct(shape, jnp.float32), jax.ShapeDtypeStruct(shape, jnp.float32)),
+        out_shape=jax.ShapeDtypeStruct((2, *shape), jnp.float32),
         in_specs=[pl.BlockSpec(memory_space=pltpu.VMEM)] * 6,
-        out_specs=(pl.BlockSpec(memory_space=pltpu.VMEM), pl.BlockSpec(memory_space=pltpu.VMEM)),
+        out_specs=pl.BlockSpec(memory_space=pltpu.VMEM),
         scratch_shapes=[pltpu.VMEM((band_count, total, rows, lanes), jnp.float32)] * 3
         + [pltpu.VMEM((total, rows, lanes), jnp.float32)],
         cost_estimate=pl.CostEstimate(flops=30 * cells * 4, transcendentals=0, bytes_accessed=4 * cells * 3),
@@ -106,8 +106,8 @@
 def rayleigh_ritz_kernel(scale, first_ref, packed_ref, projected_ref, residual_ref, projected_buf, residual_buf):
     size = packed_ref.shape[0]
     work = packed_ref[:, 0:size] * scale
-    rest = packed_ref[:, size : 2 * size] * scale
-    norms = packed_ref[:, 2 * size : 2 * size + 1] * scale
+    rest = packed_ref[:, 128 : 128 + size] * scale
+    norms = packed_ref[:, 192:193] * scale
     rows = lax.broadcasted_iota(jnp.int32, (size, size), 0)
     cols = lax.broadcasted_iota(jnp.int32, (size, size), 1)
     row_index = rows[:, :1]
@@ -135,7 +135,9 @@
     first = first_ref[0]
     count = projected_ref.shape[0]
     projected_ref[...] = projected_buf[pl.ds(first, count), :]
-    residual_ref[...] = residual_buf[pl.ds(first, count), :]
+    picked = jnp.broadcast_to(residual_buf[pl.ds(first, count), :], (count, count))
+    diagonal = lax.broadcasted_iota(jnp.int32, (count, count), 0) == lax.broadcasted_iota(jnp.int32, (count, count), 1)
+    residual_ref[...] = jnp.sum(jnp.where(diagonal, picked, 0.0), axis=0, keepdims=True)
 
 
 def rayleigh_ritz(first_band, band_count, packed, scale):
@@ -143,7 +145,7 @@
     return pl.pallas_call(
         functools.partial(rayleigh_ritz_kernel, scale),
         out_shape=(jax.ShapeDtypeStruct((band_count, size), jnp.float32),
-                   jax.ShapeDtypeStruct((band_count, 1), jnp.float32)),
+                   jax.ShapeDtypeStruct((1, band_count), jnp.float32)),
         in_specs=[pl.BlockSpec(memory_space=pltpu.SMEM), pl.BlockSpec(memory_space=pltpu.VMEM)],
         out_specs=(pl.BlockSpec(memory_space=pltpu.VMEM), pl.BlockSpec(memory_space=pltpu.VMEM)),
         scratch_shapes=[pltpu.VMEM((size, size), jnp.float32), pltpu.VMEM((size, 1), jnp.float32)],
@@ -171,16 +173,15 @@
     above = lax.ppermute(trial_bands[:, :width], "grid", [((i + 1) % count, i) for i in range(count)])
     below_pot = lax.ppermute(potential[potential.shape[0] - width :], ("band", "grid"), replica_pairs(1))
     above_pot = lax.ppermute(potential[:width], ("band", "grid"), replica_pairs(-1))
-    current, applied = filter_and_image(below, trial_bands, above, below_pot, potential, above_pot)
+    stacked = filter_and_image(below, trial_bands, above, below_pot, potential, above_pot)
+    current = stacked[0]
     band_devices = lax.axis_size("band")
     total_bands = band_count * band_devices
     cell_count = current.shape[1] * current.shape[2] * current.shape[3]
     cell_total = cell_count * lax.axis_size("grid")
     inverse_cells = 1.0 / cell_total
     first_band = lax.axis_index("band") * band_count
-    both = jnp.stack(
-        [current.reshape(band_count, cell_count), applied.reshape(band_count, cell_count)]
-    ).reshape(2, band_count, band_devices, cell_count // band_devices)
+    both = stacked.reshape(2, band_count, band_devices, cell_count // band_devices)
     moved = lax.all_to_all(both, "band", 2, 1, tiled=True)
     bands_here = moved[0].reshape(total_bands, -1)
     image_here = moved[1].reshape(total_bands, -1)
@@ -191,10 +192,15 @@
         image_here, bands_here.T, precision=lax.Precision.HIGHEST, preferred_element_type=jnp.float32
     )
     norm_part = jnp.sum(image_here * image_here, axis=1)
+    size = total_bands
     margin_part = (margin_part + margin_part.T) / 2
-    packed = jnp.concatenate([margin_part, image_part, norm_part[:, None]], axis=1)
+    packed = jnp.concatenate(
+        [margin_part, jnp.zeros((size, 128 - size), jnp.float32), image_part, norm_part[:, None],
+         jnp.zeros((size, 63), jnp.float32)],
+        axis=1,
+    )
+    packed = butterfly_sum(packed, "band", [flip(1), flip(2), flip(4), flip(8), ring_of_four(0, 8)])
     packed = butterfly_sum(packed, "grid", [flip(1), flip(2), ring_of_four(0, 2), flip(8)])
-    packed = butterfly_sum(packed, "band", [flip(1), flip(2), flip(4), flip(8), ring_of_four(0, 8)])
     projected_rows, residual_rows = rayleigh_ritz(first_band, band_count, packed, inverse_cells)
     residual_rows = residual_rows.reshape(-1)
     return (current, projected_rows, residual_rows)

time: 176 us -> 167 us (0.949)
  waiting for transfers between devices: 58.2 us -> 43.1 us
  starting transfers between devices: 59.6 us -> 68.6 us
  Pallas kernels: 16.8 us -> 14.4 us
    ppermute x9, waiting for transfers between devices: 47.6 us -> 32.4 us  [butterfly_sum(): values = values + lax.ppermute(values, axis, pairs)]
    ppermute x9, starting transfers between devices: 38.3 us -> 47.4 us  [butterfly_sum(): values = values + lax.ppermute(values, axis, pairs)]
    pallas_call x1, Pallas kernels: 11 us -> 8.48 us  [rayleigh_ritz(): pl.pallas_call(functools.partial(rayleigh_ritz_kernel, scale), out_shape=...]
where the time goes in v18:
time: 167 us; the launch traced here: 166 us
  starting transfers between devices  68.6 us (41%)
  waiting for transfers between devices  43.1 us (26%)
  blocking collectives  32.5 us (19%)
  Pallas kernels  14.4 us (9%)
  local copies, waits for them, and re-layouts  4.65 us (3%)
    ppermute x9, starting transfers between devices, butterfly_sum(): values = values + lax.ppermute(values, axis, pairs)  47.4 us
    all_to_all x1, blocking collectives, on_device(): moved = lax.all_to_all(both, 'band', 2, 1, tiled=True)  32.5 us
    ppermute x9, waiting for transfers between devices, butterfly_sum(): values = values + lax.ppermute(values, axis, pairs)  32.4 us
    ppermute x1, starting transfers between devices, on_device(): lax.ppermute(potential[potential.shape[0] - width:], ('band', 'grid'), re...  13.8 us
    ppermute x1, waiting for transfers between devices, on_device(): lax.ppermute(potential[:width], ('band', 'grid'), replica_pairs(-1))  10.6 us
    pallas_call x1, Pallas kernels, rayleigh_ritz(): pl.pallas_call(functools.partial(rayleigh_ritz_kernel, scale), out_shape=...  8.48 us
    pallas_call x1, Pallas kernels, filter_and_image(): pl.pallas_call(filter_kernel, out_shape=jax.ShapeDtypeStruct((2, *shape),...  5.88 us
    ppermute x1, starting transfers between devices, on_device(): lax.ppermute(trial_bands[:, :width], 'grid', [((i + 1) % count, i) for i...  3.64 us
  transfers between devices with their start and end apart: 13, of which 10 were waited for; matrix products, arithmetic and copies ran while one was open for 0% of the time, Pallas kernels for 0%

profile of v18, /device:TPU:24, one launch (start us, length us, event | category | flops | bytes accessed | tf_op | source)
XLA Modules:
  0.0 165.9 jit_solution(14219222036060918202)
XLA Ops:
  0.6 1.9 %collective-permute-start = (f32[2,10,32,128]{3,2,1,0:T(8,128)}, f32[2,10,32,128]{3,2,1,0:T(8,128)S(1)}, u32[]{:S(2)}, u32[]{:S(2)}) collective-permute-start(f32[2,10,32,128]{3,2,1,0:T(8,128)} %own_ref.1), channel_id=1, source_target_pairs={{0,1},{1,2},{2,3},{3,4},{4,5},{5,6},{6,7},{7,8},{8,9},{9,10},{10,1... | collective-permute-start | bytes 983048 | tf_op jit(solution)/shard_map/ppermute | solution.py:172
  2.6 3.6 %collective-permute-start.1 = (f32[2,10,32,128]{3,2,1,0:T(8,128)}, f32[2,10,32,128]{3,2,1,0:T(8,128)S(1)}, u32[]{:S(2)}, u32[]{:S(2)}) collective-permute-start(f32[2,10,32,128]{3,2,1,0:T(8,128)} %own_ref.1), channel_id=1, source_target_pairs={{1,0},{2,1},{3,2},{4,3},{5,4},{6,5},{7,6},{8,7},{9,8},{10,9},{11,1... | collective-permute-start | bytes 983048 | tf_op jit(solution)/shard_map/ppermute | solution.py:173
  6.2 13.8 %collective-permute-start.2 = (f32[10,32,128]{2,1,0:T(8,128)}, f32[10,32,128]{2,1,0:T(8,128)S(1)}, u32[]{:S(2)}, u32[]{:S(2)}) collective-permute-start(f32[10,32,128]{2,1,0:T(8,128)} %own_pot.1), channel_id=1, source_target_pairs={{79,0},{95,16},{111,32},{127,48},{15,64},{31,80},{47,96},{63,112},... | collective-permute-start | bytes 491528 | tf_op jit(solution)/shard_map/ppermute | solution.py:174
  20.0 1.9 %collective-permute-start.3 = (f32[10,32,128]{2,1,0:T(8,128)}, f32[10,32,128]{2,1,0:T(8,128)S(1)}, u32[]{:S(2)}, u32[]{:S(2)}) collective-permute-start(f32[10,32,128]{2,1,0:T(8,128)} %own_pot.1), channel_id=1, source_target_pairs={{1,0},{17,16},{33,32},{49,48},{65,64},{81,80},{97,96},{113,112},{1... | collective-permute-start | bytes 491528 | tf_op jit(solution)/shard_map/ppermute | solution.py:175
  21.9 10.6 %collective-permute-done.3.above_pot = f32[10,32,128]{2,1,0:T(8,128)S(1)} collective-permute-done((f32[10,32,128]{2,1,0:T(8,128)}, f32[10,32,128]{2,1,0:T(8,128)S(1)}, u32[]{:S(2)}, u32[]{:S(2)}) %collective-permute-start.3) | collective-permute-done | bytes 163872 | tf_op jit(solution)/shard_map/ppermute | solution.py:175
  32.6 0.6 copy-done.4
  33.3 0.7 copy-done.2
  34.1 5.9 %shard_map.49 = f32[2,2,10,32,128]{4,3,2,1,0:T(8,128)} custom-call(f32[2,10,32,128]{3,2,1,0:T(8,128)} %copy-done.1, f32[2,10,32,128]{3,2,1,0:T(8,128)} %own_ref.1, f32[2,10,32,128]{3,2,1,0:T(8,128)} %copy-done.2, f32[10,32,128]{2,1,0:T(8,128)} %copy-done.3, f32[10,32,128]{2,1,0:T(8,128)} %own_pot.1, f32[10,32,128]{2,1,0:T(8,128)} %copy-done.4), custom_call_target="tpu_custom_call" | custom-call | flops 29491200 | bytes 2949120 | tf_op jit(solution)/shard_map/pallas_call | solution.py:95
  39.9 1.2 reshape.22
  41.1 0.5 copy.10
  41.7 32.5 %all_to_all.15 = f32[2,2,32,1280]{3,1,0,2:T(2,128)S(1)} all-to-all(f32[2,2,32,1280]{3,1,0,2:T(2,128)S(1)} %copy.10), channel_id=1, replica_groups=mesh['band'=32,'grid'=16] {'band'}, dimensions={2} | all-to-all | bytes 1310720 | tf_op jit(solution)/shard_map/all_to_all | solution.py:185
  76.0 1.9 %collective-permute-start.4 = (f32[64,256]{1,0:T(8,128)S(1)}, f32[64,256]{1,0:T(8,128)S(1)}, u32[]{:S(2)}, u32[]{:S(2)}) collective-permute-start(f32[64,256]{1,0:T(8,128)S(1)} %concatenate.3), channel_id=1, source_target_pairs={{0,16},{16,0},{32,48},{48,32},{64,80},{80,64},{96,112},{112,96},{1... | collective-permute-start | bytes 196616 | tf_op jit(solution)/shard_map/ppermute | solution.py:23
  77.9 4.5 %collective-permute-done.4 = f32[64,256]{1,0:T(8,128)S(1)} collective-permute-done((f32[64,256]{1,0:T(8,128)S(1)}, f32[64,256]{1,0:T(8,128)S(1)}, u32[]{:S(2)}, u32[]{:S(2)}) %collective-permute-start.4) | collective-permute-done | bytes 65568 | tf_op jit(solution)/shard_map/ppermute | solution.py:23
  82.4 4.5 %collective-permute-start.5 = (f32[64,256]{1,0:T(8,128)S(1)}, f32[64,256]{1,0:T(8,128)S(1)}, u32[]{:S(2)}, u32[]{:S(2)}) collective-permute-start(f32[64,256]{1,0:T(8,128)S(1)} %add.31), channel_id=1, source_target_pairs={{0,32},{16,48},{32,0},{48,16},{64,96},{80,112},{96,64},{112,80},{1... | collective-permute-start | bytes 196616 | tf_op jit(solution)/shard_map/ppermute | solution.py:23
  86.9 2.7 %collective-permute-done.5 = f32[64,256]{1,0:T(8,128)S(1)} collective-permute-done((f32[64,256]{1,0:T(8,128)S(1)}, f32[64,256]{1,0:T(8,128)S(1)}, u32[]{:S(2)}, u32[]{:S(2)}) %collective-permute-start.5) | collective-permute-done | bytes 65568 | tf_op jit(solution)/shard_map/ppermute | solution.py:23
  89.6 6.5 %collective-permute-start.6 = (f32[64,256]{1,0:T(8,128)S(1)}, f32[64,256]{1,0:T(8,128)S(1)}, u32[]{:S(2)}, u32[]{:S(2)}) collective-permute-start(f32[64,256]{1,0:T(8,128)S(1)} %add.32), channel_id=1, source_target_pairs={{0,64},{16,80},{32,96},{48,112},{64,0},{80,16},{96,32},{112,48},{1... | collective-permute-start | bytes 196616 | tf_op jit(solution)/shard_map/ppermute | solution.py:23
  96.0 4.6 %collective-permute-done.6 = f32[64,256]{1,0:T(8,128)S(1)} collective-permute-done((f32[64,256]{1,0:T(8,128)S(1)}, f32[64,256]{1,0:T(8,128)S(1)}, u32[]{:S(2)}, u32[]{:S(2)}) %collective-permute-start.6) | collective-permute-done | bytes 65568 | tf_op jit(solution)/shard_map/ppermute | solution.py:23
  100.7 1.9 %collective-permute-start.7 = (f32[64,256]{1,0:T(8,128)S(1)}, f32[64,256]{1,0:T(8,128)S(1)}, u32[]{:S(2)}, u32[]{:S(2)}) collective-permute-start(f32[64,256]{1,0:T(8,128)S(1)} %add.33), channel_id=1, source_target_pairs={{0,128},{16,144},{32,160},{48,176},{64,192},{80,208},{96,224},{112... | collective-permute-start | bytes 196616 | tf_op jit(solution)/shard_map/ppermute | solution.py:23
  102.6 4.2 %collective-permute-done.7 = f32[64,256]{1,0:T(8,128)S(1)} collective-permute-done((f32[64,256]{1,0:T(8,128)S(1)}, f32[64,256]{1,0:T(8,128)S(1)}, u32[]{:S(2)}, u32[]{:S(2)}) %collective-permute-start.7) | collective-permute-done | bytes 65568 | tf_op jit(solution)/shard_map/ppermute | solution.py:23
  106.9 2.3 %collective-permute-start.8 = (f32[64,256]{1,0:T(8,128)S(1)}, f32[64,256]{1,0:T(8,128)S(1)}, u32[]{:S(2)}, u32[]{:S(2)}) collective-permute-start(f32[64,256]{1,0:T(8,128)S(1)} %add.34), channel_id=1, source_target_pairs={{0,384},{16,400},{32,416},{48,432},{64,448},{80,464},{96,480},{112... | collective-permute-start | bytes 196616 | tf_op jit(solution)/shard_map/ppermute | solution.py:23
  109.1 5.1 %collective-permute-done.8 = f32[64,256]{1,0:T(8,128)S(1)} collective-permute-done((f32[64,256]{1,0:T(8,128)S(1)}, f32[64,256]{1,0:T(8,128)S(1)}, u32[]{:S(2)}, u32[]{:S(2)}) %collective-permute-start.8) | collective-permute-done | bytes 65568 | tf_op jit(solution)/shard_map/ppermute | solution.py:23
  114.3 12.7 %collective-permute-start.9 = (f32[64,256]{1,0:T(8,128)S(1)}, f32[64,256]{1,0:T(8,128)S(1)}, u32[]{:S(2)}, u32[]{:S(2)}) collective-permute-start(f32[64,256]{1,0:T(8,128)S(1)} %add.35), channel_id=1, source_target_pairs={{0,1},{1,0},{2,3},{3,2},{4,5},{5,4},{6,7},{7,6},{8,9},{9,8},{10,11... | collective-permute-start | bytes 196616 | tf_op jit(solution)/shard_map/ppermute | solution.py:23
  127.0 0.9 collective-permute-done.9
  127.9 1.9 %collective-permute-start.10 = (f32[64,256]{1,0:T(8,128)S(1)}, f32[64,256]{1,0:T(8,128)S(1)}, u32[]{:S(2)}, u32[]{:S(2)}) collective-permute-start(f32[64,256]{1,0:T(8,128)S(1)} %add.36), channel_id=1, source_target_pairs={{0,2},{1,3},{2,0},{3,1},{4,6},{5,7},{6,4},{7,5},{8,10},{9,11},{10,... | collective-permute-start | bytes 196616 | tf_op jit(solution)/shard_map/ppermute | solution.py:23
  129.8 4.3 %collective-permute-done.10 = f32[64,256]{1,0:T(8,128)S(1)} collective-permute-done((f32[64,256]{1,0:T(8,128)S(1)}, f32[64,256]{1,0:T(8,128)S(1)}, u32[]{:S(2)}, u32[]{:S(2)}) %collective-permute-start.10) | collective-permute-done | bytes 65568 | tf_op jit(solution)/shard_map/ppermute | solution.py:23
  134.1 5.1 %collective-permute-start.11 = (f32[64,256]{1,0:T(8,128)S(1)}, f32[64,256]{1,0:T(8,128)S(1)}, u32[]{:S(2)}, u32[]{:S(2)}) collective-permute-start(f32[64,256]{1,0:T(8,128)S(1)} %add.37), channel_id=1, source_target_pairs={{0,6},{1,7},{2,4},{3,5},{4,2},{5,3},{6,0},{7,1},{8,14},{9,15},{10,... | collective-permute-start | bytes 196616 | tf_op jit(solution)/shard_map/ppermute | solution.py:23
  139.3 2.2 %collective-permute-done.11 = f32[64,256]{1,0:T(8,128)S(1)} collective-permute-done((f32[64,256]{1,0:T(8,128)S(1)}, f32[64,256]{1,0:T(8,128)S(1)}, u32[]{:S(2)}, u32[]{:S(2)}) %collective-permute-start.11) | collective-permute-done | bytes 65568 | tf_op jit(solution)/shard_map/ppermute | solution.py:23
  141.5 10.6 %collective-permute-start.12 = (f32[64,256]{1,0:T(8,128)S(1)}, f32[64,256]{1,0:T(8,128)S(1)}, u32[]{:S(2)}, u32[]{:S(2)}) collective-permute-start(f32[64,256]{1,0:T(8,128)S(1)} %add.38), channel_id=1, source_target_pairs={{0,8},{1,9},{2,10},{3,11},{4,12},{5,13},{6,14},{7,15},{8,0},{9,1},... | collective-permute-start | bytes 196616 | tf_op jit(solution)/shard_map/ppermute | solution.py:23
  152.1 0.7 slice_bitcast_fusion
  152.8 3.9 %collective-permute-done.12 = f32[64,256]{1,0:T(8,128)S(1)} collective-permute-done((f32[64,256]{1,0:T(8,128)S(1)}, f32[64,256]{1,0:T(8,128)S(1)}, u32[]{:S(2)}, u32[]{:S(2)}) %collective-permute-start.12) | collective-permute-done | bytes 65568 | tf_op jit(solution)/shard_map/ppermute | solution.py:23
  156.7 0.6 add.39.packed_ref
  157.4 8.5 %shard_map.50 = (f32[2,64]{1,0:T(2,128)}, f32[1,2]{1,0:T(1,128)}) custom-call(s32[1]{0:T(128)} %bitcast.1.first_ref, f32[64,256]{1,0:T(8,128)} %add.39.packed_ref), custom_call_target="tpu_custom_call" | custom-call | flops 1572864 | bytes 65536 | tf_op jit(solution)/shard_map/pallas_call | solution.py:145
  (30 shorter events, 2.0 us)
Async XLA Ops:
  0.6 31.9 %collective-permute-start = (f32[2,10,32,128]{3,2,1,0:T(8,128)}, f32[2,10,32,128]{3,2,1,0:T(8,128)S(1)}, u32[]{:S(2)}, u32[]{:S(2)}) collective-permute-start(f32[2,10,32,128]{3,2,1,0:T(8,128)} %own_ref.1), channel_id=1, source_target_pairs={{0,1},{1,2},{2,3},{3,4},{4,5},{5,6},{6,7},{7,8},{8,9},{9,10},{10,1... | collective-permute-start | bytes 983048 | tf_op jit(solution)/shard_map/ppermute | solution.py:172
  2.6 30.0 %collective-permute-start.1 = (f32[2,10,32,128]{3,2,1,0:T(8,128)}, f32[2,10,32,128]{3,2,1,0:T(8,128)S(1)}, u32[]{:S(2)}, u32[]{:S(2)}) collective-permute-start(f32[2,10,32,128]{3,2,1,0:T(8,128)} %own_ref.1), channel_id=1, source_target_pairs={{1,0},{2,1},{3,2},{4,3},{5,4},{6,5},{7,6},{8,7},{9,8},{10,9},{11,1... | collective-permute-start | bytes 983048 | tf_op jit(solution)/shard_map/ppermute | solution.py:173
  6.2 15.7 %collective-permute-start.2 = (f32[10,32,128]{2,1,0:T(8,128)}, f32[10,32,128]{2,1,0:T(8,128)S(1)}, u32[]{:S(2)}, u32[]{:S(2)}) collective-permute-start(f32[10,32,128]{2,1,0:T(8,128)} %own_pot.1), channel_id=1, source_target_pairs={{79,0},{95,16},{111,32},{127,48},{15,64},{31,80},{47,96},{63,112},... | collective-permute-start | bytes 491528 | tf_op jit(solution)/shard_map/ppermute | solution.py:174
  20.0 12.6 %collective-permute-start.3 = (f32[10,32,128]{2,1,0:T(8,128)}, f32[10,32,128]{2,1,0:T(8,128)S(1)}, u32[]{:S(2)}, u32[]{:S(2)}) collective-permute-start(f32[10,32,128]{2,1,0:T(8,128)} %own_pot.1), channel_id=1, source_target_pairs={{1,0},{17,16},{33,32},{49,48},{65,64},{81,80},{97,96},{113,112},{1... | collective-permute-start | bytes 491528 | tf_op jit(solution)/shard_map/ppermute | solution.py:175
  21.9 10.6 %copy-start.3 = (f32[10,32,128]{2,1,0:T(8,128)}, f32[10,32,128]{2,1,0:T(8,128)S(1)}, u32[]{:S(2)}) copy-start(f32[10,32,128]{2,1,0:T(8,128)S(1)} %collective-permute-done.2.below_pot) | copy-start | bytes 491524
  32.5 0.7 copy-start.4
  32.6 0.8 copy-start.1
  33.3 0.7 copy-start.2
  76.0 6.4 %collective-permute-start.4 = (f32[64,256]{1,0:T(8,128)S(1)}, f32[64,256]{1,0:T(8,128)S(1)}, u32[]{:S(2)}, u32[]{:S(2)}) collective-permute-start(f32[64,256]{1,0:T(8,128)S(1)} %concatenate.3), channel_id=1, source_target_pairs={{0,16},{16,0},{32,48},{48,32},{64,80},{80,64},{96,112},{112,96},{1... | collective-permute-start | bytes 196616 | tf_op jit(solution)/shard_map/ppermute | solution.py:23
  82.4 69.7 %copy-start = (f32[2,2,10,32,128]{4,3,2,1,0:T(8,128)S(1)}, f32[2,2,10,32,128]{4,3,2,1,0:T(8,128)}, u32[]{:S(2)}) copy-start(f32[2,2,10,32,128]{4,3,2,1,0:T(8,128)} %shard_map.49) | copy-start | bytes 1966084
  82.4 7.2 %collective-permute-start.5 = (f32[64,256]{1,0:T(8,128)S(1)}, f32[64,256]{1,0:T(8,128)S(1)}, u32[]{:S(2)}, u32[]{:S(2)}) collective-permute-start(f32[64,256]{1,0:T(8,128)S(1)} %add.31), channel_id=1, source_target_pairs={{0,32},{16,48},{32,0},{48,16},{64,96},{80,112},{96,64},{112,80},{1... | collective-permute-start | bytes 196616 | tf_op jit(solution)/shard_map/ppermute | solution.py:23
  89.6 11.1 %collective-permute-start.6 = (f32[64,256]{1,0:T(8,128)S(1)}, f32[64,256]{1,0:T(8,128)S(1)}, u32[]{:S(2)}, u32[]{:S(2)}) collective-permute-start(f32[64,256]{1,0:T(8,128)S(1)} %add.32), channel_id=1, source_target_pairs={{0,64},{16,80},{32,96},{48,112},{64,0},{80,16},{96,32},{112,48},{1... | collective-permute-start | bytes 196616 | tf_op jit(solution)/shard_map/ppermute | solution.py:23
  100.7 6.2 %collective-permute-start.7 = (f32[64,256]{1,0:T(8,128)S(1)}, f32[64,256]{1,0:T(8,128)S(1)}, u32[]{:S(2)}, u32[]{:S(2)}) collective-permute-start(f32[64,256]{1,0:T(8,128)S(1)} %add.33), channel_id=1, source_target_pairs={{0,128},{16,144},{32,160},{48,176},{64,192},{80,208},{96,224},{112... | collective-permute-start | bytes 196616 | tf_op jit(solution)/shard_map/ppermute | solution.py:23
  106.9 7.4 %collective-permute-start.8 = (f32[64,256]{1,0:T(8,128)S(1)}, f32[64,256]{1,0:T(8,128)S(1)}, u32[]{:S(2)}, u32[]{:S(2)}) collective-permute-start(f32[64,256]{1,0:T(8,128)S(1)} %add.34), channel_id=1, source_target_pairs={{0,384},{16,400},{32,416},{48,432},{64,448},{80,464},{96,480},{112... | collective-permute-start | bytes 196616 | tf_op jit(solution)/shard_map/ppermute | solution.py:23
  114.3 13.6 %collective-permute-start.9 = (f32[64,256]{1,0:T(8,128)S(1)}, f32[64,256]{1,0:T(8,128)S(1)}, u32[]{:S(2)}, u32[]{:S(2)}) collective-permute-start(f32[64,256]{1,0:T(8,128)S(1)} %add.35), channel_id=1, source_target_pairs={{0,1},{1,0},{2,3},{3,2},{4,5},{5,4},{6,7},{7,6},{8,9},{9,8},{10,11... | collective-permute-start | bytes 196616 | tf_op jit(solution)/shard_map/ppermute | solution.py:23
  127.9 6.2 %collective-permute-start.10 = (f32[64,256]{1,0:T(8,128)S(1)}, f32[64,256]{1,0:T(8,128)S(1)}, u32[]{:S(2)}, u32[]{:S(2)}) collective-permute-start(f32[64,256]{1,0:T(8,128)S(1)} %add.36), channel_id=1, source_target_pairs={{0,2},{1,3},{2,0},{3,1},{4,6},{5,7},{6,4},{7,5},{8,10},{9,11},{10,... | collective-permute-start | bytes 196616 | tf_op jit(solution)/shard_map/ppermute | solution.py:23
  134.1 7.4 %collective-permute-start.11 = (f32[64,256]{1,0:T(8,128)S(1)}, f32[64,256]{1,0:T(8,128)S(1)}, u32[]{:S(2)}, u32[]{:S(2)}) collective-permute-start(f32[64,256]{1,0:T(8,128)S(1)} %add.37), channel_id=1, source_target_pairs={{0,6},{1,7},{2,4},{3,5},{4,2},{5,3},{6,0},{7,1},{8,14},{9,15},{10,... | collective-permute-start | bytes 196616 | tf_op jit(solution)/shard_map/ppermute | solution.py:23
  141.5 15.2 %collective-permute-start.12 = (f32[64,256]{1,0:T(8,128)S(1)}, f32[64,256]{1,0:T(8,128)S(1)}, u32[]{:S(2)}, u32[]{:S(2)}) collective-permute-start(f32[64,256]{1,0:T(8,128)S(1)} %add.38), channel_id=1, source_target_pairs={{0,8},{1,9},{2,10},{3,11},{4,12},{5,13},{6,14},{7,15},{8,0},{9,1},... | collective-permute-start | bytes 196616 | tf_op jit(solution)/shard_map/ppermute | solution.py:23

commit v19 on v17

--- a/solution.py
+++ b/solution.py
@@ -192,7 +192,7 @@
     norm_part = jnp.sum(image_here * image_here, axis=1)
     packed = jnp.concatenate([margin_part.reshape(-1), image_part.reshape(-1), norm_part])
     packed = butterfly_sum(packed, "band", [flip(1), flip(2), flip(4), flip(8), ring_of_four(0, 8)])
-    packed = butterfly_sum(packed, "grid", [flip(1), flip(2), ring_of_four(0, 2), flip(8)])
+    packed = butterfly_sum(packed, "grid", [flip(2), ring_of_four(0, 2), flip(1), flip(8)])
     packed = packed * inverse_cells
     square = total_bands * total_bands
     margin = packed[:square].reshape(total_bands, total_bands)

time: 164 us -> 166 us (1.012)
  the two profiles are of different devices: /device:TPU:24 before, /device:TPU:1 now
where the time goes in v19:
time: 166 us; the launch traced here: 165 us
  starting transfers between devices  84.1 us (51%)
  blocking collectives  32.5 us (20%)
  waiting for transfers between devices  25.7 us (15%)
  Pallas kernels  14.2 us (9%)
  local copies, waits for them, and re-layouts  6.21 us (4%)
    ppermute x9, starting transfers between devices, butterfly_sum(): values = values + lax.ppermute(values, axis, pairs)  57.1 us
    all_to_all x1, blocking collectives, on_device(): moved = lax.all_to_all(both, 'band', 2, 1, tiled=True)  32.5 us
    ppermute x9, waiting for transfers between devices, butterfly_sum(): values = values + lax.ppermute(values, axis, pairs)  24.5 us
    ppermute x1, starting transfers between devices, on_device(): lax.ppermute(potential[:width], ('band', 'grid'), replica_pairs(-1))  14.5 us
    pallas_call x1, Pallas kernels, rayleigh_ritz(): pl.pallas_call(rayleigh_ritz_kernel, out_shape=(jax.ShapeDtypeStruct((ban...  8.36 us
    ppermute x1, starting transfers between devices, on_device(): lax.ppermute(trial_bands[:, :width], 'grid', [((i + 1) % count, i) for i...  6.11 us
    pallas_call x1, Pallas kernels, filter_and_image(): pl.pallas_call(filter_kernel, out_shape=jax.ShapeDtypeStruct((2, *shape),...  5.88 us
    ppermute x1, starting transfers between devices, on_device(): lax.ppermute(trial_bands[:, trial_bands.shape[1] - width:], 'grid', [(i,...  4.59 us
  transfers between devices with their start and end apart: 13, of which 10 were waited for; matrix products, arithmetic and copies ran while one was open for 0% of the time, Pallas kernels for 0%

profile of v19, /device:TPU:1, one launch (start us, length us, event | category | flops | bytes accessed | tf_op | source)
XLA Modules:
  0.0 165.5 jit_solution(5158491623593290459)
XLA Ops:
  0.6 4.6 %collective-permute-start = (f32[2,10,32,128]{3,2,1,0:T(8,128)}, f32[2,10,32,128]{3,2,1,0:T(8,128)S(1)}, u32[]{:S(2)}, u32[]{:S(2)}) collective-permute-start(f32[2,10,32,128]{3,2,1,0:T(8,128)} %own_ref.1), channel_id=1, source_target_pairs={{0,1},{1,2},{2,3},{3,4},{4,5},{5,6},{6,7},{7,8},{8,9},{9,10},{10,1... | collective-permute-start | bytes 983048 | tf_op jit(solution)/shard_map/ppermute | solution.py:170
  5.2 6.1 %collective-permute-start.1 = (f32[2,10,32,128]{3,2,1,0:T(8,128)}, f32[2,10,32,128]{3,2,1,0:T(8,128)S(1)}, u32[]{:S(2)}, u32[]{:S(2)}) collective-permute-start(f32[2,10,32,128]{3,2,1,0:T(8,128)} %own_ref.1), channel_id=1, source_target_pairs={{1,0},{2,1},{3,2},{4,3},{5,4},{6,5},{7,6},{8,7},{9,8},{10,9},{11,1... | collective-permute-start | bytes 983048 | tf_op jit(solution)/shard_map/ppermute | solution.py:171
  11.4 1.9 %collective-permute-start.2 = (f32[10,32,128]{2,1,0:T(8,128)}, f32[10,32,128]{2,1,0:T(8,128)S(1)}, u32[]{:S(2)}, u32[]{:S(2)}) collective-permute-start(f32[10,32,128]{2,1,0:T(8,128)} %own_pot.1), channel_id=1, source_target_pairs={{79,0},{95,16},{111,32},{127,48},{15,64},{31,80},{47,96},{63,112},... | collective-permute-start | bytes 491528 | tf_op jit(solution)/shard_map/ppermute | solution.py:172
  13.3 14.5 %collective-permute-start.3 = (f32[10,32,128]{2,1,0:T(8,128)}, f32[10,32,128]{2,1,0:T(8,128)S(1)}, u32[]{:S(2)}, u32[]{:S(2)}) collective-permute-start(f32[10,32,128]{2,1,0:T(8,128)} %own_pot.1), channel_id=1, source_target_pairs={{1,0},{17,16},{33,32},{49,48},{65,64},{81,80},{97,96},{113,112},{1... | collective-permute-start | bytes 491528 | tf_op jit(solution)/shard_map/ppermute | solution.py:173
  27.8 1.2 collective-permute-done.3.above_pot
  29.0 0.6 copy-done.4
  29.7 0.7 copy-done.2
  30.5 5.9 %shard_map.49 = f32[2,2,10,32,128]{4,3,2,1,0:T(8,128)} custom-call(f32[2,10,32,128]{3,2,1,0:T(8,128)} %copy-done.1, f32[2,10,32,128]{3,2,1,0:T(8,128)} %own_ref.1, f32[2,10,32,128]{3,2,1,0:T(8,128)} %copy-done.2, f32[10,32,128]{2,1,0:T(8,128)} %copy-done.3, f32[10,32,128]{2,1,0:T(8,128)} %own_pot.1, f32[10,32,128]{2,1,0:T(8,128)} %copy-done.4), custom_call_target="tpu_custom_call" | custom-call | flops 29491200 | bytes 2949120 | tf_op jit(solution)/shard_map/pallas_call | solution.py:93
  36.4 1.2 reshape.48
  38.1 32.5 %all_to_all.15 = f32[2,2,32,1280]{3,1,0,2:T(2,128)S(1)} all-to-all(f32[2,2,32,1280]{3,1,0,2:T(2,128)S(1)} %copy.10), channel_id=1, replica_groups=mesh['band'=32,'grid'=16] {'band'}, dimensions={2} | all-to-all | bytes 1310720 | tf_op jit(solution)/shard_map/all_to_all | solution.py:183
  72.4 2.0 %collective-permute-start.4 = (f32[8256]{0:T(1024)S(1)}, f32[8256]{0:T(1024)S(1)}, u32[]{:S(2)}, u32[]{:S(2)}) collective-permute-start(f32[8256]{0:T(1024)S(1)} %constant_dynamic-update-slice_fusion), channel_id=1, source_target_pairs={{0,16},{16,0},{32,48},{48,32},{64,80},{80,64},{96,112},{112,96},{1... | collective-permute-start | bytes 99080 | tf_op jit(solution)/shard_map/ppermute | solution.py:21
  74.5 3.1 %collective-permute-done.4 = f32[8256]{0:T(1024)S(1)} collective-permute-done((f32[8256]{0:T(1024)S(1)}, f32[8256]{0:T(1024)S(1)}, u32[]{:S(2)}, u32[]{:S(2)}) %collective-permute-start.4) | collective-permute-done | bytes 33056 | tf_op jit(solution)/shard_map/ppermute | solution.py:21
  77.6 2.3 %collective-permute-start.5 = (f32[8256]{0:T(1024)S(1)}, f32[8256]{0:T(1024)S(1)}, u32[]{:S(2)}, u32[]{:S(2)}) collective-permute-start(f32[8256]{0:T(1024)S(1)} %add.30), channel_id=1, source_target_pairs={{0,32},{16,48},{32,0},{48,16},{64,96},{80,112},{96,64},{112,80},{1... | collective-permute-start | bytes 99080 | tf_op jit(solution)/shard_map/ppermute | solution.py:21
  79.9 4.9 %collective-permute-done.5 = f32[8256]{0:T(1024)S(1)} collective-permute-done((f32[8256]{0:T(1024)S(1)}, f32[8256]{0:T(1024)S(1)}, u32[]{:S(2)}, u32[]{:S(2)}) %collective-permute-start.5) | collective-permute-done | bytes 33056 | tf_op jit(solution)/shard_map/ppermute | solution.py:21
  84.8 5.2 %collective-permute-start.6 = (f32[8256]{0:T(1024)S(1)}, f32[8256]{0:T(1024)S(1)}, u32[]{:S(2)}, u32[]{:S(2)}) collective-permute-start(f32[8256]{0:T(1024)S(1)} %add.31), channel_id=1, source_target_pairs={{0,64},{16,80},{32,96},{48,112},{64,0},{80,16},{96,32},{112,48},{1... | collective-permute-start | bytes 99080 | tf_op jit(solution)/shard_map/ppermute | solution.py:21
  90.0 4.0 %collective-permute-done.6 = f32[8256]{0:T(1024)S(1)} collective-permute-done((f32[8256]{0:T(1024)S(1)}, f32[8256]{0:T(1024)S(1)}, u32[]{:S(2)}, u32[]{:S(2)}) %collective-permute-start.6) | collective-permute-done | bytes 33056 | tf_op jit(solution)/shard_map/ppermute | solution.py:21
  94.0 1.9 %collective-permute-start.7 = (f32[8256]{0:T(1024)S(1)}, f32[8256]{0:T(1024)S(1)}, u32[]{:S(2)}, u32[]{:S(2)}) collective-permute-start(f32[8256]{0:T(1024)S(1)} %add.32), channel_id=1, source_target_pairs={{0,128},{16,144},{32,160},{48,176},{64,192},{80,208},{96,224},{112... | collective-permute-start | bytes 99080 | tf_op jit(solution)/shard_map/ppermute | solution.py:21
  95.9 2.8 %collective-permute-done.7 = f32[8256]{0:T(1024)S(1)} collective-permute-done((f32[8256]{0:T(1024)S(1)}, f32[8256]{0:T(1024)S(1)}, u32[]{:S(2)}, u32[]{:S(2)}) %collective-permute-start.7) | collective-permute-done | bytes 33056 | tf_op jit(solution)/shard_map/ppermute | solution.py:21
  98.7 1.9 %collective-permute-start.8 = (f32[8256]{0:T(1024)S(1)}, f32[8256]{0:T(1024)S(1)}, u32[]{:S(2)}, u32[]{:S(2)}) collective-permute-start(f32[8256]{0:T(1024)S(1)} %add.33), channel_id=1, source_target_pairs={{0,384},{16,400},{32,416},{48,432},{64,448},{80,464},{96,480},{112... | collective-permute-start | bytes 99080 | tf_op jit(solution)/shard_map/ppermute | solution.py:21
  100.6 4.0 %collective-permute-done.8 = f32[8256]{0:T(1024)S(1)} collective-permute-done((f32[8256]{0:T(1024)S(1)}, f32[8256]{0:T(1024)S(1)}, u32[]{:S(2)}, u32[]{:S(2)}) %collective-permute-start.8) | collective-permute-done | bytes 33056 | tf_op jit(solution)/shard_map/ppermute | solution.py:21
  104.6 8.0 %collective-permute-start.9 = (f32[8256]{0:T(1024)S(1)}, f32[8256]{0:T(1024)S(1)}, u32[]{:S(2)}, u32[]{:S(2)}) collective-permute-start(f32[8256]{0:T(1024)S(1)} %add.34), channel_id=1, source_target_pairs={{0,2},{1,3},{2,0},{3,1},{4,6},{5,7},{6,4},{7,5},{8,10},{9,11},{10,... | collective-permute-start | bytes 99080 | tf_op jit(solution)/shard_map/ppermute | solution.py:21
  112.7 1.3 collective-permute-done.9
  114.0 18.6 %collective-permute-start.10 = (f32[8256]{0:T(1024)S(1)}, f32[8256]{0:T(1024)S(1)}, u32[]{:S(2)}, u32[]{:S(2)}) collective-permute-start(f32[8256]{0:T(1024)S(1)} %add.35), channel_id=1, source_target_pairs={{0,6},{1,7},{2,4},{3,5},{4,2},{5,3},{6,0},{7,1},{8,14},{9,15},{10,... | collective-permute-start | bytes 99080 | tf_op jit(solution)/shard_map/ppermute | solution.py:21
  132.6 1.3 collective-permute-done.10
  133.9 6.7 %collective-permute-start.11 = (f32[8256]{0:T(1024)S(1)}, f32[8256]{0:T(1024)S(1)}, u32[]{:S(2)}, u32[]{:S(2)}) collective-permute-start(f32[8256]{0:T(1024)S(1)} %add.36), channel_id=1, source_target_pairs={{0,1},{1,0},{2,3},{3,2},{4,5},{5,4},{6,7},{7,6},{8,9},{9,8},{10,11... | collective-permute-start | bytes 99080 | tf_op jit(solution)/shard_map/ppermute | solution.py:21
  140.6 0.8 collective-permute-done.11
  141.5 10.4 %collective-permute-start.12 = (f32[8256]{0:T(1024)S(1)}, f32[8256]{0:T(1024)S(1)}, u32[]{:S(2)}, u32[]{:S(2)}) collective-permute-start(f32[8256]{0:T(1024)S(1)} %add.37), channel_id=1, source_target_pairs={{0,8},{1,9},{2,10},{3,11},{4,12},{5,13},{6,14},{7,15},{8,0},{9,1},... | collective-permute-start | bytes 99080 | tf_op jit(solution)/shard_map/ppermute | solution.py:21
  151.9 0.7 slice_bitcast_fusion
  152.6 2.3 %collective-permute-done.12 = f32[8256]{0:T(1024)S(1)} collective-permute-done((f32[8256]{0:T(1024)S(1)}, f32[8256]{0:T(1024)S(1)}, u32[]{:S(2)}, u32[]{:S(2)}) %collective-permute-start.12) | collective-permute-done | bytes 33056 | tf_op jit(solution)/shard_map/ppermute | solution.py:21
  154.9 0.7 slice.46.subspace_ref
  155.6 0.7 copy.12.norms_ref
  157.1 8.4 %shard_map.50 = (f32[2,64]{1,0:T(2,128)}, f32[1,2]{1,0:T(1,128)}) custom-call(s32[1]{0:T(128)} %bitcast.1.first_ref, f32[64,64]{1,0:T(8,128)} %fusion.margin_ref, f32[64,64]{1,0:T(8,128)} %slice.46.subspace_ref, f32[64,1]{1,0:T(8,128)} %copy.12.norms_ref), custom_call_target="tpu_custom_call" | custom-call | flops 1572864 | bytes 65536 | tf_op jit(solution)/shard_map/pallas_call | solution.py:143
  (37 shorter events, 3.3 us)
Async XLA Ops:
  0.6 28.3 %collective-permute-start = (f32[2,10,32,128]{3,2,1,0:T(8,128)}, f32[2,10,32,128]{3,2,1,0:T(8,128)S(1)}, u32[]{:S(2)}, u32[]{:S(2)}) collective-permute-start(f32[2,10,32,128]{3,2,1,0:T(8,128)} %own_ref.1), channel_id=1, source_target_pairs={{0,1},{1,2},{2,3},{3,4},{4,5},{5,6},{6,7},{7,8},{8,9},{9,10},{10,1... | collective-permute-start | bytes 983048 | tf_op jit(solution)/shard_map/ppermute | solution.py:170
  5.2 23.7 %collective-permute-start.1 = (f32[2,10,32,128]{3,2,1,0:T(8,128)}, f32[2,10,32,128]{3,2,1,0:T(8,128)S(1)}, u32[]{:S(2)}, u32[]{:S(2)}) collective-permute-start(f32[2,10,32,128]{3,2,1,0:T(8,128)} %own_ref.1), channel_id=1, source_target_pairs={{1,0},{2,1},{3,2},{4,3},{5,4},{6,5},{7,6},{8,7},{9,8},{10,9},{11,1... | collective-permute-start | bytes 983048 | tf_op jit(solution)/shard_map/ppermute | solution.py:171
  11.4 16.4 %collective-permute-start.2 = (f32[10,32,128]{2,1,0:T(8,128)}, f32[10,32,128]{2,1,0:T(8,128)S(1)}, u32[]{:S(2)}, u32[]{:S(2)}) collective-permute-start(f32[10,32,128]{2,1,0:T(8,128)} %own_pot.1), channel_id=1, source_target_pairs={{79,0},{95,16},{111,32},{127,48},{15,64},{31,80},{47,96},{63,112},... | collective-permute-start | bytes 491528 | tf_op jit(solution)/shard_map/ppermute | solution.py:172
  13.3 15.7 %collective-permute-start.3 = (f32[10,32,128]{2,1,0:T(8,128)}, f32[10,32,128]{2,1,0:T(8,128)S(1)}, u32[]{:S(2)}, u32[]{:S(2)}) collective-permute-start(f32[10,32,128]{2,1,0:T(8,128)} %own_pot.1), channel_id=1, source_target_pairs={{1,0},{17,16},{33,32},{49,48},{65,64},{81,80},{97,96},{113,112},{1... | collective-permute-start | bytes 491528 | tf_op jit(solution)/shard_map/ppermute | solution.py:173
  27.8 1.2 copy-start.3
  29.0 0.7 copy-start.4
  29.0 0.8 copy-start.1
  29.7 0.7 copy-start.2
  72.4 79.5 %copy-start = (f32[2,2,10,32,128]{4,3,2,1,0:T(8,128)S(1)}, f32[2,2,10,32,128]{4,3,2,1,0:T(8,128)}, u32[]{:S(2)}) copy-start(f32[2,2,10,32,128]{4,3,2,1,0:T(8,128)} %shard_map.49) | copy-start | bytes 1966084
  72.4 5.1 %collective-permute-start.4 = (f32[8256]{0:T(1024)S(1)}, f32[8256]{0:T(1024)S(1)}, u32[]{:S(2)}, u32[]{:S(2)}) collective-permute-start(f32[8256]{0:T(1024)S(1)} %constant_dynamic-update-slice_fusion), channel_id=1, source_target_pairs={{0,16},{16,0},{32,48},{48,32},{64,80},{80,64},{96,112},{112,96},{1... | collective-permute-start | bytes 99080 | tf_op jit(solution)/shard_map/ppermute | solution.py:21
  77.6 7.2 %collective-permute-start.5 = (f32[8256]{0:T(1024)S(1)}, f32[8256]{0:T(1024)S(1)}, u32[]{:S(2)}, u32[]{:S(2)}) collective-permute-start(f32[8256]{0:T(1024)S(1)} %add.30), channel_id=1, source_target_pairs={{0,32},{16,48},{32,0},{48,16},{64,96},{80,112},{96,64},{112,80},{1... | collective-permute-start | bytes 99080 | tf_op jit(solution)/shard_map/ppermute | solution.py:21
  84.8 9.2 %collective-permute-start.6 = (f32[8256]{0:T(1024)S(1)}, f32[8256]{0:T(1024)S(1)}, u32[]{:S(2)}, u32[]{:S(2)}) collective-permute-start(f32[8256]{0:T(1024)S(1)} %add.31), channel_id=1, source_target_pairs={{0,64},{16,80},{32,96},{48,112},{64,0},{80,16},{96,32},{112,48},{1... | collective-permute-start | bytes 99080 | tf_op jit(solution)/shard_map/ppermute | solution.py:21
  94.0 4.7 %collective-permute-start.7 = (f32[8256]{0:T(1024)S(1)}, f32[8256]{0:T(1024)S(1)}, u32[]{:S(2)}, u32[]{:S(2)}) collective-permute-start(f32[8256]{0:T(1024)S(1)} %add.32), channel_id=1, source_target_pairs={{0,128},{16,144},{32,160},{48,176},{64,192},{80,208},{96,224},{112... | collective-permute-start | bytes 99080 | tf_op jit(solution)/shard_map/ppermute | solution.py:21
  98.7 5.9 %collective-permute-start.8 = (f32[8256]{0:T(1024)S(1)}, f32[8256]{0:T(1024)S(1)}, u32[]{:S(2)}, u32[]{:S(2)}) collective-permute-start(f32[8256]{0:T(1024)S(1)} %add.33), channel_id=1, source_target_pairs={{0,384},{16,400},{32,416},{48,432},{64,448},{80,464},{96,480},{112... | collective-permute-start | bytes 99080 | tf_op jit(solution)/shard_map/ppermute | solution.py:21
  104.6 9.4 %collective-permute-start.9 = (f32[8256]{0:T(1024)S(1)}, f32[8256]{0:T(1024)S(1)}, u32[]{:S(2)}, u32[]{:S(2)}) collective-permute-start(f32[8256]{0:T(1024)S(1)} %add.34), channel_id=1, source_target_pairs={{0,2},{1,3},{2,0},{3,1},{4,6},{5,7},{6,4},{7,5},{8,10},{9,11},{10,... | collective-permute-start | bytes 99080 | tf_op jit(solution)/shard_map/ppermute | solution.py:21
  114.0 19.9 %collective-permute-start.10 = (f32[8256]{0:T(1024)S(1)}, f32[8256]{0:T(1024)S(1)}, u32[]{:S(2)}, u32[]{:S(2)}) collective-permute-start(f32[8256]{0:T(1024)S(1)} %add.35), channel_id=1, source_target_pairs={{0,6},{1,7},{2,4},{3,5},{4,2},{5,3},{6,0},{7,1},{8,14},{9,15},{10,... | collective-permute-start | bytes 99080 | tf_op jit(solution)/shard_map/ppermute | solution.py:21
  133.9 7.6 %collective-permute-start.11 = (f32[8256]{0:T(1024)S(1)}, f32[8256]{0:T(1024)S(1)}, u32[]{:S(2)}, u32[]{:S(2)}) collective-permute-start(f32[8256]{0:T(1024)S(1)} %add.36), channel_id=1, source_target_pairs={{0,1},{1,0},{2,3},{3,2},{4,5},{5,4},{6,7},{7,6},{8,9},{9,8},{10,11... | collective-permute-start | bytes 99080 | tf_op jit(solution)/shard_map/ppermute | solution.py:21
  141.5 13.4 %collective-permute-start.12 = (f32[8256]{0:T(1024)S(1)}, f32[8256]{0:T(1024)S(1)}, u32[]{:S(2)}, u32[]{:S(2)}) collective-permute-start(f32[8256]{0:T(1024)S(1)} %add.37), channel_id=1, source_target_pairs={{0,8},{1,9},{2,10},{3,11},{4,12},{5,13},{6,14},{7,15},{8,0},{9,1},... | collective-permute-start | bytes 99080 | tf_op jit(solution)/shard_map/ppermute | solution.py:21
